TPU v7x, 32 devices: a whole 2x2x4 slice. The times are simulated.
32 devices in a mesh: seq: 8 (over y, x, core), tp: 4 (over z).
Axes of the slice: x: 2, y: 2, z: 4, core: 2. Of those that a mesh axis runs over, the one named last changes fastest.
Arguments:
- hidden: bfloat16 [1024, 8192], P('seq'), may hold values from -7 to 7
- norm_gain: bfloat16 [8192], replicated, may hold values from 0.099609375 to 1.8984375
- w_query: bfloat16 [8192, 1024], P('seq', 'tp'), may hold values from -1 to 1
- w_key: bfloat16 [8192, 128], P('seq'), may hold values from -64 to 64
- w_value: bfloat16 [8192, 128], P('seq'), may hold values from -0.0625 to 0.0625
- doc_lengths: int32 [8], replicated, may hold values from 1 to 640, 1024 in all
- critic_up: bfloat16 [8192, 4608], P('seq', 'tp'), may hold values from -0.0625 to 0.0625
- critic_down: bfloat16 [4, 4608, 8192], P(None, 'tp', 'seq'), may hold values from -0.09375 to 0.09375
- rule_ids: int32 [8], replicated, may hold values from 0 to 3
Outputs:
- attention: bfloat16 [1024, 1024], P('seq', 'tp')
- critic_values: bfloat16 [8, 8192], P(None, 'seq')
Inputs may be any that keep to these rules, and one draw needn't show every extreme that they name: `doc_lengths`: the 8 lengths sum to 1024; the longest is exactly 640.
All inputs are finite; a program needn't handle non-finite values.
Results may differ from a plain program's by a relative error of at most 0.03.
The roundings to bfloat16 on the way count: a program that leaves them out, or rounds other values in their place, can miss the bound.
Values may be sent and summed in bfloat16 or wider, within the bound.
No kernel may reach another device: no remote copies, remote signals or barrier semaphores. Data moves between devices by JAX's collectives and lax.ppermute only.
A program may use at most 64 MiB of HBM per device.

v0:
```python
import math

import jax
import jax.numpy as jnp
from jax import lax
from jax.sharding import PartitionSpec as P


HEAD = 128
GROUP = 8


def rms_norm(values, norm_gain):
    widened = values.astype(jnp.float32)
    mean_square = jnp.mean(widened * widened, axis=-1, keepdims=True)
    return (widened * lax.rsqrt(mean_square + 1e-05) * norm_gain.astype(jnp.float32)).astype(
        jnp.bfloat16
    )


def xor_perm(n, pick):
    return [(j, pick(j)) for j in range(n)]


def xor_all_reduce(x, axis, n):
    k = 1
    while k < n:
        x = x + lax.ppermute(x, axis, xor_perm(n, lambda j, k=k: j ^ k))
        k = k * 2
    return x


def xor_reduce_scatter(x, axis, n):
    i = lax.axis_index(axis)
    k = n // 2
    while k >= 1:
        half = x.shape[1] // 2
        bit = (i // k) % 2
        keep = lax.dynamic_slice_in_dim(x, bit * half, half, 1)
        send = lax.dynamic_slice_in_dim(x, (1 - bit) * half, half, 1)
        x = keep + lax.ppermute(send, axis, xor_perm(n, lambda j, k=k: j ^ k))
        k = k // 2
    return x


def xor_gather_stack(x, axis, n, size):
    i = lax.axis_index(axis)
    stack = x[None]
    k = 1
    while k < size:
        other = lax.ppermute(stack, axis, xor_perm(n, lambda j, k=k: j ^ k))
        low = (i // k) % 2 == 0
        stack = jnp.where(
            low,
            jnp.concatenate([stack, other], axis=0),
            jnp.concatenate([other, stack], axis=0),
        )
        k = k * 2
    return stack


def power_of_two(n):
    return n & (n - 1) == 0


def gather_pieces(blk, n):
    i = lax.axis_index("seq")
    rows = blk.shape[0]
    if n != 8:
        full = lax.all_gather(blk, "seq", axis=0, tiled=True)
        return [(full, jnp.int32(0), n * rows)]
    core = i % 2
    chip = i // 2
    sib = lax.ppermute(blk, "seq", xor_perm(8, lambda j: j ^ 1))
    pair = jnp.concatenate([blk, sib], axis=0)
    nb = lax.ppermute(pair, "seq", xor_perm(8, lambda j: j ^ 2 if j % 2 == 0 else j ^ 4))
    dg = lax.ppermute(nb[:rows], "seq", xor_perm(8, lambda j: j ^ 5 if j % 2 == 0 else j ^ 3))
    oth = lax.ppermute(jnp.concatenate([nb, dg], axis=0), "seq", xor_perm(8, lambda j: j ^ 1))
    nb_chip = chip ^ (1 + core)
    oth_chip = chip ^ (2 - core)
    diag = chip ^ 3
    return [
        (blk, i, rows),
        (sib, i ^ 1, rows),
        (nb[:rows], 2 * nb_chip + core, rows),
        (nb[rows:], 2 * nb_chip + 1 - core, rows),
        (dg, 2 * diag + 1 - core, rows),
        (oth[:rows], 2 * oth_chip + 1 - core, rows),
        (oth[rows : 2 * rows], 2 * oth_chip + core, rows),
        (oth[2 * rows :], 2 * diag + core, rows),
    ]


def project(normed, pieces):
    total = None
    for piece, source, rows in pieces:
        cols = lax.dynamic_slice_in_dim(normed, source * rows, rows, 1)
        term = jnp.dot(cols, piece, preferred_element_type=jnp.float32)
        total = term if total is None else total + term
    return total


def body(
    hidden, norm_gain, w_query, w_key, w_value, doc_lengths, critic_up, critic_down, rule_ids
):
    n_seq = lax.axis_size("seq")
    n_tp = lax.axis_size("tp")
    seq_i = lax.axis_index("seq")
    tp_i = lax.axis_index("tp")
    normed = rms_norm(hidden, norm_gain)
    tokens_here = hidden.shape[0]
    heads_here = w_query.shape[1] // HEAD
    sharers = GROUP // heads_here
    kv_width = HEAD // sharers
    kv_head = tp_i * heads_here // GROUP
    kv_part = tp_i % sharers
    kv_start = kv_head * HEAD + kv_part * kv_width
    key_cols = lax.dynamic_slice_in_dim(w_key, kv_start, kv_width, 1)
    value_cols = lax.dynamic_slice_in_dim(w_value, kv_start, kv_width, 1)
    kv_weights = jnp.concatenate([key_cols, value_cols], axis=1)

    doc_ends = jnp.cumsum(doc_lengths) - 1
    first_row = seq_i * tokens_here
    query_pos = first_row + jnp.arange(tokens_here, dtype=jnp.int32)
    picker = (doc_ends[:, None] == query_pos[None, :]).astype(jnp.bfloat16)
    end_terms = jnp.dot(picker, normed, preferred_element_type=jnp.float32).astype(jnp.bfloat16)
    if power_of_two(n_seq):
        end_rows = xor_reduce_scatter(end_terms, "seq", n_seq)
    else:
        end_rows = lax.psum_scatter(end_terms, "seq", scatter_dimension=1, tiled=True)
    up_own = jnp.dot(end_rows, critic_up, preferred_element_type=jnp.float32)
    if power_of_two(n_seq):
        up_sum = xor_all_reduce(up_own, "seq", n_seq)
    else:
        up_sum = lax.psum(up_own, "seq")
    critic_hidden = jax.nn.silu(up_sum).astype(jnp.bfloat16)
    per_rule = jnp.einsum(
        "dc,rce->dre", critic_hidden, critic_down, preferred_element_type=jnp.float32
    )
    rule_pick = rule_ids[:, None] == jnp.arange(critic_down.shape[0], dtype=jnp.int32)[None, :]
    chosen = jnp.sum(jnp.where(rule_pick[:, :, None], per_rule, 0.0), axis=1)
    if power_of_two(n_tp):
        critic_sum = xor_all_reduce(chosen, "tp", n_tp)
    else:
        critic_sum = lax.psum(chosen, "tp")
    critic_values = critic_sum.astype(jnp.bfloat16)

    kv_pieces = gather_pieces(kv_weights, n_seq)
    kv_own = project(normed, kv_pieces).astype(jnp.bfloat16)
    kv_stack = xor_gather_stack(kv_own, "tp", n_tp, sharers)
    kv_rows = jnp.concatenate(
        [kv_stack[m, :, :kv_width] for m in range(sharers)]
        + [kv_stack[m, :, kv_width:] for m in range(sharers)],
        axis=1,
    )
    kv_all = gather_pieces(kv_rows, n_seq)
    key_block = jnp.concatenate([piece[:, :HEAD] for piece, _, _ in kv_all], axis=0)
    value_block = jnp.concatenate([piece[:, HEAD:] for piece, _, _ in kv_all], axis=0)
    key_pos = jnp.concatenate(
        [
            source * tokens_here + jnp.arange(piece.shape[0], dtype=jnp.int32)
            for piece, source, _ in kv_all
        ]
    )

    q_pieces = gather_pieces(w_query, n_seq)
    queries = project(normed, q_pieces).astype(jnp.bfloat16).reshape(tokens_here, heads_here, HEAD)

    def segment_of(positions):
        return jnp.sum((positions[:, None] > doc_ends[None, :]).astype(jnp.int32), axis=1)

    query_seg = segment_of(query_pos)
    inverse_root = 1.0 / math.sqrt(HEAD)
    allowed = (query_seg[:, None] == segment_of(key_pos)[None, :]) & (
        key_pos[None, :] <= query_pos[:, None]
    )
    allowed = allowed[:, None, :]
    scores = (
        jnp.einsum("qhd,kd->qhk", queries, key_block, preferred_element_type=jnp.float32)
        * inverse_root
    )
    scores = jnp.where(allowed, scores, -1e30)
    maxima = jnp.max(scores, axis=2)
    expanded = jnp.where(allowed, jnp.exp(scores - maxima[:, :, None]), 0.0)
    totals = jnp.sum(expanded, axis=2)
    weighted = jnp.einsum(
        "qhk,kd->qhd",
        expanded.astype(jnp.bfloat16),
        value_block,
        preferred_element_type=jnp.float32,
    )
    attention = (
        (weighted / totals[:, :, None])
        .reshape(tokens_here, heads_here * HEAD)
        .astype(jnp.bfloat16)
    )
    return (attention, critic_values)


def solution(mesh):
    return jax.shard_map(
        body,
        mesh=mesh,
        in_specs=(
            P("seq", None),
            P(),
            P("seq", "tp"),
            P("seq", None),
            P("seq", None),
            P(),
            P("seq", "tp"),
            P(None, "tp", "seq"),
            P(),
        ),
        out_specs=(P("seq", "tp"), P(None, "seq")),
        check_vma=False,
    )
```

profile of v0, /device:TPU:0, one launch (start us, length us, event | category | flops | bytes accessed | tf_op | source)
XLA Modules:
  0.0 108.7 jit_solution(7238889622306429144)
XLA Ops:
  0.7 1.4 %constant_dynamic-slice_fusion.3 = (bf16[1024,32]{1,0:T(8,128)(2,1)S(1)}, bf16[1024,32]{1,0:T(8,128)(2,1)S(1)}) fusion(bf16[1024,128]{1,0:T(8,128)(2,1)} %param.13, s32[]{:T(128)S(6)} %select_n.149, bf16[1024,128]{1,0:T(8,128)(2,1)} %param.12), kind=kLoop, calls=%fused_computation.143 | loop fusion | bytes 262148 | tf_op jit(solution)/shard_map/dynamic_slice | solution.py:119
  2.3 0.7 pad_maximum_fusion.5
  3.0 0.5 collective-permute-start.4
  3.5 0.8 reduce-window.7
  4.3 0.5 add_bitcast_fusion
  4.8 2.1 %fusion.1 = f32[128]{0:T(128)S(1)} fusion(bf16[128,8192]{1,0:T(8,128)(2,1)} %param.9), kind=kLoop, calls=%fused_computation.4 | loop fusion | flops 3145600 | bytes 2097664 | tf_op jit(solution)/shard_map/reduce_sum | solution.py:15
  7.1 0.6 copy-done.12
  7.7 2.2 %fusion.3 = bf16[128,8192]{1,0:T(8,128)(2,1)S(1)} fusion(bf16[128,8192]{1,0:T(8,128)(2,1)} %param.9, f32[8192]{0:T(1024)S(1)} %convert_element_type.43, f32[128]{0:T(128)S(1)} %add_rsqrt_fusion), kind=kLoop, calls=%fused_computation.6 | loop fusion | flops 4194304 | bytes 4227584 | tf_op jit(solution)/shard_map/convert_element_type | solution.py:16
  9.9 1.3 %copy-done.1 = bf16[128,8192]{1,0:T(8,128)(2,1)} copy-done((bf16[128,8192]{1,0:T(8,128)(2,1)}, bf16[128,8192]{1,0:T(8,128)(2,1)S(1)}, u32[]{:S(2)}) %copy-start.1) | copy-done | bytes 2097176
  11.2 1.1 %convolution_convert_fusion = bf16[8,8192]{1,0:T(8,128)(2,1)} fusion(bf16[128,8192]{1,0:T(8,128)(2,1)S(1)} %fusion.3, s32[128]{0:T(128)S(1)} %get-tuple-element.27, s32[8]{0:T(128)S(1)} %copy-done.18), kind=kOutput, calls=%fused_computation.1 | convolution fusion | flops 16843776 | bytes 2228768 | tf_op jit(solution)/shard_map/dot_general | solution.py:126
  12.3 1.5 %constant_dynamic-slice_fusion.2 = bf16[8,4096]{1,0:T(8,128)(2,1)} fusion(bf16[8,8192]{1,0:T(8,128)(2,1)} %convolution_convert_fusion, s32[]{:T(128)S(6)} %select_n.157), kind=kLoop, calls=%fused_computation.142 | loop fusion | bytes 131076 | tf_op jit(solution)/shard_map/dynamic_slice | solution.py:40
  13.8 3.0 %collective-permute-start.14 = (bf16[8,4096]{1,0:T(8,128)(2,1)}, bf16[8,4096]{1,0:T(8,128)(2,1)}, u32[]{:S(2)}, u32[]{:S(2)}) collective-permute-start(bf16[8,4096]{1,0:T(8,128)(2,1)} %constant_dynamic-slice_fusion.2), channel_id=1, source_target_pairs={{0,16},{4,20},{8,24},{12,28},{16,0},{20,4},{24,8},{28,12},{1,17},{... | collective-permute-start | bytes 196616 | tf_op jit(solution)/shard_map/ppermute | solution.py:41
  16.8 1.8 %fusion.57 = f32[128,256]{1,0:T(8,128)} fusion(bf16[1024,256]{1,0:T(8,128)(2,1)S(1)} %copy-done.3, bf16[128,8192]{1,0:T(8,128)(2,1)} %copy-done.1, s32[]{:T(128)S(6)} %select_n.134), kind=kOutput, calls=%fused_computation.72 | convolution fusion | flops 67108864 | bytes 917508 | tf_op jit(solution)/shard_map/dot_general | solution.py:98
  18.6 0.7 collective-permute-done.14
  19.3 0.9 dynamic-slice_add_fusion
  20.2 0.6 copy-done.8
  20.9 0.6 constant_dynamic-slice_fusion.1
  21.5 2.0 %collective-permute-start.15 = (bf16[8,2048]{1,0:T(8,128)(2,1)}, bf16[8,2048]{1,0:T(8,128)(2,1)}, u32[]{:S(2)}, u32[]{:S(2)}) collective-permute-start(bf16[8,2048]{1,0:T(8,128)(2,1)} %constant_dynamic-slice_fusion.1), channel_id=1, source_target_pairs={{0,8},{4,12},{8,0},{12,4},{16,24},{20,28},{24,16},{28,20},{1,9},{5... | collective-permute-start | bytes 98312 | tf_op jit(solution)/shard_map/ppermute | solution.py:41
  23.4 0.7 convert_reduce_fusion
  24.1 1.6 %collective-permute-done.15 = bf16[8,2048]{1,0:T(8,128)(2,1)} collective-permute-done((bf16[8,2048]{1,0:T(8,128)(2,1)}, bf16[8,2048]{1,0:T(8,128)(2,1)}, u32[]{:S(2)}, u32[]{:S(2)}) %collective-permute-start.15) | collective-permute-done | bytes 32800 | tf_op jit(solution)/shard_map/ppermute | solution.py:41
  25.7 0.8 dynamic-slice_add_fusion.1
  26.5 0.6 copy-done.9
  27.1 0.6 constant_dynamic-slice_fusion
  27.7 1.3 %convert_reduce_fusion.1 = s32[128]{0:T(128)} fusion(s32[128]{0:T(128)} %copy-done.15, s32[8]{0:T(128)} %add_bitcast_fusion), kind=kLoop, calls=%fused_computation.130 | loop fusion | flops 2944 | bytes 1056 | tf_op jit(solution)/shard_map/reduce_sum | solution.py:170
  29.1 1.1 %fusion.72 = f32[8,1152]{1,0:T(8,128)S(1)} fusion(bf16[1024,1152]{1,0:T(8,128)(2,1)S(1)} %copy-done, bf16[8,1024]{1,0:T(8,128)(2,1)S(1)} %collective-permute-done.16, bf16[8,2048]{1,0:T(8,128)(2,1)} %copy-done.9, s32[]{:T(128)S(6)} %select_n.161), kind=kOutput, calls=%fused_computation.112 | convolution fusion | flops 18907136 | bytes 2428932 | tf_op jit(solution)/shard_map/dot_general | solution.py:131
  30.2 0.5 collective-permute-start.17
  30.7 0.8 compare_and_fusion
  31.6 2.0 %collective-permute-start.18 = (f32[8,1152]{1,0:T(8,128)S(1)}, f32[8,1152]{1,0:T(8,128)S(1)}, u32[]{:S(2)}, u32[]{:S(2)}) collective-permute-start(f32[8,1152]{1,0:T(8,128)S(1)} %add.333), channel_id=1, source_target_pairs={{0,8},{4,12},{8,0},{12,4},{16,24},{20,28},{24,16},{28,20},{1,9},{5... | collective-permute-start | bytes 110600 | tf_op jit(solution)/shard_map/ppermute | solution.py:28
  33.6 2.0 %collective-permute-done.18 = f32[8,1152]{1,0:T(8,128)S(1)} collective-permute-done((f32[8,1152]{1,0:T(8,128)S(1)}, f32[8,1152]{1,0:T(8,128)S(1)}, u32[]{:S(2)}, u32[]{:S(2)}) %collective-permute-start.18) | collective-permute-done | bytes 36896 | tf_op jit(solution)/shard_map/ppermute | solution.py:28
  35.6 2.0 %collective-permute-start.19 = (f32[8,1152]{1,0:T(8,128)S(1)}, f32[8,1152]{1,0:T(8,128)S(1)}, u32[]{:S(2)}, u32[]{:S(2)}) collective-permute-start(f32[8,1152]{1,0:T(8,128)S(1)} %add.334), channel_id=1, source_target_pairs={{0,16},{4,20},{8,24},{12,28},{16,0},{20,4},{24,8},{28,12},{1,17},{... | collective-permute-start | bytes 110600 | tf_op jit(solution)/shard_map/ppermute | solution.py:28
  37.6 1.6 %pad_maximum_fusion.3 = bf16[2048,64]{0,1:T(8,128)(2,1)} fusion(bf16[1024,64]{0,1:T(8,128)(2,1)} %collective-permute-done.4, bf16[1024,32]{0,1:T(8,128)(2,1)S(1)} %copy.27, bf16[1024,32]{0,1:T(8,128)(2,1)S(1)} %copy.26), kind=kLoop, calls=%fused_computation.47 | loop fusion | flops 786432 | bytes 524288 | tf_op jit(solution)/shard_map/concatenate | solution.py:75
  39.2 1.5 %collective-permute-start.5 = (bf16[2048,64]{0,1:T(8,128)(2,1)}, bf16[2048,64]{0,1:T(8,128)(2,1)}, u32[]{:S(2)}, u32[]{:S(2)}) collective-permute-start(bf16[2048,64]{0,1:T(8,128)(2,1)} %pad_maximum_fusion.3), channel_id=1, source_target_pairs={{0,8},{4,20},{8,0},{12,28},{16,24},{20,4},{24,16},{28,12},{1,9},{5... | collective-permute-start | bytes 786440 | tf_op jit(solution)/shard_map/ppermute | solution.py:76
  40.7 5.6 %fusion.15 = f32[8,1024]{1,0:T(8,128)} fusion(bf16[4,1152,1024]{2,1,0:T(8,128)(2,1)} %param.16, pred[8,4]{0,1:T(4,128)(4,1)S(1)} %iota_compare_fusion, f32[8,1152]{1,0:T(8,128)S(1)} %add.334, f32[8,1152]{1,0:T(8,128)S(1)} %collective-permute-done.19), kind=kOutput, calls=%fused_computation.24 | convolution fusion | flops 75610112 | bytes 9543712 | tf_op jit(solution)/shard_map/dc,rce->dre/dot_general | solution.py:137
  46.4 1.6 %collective-permute-start.20 = (f32[8,1024]{1,0:T(8,128)}, f32[8,1024]{1,0:T(8,128)}, u32[]{:S(2)}, u32[]{:S(2)}) collective-permute-start(f32[8,1024]{1,0:T(8,128)} %fusion.15), channel_id=1, source_target_pairs={{0,1},{1,0},{2,3},{3,2},{4,5},{5,4},{6,7},{7,6},{8,9},{9,8},{10,11... | collective-permute-start | bytes 98312 | tf_op jit(solution)/shard_map/ppermute | solution.py:28
  47.9 1.8 %fusion.55 = f32[128,64]{0,1:T(8,128)} fusion(bf16[128,8192]{1,0:T(8,128)(2,1)} %copy-done.1, s32[]{:T(128)S(6)} %select_n.134, bf16[1024,32]{0,1:T(8,128)(2,1)S(1)} %copy.27, bf16[1024,32]{0,1:T(8,128)(2,1)S(1)} %copy.26), kind=kOutput, calls=%fused_computation.70 | convolution fusion | flops 17039360 | bytes 425988 | tf_op jit(solution)/shard_map/dot_general | solution.py:98
  49.7 0.9 collective-permute-done.20
  50.6 0.8 add.337
  51.4 2.8 %collective-permute-start.21 = (f32[8,1024]{1,0:T(8,128)S(1)}, f32[8,1024]{1,0:T(8,128)S(1)}, u32[]{:S(2)}, u32[]{:S(2)}) collective-permute-start(f32[8,1024]{1,0:T(8,128)S(1)} %add.337), channel_id=1, source_target_pairs={{0,2},{1,3},{2,0},{3,1},{4,6},{5,7},{6,4},{7,5},{8,10},{9,11},{10,... | collective-permute-start | bytes 98312 | tf_op jit(solution)/shard_map/ppermute | solution.py:28
  54.1 1.2 %convolution_add_fusion.3 = f32[128,64]{0,1:T(8,128)S(1)} fusion(f32[128,64]{0,1:T(8,128)} %fusion.55, bf16[1024,64]{0,1:T(8,128)(2,1)} %collective-permute-done.4, bf16[128,8192]{1,0:T(8,128)(2,1)} %copy-done.1, s32[]{:T(128)S(6)} %select_n.135), kind=kOutput, calls=%fused_computation.32 | convolution fusion | flops 16785408 | bytes 458756 | tf_op jit(solution)/shard_map/dot_general | solution.py:98
  55.4 0.9 slice.144
  56.4 0.6 add_convert_fusion
  57.0 3.8 %collective-permute-done.6 = bf16[1024,64]{0,1:T(8,128)(2,1)S(1)} collective-permute-done((bf16[1024,64]{0,1:T(8,128)(2,1)S(1)}, bf16[1024,64]{0,1:T(8,128)(2,1)S(1)}, u32[]{:S(2)}, u32[]{:S(2)}) %collective-permute-start.6) | collective-permute-done | bytes 131104 | tf_op jit(solution)/shard_map/ppermute | solution.py:77
  60.8 1.0 pad_maximum_fusion.2
  61.8 1.2 %fusion.48 = f32[128,64]{0,1:T(8,128)S(1)} fusion(bf16[128,8192]{1,0:T(8,128)(2,1)} %copy-done.1, s32[]{:T(128)S(6)} %select_n.137, bf16[2048,64]{0,1:T(8,128)(2,1)} %collective-permute-done.5), kind=kOutput, calls=%fused_computation.63 | convolution fusion | flops 16777216 | bytes 425988 | tf_op jit(solution)/shard_map/dot_general | solution.py:98
  63.3 0.3 collective-permute-done.7
  64.2 1.1 %fusion.23 = bf16[1,128,64]{1,2,0:T(8,128)(2,1)S(1)} fusion(f32[128,64]{0,1:T(8,128)S(1)} %fusion.35, f32[128,64]{0,1:T(8,128)S(1)} %fusion.38, f32[128,64]{0,1:T(8,128)S(1)} %fusion.41, f32[128,64]{0,1:T(8,128)S(1)} %fusion.44, f32[128,64]{0,1:T(8,128)S(1)} %fusion.48, f32[128,64]{0,1:T(8,128)S(1)} %convolution_add_fusion.3, ...), kind=kOutput, calls=%fused_computation.34 | convolution fusion | flops 16834560 | bytes 606212 | tf_op jit(solution)/shard_map/dot_general | solution.py:98
  65.3 1.5 %collective-permute-start.8 = (bf16[1,128,64]{1,2,0:T(8,128)(2,1)S(1)}, bf16[1,128,64]{1,2,0:T(8,128)(2,1)S(1)}, u32[]{:S(2)}, u32[]{:S(2)}) collective-permute-start(bf16[1,128,64]{1,2,0:T(8,128)(2,1)S(1)} %fusion.23), channel_id=1, source_target_pairs={{0,1},{1,0},{2,3},{3,2},{4,5},{5,4},{6,7},{7,6},{8,9},{9,8},{10,11... | collective-permute-start | bytes 49160 | tf_op jit(solution)/shard_map/ppermute | solution.py:51
  66.9 0.9 collective-permute-start.1
  67.7 1.4 %collective-permute-done.8 = bf16[1,128,64]{1,2,0:T(8,128)(2,1)S(1)} collective-permute-done((bf16[1,128,64]{1,2,0:T(8,128)(2,1)S(1)}, bf16[1,128,64]{1,2,0:T(8,128)(2,1)S(1)}, u32[]{:S(2)}, u32[]{:S(2)}) %collective-permute-start.8) | collective-permute-done | bytes 16416 | tf_op jit(solution)/shard_map/ppermute | solution.py:51
  69.6 4.4 %collective-permute-done.9 = bf16[2,128,64]{1,2,0:T(8,128)(2,1)S(1)} collective-permute-done((bf16[2,128,64]{1,2,0:T(8,128)(2,1)S(1)}, bf16[2,128,64]{1,2,0:T(8,128)(2,1)S(1)}, u32[]{:S(2)}, u32[]{:S(2)}) %collective-permute-start.9) | collective-permute-done | bytes 32800 | tf_op jit(solution)/shard_map/ppermute | solution.py:51
  74.1 7.6 %collective-permute-done.1 = bf16[2048,256]{1,0:T(8,128)(2,1)S(1)} collective-permute-done((bf16[2048,256]{1,0:T(8,128)(2,1)S(1)}, bf16[2048,256]{1,0:T(8,128)(2,1)S(1)}, u32[]{:S(2)}, u32[]{:S(2)}) %collective-permute-start.1) | collective-permute-done | bytes 1048608 | tf_op jit(solution)/shard_map/ppermute | solution.py:76
  81.8 0.9 collective-permute-start.10
  82.8 7.6 %collective-permute-done.2 = bf16[1024,256]{1,0:T(8,128)(2,1)S(1)} collective-permute-done((bf16[1024,256]{1,0:T(8,128)(2,1)S(1)}, bf16[1024,256]{1,0:T(8,128)(2,1)S(1)}, u32[]{:S(2)}, u32[]{:S(2)}) %collective-permute-start.2) | collective-permute-done | bytes 524320 | tf_op jit(solution)/shard_map/ppermute | solution.py:77
  90.6 1.0 collective-permute-start.11
  91.6 4.0 %collective-permute-done.11 = bf16[256,256]{0,1:T(8,128)(2,1)S(1)} collective-permute-done((bf16[256,256]{0,1:T(8,128)(2,1)S(1)}, bf16[256,256]{0,1:T(8,128)(2,1)S(1)}, u32[]{:S(2)}, u32[]{:S(2)}) %collective-permute-start.11) | collective-permute-done | bytes 131104 | tf_op jit(solution)/shard_map/ppermute | solution.py:76
  95.9 3.4 %collective-permute-done.12 = bf16[128,256]{0,1:T(8,128)(2,1)S(1)} collective-permute-done((bf16[128,256]{0,1:T(8,128)(2,1)S(1)}, bf16[128,256]{0,1:T(8,128)(2,1)S(1)}, u32[]{:S(2)}, u32[]{:S(2)}) %collective-permute-start.12) | collective-permute-done | bytes 65568 | tf_op jit(solution)/shard_map/ppermute | solution.py:77
  99.5 1.4 %collective-permute-done.13 = bf16[384,256]{0,1:T(8,128)(2,1)S(1)} collective-permute-done((bf16[384,256]{0,1:T(8,128)(2,1)S(1)}, bf16[384,256]{0,1:T(8,128)(2,1)S(1)}, u32[]{:S(2)}, u32[]{:S(2)}) %collective-permute-start.13) | collective-permute-done | bytes 196640 | tf_op jit(solution)/shard_map/ppermute | solution.py:78
  101.5 0.2 fusion.24
  102.2 0.3 fusion.16
  102.5 0.6 copy-done.7
  103.1 0.7 fusion.102
  103.8 1.3 %fusion.7 = f32[128,2,1024]{2,0,1:T(8,128)S(1)} fusion(pred[128,1024]{1,0:T(8,128)(4,1)S(1)} %copy-done.4, bf16[1024,128]{0,1:T(8,128)(2,1)} %copy-done.6, bf16[16,2,8,128]{3,2,1,0:T(8,128)(2,1)} %copy-done.7), kind=kOutput, calls=%fused_computation.12 | convolution fusion | flops 67633152 | bytes 1507328 | tf_op jit(solution)/shard_map/qhd,kd->qhk/dot_general | solution.py:179
  105.1 2.0 %fusion.14 = bf16[128,2,128]{0,2,1:T(8,128)(2,1)} fusion(bf16[1024,128]{0,1:T(8,128)(2,1)} %copy-done.17, f32[128,2,1024]{2,0,1:T(8,128)S(1)} %fusion.7, pred[128,1024]{1,0:T(8,128)(4,1)S(1)} %copy-done.4, f32[128,2]{0,1:T(2,128)S(1)} %fusion.102), kind=kOutput, calls=%fused_computation.23 | convolution fusion | flops 67962112 | bytes 1508352 | tf_op jit(solution)/shard_map/qhk,kd->qhd/dot_general | solution.py:186
  107.1 1.6 %copy.23 = bf16[128,256]{1,0:T(8,128)(2,1)} copy(bf16[128,256]{0,1:T(8,128)(2,1)} %bitcast.70) | data formatting | bytes 131072
  (103 shorter events, 3.8 us)
Async XLA Ops:
  0.6 28.5 %copy-start = (bf16[1024,1152]{1,0:T(8,128)(2,1)S(1)}, bf16[1024,1152]{1,0:T(8,128)(2,1)}, u32[]{:S(2)}) copy-start(bf16[1024,1152]{1,0:T(8,128)(2,1)} %param.15) | copy-start | bytes 7077892
  0.7 6.3 %copy-start.10 = (bf16[8192]{0:T(1024)(128)(2,1)S(1)}, bf16[8192]{0:T(1024)(128)(2,1)}, u32[]{:S(2)}) copy-start(bf16[8192]{0:T(1024)(128)(2,1)} %param.10) | copy-start | bytes 49156
  3.0 34.6 %collective-permute-start.4 = (bf16[1024,64]{0,1:T(8,128)(2,1)}, bf16[1024,64]{0,1:T(8,128)(2,1)}, u32[]{:S(2)}, u32[]{:S(2)}) collective-permute-start(bf16[1024,64]{0,1:T(8,128)(2,1)} %pad_maximum_fusion.5), channel_id=1, source_target_pairs={{0,4},{4,0},{8,12},{12,8},{16,20},{20,16},{24,28},{28,24},{1,5},{5... | collective-permute-start | bytes 393224 | tf_op jit(solution)/shard_map/ppermute | solution.py:74
  3.5 63.3 %collective-permute-start = (bf16[1024,256]{1,0:T(8,128)(2,1)}, bf16[1024,256]{1,0:T(8,128)(2,1)S(1)}, u32[]{:S(2)}, u32[]{:S(2)}) collective-permute-start(bf16[1024,256]{1,0:T(8,128)(2,1)} %param.11), channel_id=1, source_target_pairs={{0,4},{4,0},{8,12},{12,8},{16,20},{20,16},{24,28},{28,24},{1,5},{5... | collective-permute-start | bytes 1572872 | tf_op jit(solution)/shard_map/ppermute | solution.py:74
  7.1 0.6 copy-start.12
  7.7 2.2 %copy-start.15 = (s32[128]{0:T(128)}, s32[128]{0:T(128)S(1)}, u32[]{:S(2)}) copy-start(s32[128]{0:T(128)S(1)} %get-tuple-element.27) | copy-start | bytes 1540
  7.7 3.5 %copy-start.18 = (s32[8]{0:T(128)S(1)}, s32[8]{0:T(128)}, u32[]{:S(2)}) copy-start(s32[8]{0:T(128)} %add_bitcast_fusion) | copy-start | bytes 100
  9.9 1.3 %copy-start.1 = (bf16[128,8192]{1,0:T(8,128)(2,1)}, bf16[128,8192]{1,0:T(8,128)(2,1)S(1)}, u32[]{:S(2)}) copy-start(bf16[128,8192]{1,0:T(8,128)(2,1)S(1)} %fusion.3) | copy-start | bytes 6291460
  9.9 6.9 %copy-start.3 = (bf16[1024,256]{1,0:T(8,128)(2,1)S(1)}, bf16[1024,256]{1,0:T(8,128)(2,1)}, u32[]{:S(2)}) copy-start(bf16[1024,256]{1,0:T(8,128)(2,1)} %param.11) | copy-start | bytes 1572868
  9.9 13.6 %copy-start.13 = (s32[1024]{0:T(1024)S(1)}, s32[1024]{0:T(1024)}, u32[]{:S(2)}) copy-start(s32[1024]{0:T(1024)} %copy-done.12) | copy-start | bytes 12292
  13.8 5.6 %collective-permute-start.14 = (bf16[8,4096]{1,0:T(8,128)(2,1)}, bf16[8,4096]{1,0:T(8,128)(2,1)}, u32[]{:S(2)}, u32[]{:S(2)}) collective-permute-start(bf16[8,4096]{1,0:T(8,128)(2,1)} %constant_dynamic-slice_fusion.2), channel_id=1, source_target_pairs={{0,16},{4,20},{8,24},{12,28},{16,0},{20,4},{24,8},{28,12},{1,17},{... | collective-permute-start | bytes 196616 | tf_op jit(solution)/shard_map/ppermute | solution.py:41
  20.2 0.6 copy-start.8
  21.5 4.2 %collective-permute-start.15 = (bf16[8,2048]{1,0:T(8,128)(2,1)}, bf16[8,2048]{1,0:T(8,128)(2,1)}, u32[]{:S(2)}, u32[]{:S(2)}) collective-permute-start(bf16[8,2048]{1,0:T(8,128)(2,1)} %constant_dynamic-slice_fusion.1), channel_id=1, source_target_pairs={{0,8},{4,12},{8,0},{12,4},{16,24},{20,28},{24,16},{28,20},{1,9},{5... | collective-permute-start | bytes 98312 | tf_op jit(solution)/shard_map/ppermute | solution.py:41
  26.5 0.6 copy-start.9
  27.7 1.4 %collective-permute-start.16 = (bf16[8,1024]{1,0:T(8,128)(2,1)}, bf16[8,1024]{1,0:T(8,128)(2,1)S(1)}, u32[]{:S(2)}, u32[]{:S(2)}) collective-permute-start(bf16[8,1024]{1,0:T(8,128)(2,1)} %constant_dynamic-slice_fusion), channel_id=1, source_target_pairs={{0,4},{4,0},{8,12},{12,8},{16,20},{20,16},{24,28},{28,24},{1,5},{5... | collective-permute-start | bytes 49160 | tf_op jit(solution)/shard_map/ppermute | solution.py:41
  29.0 1.7 %copy-start.11 = (s32[1024]{0:T(1024)S(1)}, s32[1024]{0:T(1024)}, u32[]{:S(2)}) copy-start(s32[1024]{0:T(1024)} %convert_reduce_fusion) | copy-start | bytes 12292
  29.0 1.7 %copy-start.14 = (s32[1024]{0:T(1024)S(1)}, s32[1024]{0:T(1024)}, u32[]{:S(2)}) copy-start(s32[1024]{0:T(1024)} %copy-done.12) | copy-start | bytes 12292
  29.0 1.7 %copy-start.16 = (s32[128]{0:T(128)S(1)}, s32[128]{0:T(128)}, u32[]{:S(2)}) copy-start(s32[128]{0:T(128)} %copy-done.15) | copy-start | bytes 1540
  29.0 1.7 %copy-start.19 = (s32[128]{0:T(128)S(1)}, s32[128]{0:T(128)}, u32[]{:S(2)}) copy-start(s32[128]{0:T(128)} %convert_reduce_fusion.1) | copy-start | bytes 1540
  29.0 4.6 %copy-start.20 = (s32[8]{0:T(128)S(1)}, s32[8]{0:T(128)}, u32[]{:S(2)}) copy-start(s32[8]{0:T(128)} %param.17) | copy-start | bytes 100
  30.2 1.4 %collective-permute-start.17 = (f32[8,1152]{1,0:T(8,128)S(1)}, f32[8,1152]{1,0:T(8,128)S(1)}, u32[]{:S(2)}, u32[]{:S(2)}) collective-permute-start(f32[8,1152]{1,0:T(8,128)S(1)} %fusion.72), channel_id=1, source_target_pairs={{0,4},{4,0},{8,12},{12,8},{16,20},{20,16},{24,28},{28,24},{1,5},{5... | collective-permute-start | bytes 110600 | tf_op jit(solution)/shard_map/ppermute | solution.py:28
  31.6 4.0 %collective-permute-start.18 = (f32[8,1152]{1,0:T(8,128)S(1)}, f32[8,1152]{1,0:T(8,128)S(1)}, u32[]{:S(2)}, u32[]{:S(2)}) collective-permute-start(f32[8,1152]{1,0:T(8,128)S(1)} %add.333), channel_id=1, source_target_pairs={{0,8},{4,12},{8,0},{12,4},{16,24},{20,28},{24,16},{28,20},{1,9},{5... | collective-permute-start | bytes 110600 | tf_op jit(solution)/shard_map/ppermute | solution.py:28
  35.6 5.1 %collective-permute-start.19 = (f32[8,1152]{1,0:T(8,128)S(1)}, f32[8,1152]{1,0:T(8,128)S(1)}, u32[]{:S(2)}, u32[]{:S(2)}) collective-permute-start(f32[8,1152]{1,0:T(8,128)S(1)} %add.334), channel_id=1, source_target_pairs={{0,16},{4,20},{8,24},{12,28},{16,0},{20,4},{24,8},{28,12},{1,17},{... | collective-permute-start | bytes 110600 | tf_op jit(solution)/shard_map/ppermute | solution.py:28
  39.2 16.1 %collective-permute-start.5 = (bf16[2048,64]{0,1:T(8,128)(2,1)}, bf16[2048,64]{0,1:T(8,128)(2,1)}, u32[]{:S(2)}, u32[]{:S(2)}) collective-permute-start(bf16[2048,64]{0,1:T(8,128)(2,1)} %pad_maximum_fusion.3), channel_id=1, source_target_pairs={{0,8},{4,20},{8,0},{12,28},{16,24},{20,4},{24,16},{28,12},{1,9},{5... | collective-permute-start | bytes 786440 | tf_op jit(solution)/shard_map/ppermute | solution.py:76
  46.4 4.2 %collective-permute-start.20 = (f32[8,1024]{1,0:T(8,128)}, f32[8,1024]{1,0:T(8,128)}, u32[]{:S(2)}, u32[]{:S(2)}) collective-permute-start(f32[8,1024]{1,0:T(8,128)} %fusion.15), channel_id=1, source_target_pairs={{0,1},{1,0},{2,3},{3,2},{4,5},{5,4},{6,7},{7,6},{8,9},{9,8},{10,11... | collective-permute-start | bytes 98312 | tf_op jit(solution)/shard_map/ppermute | solution.py:28
  49.7 13.3 %copy-start.2 = (bf16[128,8192]{1,0:T(8,128)(2,1)S(1)}, bf16[128,8192]{1,0:T(8,128)(2,1)}, u32[]{:S(2)}) copy-start(bf16[128,8192]{1,0:T(8,128)(2,1)} %copy-done.1) | copy-start | bytes 6291460
  51.4 5.0 %collective-permute-start.21 = (f32[8,1024]{1,0:T(8,128)S(1)}, f32[8,1024]{1,0:T(8,128)S(1)}, u32[]{:S(2)}, u32[]{:S(2)}) collective-permute-start(f32[8,1024]{1,0:T(8,128)S(1)} %add.337), channel_id=1, source_target_pairs={{0,2},{1,3},{2,0},{3,1},{4,6},{5,7},{6,4},{7,5},{8,10},{9,11},{10,... | collective-permute-start | bytes 98312 | tf_op jit(solution)/shard_map/ppermute | solution.py:28
  56.3 4.4 %collective-permute-start.6 = (bf16[1024,64]{0,1:T(8,128)(2,1)S(1)}, bf16[1024,64]{0,1:T(8,128)(2,1)S(1)}, u32[]{:S(2)}, u32[]{:S(2)}) collective-permute-start(bf16[1024,64]{0,1:T(8,128)(2,1)S(1)} %slice.144), channel_id=1, source_target_pairs={{0,20},{4,8},{8,28},{12,0},{16,4},{20,24},{24,12},{28,16},{1,21},{... | collective-permute-start | bytes 393224 | tf_op jit(solution)/shard_map/ppermute | solution.py:77
  61.7 1.8 %collective-permute-start.7 = (bf16[3072,64]{0,1:T(8,128)(2,1)S(1)}, bf16[3072,64]{0,1:T(8,128)(2,1)S(1)}, u32[]{:S(2)}, u32[]{:S(2)}) collective-permute-start(bf16[3072,64]{0,1:T(8,128)(2,1)S(1)} %pad_maximum_fusion.2), channel_id=1, source_target_pairs={{0,4},{4,0},{8,12},{12,8},{16,20},{20,16},{24,28},{28,24},{1,5},{5... | collective-permute-start | bytes 1179656 | tf_op jit(solution)/shard_map/ppermute | solution.py:78
  63.2 6.1 %copy-start.5 = (f32[128,256]{1,0:T(8,128)S(1)}, f32[128,256]{1,0:T(8,128)}, u32[]{:S(2)}) copy-start(f32[128,256]{1,0:T(8,128)} %fusion.57) | copy-start | bytes 393220
  65.3 3.8 %collective-permute-start.8 = (bf16[1,128,64]{1,2,0:T(8,128)(2,1)S(1)}, bf16[1,128,64]{1,2,0:T(8,128)(2,1)S(1)}, u32[]{:S(2)}, u32[]{:S(2)}) collective-permute-start(bf16[1,128,64]{1,2,0:T(8,128)(2,1)S(1)} %fusion.23), channel_id=1, source_target_pairs={{0,1},{1,0},{2,3},{3,2},{4,5},{5,4},{6,7},{7,6},{8,9},{9,8},{10,11... | collective-permute-start | bytes 49160 | tf_op jit(solution)/shard_map/ppermute | solution.py:51
  66.9 14.9 %collective-permute-start.1 = (bf16[2048,256]{1,0:T(8,128)(2,1)S(1)}, bf16[2048,256]{1,0:T(8,128)(2,1)S(1)}, u32[]{:S(2)}, u32[]{:S(2)}) collective-permute-start(bf16[2048,256]{1,0:T(8,128)(2,1)S(1)} %pad_maximum_fusion.1), channel_id=1, source_target_pairs={{0,8},{4,20},{8,0},{12,28},{16,24},{20,4},{24,16},{28,12},{1,9},{5... | collective-permute-start | bytes 3145736 | tf_op jit(solution)/shard_map/ppermute | solution.py:76
  69.1 4.9 %collective-permute-start.9 = (bf16[2,128,64]{1,2,0:T(8,128)(2,1)S(1)}, bf16[2,128,64]{1,2,0:T(8,128)(2,1)S(1)}, u32[]{:S(2)}, u32[]{:S(2)}) collective-permute-start(bf16[2,128,64]{1,2,0:T(8,128)(2,1)S(1)} %maximum_select_fusion.1), channel_id=1, source_target_pairs={{0,2},{1,3},{2,0},{3,1},{4,6},{5,7},{6,4},{7,5},{8,10},{9,11},{10,... | collective-permute-start | bytes 98312 | tf_op jit(solution)/shard_map/ppermute | solution.py:51
  81.8 8.7 %collective-permute-start.2 = (bf16[1024,256]{1,0:T(8,128)(2,1)S(1)}, bf16[1024,256]{1,0:T(8,128)(2,1)S(1)}, u32[]{:S(2)}, u32[]{:S(2)}) collective-permute-start(bf16[1024,256]{1,0:T(8,128)(2,1)S(1)} %slice.139), channel_id=1, source_target_pairs={{0,20},{4,8},{8,28},{12,0},{16,4},{20,24},{24,12},{28,16},{1,21},{... | collective-permute-start | bytes 1572872 | tf_op jit(solution)/shard_map/ppermute | solution.py:77
  81.8 8.8 %collective-permute-start.10 = (bf16[128,256]{0,1:T(8,128)(2,1)S(1)}, bf16[128,256]{0,1:T(8,128)(2,1)S(1)}, u32[]{:S(2)}, u32[]{:S(2)}) collective-permute-start(bf16[128,256]{0,1:T(8,128)(2,1)S(1)} %constant_dynamic-update-slice_fusion.1), channel_id=1, source_target_pairs={{0,4},{4,0},{8,12},{12,8},{16,20},{20,16},{24,28},{28,24},{1,5},{5... | collective-permute-start | bytes 196616 | tf_op jit(solution)/shard_map/ppermute | solution.py:74
  90.5 10.9 %collective-permute-start.3 = (bf16[3072,256]{1,0:T(8,128)(2,1)S(1)}, bf16[3072,256]{1,0:T(8,128)(2,1)S(1)}, u32[]{:S(2)}, u32[]{:S(2)}) collective-permute-start(bf16[3072,256]{1,0:T(8,128)(2,1)S(1)} %pad_maximum_fusion), channel_id=1, source_target_pairs={{0,4},{4,0},{8,12},{12,8},{16,20},{20,16},{24,28},{28,24},{1,5},{5... | collective-permute-start | bytes 4718600 | tf_op jit(solution)/shard_map/ppermute | solution.py:78
  90.6 5.0 %collective-permute-start.11 = (bf16[256,256]{0,1:T(8,128)(2,1)S(1)}, bf16[256,256]{0,1:T(8,128)(2,1)S(1)}, u32[]{:S(2)}, u32[]{:S(2)}) collective-permute-start(bf16[256,256]{0,1:T(8,128)(2,1)S(1)} %pad_maximum_fusion.6), channel_id=1, source_target_pairs={{0,8},{4,20},{8,0},{12,28},{16,24},{20,4},{24,16},{28,12},{1,9},{5... | collective-permute-start | bytes 393224 | tf_op jit(solution)/shard_map/ppermute | solution.py:76
  95.7 3.7 %collective-permute-start.12 = (bf16[128,256]{0,1:T(8,128)(2,1)S(1)}, bf16[128,256]{0,1:T(8,128)(2,1)S(1)}, u32[]{:S(2)}, u32[]{:S(2)}) collective-permute-start(bf16[128,256]{0,1:T(8,128)(2,1)S(1)} %slice.159), channel_id=1, source_target_pairs={{0,20},{4,8},{8,28},{12,0},{16,4},{20,24},{24,12},{28,16},{1,21},{... | collective-permute-start | bytes 196616 | tf_op jit(solution)/shard_map/ppermute | solution.py:77
  99.4 1.5 %collective-permute-start.13 = (bf16[384,256]{0,1:T(8,128)(2,1)S(1)}, bf16[384,256]{0,1:T(8,128)(2,1)S(1)}, u32[]{:S(2)}, u32[]{:S(2)}) collective-permute-start(bf16[384,256]{0,1:T(8,128)(2,1)S(1)} %pad_maximum_fusion.4), channel_id=1, source_target_pairs={{0,4},{4,0},{8,12},{12,8},{16,20},{20,16},{24,28},{28,24},{1,5},{5... | collective-permute-start | bytes 589832 | tf_op jit(solution)/shard_map/ppermute | solution.py:78
  100.9 1.3 %copy-start.17 = (bf16[1024,128]{0,1:T(8,128)(2,1)}, bf16[1024,128]{0,1:T(8,128)(2,1)S(1)}, u32[]{:S(2)}) copy-start(bf16[1024,128]{0,1:T(8,128)(2,1)S(1)} %get-tuple-element.9) | copy-start | bytes 786436
  101.0 1.5 %copy-start.6 = (bf16[1024,128]{0,1:T(8,128)(2,1)}, bf16[1024,128]{0,1:T(8,128)(2,1)S(1)}, u32[]{:S(2)}) copy-start(bf16[1024,128]{0,1:T(8,128)(2,1)S(1)} %get-tuple-element.8) | copy-start | bytes 786436
  101.4 1.7 %copy-start.4 = (pred[128,1024]{1,0:T(8,128)(4,1)S(1)}, pred[128,1024]{1,0:T(8,128)(4,1)}, u32[]{:S(2)}) copy-start(pred[128,1024]{1,0:T(8,128)(4,1)} %compare_and_fusion) | copy-start | bytes 393220
  102.5 0.6 copy-start.7
where the time goes:
time: 109 us
  waiting for transfers between devices  39.2 us (36%)
  matrix products  21.6 us (20%)
  starting transfers between devices  20.8 us (19%)
  other arithmetic  15.1 us (14%)
  local copies, waits for them, and re-layouts  10.8 us (10%)
  between operations  1.22 us (1%)
    ppermute x3, waiting for transfers between devices, gather_pieces(): lax.ppermute(nb[:rows], 'seq', xor_perm(8, lambda j: j ^ 5 if j % 2 == 0...  14.8 us
    ppermute x3, waiting for transfers between devices, gather_pieces(): lax.ppermute(pair, 'seq', xor_perm(8, lambda j: j ^ 2 if j % 2 == 0 else...  11.7 us
    dot_general x16, matrix products, project(): term = jnp.dot(cols, piece, preferred_element_type=jnp.float32)  9.69 us
    ppermute x5, starting transfers between devices, xor_all_reduce(): x = x + lax.ppermute(x, axis, xor_perm(n, lambda j, k=k: j ^ k))  8.87 us
    ppermute x2, waiting for transfers between devices, xor_gather_stack(): other = lax.ppermute(stack, axis, xor_perm(n, lambda j, k=k: j ^ k))  5.78 us
    unnamed x55, local copies, waits for them, and re-layouts  5.71 us
    dot_general x1, matrix products, body(): jnp.einsum('dc,rce->dre', critic_hidden, critic_down, preferred_element_t...  5.63 us
    ppermute x3, starting transfers between devices, xor_reduce_scatter(): x = keep + lax.ppermute(send, axis, xor_perm(n, lambda j, k=k: j ^ k))  4.98 us
  transfers between devices with their start and end apart: 22, of which 14 were waited for; matrix products, arithmetic and copies ran while one was open for 32% of the time, Pallas kernels for 0%

commit v1 on v0

--- a/solution.py
+++ b/solution.py
@@ -65,36 +65,41 @@
 
 def gather_pieces(blk, n):
     i = lax.axis_index("seq")
-    rows = blk.shape[0]
     if n != 8:
-        full = lax.all_gather(blk, "seq", axis=0, tiled=True)
-        return [(full, jnp.int32(0), n * rows)]
+        full = lax.all_gather(blk, "seq", axis=0, tiled=False)
+        return [(full[m], m) for m in range(n)]
     core = i % 2
     chip = i // 2
     sib = lax.ppermute(blk, "seq", xor_perm(8, lambda j: j ^ 1))
-    pair = jnp.concatenate([blk, sib], axis=0)
-    nb = lax.ppermute(pair, "seq", xor_perm(8, lambda j: j ^ 2 if j % 2 == 0 else j ^ 4))
-    dg = lax.ppermute(nb[:rows], "seq", xor_perm(8, lambda j: j ^ 5 if j % 2 == 0 else j ^ 3))
-    oth = lax.ppermute(jnp.concatenate([nb, dg], axis=0), "seq", xor_perm(8, lambda j: j ^ 1))
+    rows = blk.shape[0]
+    nb = lax.ppermute(
+        jnp.concatenate([blk, sib], axis=0),
+        "seq",
+        xor_perm(8, lambda j: j ^ 2 if j % 2 == 0 else j ^ 4),
+    )
+    nb0, nb1 = nb[:rows], nb[rows:]
+    dg = lax.ppermute(nb0, "seq", xor_perm(8, lambda j: j ^ 5 if j % 2 == 0 else j ^ 3))
+    ot = lax.ppermute(jnp.concatenate([nb, dg], axis=0), "seq", xor_perm(8, lambda j: j ^ 1))
+    ot0, ot1, ot2 = ot[:rows], ot[rows : 2 * rows], ot[2 * rows :]
     nb_chip = chip ^ (1 + core)
     oth_chip = chip ^ (2 - core)
     diag = chip ^ 3
     return [
-        (blk, i, rows),
-        (sib, i ^ 1, rows),
-        (nb[:rows], 2 * nb_chip + core, rows),
-        (nb[rows:], 2 * nb_chip + 1 - core, rows),
-        (dg, 2 * diag + 1 - core, rows),
-        (oth[:rows], 2 * oth_chip + 1 - core, rows),
-        (oth[rows : 2 * rows], 2 * oth_chip + core, rows),
-        (oth[2 * rows :], 2 * diag + core, rows),
+        (blk, i),
+        (sib, i ^ 1),
+        (nb0, 2 * nb_chip + core),
+        (nb1, 2 * nb_chip + 1 - core),
+        (dg, 2 * diag + 1 - core),
+        (ot0, 2 * oth_chip + 1 - core),
+        (ot1, 2 * oth_chip + core),
+        (ot2, 2 * diag + core),
     ]
 
 
-def project(normed, pieces):
+def project(normed_split, pieces):
     total = None
-    for piece, source, rows in pieces:
-        cols = lax.dynamic_slice_in_dim(normed, source * rows, rows, 1)
+    for piece, source in pieces:
+        cols = lax.dynamic_index_in_dim(normed_split, source, 0, keepdims=False)
         term = jnp.dot(cols, piece, preferred_element_type=jnp.float32)
         total = term if total is None else total + term
     return total
@@ -109,6 +114,7 @@
     tp_i = lax.axis_index("tp")
     normed = rms_norm(hidden, norm_gain)
     tokens_here = hidden.shape[0]
+    d_rows = w_query.shape[0]
     heads_here = w_query.shape[1] // HEAD
     sharers = GROUP // heads_here
     kv_width = HEAD // sharers
@@ -117,7 +123,9 @@
     kv_start = kv_head * HEAD + kv_part * kv_width
     key_cols = lax.dynamic_slice_in_dim(w_key, kv_start, kv_width, 1)
     value_cols = lax.dynamic_slice_in_dim(w_value, kv_start, kv_width, 1)
-    kv_weights = jnp.concatenate([key_cols, value_cols], axis=1)
+    weights = jnp.concatenate([w_query, key_cols, value_cols], axis=1)
+    q_width = w_query.shape[1]
+    normed_split = normed.reshape(tokens_here, n_seq, d_rows).transpose(1, 0, 2)
 
     doc_ends = jnp.cumsum(doc_lengths) - 1
     first_row = seq_i * tokens_here
@@ -145,8 +153,8 @@
         critic_sum = lax.psum(chosen, "tp")
     critic_values = critic_sum.astype(jnp.bfloat16)
 
-    kv_pieces = gather_pieces(kv_weights, n_seq)
-    kv_own = project(normed, kv_pieces).astype(jnp.bfloat16)
+    projected = project(normed_split, gather_pieces(weights, n_seq))
+    kv_own = projected[:, q_width:].astype(jnp.bfloat16)
     kv_stack = xor_gather_stack(kv_own, "tp", n_tp, sharers)
     kv_rows = jnp.concatenate(
         [kv_stack[m, :, :kv_width] for m in range(sharers)]
@@ -154,17 +162,18 @@
         axis=1,
     )
     kv_all = gather_pieces(kv_rows, n_seq)
-    key_block = jnp.concatenate([piece[:, :HEAD] for piece, _, _ in kv_all], axis=0)
-    value_block = jnp.concatenate([piece[:, HEAD:] for piece, _, _ in kv_all], axis=0)
+    key_block = jnp.concatenate([piece[:, :HEAD] for piece, _ in kv_all], axis=0)
+    value_block = jnp.concatenate([piece[:, HEAD:] for piece, _ in kv_all], axis=0)
     key_pos = jnp.concatenate(
         [
             source * tokens_here + jnp.arange(piece.shape[0], dtype=jnp.int32)
-            for piece, source, _ in kv_all
+            for piece, source in kv_all
         ]
     )
 
-    q_pieces = gather_pieces(w_query, n_seq)
-    queries = project(normed, q_pieces).astype(jnp.bfloat16).reshape(tokens_here, heads_here, HEAD)
+    queries = (
+        projected[:, :q_width].astype(jnp.bfloat16).reshape(tokens_here, heads_here, HEAD)
+    )
 
     def segment_of(positions):
         return jnp.sum((positions[:, None] > doc_ends[None, :]).astype(jnp.int32), axis=1)

time: 109 us -> 114 us (1.046)
  waiting for transfers between devices: 39.2 us -> 33.9 us
  starting transfers between devices: 20.8 us -> 24.5 us
  other arithmetic: 15.1 us -> 17.2 us
  local copies, waits for them, and re-layouts: 10.8 us -> 12.9 us
  matrix products: 21.6 us -> 23.5 us
    ppermute x6 -> x4, waiting for transfers between devices: 26.5 us -> 16.8 us  [the longest x2 13.5 us: gather_pieces(): lax.ppermute(jnp.concatenate([blk, sib], axis=0), 'seq', xor_perm(8, lamb...]
    ppermute x3, waiting for transfers between devices: 2.38 us -> 6.85 us  [xor_reduce_scatter(): x = keep + lax.ppermute(send, axis, xor_perm(n, lambda j, k=k: j ^ k))]
    ppermute x2, waiting for transfers between devices: 5.78 us -> 1.99 us  [xor_gather_stack(): other = lax.ppermute(stack, axis, xor_perm(n, lambda j, k=k: j ^ k))]
    ppermute x6 -> x4, starting transfers between devices: 3.68 us -> 6.86 us  [the longest x2 3.78 us: gather_pieces(): lax.ppermute(nb0, 'seq', xor_perm(8, lambda j: j ^ 5 if j % 2 == 0 else j...]
    ppermute x5, waiting for transfers between devices: 2.87 us -> 5.78 us  [xor_all_reduce(): x = x + lax.ppermute(x, axis, xor_perm(n, lambda j, k=k: j ^ k))]
    convert_element_type x1, other arithmetic: 2.17 us -> 4.53 us  [rms_norm(): (widened * lax.rsqrt(mean_square + 1e-05) * norm_gain.astype(jnp.float32)...]
    ppermute x5, starting transfers between devices: 8.87 us -> 6.83 us  [xor_all_reduce(): x = x + lax.ppermute(x, axis, xor_perm(n, lambda j, k=k: j ^ k))]
    unnamed x55 -> x65, local copies, waits for them, and re-layouts: 5.71 us -> 7.66 us
  transfers between devices with their start and end apart: 22 -> 18, of which waited for: 14 -> 11; matrix products, arithmetic and copies ran while one was open for 32% -> 36% of each run, Pallas kernels for 0% -> 0%
where the time goes in v1:
time: 114 us; the launch traced here: 113 us
  waiting for transfers between devices  33.9 us (30%)
  starting transfers between devices  24.5 us (21%)
  matrix products  23.5 us (21%)
  other arithmetic  17.2 us (15%)
  local copies, waits for them, and re-layouts  12.9 us (11%)
  between operations  1.18 us (1%)
    ppermute x2, waiting for transfers between devices, gather_pieces(): lax.ppermute(jnp.concatenate([blk, sib], axis=0), 'seq', xor_perm(8, lamb...  13.5 us
    dot_general x8, matrix products, project(): term = jnp.dot(cols, piece, preferred_element_type=jnp.float32)  10.9 us
    unnamed x65, local copies, waits for them, and re-layouts  7.66 us
    ppermute x3, starting transfers between devices, xor_reduce_scatter(): x = keep + lax.ppermute(send, axis, xor_perm(n, lambda j, k=k: j ^ k))  6.89 us
    ppermute x3, waiting for transfers between devices, xor_reduce_scatter(): x = keep + lax.ppermute(send, axis, xor_perm(n, lambda j, k=k: j ^ k))  6.85 us
    ppermute x5, starting transfers between devices, xor_all_reduce(): x = x + lax.ppermute(x, axis, xor_perm(n, lambda j, k=k: j ^ k))  6.83 us
    ppermute x5, waiting for transfers between devices, xor_all_reduce(): x = x + lax.ppermute(x, axis, xor_perm(n, lambda j, k=k: j ^ k))  5.78 us
    dot_general x1, matrix products, body(): jnp.einsum('dc,rce->dre', critic_hidden, critic_down, preferred_element_t...  5.01 us
  transfers between devices with their start and end apart: 18, of which 11 were waited for; matrix products, arithmetic and copies ran while one was open for 36% of the time, Pallas kernels for 0%

profile of v1, /device:TPU:0, one launch (start us, length us, event | category | flops | bytes accessed | tf_op | source)
XLA Modules:
  0.0 113.2 jit_solution(18044180493250152861)
XLA Ops:
  0.7 1.4 %constant_dynamic-slice_fusion.3 = (bf16[1024,32]{1,0:T(8,128)(2,1)S(1)}, bf16[1024,32]{1,0:T(8,128)(2,1)S(1)}) fusion(bf16[1024,128]{1,0:T(8,128)(2,1)} %param.13, s32[]{:T(128)S(6)} %select_n.127, bf16[1024,128]{1,0:T(8,128)(2,1)} %param.12), kind=kLoop, calls=%fused_computation.117 | loop fusion | bytes 262148 | tf_op jit(solution)/shard_map/dynamic_slice | solution.py:125
  2.1 0.1 copy.63
  2.3 1.3 %copy.48 = bf16[1024,256]{0,1:T(8,128)(2,1)S(1)} copy(bf16[1024,256]{1,0:T(8,128)(2,1)} %param.11) | data formatting | bytes 1048576 | tf_op args[2]
  3.6 0.9 pad_maximum_fusion.2
  4.5 0.5 collective-permute-start
  5.0 0.6 convert_element_type.39
  5.6 4.1 %copy.44 = bf16[128,8192]{0,1:T(8,128)(2,1)} copy(bf16[128,8192]{1,0:T(8,128)(2,1)} %param.9) | data formatting | bytes 4194304 | tf_op args[0]
  9.7 2.8 %fusion.1 = f32[128]{0:T(128)S(1)} fusion(bf16[128,8192]{0,1:T(8,128)(2,1)} %copy.44), kind=kLoop, calls=%fused_computation.4 | loop fusion | flops 3145600 | bytes 2097664 | tf_op jit(solution)/shard_map/reduce_sum | solution.py:15
  12.7 4.5 %fusion.3 = bf16[128,8192]{0,1:T(8,128)(2,1)} fusion(bf16[128,8192]{0,1:T(8,128)(2,1)S(1)} %copy-done.1, f32[8192]{0:T(1024)} %convert_element_type.39, f32[128]{0:T(128)S(1)} %add_rsqrt_fusion), kind=kLoop, calls=%fused_computation.6 | loop fusion | flops 4194304 | bytes 4227584 | tf_op jit(solution)/shard_map/convert_element_type | solution.py:16
  17.2 0.2 reduce-window.7
  17.5 0.5 copy-done.18
  18.0 2.3 %convolution_convert_fusion = bf16[8,8192]{1,0:T(8,128)(2,1)S(1)} fusion(bf16[128,8192]{0,1:T(8,128)(2,1)} %fusion.3, s32[128]{0:T(128)S(1)} %get-tuple-element.31, s32[8]{0:T(128)S(1)} %add_bitcast_fusion), kind=kOutput, calls=%fused_computation.1 | convolution fusion | flops 16843776 | bytes 2228768 | tf_op jit(solution)/shard_map/dot_general | solution.py:134
  20.3 1.2 %pad_maximum_fusion.1 = bf16[2048,320]{0,1:T(8,128)(2,1)} fusion(bf16[1024,320]{0,1:T(8,128)(2,1)S(1)} %collective-permute-done, bf16[1024,32]{0,1:T(8,128)(2,1)S(1)} %copy-done.4, bf16[1024,32]{0,1:T(8,128)(2,1)S(1)} %copy-done.7, bf16[1024,256]{0,1:T(8,128)(2,1)S(1)} %copy.48), kind=kLoop, calls=%fused_computation.13 | loop fusion | flops 5242880 | bytes 2621440 | tf_op jit(solution)/shard_map/concatenate | solution.py:76
  21.5 2.5 %collective-permute-start.1 = (bf16[2048,320]{0,1:T(8,128)(2,1)}, bf16[2048,320]{0,1:T(8,128)(2,1)}, u32[]{:S(2)}, u32[]{:S(2)}) collective-permute-start(bf16[2048,320]{0,1:T(8,128)(2,1)} %pad_maximum_fusion.1), channel_id=1, source_target_pairs={{0,8},{4,20},{8,0},{12,28},{16,24},{20,4},{24,16},{28,12},{1,9},{5... | collective-permute-start | bytes 3932168 | tf_op jit(solution)/shard_map/ppermute | solution.py:75
  24.0 0.6 constant_dynamic-slice_fusion.2
  24.6 1.5 %collective-permute-start.10 = (bf16[8,4096]{1,0:T(8,128)(2,1)}, bf16[8,4096]{1,0:T(8,128)(2,1)}, u32[]{:S(2)}, u32[]{:S(2)}) collective-permute-start(bf16[8,4096]{1,0:T(8,128)(2,1)} %constant_dynamic-slice_fusion.2), channel_id=1, source_target_pairs={{0,16},{4,20},{8,24},{12,28},{16,0},{20,4},{24,8},{28,12},{1,17},{... | collective-permute-start | bytes 196616 | tf_op jit(solution)/shard_map/ppermute | solution.py:41
  26.1 3.8 %collective-permute-done.10 = bf16[8,4096]{1,0:T(8,128)(2,1)} collective-permute-done((bf16[8,4096]{1,0:T(8,128)(2,1)}, bf16[8,4096]{1,0:T(8,128)(2,1)}, u32[]{:S(2)}, u32[]{:S(2)}) %collective-permute-start.10) | collective-permute-done | bytes 65568 | tf_op jit(solution)/shard_map/ppermute | solution.py:41
  29.9 0.9 dynamic-slice_add_fusion
  30.8 9.1 %collective-permute-done.1 = bf16[2048,320]{0,1:T(8,128)(2,1)} collective-permute-done((bf16[2048,320]{0,1:T(8,128)(2,1)}, bf16[2048,320]{0,1:T(8,128)(2,1)}, u32[]{:S(2)}, u32[]{:S(2)}) %collective-permute-start.1) | collective-permute-done | bytes 1310752 | tf_op jit(solution)/shard_map/ppermute | solution.py:75
  39.9 2.0 %slice.126 = bf16[1024,320]{0,1:T(8,128)(2,1)} slice(bf16[2048,320]{0,1:T(8,128)(2,1)} %collective-permute-done.1), slice={[0:1024], [0:320]} | slice | bytes 1310720 | tf_op jit(solution)/shard_map/slice | solution.py:80
  41.9 3.4 %collective-permute-start.2 = (bf16[1024,320]{0,1:T(8,128)(2,1)}, bf16[1024,320]{0,1:T(8,128)(2,1)}, u32[]{:S(2)}, u32[]{:S(2)}) collective-permute-start(bf16[1024,320]{0,1:T(8,128)(2,1)} %slice.126), channel_id=1, source_target_pairs={{0,20},{4,8},{8,28},{12,0},{16,4},{20,24},{24,12},{28,16},{1,21},{... | collective-permute-start | bytes 1966088 | tf_op jit(solution)/shard_map/ppermute | solution.py:81
  45.2 0.6 constant_dynamic-slice_fusion.1
  45.8 1.5 %collective-permute-start.11 = (bf16[8,2048]{1,0:T(8,128)(2,1)}, bf16[8,2048]{1,0:T(8,128)(2,1)}, u32[]{:S(2)}, u32[]{:S(2)}) collective-permute-start(bf16[8,2048]{1,0:T(8,128)(2,1)} %constant_dynamic-slice_fusion.1), channel_id=1, source_target_pairs={{0,8},{4,12},{8,0},{12,4},{16,24},{20,28},{24,16},{28,20},{1,9},{5... | collective-permute-start | bytes 98312 | tf_op jit(solution)/shard_map/ppermute | solution.py:41
  47.3 3.1 %collective-permute-done.11 = bf16[8,2048]{1,0:T(8,128)(2,1)} collective-permute-done((bf16[8,2048]{1,0:T(8,128)(2,1)}, bf16[8,2048]{1,0:T(8,128)(2,1)}, u32[]{:S(2)}, u32[]{:S(2)}) %collective-permute-start.11) | collective-permute-done | bytes 32800 | tf_op jit(solution)/shard_map/ppermute | solution.py:41
  50.4 0.8 dynamic-slice_add_fusion.1
  51.2 0.6 copy-done.12
  51.8 0.6 constant_dynamic-slice_fusion
  52.4 3.9 %collective-permute-start.12 = (bf16[8,1024]{1,0:T(8,128)(2,1)}, bf16[8,1024]{1,0:T(8,128)(2,1)S(1)}, u32[]{:S(2)}, u32[]{:S(2)}) collective-permute-start(bf16[8,1024]{1,0:T(8,128)(2,1)} %constant_dynamic-slice_fusion), channel_id=1, source_target_pairs={{0,4},{4,0},{8,12},{12,8},{16,20},{20,16},{24,28},{28,24},{1,5},{5... | collective-permute-start | bytes 49160 | tf_op jit(solution)/shard_map/ppermute | solution.py:41
  56.3 3.0 %pad_maximum_fusion = bf16[3072,320]{0,1:T(8,128)(2,1)} fusion(bf16[1024,320]{0,1:T(8,128)(2,1)} %collective-permute-done.2, bf16[2048,320]{0,1:T(8,128)(2,1)} %collective-permute-done.1), kind=kLoop, calls=%fused_computation.7 | loop fusion | flops 3932160 | bytes 3932160 | tf_op jit(solution)/shard_map/concatenate | solution.py:82
  59.3 1.2 %iota_compare_fusion = pred[8,4]{0,1:T(4,128)(4,1)} fusion(s32[8]{0:T(128)} %param.17), kind=kLoop, calls=%fused_computation.122 | loop fusion | flops 32 | bytes 64 | tf_op jit(solution)/shard_map/eq | solution.py:148
  60.5 1.2 %fusion.48 = f32[8,1152]{1,0:T(8,128)S(1)} fusion(bf16[1024,1152]{1,0:T(8,128)(2,1)S(1)} %copy-done, bf16[8,1024]{1,0:T(8,128)(2,1)S(1)} %collective-permute-done.12, bf16[8,2048]{1,0:T(8,128)(2,1)} %copy-done.12, s32[]{:T(128)S(6)} %select_n.151), kind=kOutput, calls=%fused_computation.87 | convolution fusion | flops 18907136 | bytes 2428932 | tf_op jit(solution)/shard_map/dot_general | solution.py:139
  61.7 0.6 collective-permute-start.13
  62.2 2.0 %fusion.33 = f32[128,320]{0,1:T(8,128)} fusion(bf16[128,8,1024]{0,2,1:T(8,128)(2,1)} %bitcast.93, s32[]{:T(128)S(6)} %select_n.124, bf16[1024,32]{0,1:T(8,128)(2,1)S(1)} %copy-done.5, bf16[1024,32]{0,1:T(8,128)(2,1)S(1)} %copy-done.8, bf16[1024,256]{0,1:T(8,128)(2,1)S(1)} %copy.48), kind=kOutput, calls=%fused_computation.45 | convolution fusion | flops 85852160 | bytes 1081348 | tf_op jit(solution)/shard_map/dot_general | solution.py:103
  64.2 0.5 collective-permute-start.14
  64.8 3.4 %collective-permute-done.14 = f32[8,1152]{1,0:T(8,128)S(1)} collective-permute-done((f32[8,1152]{1,0:T(8,128)S(1)}, f32[8,1152]{1,0:T(8,128)S(1)}, u32[]{:S(2)}, u32[]{:S(2)}) %collective-permute-start.14) | collective-permute-done | bytes 36896 | tf_op jit(solution)/shard_map/ppermute | solution.py:28
  68.2 1.5 %collective-permute-start.15 = (f32[8,1152]{1,0:T(8,128)S(1)}, f32[8,1152]{1,0:T(8,128)S(1)}, u32[]{:S(2)}, u32[]{:S(2)}) collective-permute-start(f32[8,1152]{1,0:T(8,128)S(1)} %add.291), channel_id=1, source_target_pairs={{0,16},{4,20},{8,24},{12,28},{16,0},{20,4},{24,8},{28,12},{1,17},{... | collective-permute-start | bytes 110600 | tf_op jit(solution)/shard_map/ppermute | solution.py:28
  69.8 2.3 %collective-permute-done.15 = f32[8,1152]{1,0:T(8,128)S(1)} collective-permute-done((f32[8,1152]{1,0:T(8,128)S(1)}, f32[8,1152]{1,0:T(8,128)S(1)}, u32[]{:S(2)}, u32[]{:S(2)}) %collective-permute-start.15) | collective-permute-done | bytes 36896 | tf_op jit(solution)/shard_map/ppermute | solution.py:28
  72.2 5.0 %fusion.15 = f32[8,1024]{1,0:T(8,128)S(1)} fusion(bf16[4,1152,1024]{2,1,0:T(8,128)(2,1)} %param.16, pred[8,4]{0,1:T(4,128)(4,1)S(1)} %copy-done.23, f32[8,1152]{1,0:T(8,128)S(1)} %add.291, f32[8,1152]{1,0:T(8,128)S(1)} %collective-permute-done.15), kind=kOutput, calls=%fused_computation.25 | convolution fusion | flops 75610112 | bytes 9543712 | tf_op jit(solution)/shard_map/dc,rce->dre/dot_general | solution.py:145
  77.2 1.6 %collective-permute-start.16 = (f32[8,1024]{1,0:T(8,128)S(1)}, f32[8,1024]{1,0:T(8,128)S(1)}, u32[]{:S(2)}, u32[]{:S(2)}) collective-permute-start(f32[8,1024]{1,0:T(8,128)S(1)} %fusion.15), channel_id=1, source_target_pairs={{0,1},{1,0},{2,3},{3,2},{4,5},{5,4},{6,7},{7,6},{8,9},{9,8},{10,11... | collective-permute-start | bytes 98312 | tf_op jit(solution)/shard_map/ppermute | solution.py:28
  78.8 0.4 convolution_add_fusion.1
  79.1 1.4 %fusion.22 = f32[128,320]{0,1:T(8,128)S(1)} fusion(bf16[2048,320]{0,1:T(8,128)(2,1)} %collective-permute-done.1, bf16[128,8,1024]{0,2,1:T(8,128)(2,1)S(1)} %bitcast.95, s32[]{:T(128)S(6)} %select_n.130), kind=kOutput, calls=%fused_computation.32 | convolution fusion | flops 83886080 | bytes 1081348 | tf_op jit(solution)/shard_map/dot_general | solution.py:103
  80.6 1.4 %fusion.28 = f32[128,320]{0,1:T(8,128)S(1)} fusion(bf16[1024,320]{0,1:T(8,128)(2,1)} %collective-permute-done.2, bf16[128,8,1024]{0,2,1:T(8,128)(2,1)S(1)} %bitcast.96, s32[]{:T(128)S(6)} %select_n.131), kind=kOutput, calls=%fused_computation.40 | convolution fusion | flops 83886080 | bytes 1081348 | tf_op jit(solution)/shard_map/dot_general | solution.py:103
  82.0 1.4 %fusion.16 = f32[128,320]{0,1:T(8,128)S(1)} fusion(bf16[3072,320]{0,1:T(8,128)(2,1)} %collective-permute-done.3, bf16[128,8,1024]{0,2,1:T(8,128)(2,1)S(1)} %bitcast.97, s32[]{:T(128)S(6)} %select_n.134), kind=kOutput, calls=%fused_computation.26 | convolution fusion | flops 83886080 | bytes 1081348 | tf_op jit(solution)/shard_map/dot_general | solution.py:103
  83.5 1.4 %fusion.18 = f32[128,320]{0,1:T(8,128)S(1)} fusion(bf16[3072,320]{0,1:T(8,128)(2,1)} %collective-permute-done.3, bf16[128,8,1024]{0,2,1:T(8,128)(2,1)S(1)} %bitcast.98, s32[]{:T(128)S(6)} %select_n.133), kind=kOutput, calls=%fused_computation.28 | convolution fusion | flops 83886080 | bytes 1081348 | tf_op jit(solution)/shard_map/dot_general | solution.py:103
  84.9 1.4 %fusion.20 = f32[128,320]{0,1:T(8,128)S(1)} fusion(bf16[3072,320]{0,1:T(8,128)(2,1)} %collective-permute-done.3, bf16[128,8,1024]{0,2,1:T(8,128)(2,1)S(1)} %bitcast.99, s32[]{:T(128)S(6)} %select_n.132), kind=kOutput, calls=%fused_computation.30 | convolution fusion | flops 83886080 | bytes 1081348 | tf_op jit(solution)/shard_map/dot_general | solution.py:103
  86.4 1.5 %fusion.13 = bf16[128,320]{0,1:T(8,128)(2,1)S(1)} fusion(f32[128,320]{0,1:T(8,128)S(1)} %fusion.16, f32[128,320]{0,1:T(8,128)S(1)} %fusion.18, f32[128,320]{0,1:T(8,128)S(1)} %fusion.20, f32[128,320]{0,1:T(8,128)S(1)} %fusion.28, f32[128,320]{0,1:T(8,128)S(1)} %fusion.22, f32[128,320]{0,1:T(8,128)S(1)} %convolution_add_fusion.1, ...), kind=kOutput, calls=%fused_computation.23 | convolution fusion | flops 84172800 | bytes 1982468 | tf_op jit(solution)/shard_map/dot_general | solution.py:103
  87.8 0.5 collective-permute-start.4
  88.4 0.2 compare_and_fusion
  88.6 2.7 %collective-permute-start.17 = (f32[8,1024]{1,0:T(8,128)S(1)}, f32[8,1024]{1,0:T(8,128)S(1)}, u32[]{:S(2)}, u32[]{:S(2)}) collective-permute-start(f32[8,1024]{1,0:T(8,128)S(1)} %add.294), channel_id=1, source_target_pairs={{0,2},{1,3},{2,0},{3,1},{4,6},{5,7},{6,4},{7,5},{8,10},{9,11},{10,... | collective-permute-start | bytes 98312 | tf_op jit(solution)/shard_map/ppermute | solution.py:28
  91.3 0.4 collective-permute-done.4
  91.7 2.6 %collective-permute-start.5 = (bf16[2,128,64]{1,2,0:T(8,128)(2,1)S(1)}, bf16[2,128,64]{1,2,0:T(8,128)(2,1)S(1)}, u32[]{:S(2)}, u32[]{:S(2)}) collective-permute-start(bf16[2,128,64]{1,2,0:T(8,128)(2,1)S(1)} %maximum_select_fusion.1), channel_id=1, source_target_pairs={{0,2},{1,3},{2,0},{3,1},{4,6},{5,7},{6,4},{7,5},{8,10},{9,11},{10,... | collective-permute-start | bytes 98312 | tf_op jit(solution)/shard_map/ppermute | solution.py:51
  94.3 0.6 add_convert_fusion
  94.9 1.6 %collective-permute-done.5 = bf16[2,128,64]{1,2,0:T(8,128)(2,1)S(1)} collective-permute-done((bf16[2,128,64]{1,2,0:T(8,128)(2,1)S(1)}, bf16[2,128,64]{1,2,0:T(8,128)(2,1)S(1)}, u32[]{:S(2)}, u32[]{:S(2)}) %collective-permute-start.5) | collective-permute-done | bytes 32800 | tf_op jit(solution)/shard_map/ppermute | solution.py:51
  96.8 1.2 %collective-permute-done.6 = bf16[128,256]{0,1:T(8,128)(2,1)S(1)} collective-permute-done((bf16[128,256]{0,1:T(8,128)(2,1)S(1)}, bf16[128,256]{0,1:T(8,128)(2,1)S(1)}, u32[]{:S(2)}, u32[]{:S(2)}) %collective-permute-start.6) | collective-permute-done | bytes 65568 | tf_op jit(solution)/shard_map/ppermute | solution.py:73
  98.0 0.6 collective-permute-start.7
  98.6 4.4 %collective-permute-done.7 = bf16[256,256]{0,1:T(8,128)(2,1)S(1)} collective-permute-done((bf16[256,256]{0,1:T(8,128)(2,1)S(1)}, bf16[256,256]{0,1:T(8,128)(2,1)S(1)}, u32[]{:S(2)}, u32[]{:S(2)}) %collective-permute-start.7) | collective-permute-done | bytes 131104 | tf_op jit(solution)/shard_map/ppermute | solution.py:75
  103.0 0.4 collective-permute-start.8
  103.5 3.3 %collective-permute-done.8 = bf16[128,256]{0,1:T(8,128)(2,1)S(1)} collective-permute-done((bf16[128,256]{0,1:T(8,128)(2,1)S(1)}, bf16[128,256]{0,1:T(8,128)(2,1)S(1)}, u32[]{:S(2)}, u32[]{:S(2)}) %collective-permute-start.8) | collective-permute-done | bytes 65568 | tf_op jit(solution)/shard_map/ppermute | solution.py:81
  106.8 0.2 collective-permute-start.9
  107.0 1.3 %collective-permute-done.9 = bf16[384,256]{0,1:T(8,128)(2,1)S(1)} collective-permute-done((bf16[384,256]{0,1:T(8,128)(2,1)S(1)}, bf16[384,256]{0,1:T(8,128)(2,1)S(1)}, u32[]{:S(2)}, u32[]{:S(2)}) %collective-permute-start.9) | collective-permute-done | bytes 196640 | tf_op jit(solution)/shard_map/ppermute | solution.py:82
  108.3 0.7 fusion.69
  109.0 1.4 %fusion.7 = f32[128,2,1024]{2,0,1:T(8,128)} fusion(bf16[128,2,128]{0,2,1:T(8,128)(2,1)S(1)} %bitcast.102, pred[128,1024]{1,0:T(8,128)(4,1)S(1)} %compare_and_fusion, bf16[1024,128]{0,1:T(8,128)(2,1)S(1)} %get-tuple-element.12), kind=kOutput, calls=%fused_computation.12 | convolution fusion | flops 67633152 | bytes 1507328 | tf_op jit(solution)/shard_map/qhd,kd->qhk/dot_general | solution.py:188
  110.4 2.0 %fusion.14 = bf16[128,2,128]{0,2,1:T(8,128)(2,1)S(1)} fusion(bf16[1024,128]{0,1:T(8,128)(2,1)S(1)} %get-tuple-element.13, f32[128,2,1024]{2,0,1:T(8,128)} %fusion.7, pred[128,1024]{1,0:T(8,128)(4,1)S(1)} %compare_and_fusion, f32[128,2]{0,1:T(2,128)S(1)} %fusion.69), kind=kOutput, calls=%fused_computation.24 | convolution fusion | flops 67962112 | bytes 1508352 | tf_op jit(solution)/shard_map/qhk,kd->qhd/dot_general | solution.py:195
  112.4 0.7 copy.58
  (96 shorter events, 0.8 us)
Async XLA Ops:
  0.6 59.9 %copy-start = (bf16[1024,1152]{1,0:T(8,128)(2,1)S(1)}, bf16[1024,1152]{1,0:T(8,128)(2,1)}, u32[]{:S(2)}) copy-start(bf16[1024,1152]{1,0:T(8,128)(2,1)} %param.15) | copy-start | bytes 7077892
  0.7 4.4 %copy-start.13 = (bf16[8192]{0:T(1024)(128)(2,1)S(1)}, bf16[8192]{0:T(1024)(128)(2,1)}, u32[]{:S(2)}) copy-start(bf16[8192]{0:T(1024)(128)(2,1)} %param.10) | copy-start | bytes 49156
  2.2 1.4 %copy-start.3 = (bf16[1024,32]{0,1:T(8,128)(2,1)}, bf16[1024,32]{0,1:T(8,128)(2,1)S(1)}, u32[]{:S(2)}) copy-start(bf16[1024,32]{0,1:T(8,128)(2,1)S(1)} %copy.63) | copy-start | bytes 196612
  2.3 1.3 %copy-start.6 = (bf16[1024,32]{0,1:T(8,128)(2,1)}, bf16[1024,32]{0,1:T(8,128)(2,1)S(1)}, u32[]{:S(2)}) copy-start(bf16[1024,32]{0,1:T(8,128)(2,1)S(1)} %copy.62) | copy-start | bytes 196612
  4.5 15.8 %collective-permute-start = (bf16[1024,320]{0,1:T(8,128)(2,1)}, bf16[1024,320]{0,1:T(8,128)(2,1)S(1)}, u32[]{:S(2)}, u32[]{:S(2)}) collective-permute-start(bf16[1024,320]{0,1:T(8,128)(2,1)} %pad_maximum_fusion.2), channel_id=1, source_target_pairs={{0,4},{4,0},{8,12},{12,8},{16,20},{20,16},{24,28},{28,24},{1,5},{5... | collective-permute-start | bytes 1966088 | tf_op jit(solution)/shard_map/ppermute | solution.py:73
  5.6 6.9 %copy-start.14 = (s32[1024]{0:T(1024)S(1)}, s32[1024]{0:T(1024)}, u32[]{:S(2)}) copy-start(s32[1024]{0:T(1024)} %custom-call.3) | copy-start | bytes 12292
  9.7 2.9 %copy-start.1 = (bf16[128,8192]{0,1:T(8,128)(2,1)S(1)}, bf16[128,8192]{0,1:T(8,128)(2,1)}, u32[]{:S(2)}) copy-start(bf16[128,8192]{0,1:T(8,128)(2,1)} %copy.44) | copy-start | bytes 6291460
  12.7 4.6 %copy-start.24 = (s32[8]{0:T(128)S(1)}, s32[8]{0:T(128)}, u32[]{:S(2)}) copy-start(s32[8]{0:T(128)} %param.14) | copy-start | bytes 100
  17.4 2.9 %copy-start.4 = (bf16[1024,32]{0,1:T(8,128)(2,1)S(1)}, bf16[1024,32]{0,1:T(8,128)(2,1)}, u32[]{:S(2)}) copy-start(bf16[1024,32]{0,1:T(8,128)(2,1)} %copy-done.3) | copy-start | bytes 196612
  17.4 2.9 %copy-start.7 = (bf16[1024,32]{0,1:T(8,128)(2,1)S(1)}, bf16[1024,32]{0,1:T(8,128)(2,1)}, u32[]{:S(2)}) copy-start(bf16[1024,32]{0,1:T(8,128)(2,1)} %copy-done.6) | copy-start | bytes 196612
  17.4 0.6 copy-start.18
  17.4 4.1 %copy-start.15 = (s32[1024]{0:T(1024)}, s32[1024]{0:T(1024)S(1)}, u32[]{:S(2)}) copy-start(s32[1024]{0:T(1024)S(1)} %get-tuple-element.30) | copy-start | bytes 12292
  17.4 2.8 %copy-start.21 = (s32[8]{0:T(128)}, s32[8]{0:T(128)S(1)}, u32[]{:S(2)}) copy-start(s32[8]{0:T(128)S(1)} %add_bitcast_fusion) | copy-start | bytes 100
  20.3 3.7 %copy-start.9 = (bf16[8,8192]{1,0:T(8,128)(2,1)}, bf16[8,8192]{1,0:T(8,128)(2,1)S(1)}, u32[]{:S(2)}) copy-start(bf16[8,8192]{1,0:T(8,128)(2,1)S(1)} %convolution_convert_fusion) | copy-start | bytes 393220
  21.5 18.4 %collective-permute-start.1 = (bf16[2048,320]{0,1:T(8,128)(2,1)}, bf16[2048,320]{0,1:T(8,128)(2,1)}, u32[]{:S(2)}, u32[]{:S(2)}) collective-permute-start(bf16[2048,320]{0,1:T(8,128)(2,1)} %pad_maximum_fusion.1), channel_id=1, source_target_pairs={{0,8},{4,20},{8,0},{12,28},{16,24},{20,4},{24,16},{28,12},{1,9},{5... | collective-permute-start | bytes 3932168 | tf_op jit(solution)/shard_map/ppermute | solution.py:75
  24.6 5.3 %collective-permute-start.10 = (bf16[8,4096]{1,0:T(8,128)(2,1)}, bf16[8,4096]{1,0:T(8,128)(2,1)}, u32[]{:S(2)}, u32[]{:S(2)}) collective-permute-start(bf16[8,4096]{1,0:T(8,128)(2,1)} %constant_dynamic-slice_fusion.2), channel_id=1, source_target_pairs={{0,16},{4,20},{8,24},{12,28},{16,0},{20,4},{24,8},{28,12},{1,17},{... | collective-permute-start | bytes 196616 | tf_op jit(solution)/shard_map/ppermute | solution.py:41
  30.8 14.4 %copy-start.10 = (bf16[8,4096]{1,0:T(8,128)(2,1)}, bf16[8,4096]{1,0:T(8,128)(2,1)S(1)}, u32[]{:S(2)}) copy-start(bf16[8,4096]{1,0:T(8,128)(2,1)S(1)} %dynamic-slice_add_fusion) | copy-start | bytes 196612
  41.9 14.4 %collective-permute-start.2 = (bf16[1024,320]{0,1:T(8,128)(2,1)}, bf16[1024,320]{0,1:T(8,128)(2,1)}, u32[]{:S(2)}, u32[]{:S(2)}) collective-permute-start(bf16[1024,320]{0,1:T(8,128)(2,1)} %slice.126), channel_id=1, source_target_pairs={{0,20},{4,8},{8,28},{12,0},{16,4},{20,24},{24,12},{28,16},{1,21},{... | collective-permute-start | bytes 1966088 | tf_op jit(solution)/shard_map/ppermute | solution.py:81
  45.8 4.6 %collective-permute-start.11 = (bf16[8,2048]{1,0:T(8,128)(2,1)}, bf16[8,2048]{1,0:T(8,128)(2,1)}, u32[]{:S(2)}, u32[]{:S(2)}) collective-permute-start(bf16[8,2048]{1,0:T(8,128)(2,1)} %constant_dynamic-slice_fusion.1), channel_id=1, source_target_pairs={{0,8},{4,12},{8,0},{12,4},{16,24},{20,28},{24,16},{28,20},{1,9},{5... | collective-permute-start | bytes 98312 | tf_op jit(solution)/shard_map/ppermute | solution.py:41
  51.2 0.6 copy-start.12
  52.4 8.1 %collective-permute-start.12 = (bf16[8,1024]{1,0:T(8,128)(2,1)}, bf16[8,1024]{1,0:T(8,128)(2,1)S(1)}, u32[]{:S(2)}, u32[]{:S(2)}) collective-permute-start(bf16[8,1024]{1,0:T(8,128)(2,1)} %constant_dynamic-slice_fusion), channel_id=1, source_target_pairs={{0,4},{4,0},{8,12},{12,8},{16,20},{20,16},{24,28},{28,24},{1,5},{5... | collective-permute-start | bytes 49160 | tf_op jit(solution)/shard_map/ppermute | solution.py:41
  59.3 22.8 %collective-permute-start.3 = (bf16[3072,320]{0,1:T(8,128)(2,1)}, bf16[3072,320]{0,1:T(8,128)(2,1)}, u32[]{:S(2)}, u32[]{:S(2)}) collective-permute-start(bf16[3072,320]{0,1:T(8,128)(2,1)} %pad_maximum_fusion), channel_id=1, source_target_pairs={{0,4},{4,0},{8,12},{12,8},{16,20},{20,16},{24,28},{28,24},{1,5},{5... | collective-permute-start | bytes 5898248 | tf_op jit(solution)/shard_map/ppermute | solution.py:82
  60.5 1.8 %copy-start.5 = (bf16[1024,32]{0,1:T(8,128)(2,1)S(1)}, bf16[1024,32]{0,1:T(8,128)(2,1)}, u32[]{:S(2)}) copy-start(bf16[1024,32]{0,1:T(8,128)(2,1)} %copy-done.3) | copy-start | bytes 196612
  60.5 1.8 %copy-start.8 = (bf16[1024,32]{0,1:T(8,128)(2,1)S(1)}, bf16[1024,32]{0,1:T(8,128)(2,1)}, u32[]{:S(2)}) copy-start(bf16[1024,32]{0,1:T(8,128)(2,1)} %copy-done.6) | copy-start | bytes 196612
  60.5 4.2 %copy-start.16 = (s32[1024]{0:T(1024)S(1)}, s32[1024]{0:T(1024)}, u32[]{:S(2)}) copy-start(s32[1024]{0:T(1024)} %copy-done.15) | copy-start | bytes 12292
  60.5 4.2 %copy-start.22 = (s32[8]{0:T(128)S(1)}, s32[8]{0:T(128)}, u32[]{:S(2)}) copy-start(s32[8]{0:T(128)} %copy-done.21) | copy-start | bytes 100
  60.5 9.3 %copy-start.19 = (s32[128]{0:T(128)S(1)}, s32[128]{0:T(128)}, u32[]{:S(2)}) copy-start(s32[128]{0:T(128)} %copy-done.18) | copy-start | bytes 1540
  61.7 10.5 %copy-start.23 = (pred[8,4]{0,1:T(4,128)(4,1)S(1)}, pred[8,4]{0,1:T(4,128)(4,1)}, u32[]{:S(2)}) copy-start(pred[8,4]{0,1:T(4,128)(4,1)} %iota_compare_fusion) | copy-start | bytes 100
  61.7 2.5 %collective-permute-start.13 = (f32[8,1152]{1,0:T(8,128)S(1)}, f32[8,1152]{1,0:T(8,128)S(1)}, u32[]{:S(2)}, u32[]{:S(2)}) collective-permute-start(f32[8,1152]{1,0:T(8,128)S(1)} %fusion.48), channel_id=1, source_target_pairs={{0,4},{4,0},{8,12},{12,8},{16,20},{20,16},{24,28},{28,24},{1,5},{5... | collective-permute-start | bytes 110600 | tf_op jit(solution)/shard_map/ppermute | solution.py:28
  64.2 4.0 %collective-permute-start.14 = (f32[8,1152]{1,0:T(8,128)S(1)}, f32[8,1152]{1,0:T(8,128)S(1)}, u32[]{:S(2)}, u32[]{:S(2)}) collective-permute-start(f32[8,1152]{1,0:T(8,128)S(1)} %add.290), channel_id=1, source_target_pairs={{0,8},{4,12},{8,0},{12,4},{16,24},{20,28},{24,16},{28,20},{1,9},{5... | collective-permute-start | bytes 110600 | tf_op jit(solution)/shard_map/ppermute | solution.py:28
  68.2 4.0 %collective-permute-start.15 = (f32[8,1152]{1,0:T(8,128)S(1)}, f32[8,1152]{1,0:T(8,128)S(1)}, u32[]{:S(2)}, u32[]{:S(2)}) collective-permute-start(f32[8,1152]{1,0:T(8,128)S(1)} %add.291), channel_id=1, source_target_pairs={{0,16},{4,20},{8,24},{12,28},{16,0},{20,4},{24,8},{28,12},{1,17},{... | collective-permute-start | bytes 110600 | tf_op jit(solution)/shard_map/ppermute | solution.py:28
  69.8 9.0 %copy-start.2 = (bf16[128,8192]{0,1:T(8,128)(2,1)S(1)}, bf16[128,8192]{0,1:T(8,128)(2,1)}, u32[]{:S(2)}) copy-start(bf16[128,8192]{0,1:T(8,128)(2,1)} %fusion.3) | copy-start | bytes 6291460
  69.8 9.0 %copy-start.11 = (f32[128,320]{0,1:T(8,128)S(1)}, f32[128,320]{0,1:T(8,128)}, u32[]{:S(2)}) copy-start(f32[128,320]{0,1:T(8,128)} %fusion.33) | copy-start | bytes 491524
  77.2 11.4 %collective-permute-start.16 = (f32[8,1024]{1,0:T(8,128)S(1)}, f32[8,1024]{1,0:T(8,128)S(1)}, u32[]{:S(2)}, u32[]{:S(2)}) collective-permute-start(f32[8,1024]{1,0:T(8,128)S(1)} %fusion.15), channel_id=1, source_target_pairs={{0,1},{1,0},{2,3},{3,2},{4,5},{5,4},{6,7},{7,6},{8,9},{9,8},{10,11... | collective-permute-start | bytes 98312 | tf_op jit(solution)/shard_map/ppermute | solution.py:28
  83.5 4.9 %copy-start.17 = (s32[1024]{0:T(1024)S(1)}, s32[1024]{0:T(1024)}, u32[]{:S(2)}) copy-start(s32[1024]{0:T(1024)} %copy-done.15) | copy-start | bytes 12292
  83.5 4.9 %copy-start.20 = (s32[128]{0:T(128)S(1)}, s32[128]{0:T(128)}, u32[]{:S(2)}) copy-start(s32[128]{0:T(128)} %copy-done.18) | copy-start | bytes 1540
  87.8 3.8 %collective-permute-start.4 = (bf16[1,128,64]{1,2,0:T(8,128)(2,1)S(1)}, bf16[1,128,64]{1,2,0:T(8,128)(2,1)S(1)}, u32[]{:S(2)}, u32[]{:S(2)}) collective-permute-start(bf16[1,128,64]{1,2,0:T(8,128)(2,1)S(1)} %slice_bitcast_fusion), channel_id=1, source_target_pairs={{0,1},{1,0},{2,3},{3,2},{4,5},{5,4},{6,7},{7,6},{8,9},{9,8},{10,11... | collective-permute-start | bytes 49160 | tf_op jit(solution)/shard_map/ppermute | solution.py:51
  88.6 5.7 %collective-permute-start.17 = (f32[8,1024]{1,0:T(8,128)S(1)}, f32[8,1024]{1,0:T(8,128)S(1)}, u32[]{:S(2)}, u32[]{:S(2)}) collective-permute-start(f32[8,1024]{1,0:T(8,128)S(1)} %add.294), channel_id=1, source_target_pairs={{0,2},{1,3},{2,0},{3,1},{4,6},{5,7},{6,4},{7,5},{8,10},{9,11},{10,... | collective-permute-start | bytes 98312 | tf_op jit(solution)/shard_map/ppermute | solution.py:28
  91.7 4.9 %collective-permute-start.5 = (bf16[2,128,64]{1,2,0:T(8,128)(2,1)S(1)}, bf16[2,128,64]{1,2,0:T(8,128)(2,1)S(1)}, u32[]{:S(2)}, u32[]{:S(2)}) collective-permute-start(bf16[2,128,64]{1,2,0:T(8,128)(2,1)S(1)} %maximum_select_fusion.1), channel_id=1, source_target_pairs={{0,2},{1,3},{2,0},{3,1},{4,6},{5,7},{6,4},{7,5},{8,10},{9,11},{10,... | collective-permute-start | bytes 98312 | tf_op jit(solution)/shard_map/ppermute | solution.py:51
  96.7 1.3 %collective-permute-start.6 = (bf16[128,256]{0,1:T(8,128)(2,1)S(1)}, bf16[128,256]{0,1:T(8,128)(2,1)S(1)}, u32[]{:S(2)}, u32[]{:S(2)}) collective-permute-start(bf16[128,256]{0,1:T(8,128)(2,1)S(1)} %constant_dynamic-update-slice_fusion.1), channel_id=1, source_target_pairs={{0,4},{4,0},{8,12},{12,8},{16,20},{20,16},{24,28},{28,24},{1,5},{5... | collective-permute-start | bytes 196616 | tf_op jit(solution)/shard_map/ppermute | solution.py:73
  98.0 5.0 %collective-permute-start.7 = (bf16[256,256]{0,1:T(8,128)(2,1)S(1)}, bf16[256,256]{0,1:T(8,128)(2,1)S(1)}, u32[]{:S(2)}, u32[]{:S(2)}) collective-permute-start(bf16[256,256]{0,1:T(8,128)(2,1)S(1)} %pad_maximum_fusion.4), channel_id=1, source_target_pairs={{0,8},{4,20},{8,0},{12,28},{16,24},{20,4},{24,16},{28,12},{1,9},{5... | collective-permute-start | bytes 393224 | tf_op jit(solution)/shard_map/ppermute | solution.py:75
  103.0 3.7 %collective-permute-start.8 = (bf16[128,256]{0,1:T(8,128)(2,1)S(1)}, bf16[128,256]{0,1:T(8,128)(2,1)S(1)}, u32[]{:S(2)}, u32[]{:S(2)}) collective-permute-start(bf16[128,256]{0,1:T(8,128)(2,1)S(1)} %slice.143), channel_id=1, source_target_pairs={{0,20},{4,8},{8,28},{12,0},{16,4},{20,24},{24,12},{28,16},{1,21},{... | collective-permute-start | bytes 196616 | tf_op jit(solution)/shard_map/ppermute | solution.py:81
  106.8 1.5 %collective-permute-start.9 = (bf16[384,256]{0,1:T(8,128)(2,1)S(1)}, bf16[384,256]{0,1:T(8,128)(2,1)S(1)}, u32[]{:S(2)}, u32[]{:S(2)}) collective-permute-start(bf16[384,256]{0,1:T(8,128)(2,1)S(1)} %pad_maximum_fusion.3), channel_id=1, source_target_pairs={{0,4},{4,0},{8,12},{12,8},{16,20},{20,16},{24,28},{28,24},{1,5},{5... | collective-permute-start | bytes 589832 | tf_op jit(solution)/shard_map/ppermute | solution.py:82

commit v2 on v0

--- a/solution.py
+++ b/solution.py
@@ -163,8 +163,12 @@
         ]
     )
 
-    q_pieces = gather_pieces(w_query, n_seq)
-    queries = project(normed, q_pieces).astype(jnp.bfloat16).reshape(tokens_here, heads_here, HEAD)
+    q_weights = lax.all_gather(w_query, "seq", axis=0, tiled=True)
+    queries = (
+        jnp.dot(normed, q_weights, preferred_element_type=jnp.float32)
+        .astype(jnp.bfloat16)
+        .reshape(tokens_here, heads_here, HEAD)
+    )
 
     def segment_of(positions):
         return jnp.sum((positions[:, None] > doc_ends[None, :]).astype(jnp.int32), axis=1)

time: 109 us -> 92.7 us (0.85)
  waiting for transfers between devices: 39.2 us -> 21.8 us
  between operations: 1.22 us -> 14.6 us
  other arithmetic: 15.1 us -> 8.21 us
  local copies, waits for them, and re-layouts: 10.8 us -> 6.67 us
  matrix products: 21.6 us -> 19.6 us
    ppermute x3 -> x2, waiting for transfers between devices: 14.8 us -> 2.23 us  [gather_pieces(): lax.ppermute(nb[:rows], 'seq', xor_perm(8, lambda j: j ^ 5 if j % 2 == 0...]
    ppermute x3 -> x2, waiting for transfers between devices: 11.7 us -> 2.55 us  [gather_pieces(): lax.ppermute(pair, 'seq', xor_perm(8, lambda j: j ^ 2 if j % 2 == 0 else...]
    dot_general x16 -> x8, matrix products: 9.69 us -> 3.59 us  [project(): term = jnp.dot(cols, piece, preferred_element_type=jnp.float32)]
    ppermute x3, waiting for transfers between devices: 2.38 us -> 7.73 us  [xor_reduce_scatter(): x = keep + lax.ppermute(send, axis, xor_perm(n, lambda j, k=k: j ^ k))]
    ppermute x2, waiting for transfers between devices: 5.78 us -> 1.72 us  [xor_gather_stack(): other = lax.ppermute(stack, axis, xor_perm(n, lambda j, k=k: j ^ k))]
    dot_general x0 -> x1, matrix products: none -> 3.53 us  [body(): jnp.dot(normed, q_weights, preferred_element_type=jnp.float32)]
    dynamic_slice x3, local copies, waits for them, and re-layouts: 2.69 us -> 0.03 us  [xor_reduce_scatter(): send = lax.dynamic_slice_in_dim(x, (1 - bit) * half, half, 1)]
    ppermute x5, waiting for transfers between devices: 2.87 us -> 5.43 us  [xor_all_reduce(): x = x + lax.ppermute(x, axis, xor_perm(n, lambda j, k=k: j ^ k))]
  transfers between devices with their start and end apart: 22 -> 19, of which waited for: 14 -> 11; matrix products, arithmetic and copies ran while one was open for 32% -> 24% of each run, Pallas kernels for 0% -> 0%
where the time goes in v2:
time: 92.7 us; the launch traced here: 92.3 us
  waiting for transfers between devices  21.8 us (24%)
  starting transfers between devices  21.3 us (23%)
  matrix products  19.6 us (21%)
  between operations  14.6 us (16%)
  other arithmetic  8.21 us (9%)
  local copies, waits for them, and re-layouts  6.67 us (7%)
    ppermute x5, starting transfers between devices, xor_all_reduce(): x = x + lax.ppermute(x, axis, xor_perm(n, lambda j, k=k: j ^ k))  8.87 us
    ppermute x3, waiting for transfers between devices, xor_reduce_scatter(): x = keep + lax.ppermute(send, axis, xor_perm(n, lambda j, k=k: j ^ k))  7.73 us
    ppermute x5, waiting for transfers between devices, xor_all_reduce(): x = x + lax.ppermute(x, axis, xor_perm(n, lambda j, k=k: j ^ k))  5.43 us
    dot_general x1, matrix products, body(): jnp.einsum('dc,rce->dre', critic_hidden, critic_down, preferred_element_t...  5.08 us
    unnamed x25, local copies, waits for them, and re-layouts  4.5 us
    ppermute x3, starting transfers between devices, xor_reduce_scatter(): x = keep + lax.ppermute(send, axis, xor_perm(n, lambda j, k=k: j ^ k))  4.14 us
    dot_general x8, matrix products, project(): term = jnp.dot(cols, piece, preferred_element_type=jnp.float32)  3.59 us
    dot_general x1, matrix products, body(): jnp.dot(normed, q_weights, preferred_element_type=jnp.float32)  3.53 us
  transfers between devices with their start and end apart: 19, of which 11 were waited for; matrix products, arithmetic and copies ran while one was open for 24% of the time, Pallas kernels for 0%

profile of v2, /device:TPU:0, one launch (start us, length us, event | category | flops | bytes accessed | tf_op | source)
XLA Modules:
  0.0 92.3 jit_solution(14732758478523165501)
XLA Ops:
  7.2 0.0 all-gather.2.cloned.1.call-start
  7.3 1.4 %constant_dynamic-slice_fusion.3 = (bf16[1024,32]{1,0:T(8,128)(2,1)S(1)}, bf16[1024,32]{1,0:T(8,128)(2,1)S(1)}) fusion(bf16[1024,128]{1,0:T(8,128)(2,1)} %param.13, s32[]{:T(128)S(6)} %select_n.131, bf16[1024,128]{1,0:T(8,128)(2,1)} %param.12), kind=kLoop, calls=%fused_computation.115 | loop fusion | bytes 262148 | tf_op jit(solution)/shard_map/dynamic_slice | solution.py:119
  8.7 0.1 copy.27
  8.8 0.1 copy.26
  8.9 0.6 collective-permute-start
  9.5 0.0 all-gather.2.cloned.1.call-update
  9.6 2.1 %fusion.1 = f32[128]{0:T(128)S(1)} fusion(bf16[128,8192]{1,0:T(8,128)(2,1)} %param.9), kind=kLoop, calls=%fused_computation.4 | loop fusion | flops 3145600 | bytes 2097664 | tf_op jit(solution)/shard_map/reduce_sum | solution.py:15
  11.7 0.2 reduce-window.7
  11.9 3.5 %fusion.3 = bf16[128,8192]{1,0:T(8,128)(2,1)} fusion(bf16[128,8192]{1,0:T(8,128)(2,1)} %param.9, f32[8192]{0:T(1024)S(1)} %convert_element_type.43, f32[128]{0:T(128)S(1)} %add_rsqrt_fusion), kind=kLoop, calls=%fused_computation.6 | loop fusion | flops 4194304 | bytes 4227584 | tf_op jit(solution)/shard_map/convert_element_type | solution.py:16
  15.5 2.0 %convolution_convert_fusion = bf16[8,8192]{1,0:T(8,128)(2,1)S(1)} fusion(bf16[128,8192]{1,0:T(8,128)(2,1)} %fusion.3, s32[128]{0:T(128)S(1)} %get-tuple-element.27, s32[8]{0:T(128)S(1)} %add_bitcast_fusion), kind=kOutput, calls=%fused_computation.1 | convolution fusion | flops 16843776 | bytes 2228768 | tf_op jit(solution)/shard_map/dot_general | solution.py:126
  17.6 2.6 %collective-permute-start.10 = (bf16[8,4096]{1,0:T(8,128)(2,1)S(1)}, bf16[8,4096]{1,0:T(8,128)(2,1)S(1)}, u32[]{:S(2)}, u32[]{:S(2)}) collective-permute-start(bf16[8,4096]{1,0:T(8,128)(2,1)S(1)} %constant_dynamic-slice_fusion.2), channel_id=1, source_target_pairs={{0,16},{4,20},{8,24},{12,28},{16,0},{20,4},{24,8},{28,12},{1,17},{... | collective-permute-start | bytes 196616 | tf_op jit(solution)/shard_map/ppermute | solution.py:41
  20.1 3.4 %collective-permute-done.10 = bf16[8,4096]{1,0:T(8,128)(2,1)S(1)} collective-permute-done((bf16[8,4096]{1,0:T(8,128)(2,1)S(1)}, bf16[8,4096]{1,0:T(8,128)(2,1)S(1)}, u32[]{:S(2)}, u32[]{:S(2)}) %collective-permute-start.10) | collective-permute-done | bytes 65568 | tf_op jit(solution)/shard_map/ppermute | solution.py:41
  23.6 1.5 %collective-permute-start.11 = (bf16[8,2048]{1,0:T(8,128)(2,1)S(1)}, bf16[8,2048]{1,0:T(8,128)(2,1)S(1)}, u32[]{:S(2)}, u32[]{:S(2)}) collective-permute-start(bf16[8,2048]{1,0:T(8,128)(2,1)S(1)} %constant_dynamic-slice_fusion.1), channel_id=1, source_target_pairs={{0,8},{4,12},{8,0},{12,4},{16,24},{20,28},{24,16},{28,20},{1,9},{5... | collective-permute-start | bytes 98312 | tf_op jit(solution)/shard_map/ppermute | solution.py:41
  25.1 0.1 convert_reduce_fusion
  25.2 3.2 %collective-permute-done.11 = bf16[8,2048]{1,0:T(8,128)(2,1)S(1)} collective-permute-done((bf16[8,2048]{1,0:T(8,128)(2,1)S(1)}, bf16[8,2048]{1,0:T(8,128)(2,1)S(1)}, u32[]{:S(2)}, u32[]{:S(2)}) %collective-permute-start.11) | collective-permute-done | bytes 32800 | tf_op jit(solution)/shard_map/ppermute | solution.py:41
  28.5 0.1 collective-permute-start.12
  28.5 0.1 convert_reduce_fusion.1
  28.6 1.1 %collective-permute-done.12 = bf16[8,1024]{1,0:T(8,128)(2,1)S(1)} collective-permute-done((bf16[8,1024]{1,0:T(8,128)(2,1)S(1)}, bf16[8,1024]{1,0:T(8,128)(2,1)S(1)}, u32[]{:S(2)}, u32[]{:S(2)}) %collective-permute-start.12) | collective-permute-done | bytes 16416 | tf_op jit(solution)/shard_map/ppermute | solution.py:41
  29.7 0.4 fusion.48
  30.1 0.2 collective-permute-start.13
  30.3 1.1 %collective-permute-start.1 = (bf16[2048,64]{0,1:T(8,128)(2,1)S(1)}, bf16[2048,64]{0,1:T(8,128)(2,1)S(1)}, u32[]{:S(2)}, u32[]{:S(2)}) collective-permute-start(bf16[2048,64]{0,1:T(8,128)(2,1)S(1)} %pad_maximum_fusion.1), channel_id=1, source_target_pairs={{0,8},{4,20},{8,0},{12,28},{16,24},{20,4},{24,16},{28,12},{1,9},{5... | collective-permute-start | bytes 786440 | tf_op jit(solution)/shard_map/ppermute | solution.py:76
  31.5 1.0 %collective-permute-start.14 = (f32[8,1152]{1,0:T(8,128)S(1)}, f32[8,1152]{1,0:T(8,128)S(1)}, u32[]{:S(2)}, u32[]{:S(2)}) collective-permute-start(f32[8,1152]{1,0:T(8,128)S(1)} %add.289), channel_id=1, source_target_pairs={{0,8},{4,12},{8,0},{12,4},{16,24},{20,28},{24,16},{28,20},{1,9},{5... | collective-permute-start | bytes 110600 | tf_op jit(solution)/shard_map/ppermute | solution.py:28
  32.5 1.2 %fusion.33 = f32[128,64]{0,1:T(8,128)S(1)} fusion(bf16[128,8192]{1,0:T(8,128)(2,1)} %fusion.3, s32[]{:T(128)S(6)} %select_n.128, bf16[1024,32]{0,1:T(8,128)(2,1)S(1)} %copy.27, bf16[1024,32]{0,1:T(8,128)(2,1)S(1)} %copy.26), kind=kOutput, calls=%fused_computation.45 | convolution fusion | flops 17039360 | bytes 425988 | tf_op jit(solution)/shard_map/dot_general | solution.py:98
  33.7 3.8 %collective-permute-done.14 = f32[8,1152]{1,0:T(8,128)S(1)} collective-permute-done((f32[8,1152]{1,0:T(8,128)S(1)}, f32[8,1152]{1,0:T(8,128)S(1)}, u32[]{:S(2)}, u32[]{:S(2)}) %collective-permute-start.14) | collective-permute-done | bytes 36896 | tf_op jit(solution)/shard_map/ppermute | solution.py:28
  37.6 3.4 %collective-permute-start.15 = (f32[8,1152]{1,0:T(8,128)S(1)}, f32[8,1152]{1,0:T(8,128)S(1)}, u32[]{:S(2)}, u32[]{:S(2)}) collective-permute-start(f32[8,1152]{1,0:T(8,128)S(1)} %add.290), channel_id=1, source_target_pairs={{0,16},{4,20},{8,24},{12,28},{16,0},{20,4},{24,8},{28,12},{1,17},{... | collective-permute-start | bytes 110600 | tf_op jit(solution)/shard_map/ppermute | solution.py:28
  40.9 1.2 %convolution_add_fusion.1 = f32[128,64]{0,1:T(8,128)S(1)} fusion(f32[128,64]{0,1:T(8,128)S(1)} %fusion.33, bf16[1024,64]{0,1:T(8,128)(2,1)S(1)} %collective-permute-done, bf16[128,8192]{1,0:T(8,128)(2,1)} %fusion.3, s32[]{:T(128)S(6)} %select_n.132), kind=kOutput, calls=%fused_computation.24 | convolution fusion | flops 16785408 | bytes 458756 | tf_op jit(solution)/shard_map/dot_general | solution.py:98
  42.1 0.1 collective-permute-start.2
  42.2 1.6 %collective-permute-done.15 = f32[8,1152]{1,0:T(8,128)S(1)} collective-permute-done((f32[8,1152]{1,0:T(8,128)S(1)}, f32[8,1152]{1,0:T(8,128)S(1)}, u32[]{:S(2)}, u32[]{:S(2)}) %collective-permute-start.15) | collective-permute-done | bytes 36896 | tf_op jit(solution)/shard_map/ppermute | solution.py:28
  43.8 5.1 %fusion.9 = f32[8,1024]{1,0:T(8,128)S(1)} fusion(bf16[4,1152,1024]{2,1,0:T(8,128)(2,1)} %param.16, pred[8,4]{0,1:T(4,128)(4,1)S(1)} %iota_compare_fusion, f32[8,1152]{1,0:T(8,128)S(1)} %add.290, f32[8,1152]{1,0:T(8,128)S(1)} %collective-permute-done.15), kind=kOutput, calls=%fused_computation.16 | convolution fusion | flops 75610112 | bytes 9543712 | tf_op jit(solution)/shard_map/dc,rce->dre/dot_general | solution.py:137
  48.9 1.5 %collective-permute-start.16 = (f32[8,1024]{1,0:T(8,128)S(1)}, f32[8,1024]{1,0:T(8,128)S(1)}, u32[]{:S(2)}, u32[]{:S(2)}) collective-permute-start(f32[8,1024]{1,0:T(8,128)S(1)} %fusion.9), channel_id=1, source_target_pairs={{0,1},{1,0},{2,3},{3,2},{4,5},{5,4},{6,7},{7,6},{8,9},{9,8},{10,11... | collective-permute-start | bytes 98312 | tf_op jit(solution)/shard_map/ppermute | solution.py:28
  50.4 0.1 collective-permute-start.3
  50.5 0.2 fusion.29
  50.7 0.2 fusion.27
  51.0 1.5 %collective-permute-done.3 = bf16[3072,64]{0,1:T(8,128)(2,1)S(1)} collective-permute-done((bf16[3072,64]{0,1:T(8,128)(2,1)S(1)}, bf16[3072,64]{0,1:T(8,128)(2,1)S(1)}, u32[]{:S(2)}, u32[]{:S(2)}) %collective-permute-start.3) | collective-permute-done | bytes 393248 | tf_op jit(solution)/shard_map/ppermute | solution.py:78
  52.5 0.2 fusion.21
  52.7 0.2 fusion.23
  52.9 0.2 fusion.25
  53.1 0.2 fusion.17
  53.4 0.4 collective-permute-start.4
  53.8 0.2 compare_and_fusion
  54.1 2.8 %collective-permute-start.17 = (f32[8,1024]{1,0:T(8,128)S(1)}, f32[8,1024]{1,0:T(8,128)S(1)}, u32[]{:S(2)}, u32[]{:S(2)}) collective-permute-start(f32[8,1024]{1,0:T(8,128)S(1)} %add.293), channel_id=1, source_target_pairs={{0,2},{1,3},{2,0},{3,1},{4,6},{5,7},{6,4},{7,5},{8,10},{9,11},{10,... | collective-permute-start | bytes 98312 | tf_op jit(solution)/shard_map/ppermute | solution.py:28
  56.8 0.4 collective-permute-done.4
  57.2 3.0 %collective-permute-start.5 = (bf16[2,128,64]{1,2,0:T(8,128)(2,1)S(1)}, bf16[2,128,64]{1,2,0:T(8,128)(2,1)S(1)}, u32[]{:S(2)}, u32[]{:S(2)}) collective-permute-start(bf16[2,128,64]{1,2,0:T(8,128)(2,1)S(1)} %maximum_select_fusion.1), channel_id=1, source_target_pairs={{0,2},{1,3},{2,0},{3,1},{4,6},{5,7},{6,4},{7,5},{8,10},{9,11},{10,... | collective-permute-start | bytes 98312 | tf_op jit(solution)/shard_map/ppermute | solution.py:51
  60.2 0.6 add_convert_fusion
  60.9 1.4 %collective-permute-done.5 = bf16[2,128,64]{1,2,0:T(8,128)(2,1)S(1)} collective-permute-done((bf16[2,128,64]{1,2,0:T(8,128)(2,1)S(1)}, bf16[2,128,64]{1,2,0:T(8,128)(2,1)S(1)}, u32[]{:S(2)}, u32[]{:S(2)}) %collective-permute-start.5) | collective-permute-done | bytes 32800 | tf_op jit(solution)/shard_map/ppermute | solution.py:51
  62.3 0.1 collective-permute-start.6
  62.4 0.6 constant_dynamic-update-slice_fusion.11
  63.1 0.6 constant_dynamic-update-slice_fusion.14
  63.7 1.8 %collective-permute-start.7 = (bf16[256,256]{0,1:T(8,128)(2,1)S(1)}, bf16[256,256]{0,1:T(8,128)(2,1)S(1)}, u32[]{:S(2)}, u32[]{:S(2)}) collective-permute-start(bf16[256,256]{0,1:T(8,128)(2,1)S(1)} %pad_maximum_fusion.4), channel_id=1, source_target_pairs={{0,8},{4,20},{8,0},{12,28},{16,24},{20,4},{24,16},{28,12},{1,9},{5... | collective-permute-start | bytes 393224 | tf_op jit(solution)/shard_map/ppermute | solution.py:76
  65.5 0.7 constant_dynamic-update-slice_fusion.10
  66.2 2.5 %collective-permute-done.7 = bf16[256,256]{0,1:T(8,128)(2,1)S(1)} collective-permute-done((bf16[256,256]{0,1:T(8,128)(2,1)S(1)}, bf16[256,256]{0,1:T(8,128)(2,1)S(1)}, u32[]{:S(2)}, u32[]{:S(2)}) %collective-permute-start.7) | collective-permute-done | bytes 131104 | tf_op jit(solution)/shard_map/ppermute | solution.py:76
  68.7 0.8 collective-permute-start.8
  69.5 0.7 slice_dynamic-update-slice_fusion.3
  70.2 2.2 %collective-permute-done.8 = bf16[128,256]{0,1:T(8,128)(2,1)S(1)} collective-permute-done((bf16[128,256]{0,1:T(8,128)(2,1)S(1)}, bf16[128,256]{0,1:T(8,128)(2,1)S(1)}, u32[]{:S(2)}, u32[]{:S(2)}) %collective-permute-start.8) | collective-permute-done | bytes 65568 | tf_op jit(solution)/shard_map/ppermute | solution.py:77
  72.5 0.2 collective-permute-start.9
  72.7 0.6 constant_dynamic-update-slice_fusion.9
  73.3 0.6 collective-permute-done.9
  74.0 0.7 slice_dynamic-update-slice_fusion.1
  74.7 3.5 %fusion.10 = bf16[16,2,8,128]{3,2,1,0:T(8,128)(2,1)S(1)} fusion(bf16[128,8192]{1,0:T(8,128)(2,1)} %fusion.3, bf16[8192,256]{1,0:T(8,128)(2,1)} %all-gather.2.cloned.1.call-done), kind=kOutput, calls=%fused_computation.17 | convolution fusion | flops 536903680 | bytes 6356992 | tf_op jit(solution)/shard_map/dot_general | solution.py:168
  78.2 0.6 copy-done.2
  78.9 1.3 %fusion.7 = f32[128,2,1024]{2,0,1:T(8,128)S(1)} fusion(pred[128,1024]{1,0:T(8,128)(4,1)S(1)} %compare_and_fusion, bf16[1024,128]{0,1:T(8,128)(2,1)} %get-tuple-element.8, bf16[16,2,8,128]{3,2,1,0:T(8,128)(2,1)S(1)} %fusion.10), kind=kOutput, calls=%fused_computation.11 | convolution fusion | flops 67633152 | bytes 1507328 | tf_op jit(solution)/shard_map/qhd,kd->qhk/dot_general | solution.py:183
  80.1 1.7 %fusion.69 = f32[128,2]{0,1:T(2,128)S(1)} fusion(pred[128,1024]{1,0:T(8,128)(4,1)S(1)} %compare_and_fusion, bf16[1024,128]{0,1:T(8,128)(2,1)} %get-tuple-element.8, bf16[16,2,8,128]{3,2,1,0:T(8,128)(2,1)} %copy-done.2), kind=kOutput, calls=%fused_computation.131 | convolution fusion | flops 68420608 | bytes 459776 | tf_op jit(solution)/shard_map/sub | solution.py:188
  81.8 2.0 %fusion.8 = bf16[128,2,128]{0,2,1:T(8,128)(2,1)} fusion(bf16[1024,128]{0,1:T(8,128)(2,1)} %get-tuple-element.9, f32[128,2,1024]{2,0,1:T(8,128)S(1)} %fusion.7, pred[128,1024]{1,0:T(8,128)(4,1)S(1)} %compare_and_fusion, f32[128,2]{0,1:T(2,128)S(1)} %fusion.69), kind=kOutput, calls=%fused_computation.14 | convolution fusion | flops 67962112 | bytes 1508352 | tf_op jit(solution)/shard_map/qhk,kd->qhd/dot_general | solution.py:190
  83.8 1.6 %copy.23 = bf16[128,256]{1,0:T(8,128)(2,1)} copy(bf16[128,256]{0,1:T(8,128)(2,1)} %bitcast.69) | data formatting | bytes 131072
  (58 shorter events, 0.4 us)
Async XLA Ops:
  7.2 22.5 %copy-start = (bf16[1024,1152]{1,0:T(8,128)(2,1)S(1)}, bf16[1024,1152]{1,0:T(8,128)(2,1)}, u32[]{:S(2)}) copy-start(bf16[1024,1152]{1,0:T(8,128)(2,1)} %param.15) | copy-start | bytes 7077892
  7.2 2.4 %copy-start.3 = (bf16[8192]{0:T(1024)(128)(2,1)S(1)}, bf16[8192]{0:T(1024)(128)(2,1)}, u32[]{:S(2)}) copy-start(bf16[8192]{0:T(1024)(128)(2,1)} %param.10) | copy-start | bytes 49156
  7.2 67.5 %all-gather.2.cloned.1.call-start = ((), (), s32[]{:S(2)}) async-start(), calls=%async_computation | async-start | bytes 4718592 | tf_op jit(solution)/shard_map/all_gather | solution.py:166
  8.7 3.1 %copy-start.4 = (s32[8]{0:T(128)S(1)}, s32[8]{0:T(128)}, u32[]{:S(2)}) copy-start(s32[8]{0:T(128)} %param.14) | copy-start | bytes 100
  8.9 21.4 %collective-permute-start = (bf16[1024,64]{0,1:T(8,128)(2,1)S(1)}, bf16[1024,64]{0,1:T(8,128)(2,1)S(1)}, u32[]{:S(2)}, u32[]{:S(2)}) collective-permute-start(bf16[1024,64]{0,1:T(8,128)(2,1)S(1)} %pad_maximum_fusion.3), channel_id=1, source_target_pairs={{0,4},{4,0},{8,12},{12,8},{16,20},{20,16},{24,28},{28,24},{1,5},{5... | collective-permute-start | bytes 393224 | tf_op jit(solution)/shard_map/ppermute | solution.py:74
  15.4 4.7 %copy-start.5 = (s32[8]{0:T(128)S(1)}, s32[8]{0:T(128)}, u32[]{:S(2)}) copy-start(s32[8]{0:T(128)} %param.17) | copy-start | bytes 100
  17.6 6.0 %collective-permute-start.10 = (bf16[8,4096]{1,0:T(8,128)(2,1)S(1)}, bf16[8,4096]{1,0:T(8,128)(2,1)S(1)}, u32[]{:S(2)}, u32[]{:S(2)}) collective-permute-start(bf16[8,4096]{1,0:T(8,128)(2,1)S(1)} %constant_dynamic-slice_fusion.2), channel_id=1, source_target_pairs={{0,16},{4,20},{8,24},{12,28},{16,0},{20,4},{24,8},{28,12},{1,17},{... | collective-permute-start | bytes 196616 | tf_op jit(solution)/shard_map/ppermute | solution.py:41
  23.6 4.8 %collective-permute-start.11 = (bf16[8,2048]{1,0:T(8,128)(2,1)S(1)}, bf16[8,2048]{1,0:T(8,128)(2,1)S(1)}, u32[]{:S(2)}, u32[]{:S(2)}) collective-permute-start(bf16[8,2048]{1,0:T(8,128)(2,1)S(1)} %constant_dynamic-slice_fusion.1), channel_id=1, source_target_pairs={{0,8},{4,12},{8,0},{12,4},{16,24},{20,28},{24,16},{28,20},{1,9},{5... | collective-permute-start | bytes 98312 | tf_op jit(solution)/shard_map/ppermute | solution.py:41
  28.5 1.2 %collective-permute-start.12 = (bf16[8,1024]{1,0:T(8,128)(2,1)S(1)}, bf16[8,1024]{1,0:T(8,128)(2,1)S(1)}, u32[]{:S(2)}, u32[]{:S(2)}) collective-permute-start(bf16[8,1024]{1,0:T(8,128)(2,1)S(1)} %constant_dynamic-slice_fusion), channel_id=1, source_target_pairs={{0,4},{4,0},{8,12},{12,8},{16,20},{20,16},{24,28},{28,24},{1,5},{5... | collective-permute-start | bytes 49160 | tf_op jit(solution)/shard_map/ppermute | solution.py:41
  30.1 1.3 %collective-permute-start.13 = (f32[8,1152]{1,0:T(8,128)S(1)}, f32[8,1152]{1,0:T(8,128)S(1)}, u32[]{:S(2)}, u32[]{:S(2)}) collective-permute-start(f32[8,1152]{1,0:T(8,128)S(1)} %fusion.48), channel_id=1, source_target_pairs={{0,4},{4,0},{8,12},{12,8},{16,20},{20,16},{24,28},{28,24},{1,5},{5... | collective-permute-start | bytes 110600 | tf_op jit(solution)/shard_map/ppermute | solution.py:28
  30.3 11.8 %collective-permute-start.1 = (bf16[2048,64]{0,1:T(8,128)(2,1)S(1)}, bf16[2048,64]{0,1:T(8,128)(2,1)S(1)}, u32[]{:S(2)}, u32[]{:S(2)}) collective-permute-start(bf16[2048,64]{0,1:T(8,128)(2,1)S(1)} %pad_maximum_fusion.1), channel_id=1, source_target_pairs={{0,8},{4,20},{8,0},{12,28},{16,24},{20,4},{24,16},{28,12},{1,9},{5... | collective-permute-start | bytes 786440 | tf_op jit(solution)/shard_map/ppermute | solution.py:76
  31.5 6.1 %collective-permute-start.14 = (f32[8,1152]{1,0:T(8,128)S(1)}, f32[8,1152]{1,0:T(8,128)S(1)}, u32[]{:S(2)}, u32[]{:S(2)}) collective-permute-start(f32[8,1152]{1,0:T(8,128)S(1)} %add.289), channel_id=1, source_target_pairs={{0,8},{4,12},{8,0},{12,4},{16,24},{20,28},{24,16},{28,20},{1,9},{5... | collective-permute-start | bytes 110600 | tf_op jit(solution)/shard_map/ppermute | solution.py:28
  37.6 6.2 %collective-permute-start.15 = (f32[8,1152]{1,0:T(8,128)S(1)}, f32[8,1152]{1,0:T(8,128)S(1)}, u32[]{:S(2)}, u32[]{:S(2)}) collective-permute-start(f32[8,1152]{1,0:T(8,128)S(1)} %add.290), channel_id=1, source_target_pairs={{0,16},{4,20},{8,24},{12,28},{16,0},{20,4},{24,8},{28,12},{1,17},{... | collective-permute-start | bytes 110600 | tf_op jit(solution)/shard_map/ppermute | solution.py:28
  42.1 8.4 %copy-start.1 = (bf16[128,8192]{1,0:T(8,128)(2,1)S(1)}, bf16[128,8192]{1,0:T(8,128)(2,1)}, u32[]{:S(2)}) copy-start(bf16[128,8192]{1,0:T(8,128)(2,1)} %fusion.3) | copy-start | bytes 6291460
  42.1 8.2 %collective-permute-start.2 = (bf16[1024,64]{0,1:T(8,128)(2,1)S(1)}, bf16[1024,64]{0,1:T(8,128)(2,1)S(1)}, u32[]{:S(2)}, u32[]{:S(2)}) collective-permute-start(bf16[1024,64]{0,1:T(8,128)(2,1)S(1)} %slice.118), channel_id=1, source_target_pairs={{0,20},{4,8},{8,28},{12,0},{16,4},{20,24},{24,12},{28,16},{1,21},{... | collective-permute-start | bytes 393224 | tf_op jit(solution)/shard_map/ppermute | solution.py:77
  48.9 5.2 %collective-permute-start.16 = (f32[8,1024]{1,0:T(8,128)S(1)}, f32[8,1024]{1,0:T(8,128)S(1)}, u32[]{:S(2)}, u32[]{:S(2)}) collective-permute-start(f32[8,1024]{1,0:T(8,128)S(1)} %fusion.9), channel_id=1, source_target_pairs={{0,1},{1,0},{2,3},{3,2},{4,5},{5,4},{6,7},{7,6},{8,9},{9,8},{10,11... | collective-permute-start | bytes 98312 | tf_op jit(solution)/shard_map/ppermute | solution.py:28
  50.4 2.1 %collective-permute-start.3 = (bf16[3072,64]{0,1:T(8,128)(2,1)S(1)}, bf16[3072,64]{0,1:T(8,128)(2,1)S(1)}, u32[]{:S(2)}, u32[]{:S(2)}) collective-permute-start(bf16[3072,64]{0,1:T(8,128)(2,1)S(1)} %pad_maximum_fusion), channel_id=1, source_target_pairs={{0,4},{4,0},{8,12},{12,8},{16,20},{20,16},{24,28},{28,24},{1,5},{5... | collective-permute-start | bytes 1179656 | tf_op jit(solution)/shard_map/ppermute | solution.py:78
  53.4 3.8 %collective-permute-start.4 = (bf16[1,128,64]{1,2,0:T(8,128)(2,1)S(1)}, bf16[1,128,64]{1,2,0:T(8,128)(2,1)S(1)}, u32[]{:S(2)}, u32[]{:S(2)}) collective-permute-start(bf16[1,128,64]{1,2,0:T(8,128)(2,1)S(1)} %fusion.17), channel_id=1, source_target_pairs={{0,1},{1,0},{2,3},{3,2},{4,5},{5,4},{6,7},{7,6},{8,9},{9,8},{10,11... | collective-permute-start | bytes 49160 | tf_op jit(solution)/shard_map/ppermute | solution.py:51
  54.1 6.2 %collective-permute-start.17 = (f32[8,1024]{1,0:T(8,128)S(1)}, f32[8,1024]{1,0:T(8,128)S(1)}, u32[]{:S(2)}, u32[]{:S(2)}) collective-permute-start(f32[8,1024]{1,0:T(8,128)S(1)} %add.293), channel_id=1, source_target_pairs={{0,2},{1,3},{2,0},{3,1},{4,6},{5,7},{6,4},{7,5},{8,10},{9,11},{10,... | collective-permute-start | bytes 98312 | tf_op jit(solution)/shard_map/ppermute | solution.py:28
  57.2 5.0 %collective-permute-start.5 = (bf16[2,128,64]{1,2,0:T(8,128)(2,1)S(1)}, bf16[2,128,64]{1,2,0:T(8,128)(2,1)S(1)}, u32[]{:S(2)}, u32[]{:S(2)}) collective-permute-start(bf16[2,128,64]{1,2,0:T(8,128)(2,1)S(1)} %maximum_select_fusion.1), channel_id=1, source_target_pairs={{0,2},{1,3},{2,0},{3,1},{4,6},{5,7},{6,4},{7,5},{8,10},{9,11},{10,... | collective-permute-start | bytes 98312 | tf_op jit(solution)/shard_map/ppermute | solution.py:51
  62.3 1.3 %collective-permute-start.6 = (bf16[128,256]{0,1:T(8,128)(2,1)S(1)}, bf16[128,256]{0,1:T(8,128)(2,1)S(1)}, u32[]{:S(2)}, u32[]{:S(2)}) collective-permute-start(bf16[128,256]{0,1:T(8,128)(2,1)S(1)} %constant_dynamic-update-slice_fusion.1), channel_id=1, source_target_pairs={{0,4},{4,0},{8,12},{12,8},{16,20},{20,16},{24,28},{28,24},{1,5},{5... | collective-permute-start | bytes 196616 | tf_op jit(solution)/shard_map/ppermute | solution.py:74
  63.7 5.0 %collective-permute-start.7 = (bf16[256,256]{0,1:T(8,128)(2,1)S(1)}, bf16[256,256]{0,1:T(8,128)(2,1)S(1)}, u32[]{:S(2)}, u32[]{:S(2)}) collective-permute-start(bf16[256,256]{0,1:T(8,128)(2,1)S(1)} %pad_maximum_fusion.4), channel_id=1, source_target_pairs={{0,8},{4,20},{8,0},{12,28},{16,24},{20,4},{24,16},{28,12},{1,9},{5... | collective-permute-start | bytes 393224 | tf_op jit(solution)/shard_map/ppermute | solution.py:76
  68.7 3.7 %collective-permute-start.8 = (bf16[128,256]{0,1:T(8,128)(2,1)S(1)}, bf16[128,256]{0,1:T(8,128)(2,1)S(1)}, u32[]{:S(2)}, u32[]{:S(2)}) collective-permute-start(bf16[128,256]{0,1:T(8,128)(2,1)S(1)} %slice.133), channel_id=1, source_target_pairs={{0,20},{4,8},{8,28},{12,0},{16,4},{20,24},{24,12},{28,16},{1,21},{... | collective-permute-start | bytes 196616 | tf_op jit(solution)/shard_map/ppermute | solution.py:77
  72.5 1.5 %collective-permute-start.9 = (bf16[384,256]{0,1:T(8,128)(2,1)S(1)}, bf16[384,256]{0,1:T(8,128)(2,1)S(1)}, u32[]{:S(2)}, u32[]{:S(2)}) collective-permute-start(bf16[384,256]{0,1:T(8,128)(2,1)S(1)} %pad_maximum_fusion.2), channel_id=1, source_target_pairs={{0,4},{4,0},{8,12},{12,8},{16,20},{20,16},{24,28},{28,24},{1,5},{5... | collective-permute-start | bytes 589832 | tf_op jit(solution)/shard_map/ppermute | solution.py:78
  78.2 0.6 copy-start.2
Sparse Core Ops, SparseCore 0:
  9.9 42.7 all-gather.1

commit v3 on v2

--- a/solution.py
+++ b/solution.py
@@ -43,22 +43,6 @@
     return x
 
 
-def xor_gather_stack(x, axis, n, size):
-    i = lax.axis_index(axis)
-    stack = x[None]
-    k = 1
-    while k < size:
-        other = lax.ppermute(stack, axis, xor_perm(n, lambda j, k=k: j ^ k))
-        low = (i // k) % 2 == 0
-        stack = jnp.where(
-            low,
-            jnp.concatenate([stack, other], axis=0),
-            jnp.concatenate([other, stack], axis=0),
-        )
-        k = k * 2
-    return stack
-
-
 def power_of_two(n):
     return n & (n - 1) == 0
 
@@ -67,8 +51,8 @@
     i = lax.axis_index("seq")
     rows = blk.shape[0]
     if n != 8:
-        full = lax.all_gather(blk, "seq", axis=0, tiled=True)
-        return [(full, jnp.int32(0), n * rows)]
+        full = lax.all_gather(blk, "seq", axis=0, tiled=False)
+        return [(full[m], m, rows) for m in range(n)]
     core = i % 2
     chip = i // 2
     sib = lax.ppermute(blk, "seq", xor_perm(8, lambda j: j ^ 1))
@@ -91,10 +75,10 @@
     ]
 
 
-def project(normed, pieces):
+def project(normed, pieces, stride, offset=0):
     total = None
     for piece, source, rows in pieces:
-        cols = lax.dynamic_slice_in_dim(normed, source * rows, rows, 1)
+        cols = lax.dynamic_slice_in_dim(normed, source * stride + offset, rows, 1)
         term = jnp.dot(cols, piece, preferred_element_type=jnp.float32)
         total = term if total is None else total + term
     return total
@@ -109,15 +93,19 @@
     tp_i = lax.axis_index("tp")
     normed = rms_norm(hidden, norm_gain)
     tokens_here = hidden.shape[0]
+    d_rows = w_query.shape[0]
     heads_here = w_query.shape[1] // HEAD
     sharers = GROUP // heads_here
-    kv_width = HEAD // sharers
+    kv_rows_here = d_rows // sharers
     kv_head = tp_i * heads_here // GROUP
     kv_part = tp_i % sharers
-    kv_start = kv_head * HEAD + kv_part * kv_width
-    key_cols = lax.dynamic_slice_in_dim(w_key, kv_start, kv_width, 1)
-    value_cols = lax.dynamic_slice_in_dim(w_value, kv_start, kv_width, 1)
-    kv_weights = jnp.concatenate([key_cols, value_cols], axis=1)
+    kv_weights = jnp.concatenate(
+        [
+            lax.dynamic_slice(w_key, (kv_part * kv_rows_here, kv_head * HEAD), (kv_rows_here, HEAD)),
+            lax.dynamic_slice(w_value, (kv_part * kv_rows_here, kv_head * HEAD), (kv_rows_here, HEAD)),
+        ],
+        axis=1,
+    )
 
     doc_ends = jnp.cumsum(doc_lengths) - 1
     first_row = seq_i * tokens_here
@@ -146,13 +134,13 @@
     critic_values = critic_sum.astype(jnp.bfloat16)
 
     kv_pieces = gather_pieces(kv_weights, n_seq)
-    kv_own = project(normed, kv_pieces).astype(jnp.bfloat16)
-    kv_stack = xor_gather_stack(kv_own, "tp", n_tp, sharers)
-    kv_rows = jnp.concatenate(
-        [kv_stack[m, :, :kv_width] for m in range(sharers)]
-        + [kv_stack[m, :, kv_width:] for m in range(sharers)],
-        axis=1,
-    )
+    kv_part_sum = project(normed, kv_pieces, d_rows, kv_part * kv_rows_here)
+    kv_rows = kv_part_sum
+    k = 1
+    while k < sharers:
+        kv_rows = kv_rows + lax.ppermute(kv_rows, "tp", xor_perm(n_tp, lambda j, k=k: j ^ k))
+        k *= 2
+    kv_rows = kv_rows.astype(jnp.bfloat16)
     kv_all = gather_pieces(kv_rows, n_seq)
     key_block = jnp.concatenate([piece[:, :HEAD] for piece, _, _ in kv_all], axis=0)
     value_block = jnp.concatenate([piece[:, HEAD:] for piece, _, _ in kv_all], axis=0)
@@ -178,26 +166,21 @@
     allowed = (query_seg[:, None] == segment_of(key_pos)[None, :]) & (
         key_pos[None, :] <= query_pos[:, None]
     )
-    allowed = allowed[:, None, :]
-    scores = (
-        jnp.einsum("qhd,kd->qhk", queries, key_block, preferred_element_type=jnp.float32)
-        * inverse_root
-    )
-    scores = jnp.where(allowed, scores, -1e30)
-    maxima = jnp.max(scores, axis=2)
-    expanded = jnp.where(allowed, jnp.exp(scores - maxima[:, :, None]), 0.0)
-    totals = jnp.sum(expanded, axis=2)
-    weighted = jnp.einsum(
-        "qhk,kd->qhd",
-        expanded.astype(jnp.bfloat16),
-        value_block,
-        preferred_element_type=jnp.float32,
-    )
-    attention = (
-        (weighted / totals[:, :, None])
-        .reshape(tokens_here, heads_here * HEAD)
-        .astype(jnp.bfloat16)
-    )
+    outs = []
+    for h in range(heads_here):
+        scores = (
+            jnp.dot(queries[:, h, :], key_block.T, preferred_element_type=jnp.float32)
+            * inverse_root
+        )
+        scores = jnp.where(allowed, scores, -1e30)
+        maxima = jnp.max(scores, axis=1, keepdims=True)
+        expanded = jnp.where(allowed, jnp.exp(scores - maxima), 0.0)
+        totals = jnp.sum(expanded, axis=1, keepdims=True)
+        weighted = jnp.dot(
+            expanded.astype(jnp.bfloat16), value_block, preferred_element_type=jnp.float32
+        )
+        outs.append((weighted / totals).astype(jnp.bfloat16))
+    attention = jnp.concatenate(outs, axis=1)
     return (attention, critic_values)
 
 

time: 92.7 us -> 96.7 us (1.043)
  waiting for transfers between devices: 21.8 us -> 28.1 us
  local copies, waits for them, and re-layouts: 6.67 us -> 1.89 us
  starting transfers between devices: 21.3 us -> 23.1 us
    ppermute x2, waiting for transfers between devices: 1.72 us -> 7.37 us  [body(): lax.ppermute(kv_rows, 'tp', xor_perm(n_tp, lambda j, k=k: j ^ k))]
    dot_general x8, matrix products: 3.59 us -> 8.02 us  [project(): term = jnp.dot(cols, piece, preferred_element_type=jnp.float32)]
    unnamed x25 -> x11, local copies, waits for them, and re-layouts: 4.5 us -> 0.81 us
    dot_general x2 -> x4, matrix products: 3.31 us -> 1.44 us  [the longest x2 0.76 us: body(): jnp.dot(expanded.astype(jnp.bfloat16), value_block, preferred_element_typ...]
    sub x1 -> x0, matrix products: 1.66 us -> none  [body(): expanded = jnp.where(allowed, jnp.exp(scores - maxima[:, :, None]), 0.0)]
    ppermute x3, waiting for transfers between devices: 7.73 us -> 6.32 us  [xor_reduce_scatter(): x = keep + lax.ppermute(send, axis, xor_perm(n, lambda j, k=k: j ^ k))]
    unnamed x10 -> x8, other arithmetic: 1.3 us -> 0.06 us
    ppermute x2, waiting for transfers between devices: 0.01 us -> 1.23 us  [gather_pieces(): sib = lax.ppermute(blk, 'seq', xor_perm(8, lambda j: j ^ 1))]
  transfers between devices with their start and end apart: 19 -> 19, of which waited for: 11 -> 11; matrix products, arithmetic and copies ran while one was open for 24% -> 25% of each run, Pallas kernels for 0% -> 0%
where the time goes in v3:
time: 96.7 us; the launch traced here: 96 us
  waiting for transfers between devices  28.1 us (29%)
  starting transfers between devices  23.1 us (24%)
  matrix products  20.5 us (21%)
  between operations  14.6 us (15%)
  other arithmetic  7.91 us (8%)
  local copies, waits for them, and re-layouts  1.89 us (2%)
    ppermute x5, starting transfers between devices, xor_all_reduce(): x = x + lax.ppermute(x, axis, xor_perm(n, lambda j, k=k: j ^ k))  8.86 us
    dot_general x8, matrix products, project(): term = jnp.dot(cols, piece, preferred_element_type=jnp.float32)  8.02 us
    ppermute x2, waiting for transfers between devices, body(): lax.ppermute(kv_rows, 'tp', xor_perm(n_tp, lambda j, k=k: j ^ k))  7.37 us
    ppermute x3, waiting for transfers between devices, xor_reduce_scatter(): x = keep + lax.ppermute(send, axis, xor_perm(n, lambda j, k=k: j ^ k))  6.32 us
    ppermute x5, waiting for transfers between devices, xor_all_reduce(): x = x + lax.ppermute(x, axis, xor_perm(n, lambda j, k=k: j ^ k))  5.74 us
    dot_general x1, matrix products, body(): jnp.einsum('dc,rce->dre', critic_hidden, critic_down, preferred_element_t...  5.08 us
    ppermute x3, starting transfers between devices, xor_reduce_scatter(): x = keep + lax.ppermute(send, axis, xor_perm(n, lambda j, k=k: j ^ k))  4.59 us
    ppermute x2, starting transfers between devices, body(): lax.ppermute(kv_rows, 'tp', xor_perm(n_tp, lambda j, k=k: j ^ k))  3.65 us
  transfers between devices with their start and end apart: 19, of which 11 were waited for; matrix products, arithmetic and copies ran while one was open for 25% of the time, Pallas kernels for 0%

profile of v3, /device:TPU:0, one launch (start us, length us, event | category | flops | bytes accessed | tf_op | source)
XLA Modules:
  0.0 96.0 jit_solution(6502058154496584416)
XLA Ops:
  7.2 0.0 copy-start
  7.2 0.0 all-gather.2.cloned.1.call-start
  7.2 0.7 all-gather.2.cloned.1.call-update
  8.0 0.7 convert_element_type.46
  8.7 2.1 %fusion = f32[128]{0:T(128)S(1)} fusion(bf16[128,8192]{1,0:T(8,128)(2,1)} %param.9), kind=kLoop, calls=%fused_computation.3 | loop fusion | flops 3145600 | bytes 2097664 | tf_op jit(solution)/shard_map/reduce_sum | solution.py:15
  10.8 0.2 reduce-window.7
  11.0 3.5 %fusion.2 = bf16[128,8192]{1,0:T(8,128)(2,1)} fusion(bf16[128,8192]{1,0:T(8,128)(2,1)} %param.9, f32[8192]{0:T(1024)S(1)} %convert_element_type.46, f32[128]{0:T(128)S(1)} %add_rsqrt_fusion), kind=kLoop, calls=%fused_computation.5 | loop fusion | flops 4194304 | bytes 4227584 | tf_op jit(solution)/shard_map/convert_element_type | solution.py:16
  14.6 2.0 %convolution_convert_fusion = bf16[8,8192]{1,0:T(8,128)(2,1)S(1)} fusion(bf16[128,8192]{1,0:T(8,128)(2,1)} %fusion.2, s32[128]{0:T(128)S(1)} %get-tuple-element.29, s32[8]{0:T(128)S(1)} %add_bitcast_fusion), kind=kOutput, calls=%fused_computation | convolution fusion | flops 16843776 | bytes 2228768 | tf_op jit(solution)/shard_map/dot_general | solution.py:114
  16.7 3.1 %collective-permute-start.10 = (bf16[8,4096]{1,0:T(8,128)(2,1)S(1)}, bf16[8,4096]{1,0:T(8,128)(2,1)S(1)}, u32[]{:S(2)}, u32[]{:S(2)}) collective-permute-start(bf16[8,4096]{1,0:T(8,128)(2,1)S(1)} %constant_dynamic-slice_fusion.2), channel_id=1, source_target_pairs={{0,16},{4,20},{8,24},{12,28},{16,0},{20,4},{24,8},{28,12},{1,17},{... | collective-permute-start | bytes 196616 | tf_op jit(solution)/shard_map/ppermute | solution.py:41
  19.7 0.9 constant_dynamic-slice_fusion.3
  20.6 2.0 %collective-permute-done.10 = bf16[8,4096]{1,0:T(8,128)(2,1)S(1)} collective-permute-done((bf16[8,4096]{1,0:T(8,128)(2,1)S(1)}, bf16[8,4096]{1,0:T(8,128)(2,1)S(1)}, u32[]{:S(2)}, u32[]{:S(2)}) %collective-permute-start.10) | collective-permute-done | bytes 65568 | tf_op jit(solution)/shard_map/ppermute | solution.py:41
  22.6 1.5 %collective-permute-start.11 = (bf16[8,2048]{1,0:T(8,128)(2,1)S(1)}, bf16[8,2048]{1,0:T(8,128)(2,1)S(1)}, u32[]{:S(2)}, u32[]{:S(2)}) collective-permute-start(bf16[8,2048]{1,0:T(8,128)(2,1)S(1)} %constant_dynamic-slice_fusion.1), channel_id=1, source_target_pairs={{0,8},{4,12},{8,0},{12,4},{16,24},{20,28},{24,16},{28,20},{1,9},{5... | collective-permute-start | bytes 98312 | tf_op jit(solution)/shard_map/ppermute | solution.py:41
  24.1 0.1 collective-permute-start
  24.2 3.2 %collective-permute-done.11 = bf16[8,2048]{1,0:T(8,128)(2,1)S(1)} collective-permute-done((bf16[8,2048]{1,0:T(8,128)(2,1)S(1)}, bf16[8,2048]{1,0:T(8,128)(2,1)S(1)}, u32[]{:S(2)}, u32[]{:S(2)}) %collective-permute-start.11) | collective-permute-done | bytes 32800 | tf_op jit(solution)/shard_map/ppermute | solution.py:41
  27.5 0.1 collective-permute-start.12
  27.6 1.1 %collective-permute-done.12 = bf16[8,1024]{1,0:T(8,128)(2,1)S(1)} collective-permute-done((bf16[8,1024]{1,0:T(8,128)(2,1)S(1)}, bf16[8,1024]{1,0:T(8,128)(2,1)S(1)}, u32[]{:S(2)}, u32[]{:S(2)}) %collective-permute-start.12) | collective-permute-done | bytes 16416 | tf_op jit(solution)/shard_map/ppermute | solution.py:41
  28.7 0.4 fusion.42
  29.1 0.2 collective-permute-start.13
  29.3 0.0 collective-permute-done
  29.3 1.5 %collective-permute-start.1 = (bf16[512,256]{1,0:T(8,128)(2,1)S(1)}, bf16[512,256]{1,0:T(8,128)(2,1)S(1)}, u32[]{:S(2)}, u32[]{:S(2)}) collective-permute-start(bf16[512,256]{1,0:T(8,128)(2,1)S(1)} %pad_maximum_fusion.1), channel_id=1, source_target_pairs={{0,8},{4,20},{8,0},{12,28},{16,24},{20,4},{24,16},{28,12},{1,9},{5... | collective-permute-start | bytes 786440 | tf_op jit(solution)/shard_map/ppermute | solution.py:60
  30.8 0.0 collective-permute-done.13
  30.8 0.9 collective-permute-start.14
  31.7 1.0 %fusion.39 = f32[128,256]{1,0:T(8,128)S(1)} fusion(bf16[128,8192]{1,0:T(8,128)(2,1)} %fusion.2, s32[]{:T(128)S(6)} %select_n.102, bf16[256,128]{1,0:T(8,128)(2,1)S(1)} %get-tuple-element.26, bf16[256,128]{1,0:T(8,128)(2,1)S(1)} %get-tuple-element.27), kind=kOutput, calls=%fused_computation.63 | convolution fusion | flops 17039360 | bytes 327684 | tf_op jit(solution)/shard_map/dot_general | solution.py:82
  32.8 4.0 %collective-permute-done.14 = f32[8,1152]{1,0:T(8,128)S(1)} collective-permute-done((f32[8,1152]{1,0:T(8,128)S(1)}, f32[8,1152]{1,0:T(8,128)S(1)}, u32[]{:S(2)}, u32[]{:S(2)}) %collective-permute-start.14) | collective-permute-done | bytes 36896 | tf_op jit(solution)/shard_map/ppermute | solution.py:28
  36.8 3.4 %collective-permute-start.15 = (f32[8,1152]{1,0:T(8,128)S(1)}, f32[8,1152]{1,0:T(8,128)S(1)}, u32[]{:S(2)}, u32[]{:S(2)}) collective-permute-start(f32[8,1152]{1,0:T(8,128)S(1)} %add.318), channel_id=1, source_target_pairs={{0,16},{4,20},{8,24},{12,28},{16,0},{20,4},{24,8},{28,12},{1,17},{... | collective-permute-start | bytes 110600 | tf_op jit(solution)/shard_map/ppermute | solution.py:28
  40.2 1.0 %convolution_add_fusion.1 = f32[128,256]{1,0:T(8,128)S(1)} fusion(f32[128,256]{1,0:T(8,128)S(1)} %fusion.39, bf16[256,256]{1,0:T(8,128)(2,1)S(1)} %collective-permute-done, bf16[128,8192]{1,0:T(8,128)(2,1)} %fusion.2, s32[]{:T(128)S(6)} %select_n.104), kind=kOutput, calls=%fused_computation.12 | convolution fusion | flops 16809984 | bytes 458756 | tf_op jit(solution)/shard_map/dot_general | solution.py:82
  41.2 0.1 collective-permute-start.2
  41.3 1.8 %collective-permute-done.15 = f32[8,1152]{1,0:T(8,128)S(1)} collective-permute-done((f32[8,1152]{1,0:T(8,128)S(1)}, f32[8,1152]{1,0:T(8,128)S(1)}, u32[]{:S(2)}, u32[]{:S(2)}) %collective-permute-start.15) | collective-permute-done | bytes 36896 | tf_op jit(solution)/shard_map/ppermute | solution.py:28
  43.0 5.1 %fusion.10 = f32[8,1024]{1,0:T(8,128)S(1)} fusion(bf16[4,1152,1024]{2,1,0:T(8,128)(2,1)} %param.16, pred[8,4]{0,1:T(4,128)(4,1)S(1)} %iota_compare_fusion, f32[8,1152]{1,0:T(8,128)S(1)} %add.318, f32[8,1152]{1,0:T(8,128)S(1)} %collective-permute-done.15), kind=kOutput, calls=%fused_computation.19 | convolution fusion | flops 75610112 | bytes 9543712 | tf_op jit(solution)/shard_map/dc,rce->dre/dot_general | solution.py:125
  48.1 1.2 %collective-permute-start.16 = (f32[8,1024]{1,0:T(8,128)S(1)}, f32[8,1024]{1,0:T(8,128)S(1)}, u32[]{:S(2)}, u32[]{:S(2)}) collective-permute-start(f32[8,1024]{1,0:T(8,128)S(1)} %fusion.10), channel_id=1, source_target_pairs={{0,1},{1,0},{2,3},{3,2},{4,5},{5,4},{6,7},{7,6},{8,9},{9,8},{10,11... | collective-permute-start | bytes 98312 | tf_op jit(solution)/shard_map/ppermute | solution.py:28
  49.3 0.0 collective-permute-done.2
  49.3 0.6 collective-permute-start.3
  50.0 1.0 %fusion.29 = f32[128,256]{1,0:T(8,128)S(1)} fusion(bf16[512,256]{1,0:T(8,128)(2,1)S(1)} %collective-permute-done.1, bf16[128,8192]{1,0:T(8,128)(2,1)} %fusion.2, s32[]{:T(128)S(6)} %select_n.106), kind=kOutput, calls=%fused_computation.44 | convolution fusion | flops 16777216 | bytes 327684 | tf_op jit(solution)/shard_map/dot_general | solution.py:82
  51.0 1.0 %fusion.34 = f32[128,256]{1,0:T(8,128)S(1)} fusion(bf16[256,256]{1,0:T(8,128)(2,1)S(1)} %collective-permute-done.2, bf16[128,8192]{1,0:T(8,128)(2,1)} %fusion.2, s32[]{:T(128)S(6)} %select_n.107), kind=kOutput, calls=%fused_computation.58 | convolution fusion | flops 16777216 | bytes 327684 | tf_op jit(solution)/shard_map/dot_general | solution.py:82
  52.0 1.0 %fusion.23 = f32[128,256]{1,0:T(8,128)S(1)} fusion(bf16[768,256]{1,0:T(8,128)(2,1)S(1)} %collective-permute-done.3, bf16[128,8192]{1,0:T(8,128)(2,1)} %fusion.2, s32[]{:T(128)S(6)} %select_n.110), kind=kOutput, calls=%fused_computation.38 | convolution fusion | flops 16777216 | bytes 327684 | tf_op jit(solution)/shard_map/dot_general | solution.py:82
  53.0 1.0 %fusion.25 = f32[128,256]{1,0:T(8,128)S(1)} fusion(bf16[768,256]{1,0:T(8,128)(2,1)S(1)} %collective-permute-done.3, bf16[128,8192]{1,0:T(8,128)(2,1)} %fusion.2, s32[]{:T(128)S(6)} %select_n.109), kind=kOutput, calls=%fused_computation.40 | convolution fusion | flops 16777216 | bytes 327684 | tf_op jit(solution)/shard_map/dot_general | solution.py:82
  54.0 1.0 %fusion.27 = f32[128,256]{1,0:T(8,128)S(1)} fusion(bf16[768,256]{1,0:T(8,128)(2,1)S(1)} %collective-permute-done.3, bf16[128,8192]{1,0:T(8,128)(2,1)} %fusion.2, s32[]{:T(128)S(6)} %select_n.108), kind=kOutput, calls=%fused_computation.42 | convolution fusion | flops 16777216 | bytes 327684 | tf_op jit(solution)/shard_map/dot_general | solution.py:82
  55.0 1.0 %fusion.9 = f32[128,256]{1,0:T(8,128)S(1)} fusion(f32[128,256]{1,0:T(8,128)S(1)} %fusion.23, f32[128,256]{1,0:T(8,128)S(1)} %fusion.25, f32[128,256]{1,0:T(8,128)S(1)} %fusion.27, f32[128,256]{1,0:T(8,128)S(1)} %fusion.34, f32[128,256]{1,0:T(8,128)S(1)} %fusion.29, f32[128,256]{1,0:T(8,128)S(1)} %convolution_add_fusion.1, bf16[128,8192]{1,0:T(8,128)(2,1)} %fusion.2, ...), kind=kOutput, calls=%fused_computation.17 | convolution fusion | flops 16973824 | bytes 1114116 | tf_op jit(solution)/shard_map/dot_general | solution.py:82
  56.0 0.4 collective-permute-start.4
  56.4 0.1 convert_reduce_fusion
  56.5 3.1 %collective-permute-start.17 = (f32[8,1024]{1,0:T(8,128)S(1)}, f32[8,1024]{1,0:T(8,128)S(1)}, u32[]{:S(2)}, u32[]{:S(2)}) collective-permute-start(f32[8,1024]{1,0:T(8,128)S(1)} %add.321), channel_id=1, source_target_pairs={{0,2},{1,3},{2,0},{3,1},{4,6},{5,7},{6,4},{7,5},{8,10},{9,11},{10,... | collective-permute-start | bytes 98312 | tf_op jit(solution)/shard_map/ppermute | solution.py:28
  59.7 0.1 convert_reduce_fusion.1
  59.8 2.5 %collective-permute-done.4 = f32[128,256]{1,0:T(8,128)S(1)} collective-permute-done((f32[128,256]{1,0:T(8,128)S(1)}, f32[128,256]{1,0:T(8,128)S(1)}, u32[]{:S(2)}, u32[]{:S(2)}) %collective-permute-start.4) | collective-permute-done | bytes 131104 | tf_op jit(solution)/shard_map/ppermute | solution.py:141
  62.2 3.3 %collective-permute-start.5 = (f32[128,256]{1,0:T(8,128)S(1)}, f32[128,256]{1,0:T(8,128)S(1)}, u32[]{:S(2)}, u32[]{:S(2)}) collective-permute-start(f32[128,256]{1,0:T(8,128)S(1)} %add.304), channel_id=1, source_target_pairs={{0,2},{1,3},{2,0},{3,1},{4,6},{5,7},{6,4},{7,5},{8,10},{9,11},{10,... | collective-permute-start | bytes 393224 | tf_op jit(solution)/shard_map/ppermute | solution.py:141
  65.5 0.0 collective-permute-done.17
  65.5 0.6 add_convert_fusion.1
  66.1 4.9 %collective-permute-done.5 = f32[128,256]{1,0:T(8,128)S(1)} collective-permute-done((f32[128,256]{1,0:T(8,128)S(1)}, f32[128,256]{1,0:T(8,128)S(1)}, u32[]{:S(2)}, u32[]{:S(2)}) %collective-permute-start.5) | collective-permute-done | bytes 131104 | tf_op jit(solution)/shard_map/ppermute | solution.py:141
  71.1 0.1 collective-permute-start.6
  71.2 1.2 %collective-permute-done.6 = bf16[128,256]{1,0:T(8,128)(2,1)S(1)} collective-permute-done((bf16[128,256]{1,0:T(8,128)(2,1)S(1)}, bf16[128,256]{1,0:T(8,128)(2,1)S(1)}, u32[]{:S(2)}, u32[]{:S(2)}) %collective-permute-start.6) | collective-permute-done | bytes 65568 | tf_op jit(solution)/shard_map/ppermute | solution.py:58
  72.4 1.9 %collective-permute-start.7 = (bf16[256,256]{1,0:T(8,128)(2,1)S(1)}, bf16[256,256]{1,0:T(8,128)(2,1)S(1)}, u32[]{:S(2)}, u32[]{:S(2)}) collective-permute-start(bf16[256,256]{1,0:T(8,128)(2,1)S(1)} %pad_maximum_fusion.4), channel_id=1, source_target_pairs={{0,8},{4,20},{8,0},{12,28},{16,24},{20,4},{24,16},{28,12},{1,9},{5... | collective-permute-start | bytes 393224 | tf_op jit(solution)/shard_map/ppermute | solution.py:60
  74.3 3.1 %collective-permute-done.7 = bf16[256,256]{1,0:T(8,128)(2,1)S(1)} collective-permute-done((bf16[256,256]{1,0:T(8,128)(2,1)S(1)}, bf16[256,256]{1,0:T(8,128)(2,1)S(1)}, u32[]{:S(2)}, u32[]{:S(2)}) %collective-permute-start.7) | collective-permute-done | bytes 131104 | tf_op jit(solution)/shard_map/ppermute | solution.py:60
  77.4 1.1 %collective-permute-start.8 = (bf16[128,256]{1,0:T(8,128)(2,1)S(1)}, bf16[128,256]{1,0:T(8,128)(2,1)S(1)}, u32[]{:S(2)}, u32[]{:S(2)}) collective-permute-start(bf16[128,256]{1,0:T(8,128)(2,1)S(1)} %slice.107), channel_id=1, source_target_pairs={{0,20},{4,8},{8,28},{12,0},{16,4},{20,24},{24,12},{28,16},{1,21},{... | collective-permute-start | bytes 196616 | tf_op jit(solution)/shard_map/ppermute | solution.py:61
  78.6 2.6 %collective-permute-done.8 = bf16[128,256]{1,0:T(8,128)(2,1)S(1)} collective-permute-done((bf16[128,256]{1,0:T(8,128)(2,1)S(1)}, bf16[128,256]{1,0:T(8,128)(2,1)S(1)}, u32[]{:S(2)}, u32[]{:S(2)}) %collective-permute-start.8) | collective-permute-done | bytes 65568 | tf_op jit(solution)/shard_map/ppermute | solution.py:61
  81.1 0.6 collective-permute-start.9
  81.8 1.1 %collective-permute-done.9 = bf16[384,256]{1,0:T(8,128)(2,1)S(1)} collective-permute-done((bf16[384,256]{1,0:T(8,128)(2,1)S(1)}, bf16[384,256]{1,0:T(8,128)(2,1)S(1)}, u32[]{:S(2)}, u32[]{:S(2)}) %collective-permute-start.9) | collective-permute-done | bytes 196640 | tf_op jit(solution)/shard_map/ppermute | solution.py:62
  82.9 0.0 all-gather.2.cloned.1.call-done
  82.9 3.5 %convolution_convert_fusion.1 = bf16[128,256]{1,0:T(8,128)(2,1)S(1)} fusion(bf16[128,8192]{1,0:T(8,128)(2,1)} %fusion.2, bf16[8192,256]{1,0:T(8,128)(2,1)} %all-gather.2.cloned.1.call-done), kind=kOutput, calls=%fused_computation.18 | convolution fusion | flops 536903680 | bytes 6356992 | tf_op jit(solution)/shard_map/dot_general | solution.py:156
  86.5 0.1 fusion.61
  86.6 0.3 fusion.62
  86.9 0.3 fusion.63
  87.3 0.4 fusion.13
  87.7 0.4 fusion.12
  88.0 0.4 fusion.11
  88.5 0.7 copy.17
  (44 shorter events, 0.4 us)
Async XLA Ops:
  7.2 21.5 %copy-start = (bf16[1024,1152]{1,0:T(8,128)(2,1)S(1)}, bf16[1024,1152]{1,0:T(8,128)(2,1)}, u32[]{:S(2)}) copy-start(bf16[1024,1152]{1,0:T(8,128)(2,1)} %param.15) | copy-start | bytes 7077892
  7.2 3.6 %copy-start.1 = (s32[8]{0:T(128)S(1)}, s32[8]{0:T(128)}, u32[]{:S(2)}) copy-start(s32[8]{0:T(128)} %param.14) | copy-start | bytes 100
  7.2 75.7 %all-gather.2.cloned.1.call-start = ((), (), s32[]{:S(2)}) async-start(), calls=%async_computation | async-start | bytes 4718592 | tf_op jit(solution)/shard_map/all_gather | solution.py:154
  14.5 13.0 %copy-start.2 = (s32[8]{0:T(128)S(1)}, s32[8]{0:T(128)}, u32[]{:S(2)}) copy-start(s32[8]{0:T(128)} %param.17) | copy-start | bytes 100
  16.7 5.9 %collective-permute-start.10 = (bf16[8,4096]{1,0:T(8,128)(2,1)S(1)}, bf16[8,4096]{1,0:T(8,128)(2,1)S(1)}, u32[]{:S(2)}, u32[]{:S(2)}) collective-permute-start(bf16[8,4096]{1,0:T(8,128)(2,1)S(1)} %constant_dynamic-slice_fusion.2), channel_id=1, source_target_pairs={{0,16},{4,20},{8,24},{12,28},{16,0},{20,4},{24,8},{28,12},{1,17},{... | collective-permute-start | bytes 196616 | tf_op jit(solution)/shard_map/ppermute | solution.py:41
  22.6 4.8 %collective-permute-start.11 = (bf16[8,2048]{1,0:T(8,128)(2,1)S(1)}, bf16[8,2048]{1,0:T(8,128)(2,1)S(1)}, u32[]{:S(2)}, u32[]{:S(2)}) collective-permute-start(bf16[8,2048]{1,0:T(8,128)(2,1)S(1)} %constant_dynamic-slice_fusion.1), channel_id=1, source_target_pairs={{0,8},{4,12},{8,0},{12,4},{16,24},{20,28},{24,16},{28,20},{1,9},{5... | collective-permute-start | bytes 98312 | tf_op jit(solution)/shard_map/ppermute | solution.py:41
  24.1 5.2 %collective-permute-start = (bf16[256,256]{1,0:T(8,128)(2,1)S(1)}, bf16[256,256]{1,0:T(8,128)(2,1)S(1)}, u32[]{:S(2)}, u32[]{:S(2)}) collective-permute-start(bf16[256,256]{1,0:T(8,128)(2,1)S(1)} %pad_maximum_fusion.3), channel_id=1, source_target_pairs={{0,4},{4,0},{8,12},{12,8},{16,20},{20,16},{24,28},{28,24},{1,5},{5... | collective-permute-start | bytes 393224 | tf_op jit(solution)/shard_map/ppermute | solution.py:58
  27.5 1.2 %collective-permute-start.12 = (bf16[8,1024]{1,0:T(8,128)(2,1)S(1)}, bf16[8,1024]{1,0:T(8,128)(2,1)S(1)}, u32[]{:S(2)}, u32[]{:S(2)}) collective-permute-start(bf16[8,1024]{1,0:T(8,128)(2,1)S(1)} %constant_dynamic-slice_fusion), channel_id=1, source_target_pairs={{0,4},{4,0},{8,12},{12,8},{16,20},{20,16},{24,28},{28,24},{1,5},{5... | collective-permute-start | bytes 49160 | tf_op jit(solution)/shard_map/ppermute | solution.py:41
  29.1 1.7 %collective-permute-start.13 = (f32[8,1152]{1,0:T(8,128)S(1)}, f32[8,1152]{1,0:T(8,128)S(1)}, u32[]{:S(2)}, u32[]{:S(2)}) collective-permute-start(f32[8,1152]{1,0:T(8,128)S(1)} %fusion.42), channel_id=1, source_target_pairs={{0,4},{4,0},{8,12},{12,8},{16,20},{20,16},{24,28},{28,24},{1,5},{5... | collective-permute-start | bytes 110600 | tf_op jit(solution)/shard_map/ppermute | solution.py:28
  29.3 11.9 %collective-permute-start.1 = (bf16[512,256]{1,0:T(8,128)(2,1)S(1)}, bf16[512,256]{1,0:T(8,128)(2,1)S(1)}, u32[]{:S(2)}, u32[]{:S(2)}) collective-permute-start(bf16[512,256]{1,0:T(8,128)(2,1)S(1)} %pad_maximum_fusion.1), channel_id=1, source_target_pairs={{0,8},{4,20},{8,0},{12,28},{16,24},{20,4},{24,16},{28,12},{1,9},{5... | collective-permute-start | bytes 786440 | tf_op jit(solution)/shard_map/ppermute | solution.py:60
  30.8 6.0 %collective-permute-start.14 = (f32[8,1152]{1,0:T(8,128)S(1)}, f32[8,1152]{1,0:T(8,128)S(1)}, u32[]{:S(2)}, u32[]{:S(2)}) collective-permute-start(f32[8,1152]{1,0:T(8,128)S(1)} %add.317), channel_id=1, source_target_pairs={{0,8},{4,12},{8,0},{12,4},{16,24},{20,28},{24,16},{28,20},{1,9},{5... | collective-permute-start | bytes 110600 | tf_op jit(solution)/shard_map/ppermute | solution.py:28
  36.8 6.2 %collective-permute-start.15 = (f32[8,1152]{1,0:T(8,128)S(1)}, f32[8,1152]{1,0:T(8,128)S(1)}, u32[]{:S(2)}, u32[]{:S(2)}) collective-permute-start(f32[8,1152]{1,0:T(8,128)S(1)} %add.318), channel_id=1, source_target_pairs={{0,16},{4,20},{8,24},{12,28},{16,0},{20,4},{24,8},{28,12},{1,17},{... | collective-permute-start | bytes 110600 | tf_op jit(solution)/shard_map/ppermute | solution.py:28
  41.2 8.1 %collective-permute-start.2 = (bf16[256,256]{1,0:T(8,128)(2,1)S(1)}, bf16[256,256]{1,0:T(8,128)(2,1)S(1)}, u32[]{:S(2)}, u32[]{:S(2)}) collective-permute-start(bf16[256,256]{1,0:T(8,128)(2,1)S(1)} %slice.99), channel_id=1, source_target_pairs={{0,20},{4,8},{8,28},{12,0},{16,4},{20,24},{24,12},{28,16},{1,21},{... | collective-permute-start | bytes 393224 | tf_op jit(solution)/shard_map/ppermute | solution.py:61
  48.1 8.4 %collective-permute-start.16 = (f32[8,1024]{1,0:T(8,128)S(1)}, f32[8,1024]{1,0:T(8,128)S(1)}, u32[]{:S(2)}, u32[]{:S(2)}) collective-permute-start(f32[8,1024]{1,0:T(8,128)S(1)} %fusion.10), channel_id=1, source_target_pairs={{0,1},{1,0},{2,3},{3,2},{4,5},{5,4},{6,7},{7,6},{8,9},{9,8},{10,11... | collective-permute-start | bytes 98312 | tf_op jit(solution)/shard_map/ppermute | solution.py:28
  49.3 2.6 %collective-permute-start.3 = (bf16[768,256]{1,0:T(8,128)(2,1)S(1)}, bf16[768,256]{1,0:T(8,128)(2,1)S(1)}, u32[]{:S(2)}, u32[]{:S(2)}) collective-permute-start(bf16[768,256]{1,0:T(8,128)(2,1)S(1)} %pad_maximum_fusion), channel_id=1, source_target_pairs={{0,4},{4,0},{8,12},{12,8},{16,20},{20,16},{24,28},{28,24},{1,5},{5... | collective-permute-start | bytes 1179656 | tf_op jit(solution)/shard_map/ppermute | solution.py:62
  56.0 6.2 %collective-permute-start.4 = (f32[128,256]{1,0:T(8,128)S(1)}, f32[128,256]{1,0:T(8,128)S(1)}, u32[]{:S(2)}, u32[]{:S(2)}) collective-permute-start(f32[128,256]{1,0:T(8,128)S(1)} %fusion.9), channel_id=1, source_target_pairs={{0,1},{1,0},{2,3},{3,2},{4,5},{5,4},{6,7},{7,6},{8,9},{9,8},{10,11... | collective-permute-start | bytes 393224 | tf_op jit(solution)/shard_map/ppermute | solution.py:141
  56.5 9.0 %collective-permute-start.17 = (f32[8,1024]{1,0:T(8,128)S(1)}, f32[8,1024]{1,0:T(8,128)S(1)}, u32[]{:S(2)}, u32[]{:S(2)}) collective-permute-start(f32[8,1024]{1,0:T(8,128)S(1)} %add.321), channel_id=1, source_target_pairs={{0,2},{1,3},{2,0},{3,1},{4,6},{5,7},{6,4},{7,5},{8,10},{9,11},{10,... | collective-permute-start | bytes 98312 | tf_op jit(solution)/shard_map/ppermute | solution.py:28
  62.2 8.8 %collective-permute-start.5 = (f32[128,256]{1,0:T(8,128)S(1)}, f32[128,256]{1,0:T(8,128)S(1)}, u32[]{:S(2)}, u32[]{:S(2)}) collective-permute-start(f32[128,256]{1,0:T(8,128)S(1)} %add.304), channel_id=1, source_target_pairs={{0,2},{1,3},{2,0},{3,1},{4,6},{5,7},{6,4},{7,5},{8,10},{9,11},{10,... | collective-permute-start | bytes 393224 | tf_op jit(solution)/shard_map/ppermute | solution.py:141
  71.1 1.3 %collective-permute-start.6 = (bf16[128,256]{1,0:T(8,128)(2,1)S(1)}, bf16[128,256]{1,0:T(8,128)(2,1)S(1)}, u32[]{:S(2)}, u32[]{:S(2)}) collective-permute-start(bf16[128,256]{1,0:T(8,128)(2,1)S(1)} %add_convert_fusion), channel_id=1, source_target_pairs={{0,4},{4,0},{8,12},{12,8},{16,20},{20,16},{24,28},{28,24},{1,5},{5... | collective-permute-start | bytes 196616 | tf_op jit(solution)/shard_map/ppermute | solution.py:58
  72.4 5.0 %collective-permute-start.7 = (bf16[256,256]{1,0:T(8,128)(2,1)S(1)}, bf16[256,256]{1,0:T(8,128)(2,1)S(1)}, u32[]{:S(2)}, u32[]{:S(2)}) collective-permute-start(bf16[256,256]{1,0:T(8,128)(2,1)S(1)} %pad_maximum_fusion.4), channel_id=1, source_target_pairs={{0,8},{4,20},{8,0},{12,28},{16,24},{20,4},{24,16},{28,12},{1,9},{5... | collective-permute-start | bytes 393224 | tf_op jit(solution)/shard_map/ppermute | solution.py:60
  77.4 3.7 %collective-permute-start.8 = (bf16[128,256]{1,0:T(8,128)(2,1)S(1)}, bf16[128,256]{1,0:T(8,128)(2,1)S(1)}, u32[]{:S(2)}, u32[]{:S(2)}) collective-permute-start(bf16[128,256]{1,0:T(8,128)(2,1)S(1)} %slice.107), channel_id=1, source_target_pairs={{0,20},{4,8},{8,28},{12,0},{16,4},{20,24},{24,12},{28,16},{1,21},{... | collective-permute-start | bytes 196616 | tf_op jit(solution)/shard_map/ppermute | solution.py:61
  81.1 1.7 %collective-permute-start.9 = (bf16[384,256]{1,0:T(8,128)(2,1)S(1)}, bf16[384,256]{1,0:T(8,128)(2,1)S(1)}, u32[]{:S(2)}, u32[]{:S(2)}) collective-permute-start(bf16[384,256]{1,0:T(8,128)(2,1)S(1)} %pad_maximum_fusion.2), channel_id=1, source_target_pairs={{0,4},{4,0},{8,12},{12,8},{16,20},{20,16},{24,28},{28,24},{1,5},{5... | collective-permute-start | bytes 589832 | tf_op jit(solution)/shard_map/ppermute | solution.py:62
Sparse Core Ops, SparseCore 0:
  9.9 42.1 all-gather.1

commit v4 on v3

--- a/solution.py
+++ b/solution.py
@@ -22,25 +22,41 @@
     return [(j, pick(j)) for j in range(n)]
 
 
-def xor_all_reduce(x, axis, n):
-    k = 1
-    while k < n:
-        x = x + lax.ppermute(x, axis, xor_perm(n, lambda j, k=k: j ^ k))
-        k = k * 2
-    return x
-
-
-def xor_reduce_scatter(x, axis, n):
-    i = lax.axis_index(axis)
-    k = n // 2
-    while k >= 1:
-        half = x.shape[1] // 2
-        bit = (i // k) % 2
-        keep = lax.dynamic_slice_in_dim(x, bit * half, half, 1)
-        send = lax.dynamic_slice_in_dim(x, (1 - bit) * half, half, 1)
-        x = keep + lax.ppermute(send, axis, xor_perm(n, lambda j, k=k: j ^ k))
-        k = k // 2
-    return x
+def seq_all_reduce(x):
+    x = x + lax.ppermute(x, "seq", xor_perm(8, lambda j: j ^ 1))
+    got = [lax.ppermute(x, "seq", xor_perm(8, lambda j, m=m: j ^ m)) for m in (2, 4, 6)]
+    return x + got[0] + got[1] + got[2]
+
+
+def seq_reduce_scatter(x):
+    i = lax.axis_index("seq")
+    chip_cols = x.shape[1] // 4
+    own = lax.dynamic_slice_in_dim(x, (i // 2) * chip_cols, chip_cols, 1).astype(jnp.float32)
+    for m in (2, 4, 6):
+        part = lax.dynamic_slice_in_dim(x, ((i ^ m) // 2) * chip_cols, chip_cols, 1)
+        own = own + lax.ppermute(part, "seq", xor_perm(8, lambda j, m=m: j ^ m)).astype(jnp.float32)
+    half = chip_cols // 2
+    core = i % 2
+    keep = lax.dynamic_slice_in_dim(own, core * half, half, 1)
+    send = lax.dynamic_slice_in_dim(own, (1 - core) * half, half, 1)
+    return keep + lax.ppermute(send, "seq", xor_perm(8, lambda j: j ^ 1))
+
+
+def group_sum(x, axis, n, size, canonical):
+    got = [x] + [lax.ppermute(x, axis, xor_perm(n, lambda j, k=k: j ^ k)) for k in range(1, size)]
+    if not canonical:
+        total = got[0]
+        for g in got[1:]:
+            total = total + g
+        return total
+    me = lax.axis_index(axis) % size
+    total = None
+    for m in range(size):
+        value = got[0]
+        for k in range(1, size):
+            value = jnp.where((me ^ k) == m, got[k], value)
+        total = value if total is None else total + value
+    return total
 
 
 def power_of_two(n):
@@ -53,26 +69,13 @@
     if n != 8:
         full = lax.all_gather(blk, "seq", axis=0, tiled=False)
         return [(full[m], m, rows) for m in range(n)]
-    core = i % 2
-    chip = i // 2
     sib = lax.ppermute(blk, "seq", xor_perm(8, lambda j: j ^ 1))
     pair = jnp.concatenate([blk, sib], axis=0)
-    nb = lax.ppermute(pair, "seq", xor_perm(8, lambda j: j ^ 2 if j % 2 == 0 else j ^ 4))
-    dg = lax.ppermute(nb[:rows], "seq", xor_perm(8, lambda j: j ^ 5 if j % 2 == 0 else j ^ 3))
-    oth = lax.ppermute(jnp.concatenate([nb, dg], axis=0), "seq", xor_perm(8, lambda j: j ^ 1))
-    nb_chip = chip ^ (1 + core)
-    oth_chip = chip ^ (2 - core)
-    diag = chip ^ 3
-    return [
-        (blk, i, rows),
-        (sib, i ^ 1, rows),
-        (nb[:rows], 2 * nb_chip + core, rows),
-        (nb[rows:], 2 * nb_chip + 1 - core, rows),
-        (dg, 2 * diag + 1 - core, rows),
-        (oth[:rows], 2 * oth_chip + 1 - core, rows),
-        (oth[rows : 2 * rows], 2 * oth_chip + core, rows),
-        (oth[2 * rows :], 2 * diag + core, rows),
-    ]
+    pieces = [(blk, i, rows), (sib, i ^ 1, rows)]
+    for m in (2, 4, 6):
+        got = lax.ppermute(pair, "seq", xor_perm(8, lambda j, m=m: j ^ m))
+        pieces += [(got[:rows], i ^ m, rows), (got[rows:], i ^ m ^ 1, rows)]
+    return pieces
 
 
 def project(normed, pieces, stride, offset=0):
@@ -112,13 +115,13 @@
     query_pos = first_row + jnp.arange(tokens_here, dtype=jnp.int32)
     picker = (doc_ends[:, None] == query_pos[None, :]).astype(jnp.bfloat16)
     end_terms = jnp.dot(picker, normed, preferred_element_type=jnp.float32).astype(jnp.bfloat16)
-    if power_of_two(n_seq):
-        end_rows = xor_reduce_scatter(end_terms, "seq", n_seq)
+    if n_seq == 8:
+        end_rows = seq_reduce_scatter(end_terms).astype(jnp.bfloat16)
     else:
         end_rows = lax.psum_scatter(end_terms, "seq", scatter_dimension=1, tiled=True)
     up_own = jnp.dot(end_rows, critic_up, preferred_element_type=jnp.float32)
-    if power_of_two(n_seq):
-        up_sum = xor_all_reduce(up_own, "seq", n_seq)
+    if n_seq == 8:
+        up_sum = seq_all_reduce(up_own)
     else:
         up_sum = lax.psum(up_own, "seq")
     critic_hidden = jax.nn.silu(up_sum).astype(jnp.bfloat16)
@@ -127,19 +130,15 @@
     )
     rule_pick = rule_ids[:, None] == jnp.arange(critic_down.shape[0], dtype=jnp.int32)[None, :]
     chosen = jnp.sum(jnp.where(rule_pick[:, :, None], per_rule, 0.0), axis=1)
-    if power_of_two(n_tp):
-        critic_sum = xor_all_reduce(chosen, "tp", n_tp)
+    if n_tp <= 8 and power_of_two(n_tp):
+        critic_sum = group_sum(chosen, "tp", n_tp, n_tp, canonical=True)
     else:
         critic_sum = lax.psum(chosen, "tp")
     critic_values = critic_sum.astype(jnp.bfloat16)
 
     kv_pieces = gather_pieces(kv_weights, n_seq)
     kv_part_sum = project(normed, kv_pieces, d_rows, kv_part * kv_rows_here)
-    kv_rows = kv_part_sum
-    k = 1
-    while k < sharers:
-        kv_rows = kv_rows + lax.ppermute(kv_rows, "tp", xor_perm(n_tp, lambda j, k=k: j ^ k))
-        k *= 2
+    kv_rows = group_sum(kv_part_sum, "tp", n_tp, sharers, canonical=False)
     kv_rows = kv_rows.astype(jnp.bfloat16)
     kv_all = gather_pieces(kv_rows, n_seq)
     key_block = jnp.concatenate([piece[:, :HEAD] for piece, _, _ in kv_all], axis=0)

time: 96.7 us -> 93.2 us (0.964)
  waiting for transfers between devices: 28.1 us -> 23.5 us
  starting transfers between devices: 23.1 us -> 25.8 us
  matrix products: 20.5 us -> 18.9 us
  local copies, waits for them, and re-layouts: 1.89 us -> 3.33 us
  other arithmetic: 7.91 us -> 6.54 us
    ppermute x16 -> x20, waiting for transfers between devices: 26.2 us -> 22.2 us  [the longest x6 10.7 us: gather_pieces(): got = lax.ppermute(pair, 'seq', xor_perm(8, lambda j, m=m: j ^ m))]
    ppermute x16 -> x20, starting transfers between devices: 22.9 us -> 25.1 us  [the longest x6 10.1 us: group_sum(): lax.ppermute(x, axis, xor_perm(n, lambda j, k=k: j ^ k))]
    dot_general x1, matrix products: 2.01 us -> 0.43 us  [body(): jnp.dot(picker, normed, preferred_element_type=jnp.float32)]
    unnamed x11 -> x13, local copies, waits for them, and re-layouts: 0.81 us -> 2.14 us
    convert_element_type x1, other arithmetic: 3.49 us -> 2.17 us  [rms_norm(): (widened * lax.rsqrt(mean_square + 1e-05) * norm_gain.astype(jnp.float32)...]
  transfers between devices with their start and end apart: 19 -> 23, of which waited for: 11 -> 13; matrix products, arithmetic and copies ran while one was open for 25% -> 22% of each run, Pallas kernels for 0% -> 0%
where the time goes in v4:
time: 93.2 us; the launch traced here: 92.6 us
  starting transfers between devices  25.8 us (28%)
  waiting for transfers between devices  23.5 us (25%)
  matrix products  18.9 us (20%)
  between operations  14.6 us (16%)
  other arithmetic  6.54 us (7%)
  local copies, waits for them, and re-layouts  3.33 us (4%)
    ppermute x6, waiting for transfers between devices, gather_pieces(): got = lax.ppermute(pair, 'seq', xor_perm(8, lambda j, m=m: j ^ m))  10.7 us
    ppermute x6, starting transfers between devices, group_sum(): lax.ppermute(x, axis, xor_perm(n, lambda j, k=k: j ^ k))  10.1 us
    dot_general x8, matrix products, project(): term = jnp.dot(cols, piece, preferred_element_type=jnp.float32)  8.01 us
    ppermute x6, starting transfers between devices, gather_pieces(): got = lax.ppermute(pair, 'seq', xor_perm(8, lambda j, m=m: j ^ m))  7.17 us
    ppermute x6, waiting for transfers between devices, group_sum(): lax.ppermute(x, axis, xor_perm(n, lambda j, k=k: j ^ k))  6.15 us
    dot_general x1, matrix products, body(): jnp.einsum('dc,rce->dre', critic_hidden, critic_down, preferred_element_t...  5.01 us
    ppermute x3, starting transfers between devices, seq_reduce_scatter(): lax.ppermute(part, 'seq', xor_perm(8, lambda j, m=m: j ^ m))  4.15 us
    dot_general x1, matrix products, body(): jnp.dot(normed, q_weights, preferred_element_type=jnp.float32)  3.54 us
  transfers between devices with their start and end apart: 23, of which 13 were waited for; matrix products, arithmetic and copies ran while one was open for 22% of the time, Pallas kernels for 0%

profile of v4, /device:TPU:0, one launch (start us, length us, event | category | flops | bytes accessed | tf_op | source)
XLA Modules:
  0.0 92.6 jit_solution(11228532450322210957)
XLA Ops:
  7.2 0.0 all-gather.2.cloned.1.call-start
  7.3 1.0 %constant_dynamic-slice_fusion.4 = (bf16[256,128]{1,0:T(8,128)(2,1)S(1)}, bf16[256,128]{1,0:T(8,128)(2,1)S(1)}) fusion(bf16[1024,128]{1,0:T(8,128)(2,1)} %param.13, s32[]{:T(128)S(6)} %select_n.168, bf16[1024,128]{1,0:T(8,128)(2,1)} %param.12), kind=kLoop, calls=%fused_computation.100 | loop fusion | bytes 262148 | tf_op jit(solution)/shard_map/dynamic_slice | solution.py:108
  8.3 0.6 collective-permute-start
  8.9 0.0 all-gather.2.cloned.1.call-update
  9.0 0.7 convert_element_type.61
  9.7 2.1 %fusion = f32[128]{0:T(128)S(1)} fusion(bf16[128,8192]{1,0:T(8,128)(2,1)} %param.9), kind=kLoop, calls=%fused_computation.3 | loop fusion | flops 3145600 | bytes 2097664 | tf_op jit(solution)/shard_map/reduce_sum | solution.py:15
  11.8 0.2 reduce-window.7
  12.2 2.2 %fusion.2 = bf16[128,8192]{1,0:T(8,128)(2,1)S(1)} fusion(bf16[128,8192]{1,0:T(8,128)(2,1)} %param.9, f32[8192]{0:T(1024)S(1)} %convert_element_type.61, f32[128]{0:T(128)S(1)} %add_rsqrt_fusion), kind=kLoop, calls=%fused_computation.5 | loop fusion | flops 4194304 | bytes 4227584 | tf_op jit(solution)/shard_map/convert_element_type | solution.py:16
  14.4 1.3 %copy-done.1 = bf16[128,8192]{1,0:T(8,128)(2,1)} copy-done((bf16[128,8192]{1,0:T(8,128)(2,1)}, bf16[128,8192]{1,0:T(8,128)(2,1)S(1)}, u32[]{:S(2)}) %copy-start.1) | copy-done | bytes 2097176
  15.7 0.4 convolution_convert_fusion
  16.1 3.5 %collective-permute-start.13 = (bf16[8,2048]{1,0:T(8,128)(2,1)S(1)}, bf16[8,2048]{1,0:T(8,128)(2,1)S(1)}, u32[]{:S(2)}, u32[]{:S(2)}) collective-permute-start(bf16[8,2048]{1,0:T(8,128)(2,1)S(1)} %get-tuple-element.11), channel_id=1, source_target_pairs={{0,24},{4,28},{8,16},{12,20},{16,8},{20,12},{24,0},{28,4},{1,25},{... | collective-permute-start | bytes 98312 | tf_op jit(solution)/shard_map/ppermute | solution.py:37
  19.6 0.5 collective-permute-start.12
  20.1 0.1 collective-permute-start.11
  20.3 1.0 %fusion.41 = f32[128,256]{1,0:T(8,128)S(1)} fusion(bf16[128,8192]{1,0:T(8,128)(2,1)} %copy-done.1, s32[]{:T(128)S(6)} %select_n.167, bf16[256,128]{1,0:T(8,128)(2,1)S(1)} %get-tuple-element.29, bf16[256,128]{1,0:T(8,128)(2,1)S(1)} %get-tuple-element.30), kind=kOutput, calls=%fused_computation.65 | convolution fusion | flops 17039360 | bytes 327684 | tf_op jit(solution)/shard_map/dot_general | solution.py:85
  21.3 0.7 collective-permute-done.13
  22.0 2.0 %collective-permute-done.12 = bf16[8,2048]{1,0:T(8,128)(2,1)S(1)} collective-permute-done((bf16[8,2048]{1,0:T(8,128)(2,1)S(1)}, bf16[8,2048]{1,0:T(8,128)(2,1)S(1)}, u32[]{:S(2)}, u32[]{:S(2)}) %collective-permute-start.12) | collective-permute-done | bytes 32800 | tf_op jit(solution)/shard_map/ppermute | solution.py:37
  24.0 0.6 collective-permute-done.11
  24.6 0.1 collective-permute-start.14
  24.7 0.1 convert_reduce_fusion
  24.8 1.1 %collective-permute-done.14 = f32[8,1024]{1,0:T(8,128)S(1)} collective-permute-done((f32[8,1024]{1,0:T(8,128)S(1)}, f32[8,1024]{1,0:T(8,128)S(1)}, u32[]{:S(2)}, u32[]{:S(2)}) %collective-permute-start.14) | collective-permute-done | bytes 32800 | tf_op jit(solution)/shard_map/ppermute | solution.py:42
  25.9 0.4 fusion.44
  26.3 0.2 collective-permute-start.15
  26.5 0.1 convert_reduce_fusion.1
  26.6 0.9 %collective-permute-done.15 = f32[8,1152]{1,0:T(8,128)S(1)} collective-permute-done((f32[8,1152]{1,0:T(8,128)S(1)}, f32[8,1152]{1,0:T(8,128)S(1)}, u32[]{:S(2)}, u32[]{:S(2)}) %collective-permute-start.15) | collective-permute-done | bytes 36896 | tf_op jit(solution)/shard_map/ppermute | solution.py:26
  27.5 1.5 %collective-permute-start.18 = (f32[8,1152]{1,0:T(8,128)S(1)}, f32[8,1152]{1,0:T(8,128)S(1)}, u32[]{:S(2)}, u32[]{:S(2)}) collective-permute-start(f32[8,1152]{1,0:T(8,128)S(1)} %add.288), channel_id=1, source_target_pairs={{0,24},{4,28},{8,16},{12,20},{16,8},{20,12},{24,0},{28,4},{1,25},{... | collective-permute-start | bytes 110600 | tf_op jit(solution)/shard_map/ppermute | solution.py:27
  29.0 0.9 collective-permute-start.17
  29.9 1.1 %collective-permute-start.16 = (f32[8,1152]{1,0:T(8,128)S(1)}, f32[8,1152]{1,0:T(8,128)S(1)}, u32[]{:S(2)}, u32[]{:S(2)}) collective-permute-start(f32[8,1152]{1,0:T(8,128)S(1)} %add.288), channel_id=1, source_target_pairs={{0,8},{4,12},{8,0},{12,4},{16,24},{20,28},{24,16},{28,20},{1,9},{5... | collective-permute-start | bytes 110600 | tf_op jit(solution)/shard_map/ppermute | solution.py:27
  31.1 1.6 %collective-permute-start.3 = (bf16[512,256]{1,0:T(8,128)(2,1)S(1)}, bf16[512,256]{1,0:T(8,128)(2,1)S(1)}, u32[]{:S(2)}, u32[]{:S(2)}) collective-permute-start(bf16[512,256]{1,0:T(8,128)(2,1)S(1)} %pad_maximum_fusion), channel_id=1, source_target_pairs={{0,24},{4,28},{8,16},{12,20},{16,8},{20,12},{24,0},{28,4},{1,25},{... | collective-permute-start | bytes 786440 | tf_op jit(solution)/shard_map/ppermute | solution.py:76
  32.6 0.9 collective-permute-start.2
  33.5 1.0 %convolution_add_fusion.1 = f32[128,256]{1,0:T(8,128)S(1)} fusion(f32[128,256]{1,0:T(8,128)S(1)} %fusion.41, bf16[256,256]{1,0:T(8,128)(2,1)S(1)} %collective-permute-done, bf16[128,8192]{1,0:T(8,128)(2,1)} %copy-done.1, s32[]{:T(128)S(6)} %select_n.169), kind=kOutput, calls=%fused_computation.12 | convolution fusion | flops 16809984 | bytes 458756 | tf_op jit(solution)/shard_map/dot_general | solution.py:85
  34.5 1.1 %collective-permute-start.1 = (bf16[512,256]{1,0:T(8,128)(2,1)S(1)}, bf16[512,256]{1,0:T(8,128)(2,1)S(1)}, u32[]{:S(2)}, u32[]{:S(2)}) collective-permute-start(bf16[512,256]{1,0:T(8,128)(2,1)S(1)} %pad_maximum_fusion), channel_id=1, source_target_pairs={{0,8},{4,12},{8,0},{12,4},{16,24},{20,28},{24,16},{28,20},{1,9},{5... | collective-permute-start | bytes 786440 | tf_op jit(solution)/shard_map/ppermute | solution.py:76
  35.7 5.0 %fusion.10 = f32[8,1024]{1,0:T(8,128)S(1)} fusion(bf16[4,1152,1024]{2,1,0:T(8,128)(2,1)} %param.16, pred[8,4]{0,1:T(4,128)(4,1)S(1)} %iota_compare_fusion, f32[8,1152]{1,0:T(8,128)S(1)} %collective-permute-done.18, f32[8,1152]{1,0:T(8,128)S(1)} %collective-permute-done.17, f32[8,1152]{1,0:T(8,128)S(1)} %add.288, f32[8,1152]{1,0:T(8,128)S(1)} %collective-permute-done.16), kind=kOutput, calls=%fused_computation.19 | convolution fusion | flops 75628544 | bytes 9617440 | tf_op jit(solution)/shard_map/dc,rce->dre/dot_general | solution.py:128
  40.7 3.7 %collective-permute-start.19 = (f32[8,1024]{1,0:T(8,128)S(1)}, f32[8,1024]{1,0:T(8,128)S(1)}, u32[]{:S(2)}, u32[]{:S(2)}) collective-permute-start(f32[8,1024]{1,0:T(8,128)S(1)} %fusion.10), channel_id=1, source_target_pairs={{0,3},{1,2},{2,1},{3,0},{4,7},{5,6},{6,5},{7,4},{8,11},{9,10},{10,... | collective-permute-start | bytes 98312 | tf_op jit(solution)/shard_map/ppermute | solution.py:46
  44.4 0.4 collective-permute-done.3
  44.8 1.7 %collective-permute-start.21 = (f32[8,1024]{1,0:T(8,128)S(1)}, f32[8,1024]{1,0:T(8,128)S(1)}, u32[]{:S(2)}, u32[]{:S(2)}) collective-permute-start(f32[8,1024]{1,0:T(8,128)S(1)} %fusion.10), channel_id=1, source_target_pairs={{0,1},{1,0},{2,3},{3,2},{4,5},{5,4},{6,7},{7,6},{8,9},{9,8},{10,11... | collective-permute-start | bytes 98312 | tf_op jit(solution)/shard_map/ppermute | solution.py:46
  46.5 1.0 %fusion.23 = f32[128,256]{1,0:T(8,128)S(1)} fusion(bf16[512,256]{1,0:T(8,128)(2,1)S(1)} %collective-permute-done.3, bf16[128,8192]{1,0:T(8,128)(2,1)} %copy-done.1, s32[]{:T(128)S(6)} %select_n.175), kind=kOutput, calls=%fused_computation.36 | convolution fusion | flops 16777216 | bytes 327684 | tf_op jit(solution)/shard_map/dot_general | solution.py:85
  47.5 1.0 %fusion.25 = f32[128,256]{1,0:T(8,128)S(1)} fusion(bf16[512,256]{1,0:T(8,128)(2,1)S(1)} %collective-permute-done.3, bf16[128,8192]{1,0:T(8,128)(2,1)} %copy-done.1, s32[]{:T(128)S(6)} %select_n.174), kind=kOutput, calls=%fused_computation.38 | convolution fusion | flops 16777216 | bytes 327684 | tf_op jit(solution)/shard_map/dot_general | solution.py:85
  48.5 2.4 %collective-permute-done.2 = bf16[512,256]{1,0:T(8,128)(2,1)S(1)} collective-permute-done((bf16[512,256]{1,0:T(8,128)(2,1)S(1)}, bf16[512,256]{1,0:T(8,128)(2,1)S(1)}, u32[]{:S(2)}, u32[]{:S(2)}) %collective-permute-start.2) | collective-permute-done | bytes 262176 | tf_op jit(solution)/shard_map/ppermute | solution.py:76
  50.9 1.0 %fusion.27 = f32[128,256]{1,0:T(8,128)S(1)} fusion(bf16[512,256]{1,0:T(8,128)(2,1)S(1)} %collective-permute-done.2, bf16[128,8192]{1,0:T(8,128)(2,1)} %copy-done.1, s32[]{:T(128)S(6)} %select_n.173), kind=kOutput, calls=%fused_computation.40 | convolution fusion | flops 16777216 | bytes 327684 | tf_op jit(solution)/shard_map/dot_general | solution.py:85
  51.9 1.0 %fusion.29 = f32[128,256]{1,0:T(8,128)S(1)} fusion(bf16[512,256]{1,0:T(8,128)(2,1)S(1)} %collective-permute-done.2, bf16[128,8192]{1,0:T(8,128)(2,1)} %copy-done.1, s32[]{:T(128)S(6)} %select_n.172), kind=kOutput, calls=%fused_computation.42 | convolution fusion | flops 16777216 | bytes 327684 | tf_op jit(solution)/shard_map/dot_general | solution.py:85
  52.9 2.5 %collective-permute-done.1 = bf16[512,256]{1,0:T(8,128)(2,1)S(1)} collective-permute-done((bf16[512,256]{1,0:T(8,128)(2,1)S(1)}, bf16[512,256]{1,0:T(8,128)(2,1)S(1)}, u32[]{:S(2)}, u32[]{:S(2)}) %collective-permute-start.1) | collective-permute-done | bytes 262176 | tf_op jit(solution)/shard_map/ppermute | solution.py:76
  55.3 1.0 %fusion.31 = f32[128,256]{1,0:T(8,128)S(1)} fusion(bf16[512,256]{1,0:T(8,128)(2,1)S(1)} %collective-permute-done.1, bf16[128,8192]{1,0:T(8,128)(2,1)} %copy-done.1, s32[]{:T(128)S(6)} %select_n.171), kind=kOutput, calls=%fused_computation.44 | convolution fusion | flops 16777216 | bytes 327684 | tf_op jit(solution)/shard_map/dot_general | solution.py:85
  56.3 1.0 %fusion.9 = f32[128,256]{1,0:T(8,128)S(1)} fusion(f32[128,256]{1,0:T(8,128)S(1)} %fusion.23, f32[128,256]{1,0:T(8,128)S(1)} %fusion.25, f32[128,256]{1,0:T(8,128)S(1)} %fusion.27, f32[128,256]{1,0:T(8,128)S(1)} %fusion.29, f32[128,256]{1,0:T(8,128)S(1)} %fusion.31, f32[128,256]{1,0:T(8,128)S(1)} %convolution_add_fusion.1, ...), kind=kOutput, calls=%fused_computation.17 | convolution fusion | flops 16973824 | bytes 1114116 | tf_op jit(solution)/shard_map/dot_general | solution.py:85
  57.4 4.1 %collective-permute-start.6 = (f32[128,256]{1,0:T(8,128)S(1)}, f32[128,256]{1,0:T(8,128)S(1)}, u32[]{:S(2)}, u32[]{:S(2)}) collective-permute-start(f32[128,256]{1,0:T(8,128)S(1)} %fusion.9), channel_id=1, source_target_pairs={{0,3},{1,2},{2,1},{3,0},{4,7},{5,6},{6,5},{7,4},{8,11},{9,10},{10,... | collective-permute-start | bytes 393224 | tf_op jit(solution)/shard_map/ppermute | solution.py:46
  61.5 0.6 collective-permute-start.4
  62.1 0.6 add_convert_fusion.1
  62.8 2.3 %collective-permute-done.6 = f32[128,256]{1,0:T(8,128)S(1)} collective-permute-done((f32[128,256]{1,0:T(8,128)S(1)}, f32[128,256]{1,0:T(8,128)S(1)}, u32[]{:S(2)}, u32[]{:S(2)}) %collective-permute-start.6) | collective-permute-done | bytes 131104 | tf_op jit(solution)/shard_map/ppermute | solution.py:46
  65.0 3.9 %collective-permute-done.5 = f32[128,256]{1,0:T(8,128)S(1)} collective-permute-done((f32[128,256]{1,0:T(8,128)S(1)}, f32[128,256]{1,0:T(8,128)S(1)}, u32[]{:S(2)}, u32[]{:S(2)}) %collective-permute-start.5) | collective-permute-done | bytes 131104 | tf_op jit(solution)/shard_map/ppermute | solution.py:46
  68.9 0.1 collective-permute-start.7
  69.0 1.2 %collective-permute-done.7 = bf16[128,256]{1,0:T(8,128)(2,1)S(1)} collective-permute-done((bf16[128,256]{1,0:T(8,128)(2,1)S(1)}, bf16[128,256]{1,0:T(8,128)(2,1)S(1)}, u32[]{:S(2)}, u32[]{:S(2)}) %collective-permute-start.7) | collective-permute-done | bytes 65568 | tf_op jit(solution)/shard_map/ppermute | solution.py:72
  70.3 1.0 %collective-permute-start.8 = (bf16[256,256]{1,0:T(8,128)(2,1)S(1)}, bf16[256,256]{1,0:T(8,128)(2,1)S(1)}, u32[]{:S(2)}, u32[]{:S(2)}) collective-permute-start(bf16[256,256]{1,0:T(8,128)(2,1)S(1)} %pad_maximum_fusion.2), channel_id=1, source_target_pairs={{0,8},{4,12},{8,0},{12,4},{16,24},{20,28},{24,16},{28,20},{1,9},{5... | collective-permute-start | bytes 393224 | tf_op jit(solution)/shard_map/ppermute | solution.py:76
  71.3 1.1 %collective-permute-start.9 = (bf16[256,256]{1,0:T(8,128)(2,1)S(1)}, bf16[256,256]{1,0:T(8,128)(2,1)S(1)}, u32[]{:S(2)}, u32[]{:S(2)}) collective-permute-start(bf16[256,256]{1,0:T(8,128)(2,1)S(1)} %pad_maximum_fusion.2), channel_id=1, source_target_pairs={{0,16},{4,20},{8,24},{12,28},{16,0},{20,4},{24,8},{28,12},{1,17},{... | collective-permute-start | bytes 393224 | tf_op jit(solution)/shard_map/ppermute | solution.py:76
  72.4 1.4 %collective-permute-start.10 = (bf16[256,256]{1,0:T(8,128)(2,1)S(1)}, bf16[256,256]{1,0:T(8,128)(2,1)S(1)}, u32[]{:S(2)}, u32[]{:S(2)}) collective-permute-start(bf16[256,256]{1,0:T(8,128)(2,1)S(1)} %pad_maximum_fusion.2), channel_id=1, source_target_pairs={{0,24},{4,28},{8,16},{12,20},{16,8},{20,12},{24,0},{28,4},{1,25},{... | collective-permute-start | bytes 393224 | tf_op jit(solution)/shard_map/ppermute | solution.py:76
  73.8 2.9 %collective-permute-done.8 = bf16[256,256]{1,0:T(8,128)(2,1)S(1)} collective-permute-done((bf16[256,256]{1,0:T(8,128)(2,1)S(1)}, bf16[256,256]{1,0:T(8,128)(2,1)S(1)}, u32[]{:S(2)}, u32[]{:S(2)}) %collective-permute-start.8) | collective-permute-done | bytes 131104 | tf_op jit(solution)/shard_map/ppermute | solution.py:76
  76.7 2.6 %collective-permute-done.9 = bf16[256,256]{1,0:T(8,128)(2,1)S(1)} collective-permute-done((bf16[256,256]{1,0:T(8,128)(2,1)S(1)}, bf16[256,256]{1,0:T(8,128)(2,1)S(1)}, u32[]{:S(2)}, u32[]{:S(2)}) %collective-permute-start.9) | collective-permute-done | bytes 131104 | tf_op jit(solution)/shard_map/ppermute | solution.py:76
  79.4 0.0 all-gather.2.cloned.1.call-done
  79.5 3.5 %convolution_convert_fusion.1 = bf16[128,256]{1,0:T(8,128)(2,1)S(1)} fusion(bf16[128,8192]{1,0:T(8,128)(2,1)} %copy-done.1, bf16[8192,256]{1,0:T(8,128)(2,1)} %all-gather.2.cloned.1.call-done), kind=kOutput, calls=%fused_computation.18 | convolution fusion | flops 536903680 | bytes 6356992 | tf_op jit(solution)/shard_map/dot_general | solution.py:155
  83.0 0.1 fusion.60
  83.1 0.3 fusion.61
  83.5 0.3 fusion.62
  83.8 0.4 fusion.13
  84.2 0.4 fusion.12
  84.6 0.4 fusion.11
  85.0 0.7 copy.17
  (45 shorter events, 0.4 us)
Async XLA Ops:
  7.2 18.7 %copy-start = (bf16[1024,1152]{1,0:T(8,128)(2,1)S(1)}, bf16[1024,1152]{1,0:T(8,128)(2,1)}, u32[]{:S(2)}) copy-start(bf16[1024,1152]{1,0:T(8,128)(2,1)} %param.15) | copy-start | bytes 7077892
  7.2 4.7 %copy-start.2 = (s32[8]{0:T(128)S(1)}, s32[8]{0:T(128)}, u32[]{:S(2)}) copy-start(s32[8]{0:T(128)} %param.14) | copy-start | bytes 100
  7.2 72.3 %all-gather.2.cloned.1.call-start = ((), (), s32[]{:S(2)}) async-start(), calls=%async_computation | async-start | bytes 4718592 | tf_op jit(solution)/shard_map/all_gather | solution.py:153
  8.3 22.7 %collective-permute-start = (bf16[256,256]{1,0:T(8,128)(2,1)S(1)}, bf16[256,256]{1,0:T(8,128)(2,1)S(1)}, u32[]{:S(2)}, u32[]{:S(2)}) collective-permute-start(bf16[256,256]{1,0:T(8,128)(2,1)S(1)} %pad_maximum_fusion.1), channel_id=1, source_target_pairs={{0,4},{4,0},{8,12},{12,8},{16,20},{20,16},{24,28},{28,24},{1,5},{5... | collective-permute-start | bytes 393224 | tf_op jit(solution)/shard_map/ppermute | solution.py:72
  14.3 1.3 %copy-start.1 = (bf16[128,8192]{1,0:T(8,128)(2,1)}, bf16[128,8192]{1,0:T(8,128)(2,1)S(1)}, u32[]{:S(2)}) copy-start(bf16[128,8192]{1,0:T(8,128)(2,1)S(1)} %fusion.2) | copy-start | bytes 6291460
  14.3 5.9 %copy-start.3 = (s32[8]{0:T(128)S(1)}, s32[8]{0:T(128)}, u32[]{:S(2)}) copy-start(s32[8]{0:T(128)} %param.17) | copy-start | bytes 100
  16.1 5.9 %collective-permute-start.13 = (bf16[8,2048]{1,0:T(8,128)(2,1)S(1)}, bf16[8,2048]{1,0:T(8,128)(2,1)S(1)}, u32[]{:S(2)}, u32[]{:S(2)}) collective-permute-start(bf16[8,2048]{1,0:T(8,128)(2,1)S(1)} %get-tuple-element.11), channel_id=1, source_target_pairs={{0,24},{4,28},{8,16},{12,20},{16,8},{20,12},{24,0},{28,4},{1,25},{... | collective-permute-start | bytes 98312 | tf_op jit(solution)/shard_map/ppermute | solution.py:37
  19.6 4.4 %collective-permute-start.12 = (bf16[8,2048]{1,0:T(8,128)(2,1)S(1)}, bf16[8,2048]{1,0:T(8,128)(2,1)S(1)}, u32[]{:S(2)}, u32[]{:S(2)}) collective-permute-start(bf16[8,2048]{1,0:T(8,128)(2,1)S(1)} %get-tuple-element.12), channel_id=1, source_target_pairs={{0,16},{4,20},{8,24},{12,28},{16,0},{20,4},{24,8},{28,12},{1,17},{... | collective-permute-start | bytes 98312 | tf_op jit(solution)/shard_map/ppermute | solution.py:37
  20.1 4.4 %collective-permute-start.11 = (bf16[8,2048]{1,0:T(8,128)(2,1)S(1)}, bf16[8,2048]{1,0:T(8,128)(2,1)S(1)}, u32[]{:S(2)}, u32[]{:S(2)}) collective-permute-start(bf16[8,2048]{1,0:T(8,128)(2,1)S(1)} %get-tuple-element.10), channel_id=1, source_target_pairs={{0,8},{4,12},{8,0},{12,4},{16,24},{20,28},{24,16},{28,20},{1,9},{5... | collective-permute-start | bytes 98312 | tf_op jit(solution)/shard_map/ppermute | solution.py:37
  24.6 1.3 %collective-permute-start.14 = (f32[8,1024]{1,0:T(8,128)S(1)}, f32[8,1024]{1,0:T(8,128)S(1)}, u32[]{:S(2)}, u32[]{:S(2)}) collective-permute-start(f32[8,1024]{1,0:T(8,128)S(1)} %constant_dynamic-slice_fusion), channel_id=1, source_target_pairs={{0,4},{4,0},{8,12},{12,8},{16,20},{20,16},{24,28},{28,24},{1,5},{5... | collective-permute-start | bytes 98312 | tf_op jit(solution)/shard_map/ppermute | solution.py:42
  26.3 1.2 %collective-permute-start.15 = (f32[8,1152]{1,0:T(8,128)S(1)}, f32[8,1152]{1,0:T(8,128)S(1)}, u32[]{:S(2)}, u32[]{:S(2)}) collective-permute-start(f32[8,1152]{1,0:T(8,128)S(1)} %fusion.44), channel_id=1, source_target_pairs={{0,4},{4,0},{8,12},{12,8},{16,20},{20,16},{24,28},{28,24},{1,5},{5... | collective-permute-start | bytes 110600 | tf_op jit(solution)/shard_map/ppermute | solution.py:26
  27.5 7.0 %collective-permute-start.18 = (f32[8,1152]{1,0:T(8,128)S(1)}, f32[8,1152]{1,0:T(8,128)S(1)}, u32[]{:S(2)}, u32[]{:S(2)}) collective-permute-start(f32[8,1152]{1,0:T(8,128)S(1)} %add.288), channel_id=1, source_target_pairs={{0,24},{4,28},{8,16},{12,20},{16,8},{20,12},{24,0},{28,4},{1,25},{... | collective-permute-start | bytes 110600 | tf_op jit(solution)/shard_map/ppermute | solution.py:27
  29.0 6.7 %collective-permute-start.17 = (f32[8,1152]{1,0:T(8,128)S(1)}, f32[8,1152]{1,0:T(8,128)S(1)}, u32[]{:S(2)}, u32[]{:S(2)}) collective-permute-start(f32[8,1152]{1,0:T(8,128)S(1)} %add.288), channel_id=1, source_target_pairs={{0,16},{4,20},{8,24},{12,28},{16,0},{20,4},{24,8},{28,12},{1,17},{... | collective-permute-start | bytes 110600 | tf_op jit(solution)/shard_map/ppermute | solution.py:27
  29.9 5.7 %collective-permute-start.16 = (f32[8,1152]{1,0:T(8,128)S(1)}, f32[8,1152]{1,0:T(8,128)S(1)}, u32[]{:S(2)}, u32[]{:S(2)}) collective-permute-start(f32[8,1152]{1,0:T(8,128)S(1)} %add.288), channel_id=1, source_target_pairs={{0,8},{4,12},{8,0},{12,4},{16,24},{20,28},{24,16},{28,20},{1,9},{5... | collective-permute-start | bytes 110600 | tf_op jit(solution)/shard_map/ppermute | solution.py:27
  31.1 13.7 %collective-permute-start.3 = (bf16[512,256]{1,0:T(8,128)(2,1)S(1)}, bf16[512,256]{1,0:T(8,128)(2,1)S(1)}, u32[]{:S(2)}, u32[]{:S(2)}) collective-permute-start(bf16[512,256]{1,0:T(8,128)(2,1)S(1)} %pad_maximum_fusion), channel_id=1, source_target_pairs={{0,24},{4,28},{8,16},{12,20},{16,8},{20,12},{24,0},{28,4},{1,25},{... | collective-permute-start | bytes 786440 | tf_op jit(solution)/shard_map/ppermute | solution.py:76
  32.6 18.3 %collective-permute-start.2 = (bf16[512,256]{1,0:T(8,128)(2,1)S(1)}, bf16[512,256]{1,0:T(8,128)(2,1)S(1)}, u32[]{:S(2)}, u32[]{:S(2)}) collective-permute-start(bf16[512,256]{1,0:T(8,128)(2,1)S(1)} %pad_maximum_fusion), channel_id=1, source_target_pairs={{0,16},{4,20},{8,24},{12,28},{16,0},{20,4},{24,8},{28,12},{1,17},{... | collective-permute-start | bytes 786440 | tf_op jit(solution)/shard_map/ppermute | solution.py:76
  34.5 20.8 %collective-permute-start.1 = (bf16[512,256]{1,0:T(8,128)(2,1)S(1)}, bf16[512,256]{1,0:T(8,128)(2,1)S(1)}, u32[]{:S(2)}, u32[]{:S(2)}) collective-permute-start(bf16[512,256]{1,0:T(8,128)(2,1)S(1)} %pad_maximum_fusion), channel_id=1, source_target_pairs={{0,8},{4,12},{8,0},{12,4},{16,24},{20,28},{24,16},{28,20},{1,9},{5... | collective-permute-start | bytes 786440 | tf_op jit(solution)/shard_map/ppermute | solution.py:76
  40.7 20.8 %collective-permute-start.19 = (f32[8,1024]{1,0:T(8,128)S(1)}, f32[8,1024]{1,0:T(8,128)S(1)}, u32[]{:S(2)}, u32[]{:S(2)}) collective-permute-start(f32[8,1024]{1,0:T(8,128)S(1)} %fusion.10), channel_id=1, source_target_pairs={{0,3},{1,2},{2,1},{3,0},{4,7},{5,6},{6,5},{7,4},{8,11},{9,10},{10,... | collective-permute-start | bytes 98312 | tf_op jit(solution)/shard_map/ppermute | solution.py:46
  44.4 17.7 %collective-permute-start.20 = (f32[8,1024]{1,0:T(8,128)S(1)}, f32[8,1024]{1,0:T(8,128)S(1)}, u32[]{:S(2)}, u32[]{:S(2)}) collective-permute-start(f32[8,1024]{1,0:T(8,128)S(1)} %fusion.10), channel_id=1, source_target_pairs={{0,2},{1,3},{2,0},{3,1},{4,6},{5,7},{6,4},{7,5},{8,10},{9,11},{10,... | collective-permute-start | bytes 98312 | tf_op jit(solution)/shard_map/ppermute | solution.py:46
  44.8 17.4 %collective-permute-start.21 = (f32[8,1024]{1,0:T(8,128)S(1)}, f32[8,1024]{1,0:T(8,128)S(1)}, u32[]{:S(2)}, u32[]{:S(2)}) collective-permute-start(f32[8,1024]{1,0:T(8,128)S(1)} %fusion.10), channel_id=1, source_target_pairs={{0,1},{1,0},{2,3},{3,2},{4,5},{5,4},{6,7},{7,6},{8,9},{9,8},{10,11... | collective-permute-start | bytes 98312 | tf_op jit(solution)/shard_map/ppermute | solution.py:46
  57.4 7.6 %collective-permute-start.6 = (f32[128,256]{1,0:T(8,128)S(1)}, f32[128,256]{1,0:T(8,128)S(1)}, u32[]{:S(2)}, u32[]{:S(2)}) collective-permute-start(f32[128,256]{1,0:T(8,128)S(1)} %fusion.9), channel_id=1, source_target_pairs={{0,3},{1,2},{2,1},{3,0},{4,7},{5,6},{6,5},{7,4},{8,11},{9,10},{10,... | collective-permute-start | bytes 393224 | tf_op jit(solution)/shard_map/ppermute | solution.py:46
  61.5 7.4 %collective-permute-start.5 = (f32[128,256]{1,0:T(8,128)S(1)}, f32[128,256]{1,0:T(8,128)S(1)}, u32[]{:S(2)}, u32[]{:S(2)}) collective-permute-start(f32[128,256]{1,0:T(8,128)S(1)} %fusion.9), channel_id=1, source_target_pairs={{0,2},{1,3},{2,0},{3,1},{4,6},{5,7},{6,4},{7,5},{8,10},{9,11},{10,... | collective-permute-start | bytes 393224 | tf_op jit(solution)/shard_map/ppermute | solution.py:46
  61.5 7.4 %collective-permute-start.4 = (f32[128,256]{1,0:T(8,128)S(1)}, f32[128,256]{1,0:T(8,128)S(1)}, u32[]{:S(2)}, u32[]{:S(2)}) collective-permute-start(f32[128,256]{1,0:T(8,128)S(1)} %fusion.9), channel_id=1, source_target_pairs={{0,1},{1,0},{2,3},{3,2},{4,5},{5,4},{6,7},{7,6},{8,9},{9,8},{10,11... | collective-permute-start | bytes 393224 | tf_op jit(solution)/shard_map/ppermute | solution.py:46
  68.9 1.3 %collective-permute-start.7 = (bf16[128,256]{1,0:T(8,128)(2,1)S(1)}, bf16[128,256]{1,0:T(8,128)(2,1)S(1)}, u32[]{:S(2)}, u32[]{:S(2)}) collective-permute-start(bf16[128,256]{1,0:T(8,128)(2,1)S(1)} %add_convert_fusion), channel_id=1, source_target_pairs={{0,4},{4,0},{8,12},{12,8},{16,20},{20,16},{24,28},{28,24},{1,5},{5... | collective-permute-start | bytes 196616 | tf_op jit(solution)/shard_map/ppermute | solution.py:72
  70.3 6.4 %collective-permute-start.8 = (bf16[256,256]{1,0:T(8,128)(2,1)S(1)}, bf16[256,256]{1,0:T(8,128)(2,1)S(1)}, u32[]{:S(2)}, u32[]{:S(2)}) collective-permute-start(bf16[256,256]{1,0:T(8,128)(2,1)S(1)} %pad_maximum_fusion.2), channel_id=1, source_target_pairs={{0,8},{4,12},{8,0},{12,4},{16,24},{20,28},{24,16},{28,20},{1,9},{5... | collective-permute-start | bytes 393224 | tf_op jit(solution)/shard_map/ppermute | solution.py:76
  71.3 8.1 %collective-permute-start.9 = (bf16[256,256]{1,0:T(8,128)(2,1)S(1)}, bf16[256,256]{1,0:T(8,128)(2,1)S(1)}, u32[]{:S(2)}, u32[]{:S(2)}) collective-permute-start(bf16[256,256]{1,0:T(8,128)(2,1)S(1)} %pad_maximum_fusion.2), channel_id=1, source_target_pairs={{0,16},{4,20},{8,24},{12,28},{16,0},{20,4},{24,8},{28,12},{1,17},{... | collective-permute-start | bytes 393224 | tf_op jit(solution)/shard_map/ppermute | solution.py:76
  72.4 7.0 %collective-permute-start.10 = (bf16[256,256]{1,0:T(8,128)(2,1)S(1)}, bf16[256,256]{1,0:T(8,128)(2,1)S(1)}, u32[]{:S(2)}, u32[]{:S(2)}) collective-permute-start(bf16[256,256]{1,0:T(8,128)(2,1)S(1)} %pad_maximum_fusion.2), channel_id=1, source_target_pairs={{0,24},{4,28},{8,16},{12,20},{16,8},{20,12},{24,0},{28,4},{1,25},{... | collective-permute-start | bytes 393224 | tf_op jit(solution)/shard_map/ppermute | solution.py:76
Sparse Core Ops, SparseCore 0:
  9.9 48.2 all-gather.1

commit v5 on v4

--- a/solution.py
+++ b/solution.py
@@ -99,13 +99,14 @@
     d_rows = w_query.shape[0]
     heads_here = w_query.shape[1] // HEAD
     sharers = GROUP // heads_here
-    kv_rows_here = d_rows // sharers
+    kv_width = HEAD // sharers
     kv_head = tp_i * heads_here // GROUP
     kv_part = tp_i % sharers
+    kv_start = kv_head * HEAD + kv_part * kv_width
     kv_weights = jnp.concatenate(
         [
-            lax.dynamic_slice(w_key, (kv_part * kv_rows_here, kv_head * HEAD), (kv_rows_here, HEAD)),
-            lax.dynamic_slice(w_value, (kv_part * kv_rows_here, kv_head * HEAD), (kv_rows_here, HEAD)),
+            lax.dynamic_slice_in_dim(w_key, kv_start, kv_width, 1),
+            lax.dynamic_slice_in_dim(w_value, kv_start, kv_width, 1),
         ],
         axis=1,
     )
@@ -137,9 +138,20 @@
     critic_values = critic_sum.astype(jnp.bfloat16)
 
     kv_pieces = gather_pieces(kv_weights, n_seq)
-    kv_part_sum = project(normed, kv_pieces, d_rows, kv_part * kv_rows_here)
-    kv_rows = group_sum(kv_part_sum, "tp", n_tp, sharers, canonical=False)
-    kv_rows = kv_rows.astype(jnp.bfloat16)
+    kv_own = project(normed, kv_pieces, d_rows).astype(jnp.bfloat16)
+    got = [kv_own] + [
+        lax.ppermute(kv_own, "tp", xor_perm(n_tp, lambda j, k=k: j ^ k))
+        for k in range(1, sharers)
+    ]
+    shares = []
+    for m in range(sharers):
+        value = got[0]
+        for k in range(1, sharers):
+            value = jnp.where((kv_part ^ k) == m, got[k], value)
+        shares.append(value)
+    kv_rows = jnp.concatenate(
+        [v[:, :kv_width] for v in shares] + [v[:, kv_width:] for v in shares], axis=1
+    )
     kv_all = gather_pieces(kv_rows, n_seq)
     key_block = jnp.concatenate([piece[:, :HEAD] for piece, _, _ in kv_all], axis=0)
     value_block = jnp.concatenate([piece[:, HEAD:] for piece, _, _ in kv_all], axis=0)

time: 93.2 us -> 105 us (1.13)
  waiting for transfers between devices: 23.5 us -> 35 us
  other arithmetic: 6.54 us -> 8.94 us
  matrix products: 18.9 us -> 17.6 us
    ppermute x6, waiting for transfers between devices: 10.7 us -> 26.2 us  [gather_pieces(): got = lax.ppermute(pair, 'seq', xor_perm(8, lambda j, m=m: j ^ m))]
    ppermute x6 -> x3, waiting for transfers between devices: 6.15 us -> 0.01 us  [group_sum(): lax.ppermute(x, axis, xor_perm(n, lambda j, k=k: j ^ k))]
    ppermute x6 -> x3, starting transfers between devices: 10.1 us -> 5.12 us  [group_sum(): lax.ppermute(x, axis, xor_perm(n, lambda j, k=k: j ^ k))]
    ppermute x0 -> x3, starting transfers between devices: none -> 4.45 us  [body(): lax.ppermute(kv_own, 'tp', xor_perm(n_tp, lambda j, k=k: j ^ k))]
    dot_general x8, matrix products: 8.01 us -> 4.48 us  [project(): term = jnp.dot(cols, piece, preferred_element_type=jnp.float32)]
    ppermute x0 -> x3, waiting for transfers between devices: none -> 3.09 us  [body(): lax.ppermute(kv_own, 'tp', xor_perm(n_tp, lambda j, k=k: j ^ k))]
    dot_general x1, matrix products: 0.43 us -> 2.02 us  [body(): jnp.dot(picker, normed, preferred_element_type=jnp.float32)]
    convert_element_type x1, other arithmetic: 2.17 us -> 3.52 us  [rms_norm(): (widened * lax.rsqrt(mean_square + 1e-05) * norm_gain.astype(jnp.float32)...]
  transfers between devices with their start and end apart: 23 -> 23, of which waited for: 13 -> 11; matrix products, arithmetic and copies ran while one was open for 22% -> 21% of each run, Pallas kernels for 0% -> 0%
where the time goes in v5:
time: 105 us
  waiting for transfers between devices  35 us (33%)
  starting transfers between devices  25.1 us (24%)
  matrix products  17.6 us (17%)
  between operations  14.6 us (14%)
  other arithmetic  8.94 us (9%)
  local copies, waits for them, and re-layouts  3.67 us (3%)
    ppermute x6, waiting for transfers between devices, gather_pieces(): got = lax.ppermute(pair, 'seq', xor_perm(8, lambda j, m=m: j ^ m))  26.2 us
    ppermute x6, starting transfers between devices, gather_pieces(): got = lax.ppermute(pair, 'seq', xor_perm(8, lambda j, m=m: j ^ m))  7.17 us
    ppermute x3, starting transfers between devices, group_sum(): lax.ppermute(x, axis, xor_perm(n, lambda j, k=k: j ^ k))  5.12 us
    dot_general x1, matrix products, body(): jnp.einsum('dc,rce->dre', critic_hidden, critic_down, preferred_element_t...  5.02 us
    dot_general x8, matrix products, project(): term = jnp.dot(cols, piece, preferred_element_type=jnp.float32)  4.48 us
    ppermute x3, starting transfers between devices, body(): lax.ppermute(kv_own, 'tp', xor_perm(n_tp, lambda j, k=k: j ^ k))  4.45 us
    ppermute x3, starting transfers between devices, seq_reduce_scatter(): lax.ppermute(part, 'seq', xor_perm(8, lambda j, m=m: j ^ m))  4.01 us
    dot_general x1, matrix products, body(): jnp.dot(normed, q_weights, preferred_element_type=jnp.float32)  3.54 us
  transfers between devices with their start and end apart: 23, of which 11 were waited for; matrix products, arithmetic and copies ran while one was open for 21% of the time, Pallas kernels for 0%

profile of v5, /device:TPU:0, one launch (start us, length us, event | category | flops | bytes accessed | tf_op | source)
XLA Modules:
  0.0 104.9 jit_solution(4693480901862494544)
XLA Ops:
  7.2 0.0 all-gather.2.cloned.1.call-start
  7.3 1.4 %constant_dynamic-slice_fusion.4 = (bf16[1024,32]{1,0:T(8,128)(2,1)S(1)}, bf16[1024,32]{1,0:T(8,128)(2,1)S(1)}) fusion(bf16[1024,128]{1,0:T(8,128)(2,1)} %param.13, s32[]{:T(128)S(6)} %select_n.244, bf16[1024,128]{1,0:T(8,128)(2,1)} %param.12), kind=kLoop, calls=%fused_computation.112 | loop fusion | bytes 262148 | tf_op jit(solution)/shard_map/dynamic_slice | solution.py:109
  8.7 0.1 pad_maximum_fusion.1
  8.8 0.6 collective-permute-start
  9.5 2.1 %fusion = f32[128]{0:T(128)S(1)} fusion(bf16[128,8192]{1,0:T(8,128)(2,1)} %param.9), kind=kLoop, calls=%fused_computation.3 | loop fusion | flops 3145600 | bytes 2097664 | tf_op jit(solution)/shard_map/reduce_sum | solution.py:15
  11.7 0.2 reduce-window.7
  11.8 3.5 %fusion.2 = bf16[128,8192]{1,0:T(8,128)(2,1)} fusion(bf16[128,8192]{1,0:T(8,128)(2,1)} %param.9, f32[8192]{0:T(1024)S(1)} %convert_element_type.61, f32[128]{0:T(128)S(1)} %add_rsqrt_fusion), kind=kLoop, calls=%fused_computation.5 | loop fusion | flops 4194304 | bytes 4227584 | tf_op jit(solution)/shard_map/convert_element_type | solution.py:16
  15.5 2.0 %convolution_convert_fusion = bf16[8,8192]{1,0:T(8,128)(2,1)S(1)} fusion(bf16[128,8192]{1,0:T(8,128)(2,1)} %fusion.2, s32[128]{0:T(128)S(1)} %get-tuple-element.46, s32[8]{0:T(128)S(1)} %add_bitcast_fusion), kind=kOutput, calls=%fused_computation | convolution fusion | flops 16843776 | bytes 2228768 | tf_op jit(solution)/shard_map/dot_general | solution.py:118
  17.5 0.6 constant_dynamic-slice_fusion.3
  18.2 3.4 %collective-permute-start.13 = (bf16[8,2048]{1,0:T(8,128)(2,1)}, bf16[8,2048]{1,0:T(8,128)(2,1)}, u32[]{:S(2)}, u32[]{:S(2)}) collective-permute-start(bf16[8,2048]{1,0:T(8,128)(2,1)} %get-tuple-element.11), channel_id=1, source_target_pairs={{0,24},{4,28},{8,16},{12,20},{16,8},{20,12},{24,0},{28,4},{1,25},{... | collective-permute-start | bytes 98312 | tf_op jit(solution)/shard_map/ppermute | solution.py:37
  21.6 0.5 collective-permute-start.12
  22.1 0.1 collective-permute-start.11
  22.2 1.8 %fusion.42 = f32[128,64]{0,1:T(8,128)} fusion(bf16[1024,64]{1,0:T(8,128)(2,1)S(1)} %pad_maximum_fusion.1, bf16[128,8192]{1,0:T(8,128)(2,1)} %fusion.2, s32[]{:T(128)S(6)} %select_n.242), kind=kOutput, calls=%fused_computation.56 | convolution fusion | flops 16777216 | bytes 425988 | tf_op jit(solution)/shard_map/dot_general | solution.py:85
  24.0 0.7 iota_compare_fusion
  24.6 2.0 %collective-permute-done.12 = bf16[8,2048]{1,0:T(8,128)(2,1)} collective-permute-done((bf16[8,2048]{1,0:T(8,128)(2,1)}, bf16[8,2048]{1,0:T(8,128)(2,1)}, u32[]{:S(2)}, u32[]{:S(2)}) %collective-permute-start.12) | collective-permute-done | bytes 32800 | tf_op jit(solution)/shard_map/ppermute | solution.py:37
  26.6 0.4 collective-permute-done.11
  27.0 0.8 convert_add_fusion
  27.9 0.6 copy-done.2
  28.5 0.1 convert_reduce_fusion
  28.6 1.1 %collective-permute-done.14 = f32[8,1024]{1,0:T(8,128)S(1)} collective-permute-done((f32[8,1024]{1,0:T(8,128)S(1)}, f32[8,1024]{1,0:T(8,128)S(1)}, u32[]{:S(2)}, u32[]{:S(2)}) %collective-permute-start.14) | collective-permute-done | bytes 32800 | tf_op jit(solution)/shard_map/ppermute | solution.py:42
  29.7 1.2 %fusion.45 = f32[8,1152]{1,0:T(8,128)S(1)} fusion(bf16[1024,1152]{1,0:T(8,128)(2,1)S(1)} %copy-done, f32[8,1024]{1,0:T(8,128)S(1)} %collective-permute-done.14, f32[8,2048]{1,0:T(8,128)} %copy-done.2, s32[]{:T(128)S(6)} %select_n.289), kind=kOutput, calls=%fused_computation.87 | convolution fusion | flops 18890752 | bytes 2461700 | tf_op jit(solution)/shard_map/dot_general | solution.py:123
  30.9 0.2 collective-permute-start.15
  31.1 0.1 convert_reduce_fusion.1
  31.2 1.0 collective-permute-done.15
  32.1 1.5 %collective-permute-start.18 = (f32[8,1152]{1,0:T(8,128)S(1)}, f32[8,1152]{1,0:T(8,128)S(1)}, u32[]{:S(2)}, u32[]{:S(2)}) collective-permute-start(f32[8,1152]{1,0:T(8,128)S(1)} %add.246), channel_id=1, source_target_pairs={{0,24},{4,28},{8,16},{12,20},{16,8},{20,12},{24,0},{28,4},{1,25},{... | collective-permute-start | bytes 110600 | tf_op jit(solution)/shard_map/ppermute | solution.py:27
  33.6 1.1 %collective-permute-start.17 = (f32[8,1152]{1,0:T(8,128)S(1)}, f32[8,1152]{1,0:T(8,128)S(1)}, u32[]{:S(2)}, u32[]{:S(2)}) collective-permute-start(f32[8,1152]{1,0:T(8,128)S(1)} %add.246), channel_id=1, source_target_pairs={{0,16},{4,20},{8,24},{12,28},{16,0},{20,4},{24,8},{28,12},{1,17},{... | collective-permute-start | bytes 110600 | tf_op jit(solution)/shard_map/ppermute | solution.py:27
  34.7 0.9 collective-permute-start.16
  35.6 0.2 pad_maximum_fusion
  35.8 1.5 %collective-permute-start.3 = (bf16[2048,64]{1,0:T(8,128)(2,1)S(1)}, bf16[2048,64]{1,0:T(8,128)(2,1)S(1)}, u32[]{:S(2)}, u32[]{:S(2)}) collective-permute-start(bf16[2048,64]{1,0:T(8,128)(2,1)S(1)} %pad_maximum_fusion), channel_id=1, source_target_pairs={{0,24},{4,28},{8,16},{12,20},{16,8},{20,12},{24,0},{28,4},{1,25},{... | collective-permute-start | bytes 786440 | tf_op jit(solution)/shard_map/ppermute | solution.py:76
  37.4 1.1 %collective-permute-start.2 = (bf16[2048,64]{1,0:T(8,128)(2,1)S(1)}, bf16[2048,64]{1,0:T(8,128)(2,1)S(1)}, u32[]{:S(2)}, u32[]{:S(2)}) collective-permute-start(bf16[2048,64]{1,0:T(8,128)(2,1)S(1)} %pad_maximum_fusion), channel_id=1, source_target_pairs={{0,16},{4,20},{8,24},{12,28},{16,0},{20,4},{24,8},{28,12},{1,17},{... | collective-permute-start | bytes 786440 | tf_op jit(solution)/shard_map/ppermute | solution.py:76
  38.5 1.2 %convolution_add_fusion.1 = f32[128,64]{0,1:T(8,128)S(1)} fusion(f32[128,64]{0,1:T(8,128)S(1)} %copy-done.3, bf16[1024,64]{1,0:T(8,128)(2,1)S(1)} %collective-permute-done, bf16[128,8192]{1,0:T(8,128)(2,1)} %fusion.2, s32[]{:T(128)S(6)} %select_n.245), kind=kOutput, calls=%fused_computation.20 | convolution fusion | flops 16785408 | bytes 458756 | tf_op jit(solution)/shard_map/dot_general | solution.py:85
  39.7 1.0 collective-permute-start.1
  40.7 5.0 %fusion.5 = f32[8,1024]{1,0:T(8,128)S(1)} fusion(bf16[4,1152,1024]{2,1,0:T(8,128)(2,1)} %param.16, pred[8,4]{0,1:T(4,128)(4,1)S(1)} %iota_compare_fusion, f32[8,1152]{1,0:T(8,128)S(1)} %collective-permute-done.18, f32[8,1152]{1,0:T(8,128)S(1)} %collective-permute-done.17, f32[8,1152]{1,0:T(8,128)S(1)} %add.246, f32[8,1152]{1,0:T(8,128)S(1)} %collective-permute-done.16), kind=kOutput, calls=%fused_computation.12 | convolution fusion | flops 75628544 | bytes 9617440 | tf_op jit(solution)/shard_map/dc,rce->dre/dot_general | solution.py:129
  45.7 3.6 %collective-permute-start.19 = (f32[8,1024]{1,0:T(8,128)S(1)}, f32[8,1024]{1,0:T(8,128)S(1)}, u32[]{:S(2)}, u32[]{:S(2)}) collective-permute-start(f32[8,1024]{1,0:T(8,128)S(1)} %fusion.5), channel_id=1, source_target_pairs={{0,3},{1,2},{2,1},{3,0},{4,7},{5,6},{6,5},{7,4},{8,11},{9,10},{10,... | collective-permute-start | bytes 98312 | tf_op jit(solution)/shard_map/ppermute | solution.py:46
  49.3 12.7 %collective-permute-done.3 = bf16[2048,64]{1,0:T(8,128)(2,1)S(1)} collective-permute-done((bf16[2048,64]{1,0:T(8,128)(2,1)S(1)}, bf16[2048,64]{1,0:T(8,128)(2,1)S(1)}, u32[]{:S(2)}, u32[]{:S(2)}) %collective-permute-start.3) | collective-permute-done | bytes 262176 | tf_op jit(solution)/shard_map/ppermute | solution.py:76
  62.0 1.5 %collective-permute-start.21 = (f32[8,1024]{1,0:T(8,128)S(1)}, f32[8,1024]{1,0:T(8,128)S(1)}, u32[]{:S(2)}, u32[]{:S(2)}) collective-permute-start(f32[8,1024]{1,0:T(8,128)S(1)} %fusion.5), channel_id=1, source_target_pairs={{0,1},{1,0},{2,3},{3,2},{4,5},{5,4},{6,7},{7,6},{8,9},{9,8},{10,11... | collective-permute-start | bytes 98312 | tf_op jit(solution)/shard_map/ppermute | solution.py:46
  63.5 0.2 fusion.20
  63.7 0.2 fusion.22
  64.0 7.4 %collective-permute-done.2 = bf16[2048,64]{1,0:T(8,128)(2,1)S(1)} collective-permute-done((bf16[2048,64]{1,0:T(8,128)(2,1)S(1)}, bf16[2048,64]{1,0:T(8,128)(2,1)S(1)}, u32[]{:S(2)}, u32[]{:S(2)}) %collective-permute-start.2) | collective-permute-done | bytes 262176 | tf_op jit(solution)/shard_map/ppermute | solution.py:76
  71.4 0.2 fusion.24
  71.7 0.2 fusion.26
  71.9 0.2 fusion.28
  72.2 0.3 fusion.13
  72.4 3.5 %collective-permute-start.4 = (bf16[128,64]{0,1:T(8,128)(2,1)S(1)}, bf16[128,64]{0,1:T(8,128)(2,1)S(1)}, u32[]{:S(2)}, u32[]{:S(2)}) collective-permute-start(bf16[128,64]{0,1:T(8,128)(2,1)S(1)} %fusion.13), channel_id=1, source_target_pairs={{0,3},{1,2},{2,1},{3,0},{4,7},{5,6},{6,5},{7,4},{8,11},{9,10},{10,... | collective-permute-start | bytes 49160 | tf_op jit(solution)/shard_map/ppermute | solution.py:143
  76.0 0.9 collective-permute-start.6
  76.9 0.6 add_convert_fusion
  77.5 0.7 collective-permute-done.4
  78.2 2.4 %collective-permute-done.5 = bf16[128,64]{0,1:T(8,128)(2,1)S(1)} collective-permute-done((bf16[128,64]{0,1:T(8,128)(2,1)S(1)}, bf16[128,64]{0,1:T(8,128)(2,1)S(1)}, u32[]{:S(2)}, u32[]{:S(2)}) %collective-permute-start.5) | collective-permute-done | bytes 16416 | tf_op jit(solution)/shard_map/ppermute | solution.py:143
  80.7 0.1 collective-permute-start.7
  80.9 1.2 %collective-permute-done.7 = bf16[128,256]{0,1:T(8,128)(2,1)S(1)} collective-permute-done((bf16[128,256]{0,1:T(8,128)(2,1)S(1)}, bf16[128,256]{0,1:T(8,128)(2,1)S(1)}, u32[]{:S(2)}, u32[]{:S(2)}) %collective-permute-start.7) | collective-permute-done | bytes 65568 | tf_op jit(solution)/shard_map/ppermute | solution.py:72
  82.1 1.6 %collective-permute-start.8 = (bf16[256,256]{0,1:T(8,128)(2,1)S(1)}, bf16[256,256]{0,1:T(8,128)(2,1)S(1)}, u32[]{:S(2)}, u32[]{:S(2)}) collective-permute-start(bf16[256,256]{0,1:T(8,128)(2,1)S(1)} %pad_maximum_fusion.2), channel_id=1, source_target_pairs={{0,8},{4,12},{8,0},{12,4},{16,24},{20,28},{24,16},{28,20},{1,9},{5... | collective-permute-start | bytes 393224 | tf_op jit(solution)/shard_map/ppermute | solution.py:76
  83.7 0.5 collective-permute-start.9
  84.2 1.4 %collective-permute-start.10 = (bf16[256,256]{0,1:T(8,128)(2,1)S(1)}, bf16[256,256]{0,1:T(8,128)(2,1)S(1)}, u32[]{:S(2)}, u32[]{:S(2)}) collective-permute-start(bf16[256,256]{0,1:T(8,128)(2,1)S(1)} %pad_maximum_fusion.2), channel_id=1, source_target_pairs={{0,24},{4,28},{8,16},{12,20},{16,8},{20,12},{24,0},{28,4},{1,25},{... | collective-permute-start | bytes 393224 | tf_op jit(solution)/shard_map/ppermute | solution.py:76
  85.7 2.4 %collective-permute-done.8 = bf16[256,256]{0,1:T(8,128)(2,1)S(1)} collective-permute-done((bf16[256,256]{0,1:T(8,128)(2,1)S(1)}, bf16[256,256]{0,1:T(8,128)(2,1)S(1)}, u32[]{:S(2)}, u32[]{:S(2)}) %collective-permute-start.8) | collective-permute-done | bytes 131104 | tf_op jit(solution)/shard_map/ppermute | solution.py:76
  88.1 3.7 %collective-permute-done.9 = bf16[256,256]{0,1:T(8,128)(2,1)S(1)} collective-permute-done((bf16[256,256]{0,1:T(8,128)(2,1)S(1)}, bf16[256,256]{0,1:T(8,128)(2,1)S(1)}, u32[]{:S(2)}, u32[]{:S(2)}) %collective-permute-start.9) | collective-permute-done | bytes 131104 | tf_op jit(solution)/shard_map/ppermute | solution.py:76
  91.8 0.0 all-gather.2.cloned.1.call-done
  91.8 3.5 %convolution_convert_fusion.1 = bf16[128,256]{1,0:T(8,128)(2,1)S(1)} fusion(bf16[128,8192]{1,0:T(8,128)(2,1)} %fusion.2, bf16[8192,256]{1,0:T(8,128)(2,1)} %all-gather.2.cloned.1.call-done), kind=kOutput, calls=%fused_computation.11 | convolution fusion | flops 536903680 | bytes 6356992 | tf_op jit(solution)/shard_map/dot_general | solution.py:167
  95.4 0.1 fusion.61
  95.5 0.3 fusion.66
  95.8 0.3 fusion.67
  96.2 0.4 fusion.14
  96.6 0.4 fusion.7
  96.9 0.4 fusion.6
  97.3 0.7 copy.17
  (58 shorter events, 0.4 us)
Async XLA Ops:
  7.2 22.5 %copy-start = (bf16[1024,1152]{1,0:T(8,128)(2,1)S(1)}, bf16[1024,1152]{1,0:T(8,128)(2,1)}, u32[]{:S(2)}) copy-start(bf16[1024,1152]{1,0:T(8,128)(2,1)} %param.15) | copy-start | bytes 7077892
  7.2 2.3 %copy-start.4 = (bf16[8192]{0:T(1024)(128)(2,1)S(1)}, bf16[8192]{0:T(1024)(128)(2,1)}, u32[]{:S(2)}) copy-start(bf16[8192]{0:T(1024)(128)(2,1)} %param.10) | copy-start | bytes 49156
  7.2 84.6 %all-gather.2.cloned.1.call-start = ((), (), s32[]{:S(2)}) async-start(), calls=%async_computation | async-start | bytes 4718592 | tf_op jit(solution)/shard_map/all_gather | solution.py:165
  7.3 4.4 %copy-start.5 = (s32[8]{0:T(128)S(1)}, s32[8]{0:T(128)}, u32[]{:S(2)}) copy-start(s32[8]{0:T(128)} %param.14) | copy-start | bytes 100
  8.8 26.8 %collective-permute-start = (bf16[1024,64]{1,0:T(8,128)(2,1)S(1)}, bf16[1024,64]{1,0:T(8,128)(2,1)S(1)}, u32[]{:S(2)}, u32[]{:S(2)}) collective-permute-start(bf16[1024,64]{1,0:T(8,128)(2,1)S(1)} %pad_maximum_fusion.1), channel_id=1, source_target_pairs={{0,4},{4,0},{8,12},{12,8},{16,20},{20,16},{24,28},{28,24},{1,5},{5... | collective-permute-start | bytes 393224 | tf_op jit(solution)/shard_map/ppermute | solution.py:72
  18.2 6.5 %collective-permute-start.13 = (bf16[8,2048]{1,0:T(8,128)(2,1)}, bf16[8,2048]{1,0:T(8,128)(2,1)}, u32[]{:S(2)}, u32[]{:S(2)}) collective-permute-start(bf16[8,2048]{1,0:T(8,128)(2,1)} %get-tuple-element.11), channel_id=1, source_target_pairs={{0,24},{4,28},{8,16},{12,20},{16,8},{20,12},{24,0},{28,4},{1,25},{... | collective-permute-start | bytes 98312 | tf_op jit(solution)/shard_map/ppermute | solution.py:37
  21.6 5.0 %collective-permute-start.12 = (bf16[8,2048]{1,0:T(8,128)(2,1)}, bf16[8,2048]{1,0:T(8,128)(2,1)}, u32[]{:S(2)}, u32[]{:S(2)}) collective-permute-start(bf16[8,2048]{1,0:T(8,128)(2,1)} %get-tuple-element.12), channel_id=1, source_target_pairs={{0,16},{4,20},{8,24},{12,28},{16,0},{20,4},{24,8},{28,12},{1,17},{... | collective-permute-start | bytes 98312 | tf_op jit(solution)/shard_map/ppermute | solution.py:37
  22.1 4.9 %collective-permute-start.11 = (bf16[8,2048]{1,0:T(8,128)(2,1)}, bf16[8,2048]{1,0:T(8,128)(2,1)}, u32[]{:S(2)}, u32[]{:S(2)}) collective-permute-start(bf16[8,2048]{1,0:T(8,128)(2,1)} %get-tuple-element.10), channel_id=1, source_target_pairs={{0,8},{4,12},{8,0},{12,4},{16,24},{20,28},{24,16},{28,20},{1,9},{5... | collective-permute-start | bytes 98312 | tf_op jit(solution)/shard_map/ppermute | solution.py:37
  27.9 0.6 copy-start.2
  28.5 10.0 %copy-start.3 = (f32[128,64]{0,1:T(8,128)S(1)}, f32[128,64]{0,1:T(8,128)}, u32[]{:S(2)}) copy-start(f32[128,64]{0,1:T(8,128)} %fusion.42) | copy-start | bytes 98308
  28.5 1.2 %collective-permute-start.14 = (f32[8,1024]{1,0:T(8,128)S(1)}, f32[8,1024]{1,0:T(8,128)S(1)}, u32[]{:S(2)}, u32[]{:S(2)}) collective-permute-start(f32[8,1024]{1,0:T(8,128)S(1)} %constant_dynamic-slice_fusion), channel_id=1, source_target_pairs={{0,4},{4,0},{8,12},{12,8},{16,20},{20,16},{24,28},{28,24},{1,5},{5... | collective-permute-start | bytes 98312 | tf_op jit(solution)/shard_map/ppermute | solution.py:42
  30.9 1.2 %collective-permute-start.15 = (f32[8,1152]{1,0:T(8,128)S(1)}, f32[8,1152]{1,0:T(8,128)S(1)}, u32[]{:S(2)}, u32[]{:S(2)}) collective-permute-start(f32[8,1152]{1,0:T(8,128)S(1)} %fusion.45), channel_id=1, source_target_pairs={{0,4},{4,0},{8,12},{12,8},{16,20},{20,16},{24,28},{28,24},{1,5},{5... | collective-permute-start | bytes 110600 | tf_op jit(solution)/shard_map/ppermute | solution.py:26
  32.1 7.5 %collective-permute-start.18 = (f32[8,1152]{1,0:T(8,128)S(1)}, f32[8,1152]{1,0:T(8,128)S(1)}, u32[]{:S(2)}, u32[]{:S(2)}) collective-permute-start(f32[8,1152]{1,0:T(8,128)S(1)} %add.246), channel_id=1, source_target_pairs={{0,24},{4,28},{8,16},{12,20},{16,8},{20,12},{24,0},{28,4},{1,25},{... | collective-permute-start | bytes 110600 | tf_op jit(solution)/shard_map/ppermute | solution.py:27
  33.6 7.1 %collective-permute-start.17 = (f32[8,1152]{1,0:T(8,128)S(1)}, f32[8,1152]{1,0:T(8,128)S(1)}, u32[]{:S(2)}, u32[]{:S(2)}) collective-permute-start(f32[8,1152]{1,0:T(8,128)S(1)} %add.246), channel_id=1, source_target_pairs={{0,16},{4,20},{8,24},{12,28},{16,0},{20,4},{24,8},{28,12},{1,17},{... | collective-permute-start | bytes 110600 | tf_op jit(solution)/shard_map/ppermute | solution.py:27
  34.7 6.0 %collective-permute-start.16 = (f32[8,1152]{1,0:T(8,128)S(1)}, f32[8,1152]{1,0:T(8,128)S(1)}, u32[]{:S(2)}, u32[]{:S(2)}) collective-permute-start(f32[8,1152]{1,0:T(8,128)S(1)} %add.246), channel_id=1, source_target_pairs={{0,8},{4,12},{8,0},{12,4},{16,24},{20,28},{24,16},{28,20},{1,9},{5... | collective-permute-start | bytes 110600 | tf_op jit(solution)/shard_map/ppermute | solution.py:27
  35.8 26.1 %collective-permute-start.3 = (bf16[2048,64]{1,0:T(8,128)(2,1)S(1)}, bf16[2048,64]{1,0:T(8,128)(2,1)S(1)}, u32[]{:S(2)}, u32[]{:S(2)}) collective-permute-start(bf16[2048,64]{1,0:T(8,128)(2,1)S(1)} %pad_maximum_fusion), channel_id=1, source_target_pairs={{0,24},{4,28},{8,16},{12,20},{16,8},{20,12},{24,0},{28,4},{1,25},{... | collective-permute-start | bytes 786440 | tf_op jit(solution)/shard_map/ppermute | solution.py:76
  37.4 34.0 %collective-permute-start.2 = (bf16[2048,64]{1,0:T(8,128)(2,1)S(1)}, bf16[2048,64]{1,0:T(8,128)(2,1)S(1)}, u32[]{:S(2)}, u32[]{:S(2)}) collective-permute-start(bf16[2048,64]{1,0:T(8,128)(2,1)S(1)} %pad_maximum_fusion), channel_id=1, source_target_pairs={{0,16},{4,20},{8,24},{12,28},{16,0},{20,4},{24,8},{28,12},{1,17},{... | collective-permute-start | bytes 786440 | tf_op jit(solution)/shard_map/ppermute | solution.py:76
  39.7 23.8 %copy-start.1 = (bf16[128,8192]{1,0:T(8,128)(2,1)S(1)}, bf16[128,8192]{1,0:T(8,128)(2,1)}, u32[]{:S(2)}) copy-start(bf16[128,8192]{1,0:T(8,128)(2,1)} %fusion.2) | copy-start | bytes 6291460
  39.7 32.2 %collective-permute-start.1 = (bf16[2048,64]{1,0:T(8,128)(2,1)S(1)}, bf16[2048,64]{1,0:T(8,128)(2,1)S(1)}, u32[]{:S(2)}, u32[]{:S(2)}) collective-permute-start(bf16[2048,64]{1,0:T(8,128)(2,1)S(1)} %pad_maximum_fusion), channel_id=1, source_target_pairs={{0,8},{4,12},{8,0},{12,4},{16,24},{20,28},{24,16},{28,20},{1,9},{5... | collective-permute-start | bytes 786440 | tf_op jit(solution)/shard_map/ppermute | solution.py:76
  45.7 30.3 %collective-permute-start.19 = (f32[8,1024]{1,0:T(8,128)S(1)}, f32[8,1024]{1,0:T(8,128)S(1)}, u32[]{:S(2)}, u32[]{:S(2)}) collective-permute-start(f32[8,1024]{1,0:T(8,128)S(1)} %fusion.5), channel_id=1, source_target_pairs={{0,3},{1,2},{2,1},{3,0},{4,7},{5,6},{6,5},{7,4},{8,11},{9,10},{10,... | collective-permute-start | bytes 98312 | tf_op jit(solution)/shard_map/ppermute | solution.py:46
  49.3 27.6 %collective-permute-start.20 = (f32[8,1024]{1,0:T(8,128)S(1)}, f32[8,1024]{1,0:T(8,128)S(1)}, u32[]{:S(2)}, u32[]{:S(2)}) collective-permute-start(f32[8,1024]{1,0:T(8,128)S(1)} %fusion.5), channel_id=1, source_target_pairs={{0,2},{1,3},{2,0},{3,1},{4,6},{5,7},{6,4},{7,5},{8,10},{9,11},{10,... | collective-permute-start | bytes 98312 | tf_op jit(solution)/shard_map/ppermute | solution.py:46
  62.0 14.9 %collective-permute-start.21 = (f32[8,1024]{1,0:T(8,128)S(1)}, f32[8,1024]{1,0:T(8,128)S(1)}, u32[]{:S(2)}, u32[]{:S(2)}) collective-permute-start(f32[8,1024]{1,0:T(8,128)S(1)} %fusion.5), channel_id=1, source_target_pairs={{0,1},{1,0},{2,3},{3,2},{4,5},{5,4},{6,7},{7,6},{8,9},{9,8},{10,11... | collective-permute-start | bytes 98312 | tf_op jit(solution)/shard_map/ppermute | solution.py:46
  72.4 5.8 %collective-permute-start.4 = (bf16[128,64]{0,1:T(8,128)(2,1)S(1)}, bf16[128,64]{0,1:T(8,128)(2,1)S(1)}, u32[]{:S(2)}, u32[]{:S(2)}) collective-permute-start(bf16[128,64]{0,1:T(8,128)(2,1)S(1)} %fusion.13), channel_id=1, source_target_pairs={{0,3},{1,2},{2,1},{3,0},{4,7},{5,6},{6,5},{7,4},{8,11},{9,10},{10,... | collective-permute-start | bytes 49160 | tf_op jit(solution)/shard_map/ppermute | solution.py:143
  76.0 4.6 %collective-permute-start.5 = (bf16[128,64]{0,1:T(8,128)(2,1)S(1)}, bf16[128,64]{0,1:T(8,128)(2,1)S(1)}, u32[]{:S(2)}, u32[]{:S(2)}) collective-permute-start(bf16[128,64]{0,1:T(8,128)(2,1)S(1)} %fusion.13), channel_id=1, source_target_pairs={{0,2},{1,3},{2,0},{3,1},{4,6},{5,7},{6,4},{7,5},{8,10},{9,11},{10,... | collective-permute-start | bytes 49160 | tf_op jit(solution)/shard_map/ppermute | solution.py:143
  76.0 4.6 %collective-permute-start.6 = (bf16[128,64]{0,1:T(8,128)(2,1)S(1)}, bf16[128,64]{0,1:T(8,128)(2,1)S(1)}, u32[]{:S(2)}, u32[]{:S(2)}) collective-permute-start(bf16[128,64]{0,1:T(8,128)(2,1)S(1)} %fusion.13), channel_id=1, source_target_pairs={{0,1},{1,0},{2,3},{3,2},{4,5},{5,4},{6,7},{7,6},{8,9},{9,8},{10,11... | collective-permute-start | bytes 49160 | tf_op jit(solution)/shard_map/ppermute | solution.py:143
  80.7 1.3 %collective-permute-start.7 = (bf16[128,256]{0,1:T(8,128)(2,1)S(1)}, bf16[128,256]{0,1:T(8,128)(2,1)S(1)}, u32[]{:S(2)}, u32[]{:S(2)}) collective-permute-start(bf16[128,256]{0,1:T(8,128)(2,1)S(1)} %constant_dynamic-update-slice_fusion.1), channel_id=1, source_target_pairs={{0,4},{4,0},{8,12},{12,8},{16,20},{20,16},{24,28},{28,24},{1,5},{5... | collective-permute-start | bytes 196616 | tf_op jit(solution)/shard_map/ppermute | solution.py:72
  82.1 6.0 %collective-permute-start.8 = (bf16[256,256]{0,1:T(8,128)(2,1)S(1)}, bf16[256,256]{0,1:T(8,128)(2,1)S(1)}, u32[]{:S(2)}, u32[]{:S(2)}) collective-permute-start(bf16[256,256]{0,1:T(8,128)(2,1)S(1)} %pad_maximum_fusion.2), channel_id=1, source_target_pairs={{0,8},{4,12},{8,0},{12,4},{16,24},{20,28},{24,16},{28,20},{1,9},{5... | collective-permute-start | bytes 393224 | tf_op jit(solution)/shard_map/ppermute | solution.py:76
  83.7 8.1 %collective-permute-start.9 = (bf16[256,256]{0,1:T(8,128)(2,1)S(1)}, bf16[256,256]{0,1:T(8,128)(2,1)S(1)}, u32[]{:S(2)}, u32[]{:S(2)}) collective-permute-start(bf16[256,256]{0,1:T(8,128)(2,1)S(1)} %pad_maximum_fusion.2), channel_id=1, source_target_pairs={{0,16},{4,20},{8,24},{12,28},{16,0},{20,4},{24,8},{28,12},{1,17},{... | collective-permute-start | bytes 393224 | tf_op jit(solution)/shard_map/ppermute | solution.py:76
  84.2 7.6 %collective-permute-start.10 = (bf16[256,256]{0,1:T(8,128)(2,1)S(1)}, bf16[256,256]{0,1:T(8,128)(2,1)S(1)}, u32[]{:S(2)}, u32[]{:S(2)}) collective-permute-start(bf16[256,256]{0,1:T(8,128)(2,1)S(1)} %pad_maximum_fusion.2), channel_id=1, source_target_pairs={{0,24},{4,28},{8,16},{12,20},{16,8},{20,12},{24,0},{28,4},{1,25},{... | collective-permute-start | bytes 393224 | tf_op jit(solution)/shard_map/ppermute | solution.py:76
Sparse Core Ops, SparseCore 0:
  9.9 61.9 all-gather.1

commit v6 on v0

--- a/solution.py
+++ b/solution.py
@@ -109,6 +109,7 @@
     tp_i = lax.axis_index("tp")
     normed = rms_norm(hidden, norm_gain)
     tokens_here = hidden.shape[0]
+    d_rows = w_query.shape[0]
     heads_here = w_query.shape[1] // HEAD
     sharers = GROUP // heads_here
     kv_width = HEAD // sharers
@@ -163,8 +164,22 @@
         ]
     )
 
-    q_pieces = gather_pieces(w_query, n_seq)
-    queries = project(normed, q_pieces).astype(jnp.bfloat16).reshape(tokens_here, heads_here, HEAD)
+    if n_seq == 8:
+        core = seq_i % 2
+        mine = lax.all_gather(
+            w_query, "seq", axis=0, tiled=True, axis_index_groups=[[0, 2, 4, 6], [1, 3, 5, 7]]
+        )
+        theirs = lax.ppermute(mine, "seq", xor_perm(8, lambda j: j ^ 1))
+        by_core = normed.reshape(tokens_here, n_seq // 2, 2, d_rows)
+        own_cols = jnp.where(core == 0, by_core[:, :, 0, :], by_core[:, :, 1, :])
+        other_cols = jnp.where(core == 0, by_core[:, :, 1, :], by_core[:, :, 0, :])
+        query_sum = jnp.dot(
+            own_cols.reshape(tokens_here, -1), mine, preferred_element_type=jnp.float32
+        ) + jnp.dot(other_cols.reshape(tokens_here, -1), theirs, preferred_element_type=jnp.float32)
+    else:
+        q_weights = lax.all_gather(w_query, "seq", axis=0, tiled=True)
+        query_sum = jnp.dot(normed, q_weights, preferred_element_type=jnp.float32)
+    queries = query_sum.astype(jnp.bfloat16).reshape(tokens_here, heads_here, HEAD)
 
     def segment_of(positions):
         return jnp.sum((positions[:, None] > doc_ends[None, :]).astype(jnp.int32), axis=1)

time: 109 us -> 111 us (1.018)
  waiting for transfers between devices: 39.2 us -> 22.1 us
  between operations: 1.22 us -> 14.5 us
  other arithmetic: 15.1 us -> 20.6 us
  local copies, waits for them, and re-layouts: 10.8 us -> 13.5 us
  starting transfers between devices: 20.8 us -> 18.4 us
    ppermute x3 -> x2, waiting for transfers between devices: 14.8 us -> 3.66 us  [gather_pieces(): lax.ppermute(nb[:rows], 'seq', xor_perm(8, lambda j: j ^ 5 if j % 2 == 0...]
    ppermute x3 -> x2, waiting for transfers between devices: 11.7 us -> 4.15 us  [gather_pieces(): lax.ppermute(pair, 'seq', xor_perm(8, lambda j: j ^ 2 if j % 2 == 0 else...]
    ppermute x3 -> x2, waiting for transfers between devices: 0.01 us -> 3.92 us  [gather_pieces(): sib = lax.ppermute(blk, 'seq', xor_perm(8, lambda j: j ^ 1))]
    dot_general x16 -> x8, matrix products: 9.69 us -> 5.8 us  [project(): term = jnp.dot(cols, piece, preferred_element_type=jnp.float32)]
    ppermute x2, waiting for transfers between devices: 5.78 us -> 1.93 us  [xor_gather_stack(): other = lax.ppermute(stack, axis, xor_perm(n, lambda j, k=k: j ^ k))]
    unnamed x55 -> x54, local copies, waits for them, and re-layouts: 5.71 us -> 9.34 us
    dot_general x0 -> x2, matrix products: none -> 3.31 us  [the longest x1 2.1 us: body(): jnp.dot(own_cols.reshape(tokens_here, -1), mine, preferred_element_type=j...]
    select_n x0 -> x1, other arithmetic: none -> 2.7 us  [body(): other_cols = jnp.where(core == 0, by_core[:, :, 1, :], by_core[:, :, 0, :])]
  transfers between devices with their start and end apart: 22 -> 20, of which waited for: 14 -> 11; matrix products, arithmetic and copies ran while one was open for 32% -> 40% of each run, Pallas kernels for 0% -> 0%
where the time goes in v6:
time: 111 us; the launch traced here: 110 us
  waiting for transfers between devices  22.1 us (20%)
  matrix products  21.1 us (19%)
  other arithmetic  20.6 us (19%)
  starting transfers between devices  18.4 us (17%)
  between operations  14.5 us (13%)
  local copies, waits for them, and re-layouts  13.5 us (12%)
    unnamed x54, local copies, waits for them, and re-layouts  9.34 us
    ppermute x5, starting transfers between devices, xor_all_reduce(): x = x + lax.ppermute(x, axis, xor_perm(n, lambda j, k=k: j ^ k))  6.42 us
    dot_general x8, matrix products, project(): term = jnp.dot(cols, piece, preferred_element_type=jnp.float32)  5.8 us
    dot_general x1, matrix products, body(): jnp.einsum('dc,rce->dre', critic_hidden, critic_down, preferred_element_t...  5.21 us
    convert_element_type x1, other arithmetic, rms_norm(): (widened * lax.rsqrt(mean_square + 1e-05) * norm_gain.astype(jnp.float32)...  4.58 us
    ppermute x2, waiting for transfers between devices, gather_pieces(): lax.ppermute(pair, 'seq', xor_perm(8, lambda j: j ^ 2 if j % 2 == 0 else...  4.15 us
    ppermute x3, starting transfers between devices, xor_reduce_scatter(): x = keep + lax.ppermute(send, axis, xor_perm(n, lambda j, k=k: j ^ k))  4.11 us
    ppermute x2, waiting for transfers between devices, gather_pieces(): sib = lax.ppermute(blk, 'seq', xor_perm(8, lambda j: j ^ 1))  3.92 us
  transfers between devices with their start and end apart: 20, of which 11 were waited for; matrix products, arithmetic and copies ran while one was open for 40% of the time, Pallas kernels for 0%

profile of v6, /device:TPU:0, one launch (start us, length us, event | category | flops | bytes accessed | tf_op | source)
XLA Modules:
  0.0 110.3 jit_solution(15219267549992180411)
XLA Ops:
  7.2 0.7 all-gather.2.cloned.1.call-update
  8.0 1.2 %constant_dynamic-slice_fusion.3 = (bf16[1024,32]{1,0:T(8,128)(2,1)S(1)}, bf16[1024,32]{1,0:T(8,128)(2,1)S(1)}) fusion(bf16[1024,128]{1,0:T(8,128)(2,1)} %param.13, s32[]{:T(128)S(6)} %select_n.158, bf16[1024,128]{1,0:T(8,128)(2,1)} %param.12), kind=kLoop, calls=%fused_computation.118 | loop fusion | bytes 262148 | tf_op jit(solution)/shard_map/dynamic_slice | solution.py:120
  9.5 0.7 pad_maximum_fusion.3
  10.1 0.5 collective-permute-start.1
  10.8 4.1 %copy.27 = bf16[128,8192]{0,1:T(8,128)(2,1)} copy(bf16[128,8192]{1,0:T(8,128)(2,1)} %param.9) | data formatting | bytes 4194304 | tf_op args[0]
  14.9 2.7 %fusion.1 = f32[128]{0:T(128)S(1)} fusion(bf16[128,8192]{0,1:T(8,128)(2,1)} %copy.27), kind=kLoop, calls=%fused_computation.4 | loop fusion | flops 3145600 | bytes 2097664 | tf_op jit(solution)/shard_map/reduce_sum | solution.py:15
  17.7 4.6 %fusion.3 = bf16[128,8192]{0,1:T(8,128)(2,1)S(1)} fusion(bf16[128,8192]{0,1:T(8,128)(2,1)} %copy.27, f32[8192]{0:T(1024)S(1)} %convert_element_type.43, f32[128]{0:T(128)S(1)} %add_rsqrt_fusion), kind=kLoop, calls=%fused_computation.6 | loop fusion | flops 4194304 | bytes 4227584 | tf_op jit(solution)/shard_map/convert_element_type | solution.py:16
  22.3 1.3 %copy-done.1 = bf16[128,8192]{0,1:T(8,128)(2,1)} copy-done((bf16[128,8192]{0,1:T(8,128)(2,1)}, bf16[128,8192]{0,1:T(8,128)(2,1)S(1)}, u32[]{:S(2)}) %copy-start.1) | copy-done | bytes 2097176
  23.6 0.7 convolution_convert_fusion
  24.3 0.7 constant_dynamic-slice_fusion.2
  25.0 2.5 %collective-permute-start.11 = (bf16[8,4096]{1,0:T(8,128)(2,1)}, bf16[8,4096]{1,0:T(8,128)(2,1)}, u32[]{:S(2)}, u32[]{:S(2)}) collective-permute-start(bf16[8,4096]{1,0:T(8,128)(2,1)} %constant_dynamic-slice_fusion.2), channel_id=1, source_target_pairs={{0,16},{4,20},{8,24},{12,28},{16,0},{20,4},{24,8},{28,12},{1,17},{... | collective-permute-start | bytes 196616 | tf_op jit(solution)/shard_map/ppermute | solution.py:41
  27.5 2.7 %broadcast_select_fusion = (bf16[128,4,1,1024]{0,3,2,1:T(8,128)(2,1)S(1)}, bf16[128,4,1,1024]{0,3,2,1:T(8,128)(2,1)}) fusion(pred[]{:T(512)S(6)} %eq.70, bf16[128,4,2,1024]{0,3,2,1:T(8,128)(2,1)} %bitcast.74), kind=kLoop, calls=%fused_computation.28 | loop fusion | flops 1048576 | bytes 4194305 | tf_op jit(solution)/shard_map/jit(_where)/select_n | solution.py:175
  30.2 0.5 iota_compare_fusion
  30.8 0.9 dynamic-slice_add_fusion
  31.7 0.6 copy-done.7
  32.3 0.6 constant_dynamic-slice_fusion.1
  32.9 1.6 %collective-permute-start.12 = (bf16[8,2048]{1,0:T(8,128)(2,1)}, bf16[8,2048]{1,0:T(8,128)(2,1)}, u32[]{:S(2)}, u32[]{:S(2)}) collective-permute-start(bf16[8,2048]{1,0:T(8,128)(2,1)} %constant_dynamic-slice_fusion.1), channel_id=1, source_target_pairs={{0,8},{4,12},{8,0},{12,4},{16,24},{20,28},{24,16},{28,20},{1,9},{5... | collective-permute-start | bytes 98312 | tf_op jit(solution)/shard_map/ppermute | solution.py:41
  34.5 0.7 convert_reduce_fusion
  35.1 2.6 %collective-permute-done.12 = bf16[8,2048]{1,0:T(8,128)(2,1)} collective-permute-done((bf16[8,2048]{1,0:T(8,128)(2,1)}, bf16[8,2048]{1,0:T(8,128)(2,1)}, u32[]{:S(2)}, u32[]{:S(2)}) %collective-permute-start.12) | collective-permute-done | bytes 32800 | tf_op jit(solution)/shard_map/ppermute | solution.py:41
  37.8 0.8 dynamic-slice_add_fusion.1
  38.6 0.6 copy-done.8
  39.2 0.6 constant_dynamic-slice_fusion
  39.8 1.3 %convert_reduce_fusion.1 = s32[128]{0:T(128)} fusion(s32[128]{0:T(128)} %copy-done.13, s32[8]{0:T(128)} %copy-done.16), kind=kLoop, calls=%fused_computation.106 | loop fusion | flops 2944 | bytes 1056 | tf_op jit(solution)/shard_map/reduce_sum | solution.py:185
  41.2 1.1 %fusion.49 = f32[8,1152]{1,0:T(8,128)S(1)} fusion(bf16[1024,1152]{1,0:T(8,128)(2,1)S(1)} %copy-done, bf16[8,1024]{1,0:T(8,128)(2,1)S(1)} %collective-permute-done.13, bf16[8,2048]{1,0:T(8,128)(2,1)} %copy-done.8, s32[]{:T(128)S(6)} %select_n.177), kind=kOutput, calls=%fused_computation.88 | convolution fusion | flops 18907136 | bytes 2428932 | tf_op jit(solution)/shard_map/dot_general | solution.py:132
  42.3 0.4 collective-permute-start.14
  42.7 1.6 %pad_maximum_fusion.1 = bf16[2048,64]{0,1:T(8,128)(2,1)} fusion(bf16[1024,64]{0,1:T(8,128)(2,1)} %collective-permute-done.1, bf16[1024,32]{0,1:T(8,128)(2,1)S(1)} %copy.36, bf16[1024,32]{0,1:T(8,128)(2,1)S(1)} %copy.35), kind=kLoop, calls=%fused_computation.33 | loop fusion | flops 786432 | bytes 524288 | tf_op jit(solution)/shard_map/concatenate | solution.py:75
  44.4 1.7 %collective-permute-start.2 = (bf16[2048,64]{0,1:T(8,128)(2,1)}, bf16[2048,64]{0,1:T(8,128)(2,1)}, u32[]{:S(2)}, u32[]{:S(2)}) collective-permute-start(bf16[2048,64]{0,1:T(8,128)(2,1)} %pad_maximum_fusion.1), channel_id=1, source_target_pairs={{0,8},{4,20},{8,0},{12,28},{16,24},{20,4},{24,16},{28,12},{1,9},{5... | collective-permute-start | bytes 786440 | tf_op jit(solution)/shard_map/ppermute | solution.py:76
  46.1 0.6 add.294
  46.7 0.3 collective-permute-start.15
  47.0 1.7 %fusion.34 = f32[128,64]{0,1:T(8,128)} fusion(bf16[128,8192]{0,1:T(8,128)(2,1)} %copy-done.1, s32[]{:T(128)S(6)} %select_n.155, bf16[1024,32]{0,1:T(8,128)(2,1)S(1)} %copy.36, bf16[1024,32]{0,1:T(8,128)(2,1)S(1)} %copy.35), kind=kOutput, calls=%fused_computation.48 | convolution fusion | flops 17039360 | bytes 425988 | tf_op jit(solution)/shard_map/dot_general | solution.py:98
  48.8 3.1 %collective-permute-done.15 = f32[8,1152]{1,0:T(8,128)} collective-permute-done((f32[8,1152]{1,0:T(8,128)}, f32[8,1152]{1,0:T(8,128)}, u32[]{:S(2)}, u32[]{:S(2)}) %collective-permute-start.15) | collective-permute-done | bytes 36896 | tf_op jit(solution)/shard_map/ppermute | solution.py:28
  51.8 0.8 add.295
  52.6 1.5 %collective-permute-start.16 = (f32[8,1152]{1,0:T(8,128)S(1)}, f32[8,1152]{1,0:T(8,128)S(1)}, u32[]{:S(2)}, u32[]{:S(2)}) collective-permute-start(f32[8,1152]{1,0:T(8,128)S(1)} %add.295), channel_id=1, source_target_pairs={{0,16},{4,20},{8,24},{12,28},{16,0},{20,4},{24,8},{28,12},{1,17},{... | collective-permute-start | bytes 110600 | tf_op jit(solution)/shard_map/ppermute | solution.py:28
  54.1 1.2 %convolution_add_fusion.2 = f32[128,64]{0,1:T(8,128)S(1)} fusion(f32[128,64]{0,1:T(8,128)} %fusion.34, bf16[1024,64]{0,1:T(8,128)(2,1)} %collective-permute-done.1, bf16[128,8192]{0,1:T(8,128)(2,1)} %copy-done.1, s32[]{:T(128)S(6)} %select_n.159), kind=kOutput, calls=%fused_computation.25 | convolution fusion | flops 16785408 | bytes 458756 | tf_op jit(solution)/shard_map/dot_general | solution.py:98
  55.3 0.9 slice.130
  56.3 0.3 collective-permute-done.16
  56.6 5.2 %fusion.10 = f32[8,1024]{1,0:T(8,128)S(1)} fusion(bf16[4,1152,1024]{2,1,0:T(8,128)(2,1)} %param.16, pred[8,4]{0,1:T(4,128)(4,1)} %iota_compare_fusion, f32[8,1152]{1,0:T(8,128)S(1)} %add.295, f32[8,1152]{1,0:T(8,128)S(1)} %collective-permute-done.16), kind=kOutput, calls=%fused_computation.17 | convolution fusion | flops 75610112 | bytes 9543712 | tf_op jit(solution)/shard_map/dc,rce->dre/dot_general | solution.py:138
  61.8 1.5 %collective-permute-start.17 = (f32[8,1024]{1,0:T(8,128)S(1)}, f32[8,1024]{1,0:T(8,128)S(1)}, u32[]{:S(2)}, u32[]{:S(2)}) collective-permute-start(f32[8,1024]{1,0:T(8,128)S(1)} %fusion.10), channel_id=1, source_target_pairs={{0,1},{1,0},{2,3},{3,2},{4,5},{5,4},{6,7},{7,6},{8,9},{9,8},{10,11... | collective-permute-start | bytes 98312 | tf_op jit(solution)/shard_map/ppermute | solution.py:28
  63.4 1.0 pad_maximum_fusion
  64.3 1.2 %collective-permute-start.4 = (bf16[3072,64]{0,1:T(8,128)(2,1)S(1)}, bf16[3072,64]{0,1:T(8,128)(2,1)S(1)}, u32[]{:S(2)}, u32[]{:S(2)}) collective-permute-start(bf16[3072,64]{0,1:T(8,128)(2,1)S(1)} %pad_maximum_fusion), channel_id=1, source_target_pairs={{0,4},{4,0},{8,12},{12,8},{16,20},{20,16},{24,28},{28,24},{1,5},{5... | collective-permute-start | bytes 1179656 | tf_op jit(solution)/shard_map/ppermute | solution.py:78
  65.5 1.1 fusion.30
  66.6 0.2 fusion.28
  67.1 0.2 fusion.24
  67.3 0.2 fusion.26
  67.5 1.1 fusion.18
  68.6 0.5 collective-permute-start.5
  69.1 0.8 compare_and_fusion
  69.9 2.7 %collective-permute-start.18 = (f32[8,1024]{1,0:T(8,128)S(1)}, f32[8,1024]{1,0:T(8,128)S(1)}, u32[]{:S(2)}, u32[]{:S(2)}) collective-permute-start(f32[8,1024]{1,0:T(8,128)S(1)} %add.298), channel_id=1, source_target_pairs={{0,2},{1,3},{2,0},{3,1},{4,6},{5,7},{6,4},{7,5},{8,10},{9,11},{10,... | collective-permute-start | bytes 98312 | tf_op jit(solution)/shard_map/ppermute | solution.py:28
  72.6 2.4 %collective-permute-start.6 = (bf16[2,128,64]{1,2,0:T(8,128)(2,1)S(1)}, bf16[2,128,64]{1,2,0:T(8,128)(2,1)S(1)}, u32[]{:S(2)}, u32[]{:S(2)}) collective-permute-start(bf16[2,128,64]{1,2,0:T(8,128)(2,1)S(1)} %maximum_select_fusion.1), channel_id=1, source_target_pairs={{0,2},{1,3},{2,0},{3,1},{4,6},{5,7},{6,4},{7,5},{8,10},{9,11},{10,... | collective-permute-start | bytes 98312 | tf_op jit(solution)/shard_map/ppermute | solution.py:51
  75.2 0.6 add_convert_fusion
  75.8 1.9 %collective-permute-done.6 = bf16[2,128,64]{1,2,0:T(8,128)(2,1)S(1)} collective-permute-done((bf16[2,128,64]{1,2,0:T(8,128)(2,1)S(1)}, bf16[2,128,64]{1,2,0:T(8,128)(2,1)S(1)}, u32[]{:S(2)}, u32[]{:S(2)}) %collective-permute-start.6) | collective-permute-done | bytes 32800 | tf_op jit(solution)/shard_map/ppermute | solution.py:51
  77.9 0.5 collective-permute-start.7
  78.5 3.9 %collective-permute-done.7 = bf16[128,256]{0,1:T(8,128)(2,1)S(1)} collective-permute-done((bf16[128,256]{0,1:T(8,128)(2,1)S(1)}, bf16[128,256]{0,1:T(8,128)(2,1)S(1)}, u32[]{:S(2)}, u32[]{:S(2)}) %collective-permute-start.7) | collective-permute-done | bytes 65568 | tf_op jit(solution)/shard_map/ppermute | solution.py:74
  82.4 0.9 collective-permute-start.8
  83.3 4.1 %collective-permute-done.8 = bf16[256,256]{0,1:T(8,128)(2,1)S(1)} collective-permute-done((bf16[256,256]{0,1:T(8,128)(2,1)S(1)}, bf16[256,256]{0,1:T(8,128)(2,1)S(1)}, u32[]{:S(2)}, u32[]{:S(2)}) %collective-permute-start.8) | collective-permute-done | bytes 131104 | tf_op jit(solution)/shard_map/ppermute | solution.py:76
  87.5 3.7 %collective-permute-done.9 = bf16[128,256]{0,1:T(8,128)(2,1)S(1)} collective-permute-done((bf16[128,256]{0,1:T(8,128)(2,1)S(1)}, bf16[128,256]{0,1:T(8,128)(2,1)S(1)}, u32[]{:S(2)}, u32[]{:S(2)}) %collective-permute-start.9) | collective-permute-done | bytes 65568 | tf_op jit(solution)/shard_map/ppermute | solution.py:77
  91.3 1.4 %collective-permute-done.10 = bf16[384,256]{0,1:T(8,128)(2,1)S(1)} collective-permute-done((bf16[384,256]{0,1:T(8,128)(2,1)S(1)}, bf16[384,256]{0,1:T(8,128)(2,1)S(1)}, u32[]{:S(2)}, u32[]{:S(2)}) %collective-permute-start.10) | collective-permute-done | bytes 196640 | tf_op jit(solution)/shard_map/ppermute | solution.py:78
  92.7 0.7 copy-done.6
  93.5 2.1 %fusion.75 = f32[128,256]{1,0:T(8,128)S(1)} fusion(bf16[128,4096]{0,1:T(8,128)(2,1)S(1)} %bitcast.76, bf16[4096,256]{1,0:T(8,128)(2,1)} %all-gather.2.cloned.1.call-done), kind=kOutput, calls=%fused_computation.135 | convolution fusion | flops 268435456 | bytes 3276800 | tf_op jit(solution)/shard_map/dot_general | solution.py:176
  95.6 1.2 %fusion.11 = bf16[16,2,8,128]{3,2,1,0:T(8,128)(2,1)} fusion(f32[128,256]{1,0:T(8,128)S(1)} %fusion.75, bf16[128,4096]{0,1:T(8,128)(2,1)S(1)} %bitcast.75, bf16[4096,256]{1,0:T(8,128)(2,1)S(1)} %collective-permute-done), kind=kOutput, calls=%fused_computation.18 | convolution fusion | flops 268500992 | bytes 3342336 | tf_op jit(solution)/shard_map/dot_general | solution.py:178
  96.9 1.7 %fusion.70 = f32[128,2]{0,1:T(2,128)S(1)} fusion(pred[128,1024]{1,0:T(8,128)(4,1)S(1)} %copy-done.5, bf16[1024,128]{0,1:T(8,128)(2,1)} %copy-done.6, bf16[16,2,8,128]{3,2,1,0:T(8,128)(2,1)} %fusion.11), kind=kOutput, calls=%fused_computation.134 | convolution fusion | flops 68420608 | bytes 459776 | tf_op jit(solution)/shard_map/sub | solution.py:199
  98.5 1.3 %fusion.7 = f32[128,2,1024]{2,0,1:T(8,128)S(1)} fusion(pred[128,1024]{1,0:T(8,128)(4,1)S(1)} %copy-done.5, bf16[1024,128]{0,1:T(8,128)(2,1)} %copy-done.6, bf16[16,2,8,128]{3,2,1,0:T(8,128)(2,1)} %fusion.11), kind=kOutput, calls=%fused_computation.11 | convolution fusion | flops 67633152 | bytes 1507328 | tf_op jit(solution)/shard_map/qhd,kd->qhk/dot_general | solution.py:194
  99.8 2.1 %fusion.9 = bf16[128,2,128]{0,2,1:T(8,128)(2,1)} fusion(bf16[1024,128]{0,1:T(8,128)(2,1)} %copy-done.15, f32[128,2,1024]{2,0,1:T(8,128)S(1)} %fusion.7, pred[128,1024]{1,0:T(8,128)(4,1)S(1)} %copy-done.5, f32[128,2]{0,1:T(2,128)S(1)} %fusion.70), kind=kOutput, calls=%fused_computation.16 | convolution fusion | flops 67962112 | bytes 1508352 | tf_op jit(solution)/shard_map/qhk,kd->qhd/dot_general | solution.py:201
  101.9 1.6 %copy.32 = bf16[128,256]{1,0:T(8,128)(2,1)} copy(bf16[128,256]{0,1:T(8,128)(2,1)} %bitcast.77) | data formatting | bytes 131072
  (91 shorter events, 1.7 us)
Async XLA Ops:
  7.2 34.0 %copy-start = (bf16[1024,1152]{1,0:T(8,128)(2,1)S(1)}, bf16[1024,1152]{1,0:T(8,128)(2,1)}, u32[]{:S(2)}) copy-start(bf16[1024,1152]{1,0:T(8,128)(2,1)} %param.15) | copy-start | bytes 7077892
  7.2 3.5 %copy-start.18 = (s32[8]{0:T(128)S(1)}, s32[8]{0:T(128)}, u32[]{:S(2)}) copy-start(s32[8]{0:T(128)} %param.14) | copy-start | bytes 100
  7.2 3.6 %copy-start.9 = (bf16[8192]{0:T(1024)(128)(2,1)S(1)}, bf16[8192]{0:T(1024)(128)(2,1)}, u32[]{:S(2)}) copy-start(bf16[8192]{0:T(1024)(128)(2,1)} %param.10) | copy-start | bytes 49156
  7.2 70.6 %all-gather.2.cloned.1.call-start = ((), (), s32[]{:S(2)}) async-start(), calls=%async_computation | async-start | bytes 2621440 | tf_op jit(solution)/shard_map/all_gather | solution.py:169
  10.1 32.6 %collective-permute-start.1 = (bf16[1024,64]{0,1:T(8,128)(2,1)}, bf16[1024,64]{0,1:T(8,128)(2,1)}, u32[]{:S(2)}, u32[]{:S(2)}) collective-permute-start(bf16[1024,64]{0,1:T(8,128)(2,1)} %pad_maximum_fusion.3), channel_id=1, source_target_pairs={{0,4},{4,0},{8,12},{12,8},{16,20},{20,16},{24,28},{28,24},{1,5},{5... | collective-permute-start | bytes 393224 | tf_op jit(solution)/shard_map/ppermute | solution.py:74
  10.8 23.6 %copy-start.16 = (s32[8]{0:T(128)}, s32[8]{0:T(128)S(1)}, u32[]{:S(2)}) copy-start(s32[8]{0:T(128)S(1)} %add_bitcast_fusion) | copy-start | bytes 100
  17.7 4.6 %copy-start.13 = (s32[128]{0:T(128)}, s32[128]{0:T(128)S(1)}, u32[]{:S(2)}) copy-start(s32[128]{0:T(128)S(1)} %get-tuple-element.33) | copy-start | bytes 1540
  17.7 16.8 %copy-start.11 = (s32[1024]{0:T(1024)}, s32[1024]{0:T(1024)S(1)}, u32[]{:S(2)}) copy-start(s32[1024]{0:T(1024)S(1)} %get-tuple-element.32) | copy-start | bytes 12292
  22.3 1.3 %copy-start.1 = (bf16[128,8192]{0,1:T(8,128)(2,1)}, bf16[128,8192]{0,1:T(8,128)(2,1)S(1)}, u32[]{:S(2)}) copy-start(bf16[128,8192]{0,1:T(8,128)(2,1)S(1)} %fusion.3) | copy-start | bytes 6291460
  24.3 3.2 %copy-start.4 = (bf16[8,8192]{1,0:T(8,128)(2,1)}, bf16[8,8192]{1,0:T(8,128)(2,1)S(1)}, u32[]{:S(2)}) copy-start(bf16[8,8192]{1,0:T(8,128)(2,1)S(1)} %convolution_convert_fusion) | copy-start | bytes 393220
  25.0 5.8 %collective-permute-start.11 = (bf16[8,4096]{1,0:T(8,128)(2,1)}, bf16[8,4096]{1,0:T(8,128)(2,1)}, u32[]{:S(2)}, u32[]{:S(2)}) collective-permute-start(bf16[8,4096]{1,0:T(8,128)(2,1)} %constant_dynamic-slice_fusion.2), channel_id=1, source_target_pairs={{0,16},{4,20},{8,24},{12,28},{16,0},{20,4},{24,8},{28,12},{1,17},{... | collective-permute-start | bytes 196616 | tf_op jit(solution)/shard_map/ppermute | solution.py:41
  27.5 2.7 %copy-start.19 = (s32[8]{0:T(128)S(1)}, s32[8]{0:T(128)}, u32[]{:S(2)}) copy-start(s32[8]{0:T(128)} %param.17) | copy-start | bytes 100
  31.7 0.6 copy-start.7
  32.9 4.8 %collective-permute-start.12 = (bf16[8,2048]{1,0:T(8,128)(2,1)}, bf16[8,2048]{1,0:T(8,128)(2,1)}, u32[]{:S(2)}, u32[]{:S(2)}) collective-permute-start(bf16[8,2048]{1,0:T(8,128)(2,1)} %constant_dynamic-slice_fusion.1), channel_id=1, source_target_pairs={{0,8},{4,12},{8,0},{12,4},{16,24},{20,28},{24,16},{28,20},{1,9},{5... | collective-permute-start | bytes 98312 | tf_op jit(solution)/shard_map/ppermute | solution.py:41
  38.5 0.6 copy-start.8
  39.8 1.4 %collective-permute-start.13 = (bf16[8,1024]{1,0:T(8,128)(2,1)}, bf16[8,1024]{1,0:T(8,128)(2,1)S(1)}, u32[]{:S(2)}, u32[]{:S(2)}) collective-permute-start(bf16[8,1024]{1,0:T(8,128)(2,1)} %constant_dynamic-slice_fusion), channel_id=1, source_target_pairs={{0,4},{4,0},{8,12},{12,8},{16,20},{20,16},{24,28},{28,24},{1,5},{5... | collective-permute-start | bytes 49160 | tf_op jit(solution)/shard_map/ppermute | solution.py:41
  42.3 3.8 %collective-permute-start.14 = (f32[8,1152]{1,0:T(8,128)S(1)}, f32[8,1152]{1,0:T(8,128)S(1)}, u32[]{:S(2)}, u32[]{:S(2)}) collective-permute-start(f32[8,1152]{1,0:T(8,128)S(1)} %fusion.49), channel_id=1, source_target_pairs={{0,4},{4,0},{8,12},{12,8},{16,20},{20,16},{24,28},{28,24},{1,5},{5... | collective-permute-start | bytes 110600 | tf_op jit(solution)/shard_map/ppermute | solution.py:28
  44.4 10.9 %collective-permute-start.2 = (bf16[2048,64]{0,1:T(8,128)(2,1)}, bf16[2048,64]{0,1:T(8,128)(2,1)}, u32[]{:S(2)}, u32[]{:S(2)}) collective-permute-start(bf16[2048,64]{0,1:T(8,128)(2,1)} %pad_maximum_fusion.1), channel_id=1, source_target_pairs={{0,8},{4,20},{8,0},{12,28},{16,24},{20,4},{24,16},{28,12},{1,9},{5... | collective-permute-start | bytes 786440 | tf_op jit(solution)/shard_map/ppermute | solution.py:76
  46.7 5.2 %collective-permute-start.15 = (f32[8,1152]{1,0:T(8,128)}, f32[8,1152]{1,0:T(8,128)}, u32[]{:S(2)}, u32[]{:S(2)}) collective-permute-start(f32[8,1152]{1,0:T(8,128)} %add.294), channel_id=1, source_target_pairs={{0,8},{4,12},{8,0},{12,4},{16,24},{20,28},{24,16},{28,20},{1,9},{5... | collective-permute-start | bytes 110600 | tf_op jit(solution)/shard_map/ppermute | solution.py:28
  52.6 4.0 %collective-permute-start.16 = (f32[8,1152]{1,0:T(8,128)S(1)}, f32[8,1152]{1,0:T(8,128)S(1)}, u32[]{:S(2)}, u32[]{:S(2)}) collective-permute-start(f32[8,1152]{1,0:T(8,128)S(1)} %add.295), channel_id=1, source_target_pairs={{0,16},{4,20},{8,24},{12,28},{16,0},{20,4},{24,8},{28,12},{1,17},{... | collective-permute-start | bytes 110600 | tf_op jit(solution)/shard_map/ppermute | solution.py:28
  56.2 9.3 %copy-start.2 = (bf16[128,8192]{0,1:T(8,128)(2,1)S(1)}, bf16[128,8192]{0,1:T(8,128)(2,1)}, u32[]{:S(2)}) copy-start(bf16[128,8192]{0,1:T(8,128)(2,1)} %copy-done.1) | copy-start | bytes 6291460
  56.2 7.2 %collective-permute-start.3 = (bf16[1024,64]{0,1:T(8,128)(2,1)S(1)}, bf16[1024,64]{0,1:T(8,128)(2,1)S(1)}, u32[]{:S(2)}, u32[]{:S(2)}) collective-permute-start(bf16[1024,64]{0,1:T(8,128)(2,1)S(1)} %slice.130), channel_id=1, source_target_pairs={{0,20},{4,8},{8,28},{12,0},{16,4},{20,24},{24,12},{28,16},{1,21},{... | collective-permute-start | bytes 393224 | tf_op jit(solution)/shard_map/ppermute | solution.py:77
  61.8 7.3 %copy-start.10 = (s32[1024]{0:T(1024)S(1)}, s32[1024]{0:T(1024)}, u32[]{:S(2)}) copy-start(s32[1024]{0:T(1024)} %convert_reduce_fusion) | copy-start | bytes 12292
  61.8 7.3 %copy-start.12 = (s32[1024]{0:T(1024)S(1)}, s32[1024]{0:T(1024)}, u32[]{:S(2)}) copy-start(s32[1024]{0:T(1024)} %copy-done.11) | copy-start | bytes 12292
  61.8 7.3 %copy-start.14 = (s32[128]{0:T(128)S(1)}, s32[128]{0:T(128)}, u32[]{:S(2)}) copy-start(s32[128]{0:T(128)} %copy-done.13) | copy-start | bytes 1540
  61.8 7.3 %copy-start.17 = (s32[128]{0:T(128)S(1)}, s32[128]{0:T(128)}, u32[]{:S(2)}) copy-start(s32[128]{0:T(128)} %convert_reduce_fusion.1) | copy-start | bytes 1540
  61.8 8.1 %collective-permute-start.17 = (f32[8,1024]{1,0:T(8,128)S(1)}, f32[8,1024]{1,0:T(8,128)S(1)}, u32[]{:S(2)}, u32[]{:S(2)}) collective-permute-start(f32[8,1024]{1,0:T(8,128)S(1)} %fusion.10), channel_id=1, source_target_pairs={{0,1},{1,0},{2,3},{3,2},{4,5},{5,4},{6,7},{7,6},{8,9},{9,8},{10,11... | collective-permute-start | bytes 98312 | tf_op jit(solution)/shard_map/ppermute | solution.py:28
  64.3 2.5 %collective-permute-start.4 = (bf16[3072,64]{0,1:T(8,128)(2,1)S(1)}, bf16[3072,64]{0,1:T(8,128)(2,1)S(1)}, u32[]{:S(2)}, u32[]{:S(2)}) collective-permute-start(bf16[3072,64]{0,1:T(8,128)(2,1)S(1)} %pad_maximum_fusion), channel_id=1, source_target_pairs={{0,4},{4,0},{8,12},{12,8},{16,20},{20,16},{24,28},{28,24},{1,5},{5... | collective-permute-start | bytes 1179656 | tf_op jit(solution)/shard_map/ppermute | solution.py:78
  68.6 4.0 %collective-permute-start.5 = (bf16[1,128,64]{1,2,0:T(8,128)(2,1)S(1)}, bf16[1,128,64]{1,2,0:T(8,128)(2,1)S(1)}, u32[]{:S(2)}, u32[]{:S(2)}) collective-permute-start(bf16[1,128,64]{1,2,0:T(8,128)(2,1)S(1)} %fusion.18), channel_id=1, source_target_pairs={{0,1},{1,0},{2,3},{3,2},{4,5},{5,4},{6,7},{7,6},{8,9},{9,8},{10,11... | collective-permute-start | bytes 49160 | tf_op jit(solution)/shard_map/ppermute | solution.py:51
  69.9 5.2 %collective-permute-start.18 = (f32[8,1024]{1,0:T(8,128)S(1)}, f32[8,1024]{1,0:T(8,128)S(1)}, u32[]{:S(2)}, u32[]{:S(2)}) collective-permute-start(f32[8,1024]{1,0:T(8,128)S(1)} %add.298), channel_id=1, source_target_pairs={{0,2},{1,3},{2,0},{3,1},{4,6},{5,7},{6,4},{7,5},{8,10},{9,11},{10,... | collective-permute-start | bytes 98312 | tf_op jit(solution)/shard_map/ppermute | solution.py:28
  72.6 5.1 %collective-permute-start.6 = (bf16[2,128,64]{1,2,0:T(8,128)(2,1)S(1)}, bf16[2,128,64]{1,2,0:T(8,128)(2,1)S(1)}, u32[]{:S(2)}, u32[]{:S(2)}) collective-permute-start(bf16[2,128,64]{1,2,0:T(8,128)(2,1)S(1)} %maximum_select_fusion.1), channel_id=1, source_target_pairs={{0,2},{1,3},{2,0},{3,1},{4,6},{5,7},{6,4},{7,5},{8,10},{9,11},{10,... | collective-permute-start | bytes 98312 | tf_op jit(solution)/shard_map/ppermute | solution.py:51
  77.8 15.7 %copy-start.3 = (bf16[128,4,1,1024]{0,3,2,1:T(8,128)(2,1)S(1)}, bf16[128,4,1,1024]{0,3,2,1:T(8,128)(2,1)}, u32[]{:S(2)}) copy-start(bf16[128,4,1,1024]{0,3,2,1:T(8,128)(2,1)} %get-tuple-element.13) | copy-start | bytes 3145732
  77.8 17.8 %collective-permute-start = (bf16[4096,256]{1,0:T(8,128)(2,1)}, bf16[4096,256]{1,0:T(8,128)(2,1)S(1)}, u32[]{:S(2)}, u32[]{:S(2)}) collective-permute-start(bf16[4096,256]{1,0:T(8,128)(2,1)} %all-gather.2.cloned.1.call-done), channel_id=1, source_target_pairs={{0,4},{4,0},{8,12},{12,8},{16,20},{20,16},{24,28},{28,24},{1,5},{5... | collective-permute-start | bytes 6291464 | tf_op jit(solution)/shard_map/ppermute | solution.py:172
  77.9 4.4 %collective-permute-start.7 = (bf16[128,256]{0,1:T(8,128)(2,1)S(1)}, bf16[128,256]{0,1:T(8,128)(2,1)S(1)}, u32[]{:S(2)}, u32[]{:S(2)}) collective-permute-start(bf16[128,256]{0,1:T(8,128)(2,1)S(1)} %constant_dynamic-update-slice_fusion.1), channel_id=1, source_target_pairs={{0,4},{4,0},{8,12},{12,8},{16,20},{20,16},{24,28},{28,24},{1,5},{5... | collective-permute-start | bytes 196616 | tf_op jit(solution)/shard_map/ppermute | solution.py:74
  82.4 5.0 %collective-permute-start.8 = (bf16[256,256]{0,1:T(8,128)(2,1)S(1)}, bf16[256,256]{0,1:T(8,128)(2,1)S(1)}, u32[]{:S(2)}, u32[]{:S(2)}) collective-permute-start(bf16[256,256]{0,1:T(8,128)(2,1)S(1)} %pad_maximum_fusion.4), channel_id=1, source_target_pairs={{0,8},{4,20},{8,0},{12,28},{16,24},{20,4},{24,16},{28,12},{1,9},{5... | collective-permute-start | bytes 393224 | tf_op jit(solution)/shard_map/ppermute | solution.py:76
  87.4 3.7 %collective-permute-start.9 = (bf16[128,256]{0,1:T(8,128)(2,1)S(1)}, bf16[128,256]{0,1:T(8,128)(2,1)S(1)}, u32[]{:S(2)}, u32[]{:S(2)}) collective-permute-start(bf16[128,256]{0,1:T(8,128)(2,1)S(1)} %slice.145), channel_id=1, source_target_pairs={{0,20},{4,8},{8,28},{12,0},{16,4},{20,24},{24,12},{28,16},{1,21},{... | collective-permute-start | bytes 196616 | tf_op jit(solution)/shard_map/ppermute | solution.py:77
  91.2 1.5 %collective-permute-start.10 = (bf16[384,256]{0,1:T(8,128)(2,1)S(1)}, bf16[384,256]{0,1:T(8,128)(2,1)S(1)}, u32[]{:S(2)}, u32[]{:S(2)}) collective-permute-start(bf16[384,256]{0,1:T(8,128)(2,1)S(1)} %pad_maximum_fusion.2), channel_id=1, source_target_pairs={{0,4},{4,0},{8,12},{12,8},{16,20},{20,16},{24,28},{28,24},{1,5},{5... | collective-permute-start | bytes 589832 | tf_op jit(solution)/shard_map/ppermute | solution.py:78
  92.7 0.7 copy-start.6
  92.7 0.8 copy-start.15
  95.6 1.2 %copy-start.5 = (pred[128,1024]{1,0:T(8,128)(4,1)S(1)}, pred[128,1024]{1,0:T(8,128)(4,1)}, u32[]{:S(2)}) copy-start(pred[128,1024]{1,0:T(8,128)(4,1)} %compare_and_fusion) | copy-start | bytes 393220
Sparse Core Ops, SparseCore 0:
  9.9 38.2 all-gather.1

commit v7 on v2

--- a/solution.py
+++ b/solution.py
@@ -91,15 +91,6 @@
     ]
 
 
-def project(normed, pieces):
-    total = None
-    for piece, source, rows in pieces:
-        cols = lax.dynamic_slice_in_dim(normed, source * rows, rows, 1)
-        term = jnp.dot(cols, piece, preferred_element_type=jnp.float32)
-        total = term if total is None else total + term
-    return total
-
-
 def body(
     hidden, norm_gain, w_query, w_key, w_value, doc_lengths, critic_up, critic_down, rule_ids
 ):
@@ -145,8 +136,8 @@
         critic_sum = lax.psum(chosen, "tp")
     critic_values = critic_sum.astype(jnp.bfloat16)
 
-    kv_pieces = gather_pieces(kv_weights, n_seq)
-    kv_own = project(normed, kv_pieces).astype(jnp.bfloat16)
+    kv_full = lax.all_gather(kv_weights, "seq", axis=0, tiled=True)
+    kv_own = jnp.dot(normed, kv_full, preferred_element_type=jnp.float32).astype(jnp.bfloat16)
     kv_stack = xor_gather_stack(kv_own, "tp", n_tp, sharers)
     kv_rows = jnp.concatenate(
         [kv_stack[m, :, :kv_width] for m in range(sharers)]

time: 92.7 us -> 97.5 us (1.052)
  waiting for transfers between devices: 21.8 us -> 33.9 us
  starting transfers between devices: 21.3 us -> 17.5 us
  other arithmetic: 8.21 us -> 6.25 us
    all_gather x1, waiting for transfers between devices: 0.01 us -> 11.5 us  [body(): q_weights = lax.all_gather(w_query, 'seq', axis=0, tiled=True)]
    convert_element_type x1 -> x0, other arithmetic: 3.5 us -> none  [rms_norm(): (widened * lax.rsqrt(mean_square + 1e-05) * norm_gain.astype(jnp.float32)...]
    ppermute x2 -> x1, starting transfers between devices: 2.94 us -> 1.05 us  [gather_pieces(): lax.ppermute(pair, 'seq', xor_perm(8, lambda j: j ^ 2 if j % 2 == 0 else...]
    ppermute x3, waiting for transfers between devices: 7.73 us -> 6.1 us  [xor_reduce_scatter(): x = keep + lax.ppermute(send, axis, xor_perm(n, lambda j, k=k: j ^ k))]
    ppermute x2 -> x1, waiting for transfers between devices: 2.16 us -> 0.7 us  [gather_pieces(): lax.ppermute(jnp.concatenate([nb, dg], axis=0), 'seq', xor_perm(8, lambda...]
    ppermute x5, waiting for transfers between devices: 5.43 us -> 6.73 us  [xor_all_reduce(): x = x + lax.ppermute(x, axis, xor_perm(n, lambda j, k=k: j ^ k))]
    ppermute x5, starting transfers between devices: 8.87 us -> 7.79 us  [xor_all_reduce(): x = x + lax.ppermute(x, axis, xor_perm(n, lambda j, k=k: j ^ k))]
    ppermute x3, starting transfers between devices: 4.14 us -> 5.19 us  [xor_reduce_scatter(): x = keep + lax.ppermute(send, axis, xor_perm(n, lambda j, k=k: j ^ k))]
  transfers between devices with their start and end apart: 19 -> 16, of which waited for: 11 -> 13; matrix products, arithmetic and copies ran while one was open for 24% -> 20% of each run, Pallas kernels for 0% -> 0%
where the time goes in v7:
time: 97.5 us; the launch traced here: 97.1 us
  waiting for transfers between devices  33.9 us (35%)
  matrix products  18.7 us (19%)
  starting transfers between devices  17.5 us (18%)
  between operations  14.5 us (15%)
  local copies, waits for them, and re-layouts  6.28 us (6%)
  other arithmetic  6.25 us (6%)
    all_gather x1, waiting for transfers between devices, body(): q_weights = lax.all_gather(w_query, 'seq', axis=0, tiled=True)  11.5 us
    ppermute x5, starting transfers between devices, xor_all_reduce(): x = x + lax.ppermute(x, axis, xor_perm(n, lambda j, k=k: j ^ k))  7.79 us
    ppermute x5, waiting for transfers between devices, xor_all_reduce(): x = x + lax.ppermute(x, axis, xor_perm(n, lambda j, k=k: j ^ k))  6.73 us
    ppermute x3, waiting for transfers between devices, xor_reduce_scatter(): x = keep + lax.ppermute(send, axis, xor_perm(n, lambda j, k=k: j ^ k))  6.1 us
    ppermute x3, starting transfers between devices, xor_reduce_scatter(): x = keep + lax.ppermute(send, axis, xor_perm(n, lambda j, k=k: j ^ k))  5.19 us
    dot_general x1, matrix products, body(): jnp.einsum('dc,rce->dre', critic_hidden, critic_down, preferred_element_t...  5.1 us
    unnamed x19, local copies, waits for them, and re-layouts  4.17 us
    dot_general x1, matrix products, body(): jnp.dot(normed, q_weights, preferred_element_type=jnp.float32)  3.58 us
  transfers between devices with their start and end apart: 16, of which 13 were waited for; matrix products, arithmetic and copies ran while one was open for 20% of the time, Pallas kernels for 0%

profile of v7, /device:TPU:0, one launch (start us, length us, event | category | flops | bytes accessed | tf_op | source)
XLA Modules:
  0.0 97.1 jit_solution(9986044837060832174)
XLA Ops:
  7.2 0.0 copy-start
  7.2 0.0 all-gather.5.cloned.1.call-start
  7.3 1.4 %constant_dynamic-slice_fusion.3 = (bf16[1024,32]{1,0:T(8,128)(2,1)S(1)}, bf16[1024,32]{1,0:T(8,128)(2,1)S(1)}) fusion(bf16[1024,128]{1,0:T(8,128)(2,1)} %param.13, s32[]{:T(128)S(6)} %select_n.103, bf16[1024,128]{1,0:T(8,128)(2,1)} %param.12), kind=kLoop, calls=%fused_computation.84 | loop fusion | bytes 262148 | tf_op jit(solution)/shard_map/dynamic_slice | solution.py:110
  8.6 0.8 pad_maximum_fusion
  9.5 0.0 all-gather.5.cloned.1.call-update
  9.5 0.0 all-gather.3.cloned.1.call-start
  9.7 0.8 reduce-window.7
  10.6 0.7 convert_element_type.43
  11.3 2.1 %fusion.1 = f32[128]{0:T(128)S(1)} fusion(bf16[128,8192]{1,0:T(8,128)(2,1)} %param.9), kind=kLoop, calls=%fused_computation.4 | loop fusion | flops 3145600 | bytes 2097664 | tf_op jit(solution)/shard_map/reduce_sum | solution.py:15
  13.4 0.0 copy-start.3
  13.4 2.2 %convolution_convert_fusion = bf16[8,8192]{1,0:T(8,128)(2,1)S(1)} fusion(s32[128]{0:T(128)S(1)} %get-tuple-element.25, s32[8]{0:T(128)S(1)} %add_bitcast_fusion, bf16[128,8192]{1,0:T(8,128)(2,1)} %param.9, f32[8192]{0:T(1024)S(1)} %convert_element_type.43, f32[128]{0:T(128)S(1)} %add_rsqrt_fusion), kind=kOutput, calls=%fused_computation.1 | convolution fusion | flops 21038080 | bytes 2262048 | tf_op jit(solution)/shard_map/dot_general | solution.py:117
  15.7 3.1 %collective-permute-start.6 = (bf16[8,4096]{1,0:T(8,128)(2,1)S(1)}, bf16[8,4096]{1,0:T(8,128)(2,1)S(1)}, u32[]{:S(2)}, u32[]{:S(2)}) collective-permute-start(bf16[8,4096]{1,0:T(8,128)(2,1)S(1)} %constant_dynamic-slice_fusion.2), channel_id=1, source_target_pairs={{0,16},{4,20},{8,24},{12,28},{16,0},{20,4},{24,8},{28,12},{1,17},{... | collective-permute-start | bytes 196616 | tf_op jit(solution)/shard_map/ppermute | solution.py:41
  18.8 0.0 all-gather.3.cloned.1.call-update
  18.8 2.2 %collective-permute-done.6 = bf16[8,4096]{1,0:T(8,128)(2,1)S(1)} collective-permute-done((bf16[8,4096]{1,0:T(8,128)(2,1)S(1)}, bf16[8,4096]{1,0:T(8,128)(2,1)S(1)}, u32[]{:S(2)}, u32[]{:S(2)}) %collective-permute-start.6) | collective-permute-done | bytes 65568 | tf_op jit(solution)/shard_map/ppermute | solution.py:41
  21.1 2.1 %collective-permute-start.7 = (bf16[8,2048]{1,0:T(8,128)(2,1)S(1)}, bf16[8,2048]{1,0:T(8,128)(2,1)S(1)}, u32[]{:S(2)}, u32[]{:S(2)}) collective-permute-start(bf16[8,2048]{1,0:T(8,128)(2,1)S(1)} %constant_dynamic-slice_fusion.1), channel_id=1, source_target_pairs={{0,8},{4,12},{8,0},{12,4},{16,24},{20,28},{24,16},{28,20},{1,9},{5... | collective-permute-start | bytes 98312 | tf_op jit(solution)/shard_map/ppermute | solution.py:41
  23.1 2.7 %collective-permute-done.7 = bf16[8,2048]{1,0:T(8,128)(2,1)S(1)} collective-permute-done((bf16[8,2048]{1,0:T(8,128)(2,1)S(1)}, bf16[8,2048]{1,0:T(8,128)(2,1)S(1)}, u32[]{:S(2)}, u32[]{:S(2)}) %collective-permute-start.7) | collective-permute-done | bytes 32800 | tf_op jit(solution)/shard_map/ppermute | solution.py:41
  25.9 0.1 collective-permute-start.8
  26.0 1.2 %collective-permute-done.8 = bf16[8,1024]{1,0:T(8,128)(2,1)S(1)} collective-permute-done((bf16[8,1024]{1,0:T(8,128)(2,1)S(1)}, bf16[8,1024]{1,0:T(8,128)(2,1)S(1)}, u32[]{:S(2)}, u32[]{:S(2)}) %collective-permute-start.8) | collective-permute-done | bytes 16416 | tf_op jit(solution)/shard_map/ppermute | solution.py:41
  27.1 0.0 copy-done
  27.1 0.4 fusion.24
  27.6 0.2 collective-permute-start.9
  27.7 0.0 copy-done.3
  27.7 1.0 %collective-permute-done.9 = f32[8,1152]{1,0:T(8,128)S(1)} collective-permute-done((f32[8,1152]{1,0:T(8,128)S(1)}, f32[8,1152]{1,0:T(8,128)S(1)}, u32[]{:S(2)}, u32[]{:S(2)}) %collective-permute-start.9) | collective-permute-done | bytes 36896 | tf_op jit(solution)/shard_map/ppermute | solution.py:28
  28.8 1.2 %collective-permute-start.10 = (f32[8,1152]{1,0:T(8,128)S(1)}, f32[8,1152]{1,0:T(8,128)S(1)}, u32[]{:S(2)}, u32[]{:S(2)}) collective-permute-start(f32[8,1152]{1,0:T(8,128)S(1)} %add.221), channel_id=1, source_target_pairs={{0,8},{4,12},{8,0},{12,4},{16,24},{20,28},{24,16},{28,20},{1,9},{5... | collective-permute-start | bytes 110600 | tf_op jit(solution)/shard_map/ppermute | solution.py:28
  30.0 0.1 convert_reduce_fusion
  30.0 2.7 %collective-permute-done.10 = f32[8,1152]{1,0:T(8,128)S(1)} collective-permute-done((f32[8,1152]{1,0:T(8,128)S(1)}, f32[8,1152]{1,0:T(8,128)S(1)}, u32[]{:S(2)}, u32[]{:S(2)}) %collective-permute-start.10) | collective-permute-done | bytes 36896 | tf_op jit(solution)/shard_map/ppermute | solution.py:28
  32.8 1.8 %collective-permute-start.11 = (f32[8,1152]{1,0:T(8,128)S(1)}, f32[8,1152]{1,0:T(8,128)S(1)}, u32[]{:S(2)}, u32[]{:S(2)}) collective-permute-start(f32[8,1152]{1,0:T(8,128)S(1)} %add.222), channel_id=1, source_target_pairs={{0,16},{4,20},{8,24},{12,28},{16,0},{20,4},{24,8},{28,12},{1,17},{... | collective-permute-start | bytes 110600 | tf_op jit(solution)/shard_map/ppermute | solution.py:28
  34.6 0.1 convert_reduce_fusion.1
  34.7 3.0 %collective-permute-done.11 = f32[8,1152]{1,0:T(8,128)S(1)} collective-permute-done((f32[8,1152]{1,0:T(8,128)S(1)}, f32[8,1152]{1,0:T(8,128)S(1)}, u32[]{:S(2)}, u32[]{:S(2)}) %collective-permute-start.11) | collective-permute-done | bytes 36896 | tf_op jit(solution)/shard_map/ppermute | solution.py:28
  37.6 5.1 %fusion.9 = f32[8,1024]{1,0:T(8,128)S(1)} fusion(bf16[4,1152,1024]{2,1,0:T(8,128)(2,1)} %param.16, pred[8,4]{0,1:T(4,128)(4,1)S(1)} %iota_compare_fusion, f32[8,1152]{1,0:T(8,128)S(1)} %add.222, f32[8,1152]{1,0:T(8,128)S(1)} %collective-permute-done.11), kind=kOutput, calls=%fused_computation.16 | convolution fusion | flops 75610112 | bytes 9543712 | tf_op jit(solution)/shard_map/dc,rce->dre/dot_general | solution.py:128
  42.7 1.8 %collective-permute-start.12 = (f32[8,1024]{1,0:T(8,128)S(1)}, f32[8,1024]{1,0:T(8,128)S(1)}, u32[]{:S(2)}, u32[]{:S(2)}) collective-permute-start(f32[8,1024]{1,0:T(8,128)S(1)} %fusion.9), channel_id=1, source_target_pairs={{0,1},{1,0},{2,3},{3,2},{4,5},{5,4},{6,7},{7,6},{8,9},{9,8},{10,11... | collective-permute-start | bytes 98312 | tf_op jit(solution)/shard_map/ppermute | solution.py:28
  44.6 0.0 all-gather.5.cloned.1.call-done
  44.6 3.3 %fusion.11 = bf16[1,128,64]{1,2,0:T(8,128)(2,1)S(1)} fusion(bf16[8192,64]{1,0:T(8,128)(2,1)} %all-gather.5.cloned.1.call-done, bf16[128,8192]{1,0:T(8,128)(2,1)} %param.9, f32[8192]{0:T(1024)S(1)} %convert_element_type.43, f32[128]{0:T(128)S(1)} %add_rsqrt_fusion), kind=kOutput, calls=%fused_computation.19 | convolution fusion | flops 138420224 | bytes 3195392 | tf_op jit(solution)/shard_map/dot_general | solution.py:140
  47.9 0.3 collective-permute-start
  48.1 0.2 compare_and_fusion
  48.3 0.0 collective-permute-done.12
  48.4 2.8 %collective-permute-start.13 = (f32[8,1024]{1,0:T(8,128)S(1)}, f32[8,1024]{1,0:T(8,128)S(1)}, u32[]{:S(2)}, u32[]{:S(2)}) collective-permute-start(f32[8,1024]{1,0:T(8,128)S(1)} %add.225), channel_id=1, source_target_pairs={{0,2},{1,3},{2,0},{3,1},{4,6},{5,7},{6,4},{7,5},{8,10},{9,11},{10,... | collective-permute-start | bytes 98312 | tf_op jit(solution)/shard_map/ppermute | solution.py:28
  51.2 0.5 collective-permute-done
  51.7 2.5 %collective-permute-start.1 = (bf16[2,128,64]{1,2,0:T(8,128)(2,1)S(1)}, bf16[2,128,64]{1,2,0:T(8,128)(2,1)S(1)}, u32[]{:S(2)}, u32[]{:S(2)}) collective-permute-start(bf16[2,128,64]{1,2,0:T(8,128)(2,1)S(1)} %maximum_select_fusion.1), channel_id=1, source_target_pairs={{0,2},{1,3},{2,0},{3,1},{4,6},{5,7},{6,4},{7,5},{8,10},{9,11},{10,... | collective-permute-start | bytes 98312 | tf_op jit(solution)/shard_map/ppermute | solution.py:51
  54.1 0.0 collective-permute-done.13
  54.1 0.6 add_convert_fusion
  54.8 1.8 %collective-permute-done.1 = bf16[2,128,64]{1,2,0:T(8,128)(2,1)S(1)} collective-permute-done((bf16[2,128,64]{1,2,0:T(8,128)(2,1)S(1)}, bf16[2,128,64]{1,2,0:T(8,128)(2,1)S(1)}, u32[]{:S(2)}, u32[]{:S(2)}) %collective-permute-start.1) | collective-permute-done | bytes 32800 | tf_op jit(solution)/shard_map/ppermute | solution.py:51
  56.7 0.1 collective-permute-start.2
  56.8 0.6 constant_dynamic-update-slice_fusion.14
  57.4 0.6 collective-permute-done.2
  58.0 1.1 %collective-permute-start.3 = (bf16[256,256]{0,1:T(8,128)(2,1)S(1)}, bf16[256,256]{0,1:T(8,128)(2,1)S(1)}, u32[]{:S(2)}, u32[]{:S(2)}) collective-permute-start(bf16[256,256]{0,1:T(8,128)(2,1)S(1)} %pad_maximum_fusion.2), channel_id=1, source_target_pairs={{0,8},{4,20},{8,0},{12,28},{16,24},{20,4},{24,16},{28,12},{1,9},{5... | collective-permute-start | bytes 393224 | tf_op jit(solution)/shard_map/ppermute | solution.py:76
  59.1 0.6 constant_dynamic-update-slice_fusion.10
  59.7 3.4 %collective-permute-done.3 = bf16[256,256]{0,1:T(8,128)(2,1)S(1)} collective-permute-done((bf16[256,256]{0,1:T(8,128)(2,1)S(1)}, bf16[256,256]{0,1:T(8,128)(2,1)S(1)}, u32[]{:S(2)}, u32[]{:S(2)}) %collective-permute-start.3) | collective-permute-done | bytes 131104 | tf_op jit(solution)/shard_map/ppermute | solution.py:76
  63.0 0.4 collective-permute-start.4
  63.4 0.7 slice_dynamic-update-slice_fusion.3
  64.1 2.7 %collective-permute-done.4 = bf16[128,256]{0,1:T(8,128)(2,1)S(1)} collective-permute-done((bf16[128,256]{0,1:T(8,128)(2,1)S(1)}, bf16[128,256]{0,1:T(8,128)(2,1)S(1)}, u32[]{:S(2)}, u32[]{:S(2)}) %collective-permute-start.4) | collective-permute-done | bytes 65568 | tf_op jit(solution)/shard_map/ppermute | solution.py:77
  66.8 0.2 collective-permute-start.5
  66.9 0.6 constant_dynamic-update-slice_fusion.9
  67.6 0.7 collective-permute-done.5
  68.3 0.7 slice_dynamic-update-slice_fusion.1
  68.9 11.5 %all-gather.3.cloned.1.call-done = bf16[8192,256]{1,0:T(8,128)(2,1)} async-done(((bf16[1024,256]{1,0:T(8,128)(2,1)}), bf16[8192,256]{1,0:T(8,128)(2,1)}) %all-gather.3.cloned.1.call-update) | async-done | bytes 4194320 | tf_op jit(solution)/shard_map/all_gather | solution.py:157
  80.5 3.6 %fusion.10 = bf16[16,2,8,128]{3,2,1,0:T(8,128)(2,1)S(1)} fusion(bf16[8192,256]{1,0:T(8,128)(2,1)} %all-gather.3.cloned.1.call-done, bf16[128,8192]{1,0:T(8,128)(2,1)} %param.9, f32[8192]{0:T(1024)S(1)} %convert_element_type.43, f32[128]{0:T(128)S(1)} %add_rsqrt_fusion), kind=kOutput, calls=%fused_computation.17 | convolution fusion | flops 541097984 | bytes 6390272 | tf_op jit(solution)/shard_map/dot_general | solution.py:159
  84.0 0.0 copy-start.2
  84.1 0.0 copy-done.1
  84.1 0.6 copy-done.2
  84.7 0.7 fusion.39
  85.3 1.3 %fusion.7 = f32[128,2,1024]{2,0,1:T(8,128)S(1)} fusion(pred[128,1024]{1,0:T(8,128)(4,1)S(1)} %compare_and_fusion, bf16[1024,128]{0,1:T(8,128)(2,1)} %copy-done.1, bf16[16,2,8,128]{3,2,1,0:T(8,128)(2,1)} %copy-done.2), kind=kOutput, calls=%fused_computation.11 | convolution fusion | flops 67633152 | bytes 1507328 | tf_op jit(solution)/shard_map/qhd,kd->qhk/dot_general | solution.py:174
  86.7 2.0 %fusion.8 = bf16[128,2,128]{0,2,1:T(8,128)(2,1)} fusion(bf16[1024,128]{0,1:T(8,128)(2,1)} %get-tuple-element.7, f32[128,2,1024]{2,0,1:T(8,128)S(1)} %fusion.7, pred[128,1024]{1,0:T(8,128)(4,1)S(1)} %compare_and_fusion, f32[128,2]{0,1:T(2,128)S(1)} %fusion.39), kind=kOutput, calls=%fused_computation.14 | convolution fusion | flops 67962112 | bytes 1508352 | tf_op jit(solution)/shard_map/qhk,kd->qhd/dot_general | solution.py:181
  88.7 1.6 %copy.16 = bf16[128,256]{1,0:T(8,128)(2,1)} copy(bf16[128,256]{0,1:T(8,128)(2,1)} %bitcast.66) | data formatting | bytes 131072
  (36 shorter events, 0.3 us)
Async XLA Ops:
  7.2 20.0 %copy-start = (bf16[1024,1152]{1,0:T(8,128)(2,1)S(1)}, bf16[1024,1152]{1,0:T(8,128)(2,1)}, u32[]{:S(2)}) copy-start(bf16[1024,1152]{1,0:T(8,128)(2,1)} %param.15) | copy-start | bytes 7077892
  7.2 37.4 %all-gather.5.cloned.1.call-start = ((), (), s32[]{:S(2)}) async-start(), calls=%async_computation.1 | async-start | bytes 2359296 | tf_op jit(solution)/shard_map/all_gather | solution.py:139
  9.5 70.9 %all-gather.3.cloned.1.call-start = ((), (), s32[]{:S(2)}) async-start(), calls=%async_computation | async-start | bytes 4718592 | tf_op jit(solution)/shard_map/all_gather | solution.py:157
  13.4 14.3 %copy-start.3 = (s32[8]{0:T(128)S(1)}, s32[8]{0:T(128)}, u32[]{:S(2)}) copy-start(s32[8]{0:T(128)} %param.17) | copy-start | bytes 100
  15.7 5.3 %collective-permute-start.6 = (bf16[8,4096]{1,0:T(8,128)(2,1)S(1)}, bf16[8,4096]{1,0:T(8,128)(2,1)S(1)}, u32[]{:S(2)}, u32[]{:S(2)}) collective-permute-start(bf16[8,4096]{1,0:T(8,128)(2,1)S(1)} %constant_dynamic-slice_fusion.2), channel_id=1, source_target_pairs={{0,16},{4,20},{8,24},{12,28},{16,0},{20,4},{24,8},{28,12},{1,17},{... | collective-permute-start | bytes 196616 | tf_op jit(solution)/shard_map/ppermute | solution.py:41
  21.1 4.8 %collective-permute-start.7 = (bf16[8,2048]{1,0:T(8,128)(2,1)S(1)}, bf16[8,2048]{1,0:T(8,128)(2,1)S(1)}, u32[]{:S(2)}, u32[]{:S(2)}) collective-permute-start(bf16[8,2048]{1,0:T(8,128)(2,1)S(1)} %constant_dynamic-slice_fusion.1), channel_id=1, source_target_pairs={{0,8},{4,12},{8,0},{12,4},{16,24},{20,28},{24,16},{28,20},{1,9},{5... | collective-permute-start | bytes 98312 | tf_op jit(solution)/shard_map/ppermute | solution.py:41
  25.9 1.2 %collective-permute-start.8 = (bf16[8,1024]{1,0:T(8,128)(2,1)S(1)}, bf16[8,1024]{1,0:T(8,128)(2,1)S(1)}, u32[]{:S(2)}, u32[]{:S(2)}) collective-permute-start(bf16[8,1024]{1,0:T(8,128)(2,1)S(1)} %constant_dynamic-slice_fusion), channel_id=1, source_target_pairs={{0,4},{4,0},{8,12},{12,8},{16,20},{20,16},{24,28},{28,24},{1,5},{5... | collective-permute-start | bytes 49160 | tf_op jit(solution)/shard_map/ppermute | solution.py:41
  27.6 1.2 %collective-permute-start.9 = (f32[8,1152]{1,0:T(8,128)S(1)}, f32[8,1152]{1,0:T(8,128)S(1)}, u32[]{:S(2)}, u32[]{:S(2)}) collective-permute-start(f32[8,1152]{1,0:T(8,128)S(1)} %fusion.24), channel_id=1, source_target_pairs={{0,4},{4,0},{8,12},{12,8},{16,20},{20,16},{24,28},{28,24},{1,5},{5... | collective-permute-start | bytes 110600 | tf_op jit(solution)/shard_map/ppermute | solution.py:28
  28.8 4.0 %collective-permute-start.10 = (f32[8,1152]{1,0:T(8,128)S(1)}, f32[8,1152]{1,0:T(8,128)S(1)}, u32[]{:S(2)}, u32[]{:S(2)}) collective-permute-start(f32[8,1152]{1,0:T(8,128)S(1)} %add.221), channel_id=1, source_target_pairs={{0,8},{4,12},{8,0},{12,4},{16,24},{20,28},{24,16},{28,20},{1,9},{5... | collective-permute-start | bytes 110600 | tf_op jit(solution)/shard_map/ppermute | solution.py:28
  32.8 4.9 %collective-permute-start.11 = (f32[8,1152]{1,0:T(8,128)S(1)}, f32[8,1152]{1,0:T(8,128)S(1)}, u32[]{:S(2)}, u32[]{:S(2)}) collective-permute-start(f32[8,1152]{1,0:T(8,128)S(1)} %add.222), channel_id=1, source_target_pairs={{0,16},{4,20},{8,24},{12,28},{16,0},{20,4},{24,8},{28,12},{1,17},{... | collective-permute-start | bytes 110600 | tf_op jit(solution)/shard_map/ppermute | solution.py:28
  42.7 5.6 %collective-permute-start.12 = (f32[8,1024]{1,0:T(8,128)S(1)}, f32[8,1024]{1,0:T(8,128)S(1)}, u32[]{:S(2)}, u32[]{:S(2)}) collective-permute-start(f32[8,1024]{1,0:T(8,128)S(1)} %fusion.9), channel_id=1, source_target_pairs={{0,1},{1,0},{2,3},{3,2},{4,5},{5,4},{6,7},{7,6},{8,9},{9,8},{10,11... | collective-permute-start | bytes 98312 | tf_op jit(solution)/shard_map/ppermute | solution.py:28
  47.9 3.8 %collective-permute-start = (bf16[1,128,64]{1,2,0:T(8,128)(2,1)S(1)}, bf16[1,128,64]{1,2,0:T(8,128)(2,1)S(1)}, u32[]{:S(2)}, u32[]{:S(2)}) collective-permute-start(bf16[1,128,64]{1,2,0:T(8,128)(2,1)S(1)} %fusion.11), channel_id=1, source_target_pairs={{0,1},{1,0},{2,3},{3,2},{4,5},{5,4},{6,7},{7,6},{8,9},{9,8},{10,11... | collective-permute-start | bytes 49160 | tf_op jit(solution)/shard_map/ppermute | solution.py:51
  48.4 5.8 %collective-permute-start.13 = (f32[8,1024]{1,0:T(8,128)S(1)}, f32[8,1024]{1,0:T(8,128)S(1)}, u32[]{:S(2)}, u32[]{:S(2)}) collective-permute-start(f32[8,1024]{1,0:T(8,128)S(1)} %add.225), channel_id=1, source_target_pairs={{0,2},{1,3},{2,0},{3,1},{4,6},{5,7},{6,4},{7,5},{8,10},{9,11},{10,... | collective-permute-start | bytes 98312 | tf_op jit(solution)/shard_map/ppermute | solution.py:28
  51.7 4.9 %collective-permute-start.1 = (bf16[2,128,64]{1,2,0:T(8,128)(2,1)S(1)}, bf16[2,128,64]{1,2,0:T(8,128)(2,1)S(1)}, u32[]{:S(2)}, u32[]{:S(2)}) collective-permute-start(bf16[2,128,64]{1,2,0:T(8,128)(2,1)S(1)} %maximum_select_fusion.1), channel_id=1, source_target_pairs={{0,2},{1,3},{2,0},{3,1},{4,6},{5,7},{6,4},{7,5},{8,10},{9,11},{10,... | collective-permute-start | bytes 98312 | tf_op jit(solution)/shard_map/ppermute | solution.py:51
  56.7 1.3 %collective-permute-start.2 = (bf16[128,256]{0,1:T(8,128)(2,1)S(1)}, bf16[128,256]{0,1:T(8,128)(2,1)S(1)}, u32[]{:S(2)}, u32[]{:S(2)}) collective-permute-start(bf16[128,256]{0,1:T(8,128)(2,1)S(1)} %constant_dynamic-update-slice_fusion.1), channel_id=1, source_target_pairs={{0,4},{4,0},{8,12},{12,8},{16,20},{20,16},{24,28},{28,24},{1,5},{5... | collective-permute-start | bytes 196616 | tf_op jit(solution)/shard_map/ppermute | solution.py:74
  58.0 5.0 %collective-permute-start.3 = (bf16[256,256]{0,1:T(8,128)(2,1)S(1)}, bf16[256,256]{0,1:T(8,128)(2,1)S(1)}, u32[]{:S(2)}, u32[]{:S(2)}) collective-permute-start(bf16[256,256]{0,1:T(8,128)(2,1)S(1)} %pad_maximum_fusion.2), channel_id=1, source_target_pairs={{0,8},{4,20},{8,0},{12,28},{16,24},{20,4},{24,16},{28,12},{1,9},{5... | collective-permute-start | bytes 393224 | tf_op jit(solution)/shard_map/ppermute | solution.py:76
  63.0 3.7 %collective-permute-start.4 = (bf16[128,256]{0,1:T(8,128)(2,1)S(1)}, bf16[128,256]{0,1:T(8,128)(2,1)S(1)}, u32[]{:S(2)}, u32[]{:S(2)}) collective-permute-start(bf16[128,256]{0,1:T(8,128)(2,1)S(1)} %slice.107), channel_id=1, source_target_pairs={{0,20},{4,8},{8,28},{12,0},{16,4},{20,24},{24,12},{28,16},{1,21},{... | collective-permute-start | bytes 196616 | tf_op jit(solution)/shard_map/ppermute | solution.py:77
  66.8 1.5 %collective-permute-start.5 = (bf16[384,256]{0,1:T(8,128)(2,1)S(1)}, bf16[384,256]{0,1:T(8,128)(2,1)S(1)}, u32[]{:S(2)}, u32[]{:S(2)}) collective-permute-start(bf16[384,256]{0,1:T(8,128)(2,1)S(1)} %pad_maximum_fusion.1), channel_id=1, source_target_pairs={{0,4},{4,0},{8,12},{12,8},{16,20},{20,16},{24,28},{28,24},{1,5},{5... | collective-permute-start | bytes 589832 | tf_op jit(solution)/shard_map/ppermute | solution.py:78
  68.9 15.1 %copy-start.1 = (bf16[1024,128]{0,1:T(8,128)(2,1)}, bf16[1024,128]{0,1:T(8,128)(2,1)S(1)}, u32[]{:S(2)}) copy-start(bf16[1024,128]{0,1:T(8,128)(2,1)S(1)} %get-tuple-element.6) | copy-start | bytes 786436
  84.0 0.6 copy-start.2
Sparse Core Ops, SparseCore 0:
  9.9 31.7 all-gather.4
  43.6 36.7 all-gather.2

commit v8 on v5

--- a/solution.py
+++ b/solution.py
@@ -76,6 +76,34 @@
         got = lax.ppermute(pair, "seq", xor_perm(8, lambda j, m=m: j ^ m))
         pieces += [(got[:rows], i ^ m, rows), (got[rows:], i ^ m ^ 1, rows)]
     return pieces
+
+
+def gather_forward(blk, n):
+    i = lax.axis_index("seq")
+    rows = blk.shape[0]
+    if n != 8:
+        full = lax.all_gather(blk, "seq", axis=0, tiled=True)
+        return [(full, jnp.int32(0), n * rows)]
+    core = i % 2
+    chip = i // 2
+    sib = lax.ppermute(blk, "seq", xor_perm(8, lambda j: j ^ 1))
+    pair = jnp.concatenate([blk, sib], axis=0)
+    nb = lax.ppermute(pair, "seq", xor_perm(8, lambda j: j ^ 2 if j % 2 == 0 else j ^ 4))
+    dg = lax.ppermute(nb[:rows], "seq", xor_perm(8, lambda j: j ^ 5 if j % 2 == 0 else j ^ 3))
+    oth = lax.ppermute(jnp.concatenate([nb, dg], axis=0), "seq", xor_perm(8, lambda j: j ^ 1))
+    nb_chip = chip ^ (1 + core)
+    oth_chip = chip ^ (2 - core)
+    diag = chip ^ 3
+    return [
+        (blk, i, rows),
+        (sib, i ^ 1, rows),
+        (nb[:rows], 2 * nb_chip + core, rows),
+        (nb[rows:], 2 * nb_chip + 1 - core, rows),
+        (dg, 2 * diag + 1 - core, rows),
+        (oth[:rows], 2 * oth_chip + 1 - core, rows),
+        (oth[rows : 2 * rows], 2 * oth_chip + core, rows),
+        (oth[2 * rows :], 2 * diag + core, rows),
+    ]
 
 
 def project(normed, pieces, stride, offset=0):
@@ -115,7 +143,11 @@
     first_row = seq_i * tokens_here
     query_pos = first_row + jnp.arange(tokens_here, dtype=jnp.int32)
     picker = (doc_ends[:, None] == query_pos[None, :]).astype(jnp.bfloat16)
-    end_terms = jnp.dot(picker, normed, preferred_element_type=jnp.float32).astype(jnp.bfloat16)
+    picked = jnp.dot(picker, hidden, preferred_element_type=jnp.float32)
+    picked_square = jnp.mean(picked * picked, axis=-1, keepdims=True)
+    end_terms = (
+        picked * lax.rsqrt(picked_square + 1e-05) * norm_gain.astype(jnp.float32)
+    ).astype(jnp.bfloat16)
     if n_seq == 8:
         end_rows = seq_reduce_scatter(end_terms).astype(jnp.bfloat16)
     else:
@@ -137,7 +169,7 @@
         critic_sum = lax.psum(chosen, "tp")
     critic_values = critic_sum.astype(jnp.bfloat16)
 
-    kv_pieces = gather_pieces(kv_weights, n_seq)
+    kv_pieces = gather_forward(kv_weights, n_seq)
     kv_own = project(normed, kv_pieces, d_rows).astype(jnp.bfloat16)
     got = [kv_own] + [
         lax.ppermute(kv_own, "tp", xor_perm(n_tp, lambda j, k=k: j ^ k))
@@ -173,10 +205,15 @@
         return jnp.sum((positions[:, None] > doc_ends[None, :]).astype(jnp.int32), axis=1)
 
     query_seg = segment_of(query_pos)
-    inverse_root = 1.0 / math.sqrt(HEAD)
     allowed = (query_seg[:, None] == segment_of(key_pos)[None, :]) & (
         key_pos[None, :] <= query_pos[:, None]
     )
+    attention = attend(queries, key_block, value_block, allowed, heads_here)
+    return (attention, critic_values)
+
+
+def attend(queries, key_block, value_block, allowed, heads_here):
+    inverse_root = 1.0 / math.sqrt(HEAD)
     outs = []
     for h in range(heads_here):
         scores = (
@@ -191,8 +228,7 @@
             expanded.astype(jnp.bfloat16), value_block, preferred_element_type=jnp.float32
         )
         outs.append((weighted / totals).astype(jnp.bfloat16))
-    attention = jnp.concatenate(outs, axis=1)
-    return (attention, critic_values)
+    return jnp.concatenate(outs, axis=1)
 
 
 def solution(mesh):

time: 105 us -> 83.9 us (0.80)
  waiting for transfers between devices: 35 us -> 18.3 us
  other arithmetic: 8.94 us -> 7.43 us
  matrix products: 17.6 us -> 16.1 us
  local copies, waits for them, and re-layouts: 3.67 us -> 2.47 us
    ppermute x6 -> x3, waiting for transfers between devices: 26.2 us -> 5.58 us  [gather_pieces(): got = lax.ppermute(pair, 'seq', xor_perm(8, lambda j, m=m: j ^ m))]
    ppermute x0 -> x4, waiting for transfers between devices: none -> 5.15 us  [the longest x1 3.88 us: gather_forward(): lax.ppermute(pair, 'seq', xor_perm(8, lambda j: j ^ 2 if j % 2 == 0 else...]
    ppermute x6 -> x3, starting transfers between devices: 7.17 us -> 3.55 us  [gather_pieces(): got = lax.ppermute(pair, 'seq', xor_perm(8, lambda j, m=m: j ^ m))]
    ppermute x0 -> x4, starting transfers between devices: none -> 2.92 us  [the longest x1 2.01 us: gather_forward(): lax.ppermute(pair, 'seq', xor_perm(8, lambda j: j ^ 2 if j % 2 == 0 else...]
    ppermute x3, waiting for transfers between devices: 2.42 us -> 0.01 us  [seq_reduce_scatter(): lax.ppermute(part, 'seq', xor_perm(8, lambda j, m=m: j ^ m))]
    ppermute x3, waiting for transfers between devices: 0.01 us -> 2.37 us  [seq_all_reduce(): lax.ppermute(x, 'seq', xor_perm(8, lambda j, m=m: j ^ m))]
    convert_element_type x1, other arithmetic: 3.52 us -> 1.95 us  [rms_norm(): (widened * lax.rsqrt(mean_square + 1e-05) * norm_gain.astype(jnp.float32)...]
  transfers between devices with their start and end apart: 23 -> 23, of which waited for: 11 -> 9; matrix products, arithmetic and copies ran while one was open for 21% -> 20% of each run, Pallas kernels for 0% -> 0%
where the time goes in v8:
time: 83.9 us; the launch traced here: 83.5 us
  starting transfers between devices  24.5 us (29%)
  waiting for transfers between devices  18.3 us (22%)
  matrix products  16.1 us (19%)
  between operations  14.7 us (18%)
  other arithmetic  7.43 us (9%)
  local copies, waits for them, and re-layouts  2.47 us (3%)
    ppermute x3, waiting for transfers between devices, gather_pieces(): got = lax.ppermute(pair, 'seq', xor_perm(8, lambda j, m=m: j ^ m))  5.58 us
    dot_general x1, matrix products, body(): jnp.einsum('dc,rce->dre', critic_hidden, critic_down, preferred_element_t...  5.01 us
    ppermute x3, starting transfers between devices, seq_reduce_scatter(): lax.ppermute(part, 'seq', xor_perm(8, lambda j, m=m: j ^ m))  4.57 us
    ppermute x3, starting transfers between devices, body(): lax.ppermute(kv_own, 'tp', xor_perm(n_tp, lambda j, k=k: j ^ k))  4.45 us
    ppermute x3, starting transfers between devices, group_sum(): lax.ppermute(x, axis, xor_perm(n, lambda j, k=k: j ^ k))  4.39 us
    ppermute x1, waiting for transfers between devices, gather_forward(): lax.ppermute(pair, 'seq', xor_perm(8, lambda j: j ^ 2 if j % 2 == 0 else...  3.88 us
    dot_general x8, matrix products, project(): term = jnp.dot(cols, piece, preferred_element_type=jnp.float32)  3.61 us
    ppermute x3, starting transfers between devices, seq_all_reduce(): lax.ppermute(x, 'seq', xor_perm(8, lambda j, m=m: j ^ m))  3.55 us
  transfers between devices with their start and end apart: 23, of which 9 were waited for; matrix products, arithmetic and copies ran while one was open for 20% of the time, Pallas kernels for 0%

profile of v8, /device:TPU:0, one launch (start us, length us, event | category | flops | bytes accessed | tf_op | source)
XLA Modules:
  0.0 83.5 jit_solution(9747815597067742917)
XLA Ops:
  7.2 0.0 copy-start
  7.2 0.0 all-gather.2.cloned.1.call-start
  7.4 1.0 %reduce-window.7 = s32[8,1]{0,1:T(1,128)S(1)} reduce-window(s32[8,1]{0,1:T(1,128)} %bitcast.27, s32[]{:T(128)} %constant.99.clone.1), window={size=8x1 pad=7_0x0_0}, to_apply=%region_0.0 | reduce-window | flops 56 | bytes 68 | tf_op jit(solution)/shard_map/reduce-window.2
  8.4 2.1 %multiply_reduce_fusion = (f32[8]{0:T(128)S(1)}, f32[8,8192]{1,0:T(8,128)S(1)}) fusion(bf16[128,8192]{1,0:T(8,128)(2,1)} %param.9, s32[128]{0:T(128)S(1)} %get-tuple-element.50, s32[8]{0:T(128)S(1)} %add_bitcast_fusion), kind=kOutput, calls=%fused_computation.34 | convolution fusion | flops 16909304 | bytes 2359872 | tf_op jit(solution)/shard_map/dot_general | solution.py:146
  10.6 0.1 multiply_convert_fusion
  10.8 3.0 %collective-permute-start.11 = (bf16[8,2048]{1,0:T(8,128)(2,1)S(1)}, bf16[8,2048]{1,0:T(8,128)(2,1)S(1)}, u32[]{:S(2)}, u32[]{:S(2)}) collective-permute-start(bf16[8,2048]{1,0:T(8,128)(2,1)S(1)} %get-tuple-element.12), channel_id=1, source_target_pairs={{0,8},{4,12},{8,0},{12,4},{16,24},{20,28},{24,16},{28,20},{1,9},{5... | collective-permute-start | bytes 98312 | tf_op jit(solution)/shard_map/ppermute | solution.py:37
  13.8 1.5 %collective-permute-start.12 = (bf16[8,2048]{1,0:T(8,128)(2,1)S(1)}, bf16[8,2048]{1,0:T(8,128)(2,1)S(1)}, u32[]{:S(2)}, u32[]{:S(2)}) collective-permute-start(bf16[8,2048]{1,0:T(8,128)(2,1)S(1)} %get-tuple-element.14), channel_id=1, source_target_pairs={{0,16},{4,20},{8,24},{12,28},{16,0},{20,4},{24,8},{28,12},{1,17},{... | collective-permute-start | bytes 98312 | tf_op jit(solution)/shard_map/ppermute | solution.py:37
  15.3 0.0 collective-permute-start.13
  15.3 1.2 %constant_dynamic-slice_fusion.4 = (bf16[1024,32]{1,0:T(8,128)(2,1)S(1)}, bf16[1024,32]{1,0:T(8,128)(2,1)S(1)}) fusion(bf16[1024,128]{1,0:T(8,128)(2,1)S(1)} %copy-done.3, s32[]{:T(128)S(6)} %select_n.247, bf16[1024,128]{1,0:T(8,128)(2,1)} %param.12), kind=kLoop, calls=%fused_computation.112 | loop fusion | bytes 262148 | tf_op jit(solution)/shard_map/dynamic_slice | solution.py:137
  16.5 0.1 copy.26
  16.6 0.1 copy.27
  16.8 0.1 collective-permute-start
  16.9 0.0 all-gather.2.cloned.1.call-update
  16.9 0.0 copy-start.1
  16.9 2.2 %fusion = f32[128]{0:T(128)S(1)} fusion(bf16[128,8192]{1,0:T(8,128)(2,1)} %param.9), kind=kLoop, calls=%fused_computation.2 | loop fusion | flops 3145600 | bytes 2097664 | tf_op jit(solution)/shard_map/reduce_sum | solution.py:15
  19.2 1.9 %fusion.2 = bf16[128,8192]{1,0:T(8,128)(2,1)} fusion(bf16[128,8192]{1,0:T(8,128)(2,1)S(1)} %copy-done.1, f32[8192]{0:T(1024)S(1)} %convert_element_type.62, f32[128]{0:T(128)S(1)} %add_rsqrt_fusion.1), kind=kLoop, calls=%fused_computation.4 | loop fusion | flops 4194304 | bytes 4227584 | tf_op jit(solution)/shard_map/convert_element_type | solution.py:16
  21.1 0.1 convert_reduce_fusion
  21.3 0.8 convert_add_fusion
  22.1 0.6 collective-permute-start.14
  22.6 0.1 convert_reduce_fusion.1
  22.7 0.8 collective-permute-done.14
  23.5 0.4 fusion.43
  23.9 0.4 collective-permute-start.15
  24.3 2.0 %collective-permute-start.1 = (bf16[2048,64]{0,1:T(8,128)(2,1)S(1)}, bf16[2048,64]{0,1:T(8,128)(2,1)S(1)}, u32[]{:S(2)}, u32[]{:S(2)}) collective-permute-start(bf16[2048,64]{0,1:T(8,128)(2,1)S(1)} %pad_maximum_fusion.1), channel_id=1, source_target_pairs={{0,8},{4,20},{8,0},{12,28},{16,24},{20,4},{24,16},{28,12},{1,9},{5... | collective-permute-start | bytes 786440 | tf_op jit(solution)/shard_map/ppermute | solution.py:91
  26.3 1.2 %fusion.36 = f32[128,64]{0,1:T(8,128)S(1)} fusion(bf16[128,8192]{1,0:T(8,128)(2,1)} %fusion.2, s32[]{:T(128)S(6)} %select_n.245, bf16[1024,32]{0,1:T(8,128)(2,1)S(1)} %copy.27, bf16[1024,32]{0,1:T(8,128)(2,1)S(1)} %copy.26), kind=kOutput, calls=%fused_computation.51 | convolution fusion | flops 17039360 | bytes 425988 | tf_op jit(solution)/shard_map/dot_general | solution.py:113
  27.6 0.2 collective-permute-start.16
  27.7 2.0 %collective-permute-start.17 = (f32[8,1152]{1,0:T(8,128)S(1)}, f32[8,1152]{1,0:T(8,128)S(1)}, u32[]{:S(2)}, u32[]{:S(2)}) collective-permute-start(f32[8,1152]{1,0:T(8,128)S(1)} %add.284), channel_id=1, source_target_pairs={{0,16},{4,20},{8,24},{12,28},{16,0},{20,4},{24,8},{28,12},{1,17},{... | collective-permute-start | bytes 110600 | tf_op jit(solution)/shard_map/ppermute | solution.py:27
  29.7 1.4 %collective-permute-start.18 = (f32[8,1152]{1,0:T(8,128)S(1)}, f32[8,1152]{1,0:T(8,128)S(1)}, u32[]{:S(2)}, u32[]{:S(2)}) collective-permute-start(f32[8,1152]{1,0:T(8,128)S(1)} %add.284), channel_id=1, source_target_pairs={{0,24},{4,28},{8,16},{12,20},{16,8},{20,12},{24,0},{28,4},{1,25},{... | collective-permute-start | bytes 110600 | tf_op jit(solution)/shard_map/ppermute | solution.py:27
  31.1 1.2 %convolution_add_fusion.1 = f32[128,64]{0,1:T(8,128)S(1)} fusion(f32[128,64]{0,1:T(8,128)S(1)} %fusion.36, bf16[1024,64]{0,1:T(8,128)(2,1)S(1)} %collective-permute-done, bf16[128,8192]{1,0:T(8,128)(2,1)} %fusion.2, s32[]{:T(128)S(6)} %select_n.248), kind=kOutput, calls=%fused_computation.22 | convolution fusion | flops 16785408 | bytes 458756 | tf_op jit(solution)/shard_map/dot_general | solution.py:113
  32.3 3.9 %collective-permute-done.1 = bf16[2048,64]{0,1:T(8,128)(2,1)S(1)} collective-permute-done((bf16[2048,64]{0,1:T(8,128)(2,1)S(1)}, bf16[2048,64]{0,1:T(8,128)(2,1)S(1)}, u32[]{:S(2)}, u32[]{:S(2)}) %collective-permute-start.1) | collective-permute-done | bytes 262176 | tf_op jit(solution)/shard_map/ppermute | solution.py:91
  36.2 0.8 collective-permute-start.2
  37.0 2.4 %collective-permute-done.18 = f32[8,1152]{1,0:T(8,128)S(1)} collective-permute-done((f32[8,1152]{1,0:T(8,128)S(1)}, f32[8,1152]{1,0:T(8,128)S(1)}, u32[]{:S(2)}, u32[]{:S(2)}) %collective-permute-start.18) | collective-permute-done | bytes 36896 | tf_op jit(solution)/shard_map/ppermute | solution.py:27
  39.3 5.0 %fusion.5 = f32[8,1024]{1,0:T(8,128)S(1)} fusion(bf16[4,1152,1024]{2,1,0:T(8,128)(2,1)} %param.16, pred[8,4]{0,1:T(4,128)(4,1)S(1)} %iota_compare_fusion, f32[8,1152]{1,0:T(8,128)S(1)} %collective-permute-done.18, f32[8,1152]{1,0:T(8,128)S(1)} %collective-permute-done.17, f32[8,1152]{1,0:T(8,128)S(1)} %add.284, f32[8,1152]{1,0:T(8,128)S(1)} %collective-permute-done.16), kind=kOutput, calls=%fused_computation.11 | convolution fusion | flops 75628544 | bytes 9617440 | tf_op jit(solution)/shard_map/dc,rce->dre/dot_general | solution.py:161
  44.3 3.6 %collective-permute-start.19 = (f32[8,1024]{1,0:T(8,128)S(1)}, f32[8,1024]{1,0:T(8,128)S(1)}, u32[]{:S(2)}, u32[]{:S(2)}) collective-permute-start(f32[8,1024]{1,0:T(8,128)S(1)} %fusion.5), channel_id=1, source_target_pairs={{0,3},{1,2},{2,1},{3,0},{4,7},{5,6},{6,5},{7,4},{8,11},{9,10},{10,... | collective-permute-start | bytes 98312 | tf_op jit(solution)/shard_map/ppermute | solution.py:46
  47.9 0.8 collective-permute-start.21
  48.8 0.1 collective-permute-start.3
  48.9 0.2 fusion.32
  49.1 0.2 fusion.30
  49.3 1.3 %collective-permute-done.3 = bf16[3072,64]{0,1:T(8,128)(2,1)S(1)} collective-permute-done((bf16[3072,64]{0,1:T(8,128)(2,1)S(1)}, bf16[3072,64]{0,1:T(8,128)(2,1)S(1)}, u32[]{:S(2)}, u32[]{:S(2)}) %collective-permute-start.3) | collective-permute-done | bytes 393248 | tf_op jit(solution)/shard_map/ppermute | solution.py:93
  50.6 0.2 fusion.28
  50.8 0.2 fusion.26
  51.0 0.2 fusion.24
  51.2 0.2 fusion.13
  51.4 3.7 %collective-permute-start.4 = (bf16[128,64]{0,1:T(8,128)(2,1)S(1)}, bf16[128,64]{0,1:T(8,128)(2,1)S(1)}, u32[]{:S(2)}, u32[]{:S(2)}) collective-permute-start(bf16[128,64]{0,1:T(8,128)(2,1)S(1)} %fusion.13), channel_id=1, source_target_pairs={{0,3},{1,2},{2,1},{3,0},{4,7},{5,6},{6,5},{7,4},{8,11},{9,10},{10,... | collective-permute-start | bytes 49160 | tf_op jit(solution)/shard_map/ppermute | solution.py:175
  55.1 0.8 collective-permute-start.6
  55.9 0.6 add_convert_fusion
  56.5 0.5 collective-permute-done.4
  57.1 2.7 %collective-permute-done.5 = bf16[128,64]{0,1:T(8,128)(2,1)S(1)} collective-permute-done((bf16[128,64]{0,1:T(8,128)(2,1)S(1)}, bf16[128,64]{0,1:T(8,128)(2,1)S(1)}, u32[]{:S(2)}, u32[]{:S(2)}) %collective-permute-start.5) | collective-permute-done | bytes 16416 | tf_op jit(solution)/shard_map/ppermute | solution.py:175
  59.9 0.1 collective-permute-start.7
  60.0 1.2 %collective-permute-done.7 = bf16[128,256]{0,1:T(8,128)(2,1)S(1)} collective-permute-done((bf16[128,256]{0,1:T(8,128)(2,1)S(1)}, bf16[128,256]{0,1:T(8,128)(2,1)S(1)}, u32[]{:S(2)}, u32[]{:S(2)}) %collective-permute-start.7) | collective-permute-done | bytes 65568 | tf_op jit(solution)/shard_map/ppermute | solution.py:72
  61.2 1.1 %collective-permute-start.8 = (bf16[256,256]{0,1:T(8,128)(2,1)S(1)}, bf16[256,256]{0,1:T(8,128)(2,1)S(1)}, u32[]{:S(2)}, u32[]{:S(2)}) collective-permute-start(bf16[256,256]{0,1:T(8,128)(2,1)S(1)} %pad_maximum_fusion.3), channel_id=1, source_target_pairs={{0,8},{4,12},{8,0},{12,4},{16,24},{20,28},{24,16},{28,20},{1,9},{5... | collective-permute-start | bytes 393224 | tf_op jit(solution)/shard_map/ppermute | solution.py:76
  62.3 0.6 collective-permute-start.9
  62.8 1.9 %collective-permute-start.10 = (bf16[256,256]{0,1:T(8,128)(2,1)S(1)}, bf16[256,256]{0,1:T(8,128)(2,1)S(1)}, u32[]{:S(2)}, u32[]{:S(2)}) collective-permute-start(bf16[256,256]{0,1:T(8,128)(2,1)S(1)} %pad_maximum_fusion.3), channel_id=1, source_target_pairs={{0,24},{4,28},{8,16},{12,20},{16,8},{20,12},{24,0},{28,4},{1,25},{... | collective-permute-start | bytes 393224 | tf_op jit(solution)/shard_map/ppermute | solution.py:76
  64.8 2.9 %collective-permute-done.8 = bf16[256,256]{0,1:T(8,128)(2,1)S(1)} collective-permute-done((bf16[256,256]{0,1:T(8,128)(2,1)S(1)}, bf16[256,256]{0,1:T(8,128)(2,1)S(1)}, u32[]{:S(2)}, u32[]{:S(2)}) %collective-permute-start.8) | collective-permute-done | bytes 131104 | tf_op jit(solution)/shard_map/ppermute | solution.py:76
  67.7 2.7 %collective-permute-done.9 = bf16[256,256]{0,1:T(8,128)(2,1)S(1)} collective-permute-done((bf16[256,256]{0,1:T(8,128)(2,1)S(1)}, bf16[256,256]{0,1:T(8,128)(2,1)S(1)}, u32[]{:S(2)}, u32[]{:S(2)}) %collective-permute-start.9) | collective-permute-done | bytes 131104 | tf_op jit(solution)/shard_map/ppermute | solution.py:76
  70.4 0.0 all-gather.2.cloned.1.call-done
  70.4 3.5 %convolution_convert_fusion = bf16[128,256]{1,0:T(8,128)(2,1)S(1)} fusion(bf16[128,8192]{1,0:T(8,128)(2,1)} %fusion.2, bf16[8192,256]{1,0:T(8,128)(2,1)} %all-gather.2.cloned.1.call-done), kind=kOutput, calls=%fused_computation.10 | convolution fusion | flops 536903680 | bytes 6356992 | tf_op jit(solution)/shard_map/dot_general | solution.py:199
  74.0 0.1 fusion.61
  74.1 0.3 fusion.67
  74.4 0.3 fusion.66
  74.8 0.4 fusion.14
  75.2 0.4 fusion.6
  75.5 0.4 fusion.7
  75.9 0.7 copy.24
  (64 shorter events, 0.5 us)
Async XLA Ops:
  7.2 16.3 %copy-start = (bf16[1024,1152]{1,0:T(8,128)(2,1)S(1)}, bf16[1024,1152]{1,0:T(8,128)(2,1)}, u32[]{:S(2)}) copy-start(bf16[1024,1152]{1,0:T(8,128)(2,1)} %param.15) | copy-start | bytes 7077892
  7.2 3.4 %copy-start.4 = (bf16[8192]{0:T(1024)(128)(2,1)S(1)}, bf16[8192]{0:T(1024)(128)(2,1)}, u32[]{:S(2)}) copy-start(bf16[8192]{0:T(1024)(128)(2,1)} %param.10) | copy-start | bytes 49156
  7.2 8.2 %copy-start.3 = (bf16[1024,128]{1,0:T(8,128)(2,1)S(1)}, bf16[1024,128]{1,0:T(8,128)(2,1)}, u32[]{:S(2)}) copy-start(bf16[1024,128]{1,0:T(8,128)(2,1)} %param.13) | copy-start | bytes 786436
  7.2 63.2 %all-gather.2.cloned.1.call-start = ((), (), s32[]{:S(2)}) async-start(), calls=%async_computation | async-start | bytes 4718592 | tf_op jit(solution)/shard_map/all_gather | solution.py:197
  10.8 10.5 %collective-permute-start.11 = (bf16[8,2048]{1,0:T(8,128)(2,1)S(1)}, bf16[8,2048]{1,0:T(8,128)(2,1)S(1)}, u32[]{:S(2)}, u32[]{:S(2)}) collective-permute-start(bf16[8,2048]{1,0:T(8,128)(2,1)S(1)} %get-tuple-element.12), channel_id=1, source_target_pairs={{0,8},{4,12},{8,0},{12,4},{16,24},{20,28},{24,16},{28,20},{1,9},{5... | collective-permute-start | bytes 98312 | tf_op jit(solution)/shard_map/ppermute | solution.py:37
  13.8 7.4 %collective-permute-start.12 = (bf16[8,2048]{1,0:T(8,128)(2,1)S(1)}, bf16[8,2048]{1,0:T(8,128)(2,1)S(1)}, u32[]{:S(2)}, u32[]{:S(2)}) collective-permute-start(bf16[8,2048]{1,0:T(8,128)(2,1)S(1)} %get-tuple-element.14), channel_id=1, source_target_pairs={{0,16},{4,20},{8,24},{12,28},{16,0},{20,4},{24,8},{28,12},{1,17},{... | collective-permute-start | bytes 98312 | tf_op jit(solution)/shard_map/ppermute | solution.py:37
  15.3 5.9 %collective-permute-start.13 = (bf16[8,2048]{1,0:T(8,128)(2,1)S(1)}, bf16[8,2048]{1,0:T(8,128)(2,1)}, u32[]{:S(2)}, u32[]{:S(2)}) collective-permute-start(bf16[8,2048]{1,0:T(8,128)(2,1)S(1)} %get-tuple-element.13), channel_id=1, source_target_pairs={{0,24},{4,28},{8,16},{12,20},{16,8},{20,12},{24,0},{28,4},{1,25},{... | collective-permute-start | bytes 98312 | tf_op jit(solution)/shard_map/ppermute | solution.py:37
  15.3 3.8 %copy-start.5 = (s32[8]{0:T(128)S(1)}, s32[8]{0:T(128)}, u32[]{:S(2)}) copy-start(s32[8]{0:T(128)} %param.17) | copy-start | bytes 100
  16.8 7.5 %collective-permute-start = (bf16[1024,64]{0,1:T(8,128)(2,1)S(1)}, bf16[1024,64]{0,1:T(8,128)(2,1)S(1)}, u32[]{:S(2)}, u32[]{:S(2)}) collective-permute-start(bf16[1024,64]{0,1:T(8,128)(2,1)S(1)} %pad_maximum_fusion.2), channel_id=1, source_target_pairs={{0,4},{4,0},{8,12},{12,8},{16,20},{20,16},{24,28},{28,24},{1,5},{5... | collective-permute-start | bytes 393224 | tf_op jit(solution)/shard_map/ppermute | solution.py:89
  16.9 2.3 %copy-start.1 = (bf16[128,8192]{1,0:T(8,128)(2,1)S(1)}, bf16[128,8192]{1,0:T(8,128)(2,1)}, u32[]{:S(2)}) copy-start(bf16[128,8192]{1,0:T(8,128)(2,1)} %param.9) | copy-start | bytes 6291460
  22.1 1.4 %collective-permute-start.14 = (f32[8,1024]{1,0:T(8,128)S(1)}, f32[8,1024]{1,0:T(8,128)S(1)}, u32[]{:S(2)}, u32[]{:S(2)}) collective-permute-start(f32[8,1024]{1,0:T(8,128)S(1)} %constant_dynamic-slice_fusion), channel_id=1, source_target_pairs={{0,4},{4,0},{8,12},{12,8},{16,20},{20,16},{24,28},{28,24},{1,5},{5... | collective-permute-start | bytes 98312 | tf_op jit(solution)/shard_map/ppermute | solution.py:42
  23.9 3.7 %collective-permute-start.15 = (f32[8,1152]{1,0:T(8,128)S(1)}, f32[8,1152]{1,0:T(8,128)S(1)}, u32[]{:S(2)}, u32[]{:S(2)}) collective-permute-start(f32[8,1152]{1,0:T(8,128)S(1)} %fusion.43), channel_id=1, source_target_pairs={{0,4},{4,0},{8,12},{12,8},{16,20},{20,16},{24,28},{28,24},{1,5},{5... | collective-permute-start | bytes 110600 | tf_op jit(solution)/shard_map/ppermute | solution.py:26
  24.3 11.9 %collective-permute-start.1 = (bf16[2048,64]{0,1:T(8,128)(2,1)S(1)}, bf16[2048,64]{0,1:T(8,128)(2,1)S(1)}, u32[]{:S(2)}, u32[]{:S(2)}) collective-permute-start(bf16[2048,64]{0,1:T(8,128)(2,1)S(1)} %pad_maximum_fusion.1), channel_id=1, source_target_pairs={{0,8},{4,20},{8,0},{12,28},{16,24},{20,4},{24,16},{28,12},{1,9},{5... | collective-permute-start | bytes 786440 | tf_op jit(solution)/shard_map/ppermute | solution.py:91
  27.6 9.4 %collective-permute-start.16 = (f32[8,1152]{1,0:T(8,128)S(1)}, f32[8,1152]{1,0:T(8,128)S(1)}, u32[]{:S(2)}, u32[]{:S(2)}) collective-permute-start(f32[8,1152]{1,0:T(8,128)S(1)} %add.284), channel_id=1, source_target_pairs={{0,8},{4,12},{8,0},{12,4},{16,24},{20,28},{24,16},{28,20},{1,9},{5... | collective-permute-start | bytes 110600 | tf_op jit(solution)/shard_map/ppermute | solution.py:27
  27.7 9.2 %collective-permute-start.17 = (f32[8,1152]{1,0:T(8,128)S(1)}, f32[8,1152]{1,0:T(8,128)S(1)}, u32[]{:S(2)}, u32[]{:S(2)}) collective-permute-start(f32[8,1152]{1,0:T(8,128)S(1)} %add.284), channel_id=1, source_target_pairs={{0,16},{4,20},{8,24},{12,28},{16,0},{20,4},{24,8},{28,12},{1,17},{... | collective-permute-start | bytes 110600 | tf_op jit(solution)/shard_map/ppermute | solution.py:27
  29.7 9.6 %collective-permute-start.18 = (f32[8,1152]{1,0:T(8,128)S(1)}, f32[8,1152]{1,0:T(8,128)S(1)}, u32[]{:S(2)}, u32[]{:S(2)}) collective-permute-start(f32[8,1152]{1,0:T(8,128)S(1)} %add.284), channel_id=1, source_target_pairs={{0,24},{4,28},{8,16},{12,20},{16,8},{20,12},{24,0},{28,4},{1,25},{... | collective-permute-start | bytes 110600 | tf_op jit(solution)/shard_map/ppermute | solution.py:27
  36.2 12.7 %copy-start.2 = (bf16[128,8192]{1,0:T(8,128)(2,1)S(1)}, bf16[128,8192]{1,0:T(8,128)(2,1)}, u32[]{:S(2)}) copy-start(bf16[128,8192]{1,0:T(8,128)(2,1)} %fusion.2) | copy-start | bytes 6291460
  36.2 12.5 %collective-permute-start.2 = (bf16[1024,64]{0,1:T(8,128)(2,1)S(1)}, bf16[1024,64]{0,1:T(8,128)(2,1)S(1)}, u32[]{:S(2)}, u32[]{:S(2)}) collective-permute-start(bf16[1024,64]{0,1:T(8,128)(2,1)S(1)} %slice.128), channel_id=1, source_target_pairs={{0,20},{4,8},{8,28},{12,0},{16,4},{20,24},{24,12},{28,16},{1,21},{... | collective-permute-start | bytes 393224 | tf_op jit(solution)/shard_map/ppermute | solution.py:92
  44.3 10.8 %collective-permute-start.19 = (f32[8,1024]{1,0:T(8,128)S(1)}, f32[8,1024]{1,0:T(8,128)S(1)}, u32[]{:S(2)}, u32[]{:S(2)}) collective-permute-start(f32[8,1024]{1,0:T(8,128)S(1)} %fusion.5), channel_id=1, source_target_pairs={{0,3},{1,2},{2,1},{3,0},{4,7},{5,6},{6,5},{7,4},{8,11},{9,10},{10,... | collective-permute-start | bytes 98312 | tf_op jit(solution)/shard_map/ppermute | solution.py:46
  47.9 8.0 %collective-permute-start.20 = (f32[8,1024]{1,0:T(8,128)S(1)}, f32[8,1024]{1,0:T(8,128)S(1)}, u32[]{:S(2)}, u32[]{:S(2)}) collective-permute-start(f32[8,1024]{1,0:T(8,128)S(1)} %fusion.5), channel_id=1, source_target_pairs={{0,2},{1,3},{2,0},{3,1},{4,6},{5,7},{6,4},{7,5},{8,10},{9,11},{10,... | collective-permute-start | bytes 98312 | tf_op jit(solution)/shard_map/ppermute | solution.py:46
  47.9 8.0 %collective-permute-start.21 = (f32[8,1024]{1,0:T(8,128)S(1)}, f32[8,1024]{1,0:T(8,128)S(1)}, u32[]{:S(2)}, u32[]{:S(2)}) collective-permute-start(f32[8,1024]{1,0:T(8,128)S(1)} %fusion.5), channel_id=1, source_target_pairs={{0,1},{1,0},{2,3},{3,2},{4,5},{5,4},{6,7},{7,6},{8,9},{9,8},{10,11... | collective-permute-start | bytes 98312 | tf_op jit(solution)/shard_map/ppermute | solution.py:46
  48.8 1.8 %collective-permute-start.3 = (bf16[3072,64]{0,1:T(8,128)(2,1)S(1)}, bf16[3072,64]{0,1:T(8,128)(2,1)S(1)}, u32[]{:S(2)}, u32[]{:S(2)}) collective-permute-start(bf16[3072,64]{0,1:T(8,128)(2,1)S(1)} %pad_maximum_fusion), channel_id=1, source_target_pairs={{0,4},{4,0},{8,12},{12,8},{16,20},{20,16},{24,28},{28,24},{1,5},{5... | collective-permute-start | bytes 1179656 | tf_op jit(solution)/shard_map/ppermute | solution.py:93
  51.4 5.6 %collective-permute-start.4 = (bf16[128,64]{0,1:T(8,128)(2,1)S(1)}, bf16[128,64]{0,1:T(8,128)(2,1)S(1)}, u32[]{:S(2)}, u32[]{:S(2)}) collective-permute-start(bf16[128,64]{0,1:T(8,128)(2,1)S(1)} %fusion.13), channel_id=1, source_target_pairs={{0,3},{1,2},{2,1},{3,0},{4,7},{5,6},{6,5},{7,4},{8,11},{9,10},{10,... | collective-permute-start | bytes 49160 | tf_op jit(solution)/shard_map/ppermute | solution.py:175
  55.1 4.6 %collective-permute-start.5 = (bf16[128,64]{0,1:T(8,128)(2,1)S(1)}, bf16[128,64]{0,1:T(8,128)(2,1)S(1)}, u32[]{:S(2)}, u32[]{:S(2)}) collective-permute-start(bf16[128,64]{0,1:T(8,128)(2,1)S(1)} %fusion.13), channel_id=1, source_target_pairs={{0,2},{1,3},{2,0},{3,1},{4,6},{5,7},{6,4},{7,5},{8,10},{9,11},{10,... | collective-permute-start | bytes 49160 | tf_op jit(solution)/shard_map/ppermute | solution.py:175
  55.1 4.6 %collective-permute-start.6 = (bf16[128,64]{0,1:T(8,128)(2,1)S(1)}, bf16[128,64]{0,1:T(8,128)(2,1)S(1)}, u32[]{:S(2)}, u32[]{:S(2)}) collective-permute-start(bf16[128,64]{0,1:T(8,128)(2,1)S(1)} %fusion.13), channel_id=1, source_target_pairs={{0,1},{1,0},{2,3},{3,2},{4,5},{5,4},{6,7},{7,6},{8,9},{9,8},{10,11... | collective-permute-start | bytes 49160 | tf_op jit(solution)/shard_map/ppermute | solution.py:175
  59.9 1.3 %collective-permute-start.7 = (bf16[128,256]{0,1:T(8,128)(2,1)S(1)}, bf16[128,256]{0,1:T(8,128)(2,1)S(1)}, u32[]{:S(2)}, u32[]{:S(2)}) collective-permute-start(bf16[128,256]{0,1:T(8,128)(2,1)S(1)} %constant_dynamic-update-slice_fusion.1), channel_id=1, source_target_pairs={{0,4},{4,0},{8,12},{12,8},{16,20},{20,16},{24,28},{28,24},{1,5},{5... | collective-permute-start | bytes 196616 | tf_op jit(solution)/shard_map/ppermute | solution.py:72
  61.2 6.4 %collective-permute-start.8 = (bf16[256,256]{0,1:T(8,128)(2,1)S(1)}, bf16[256,256]{0,1:T(8,128)(2,1)S(1)}, u32[]{:S(2)}, u32[]{:S(2)}) collective-permute-start(bf16[256,256]{0,1:T(8,128)(2,1)S(1)} %pad_maximum_fusion.3), channel_id=1, source_target_pairs={{0,8},{4,12},{8,0},{12,4},{16,24},{20,28},{24,16},{28,20},{1,9},{5... | collective-permute-start | bytes 393224 | tf_op jit(solution)/shard_map/ppermute | solution.py:76
  62.3 8.1 %collective-permute-start.9 = (bf16[256,256]{0,1:T(8,128)(2,1)S(1)}, bf16[256,256]{0,1:T(8,128)(2,1)S(1)}, u32[]{:S(2)}, u32[]{:S(2)}) collective-permute-start(bf16[256,256]{0,1:T(8,128)(2,1)S(1)} %pad_maximum_fusion.3), channel_id=1, source_target_pairs={{0,16},{4,20},{8,24},{12,28},{16,0},{20,4},{24,8},{28,12},{1,17},{... | collective-permute-start | bytes 393224 | tf_op jit(solution)/shard_map/ppermute | solution.py:76
  62.8 7.6 %collective-permute-start.10 = (bf16[256,256]{0,1:T(8,128)(2,1)S(1)}, bf16[256,256]{0,1:T(8,128)(2,1)S(1)}, u32[]{:S(2)}, u32[]{:S(2)}) collective-permute-start(bf16[256,256]{0,1:T(8,128)(2,1)S(1)} %pad_maximum_fusion.3), channel_id=1, source_target_pairs={{0,24},{4,28},{8,16},{12,20},{16,8},{20,12},{24,0},{28,4},{1,25},{... | collective-permute-start | bytes 393224 | tf_op jit(solution)/shard_map/ppermute | solution.py:76
Sparse Core Ops, SparseCore 0:
  17.0 41.8 all-gather.1

commit v9 on v8

--- a/solution.py
+++ b/solution.py
@@ -131,23 +131,18 @@
     kv_head = tp_i * heads_here // GROUP
     kv_part = tp_i % sharers
     kv_start = kv_head * HEAD + kv_part * kv_width
-    kv_weights = jnp.concatenate(
-        [
-            lax.dynamic_slice_in_dim(w_key, kv_start, kv_width, 1),
-            lax.dynamic_slice_in_dim(w_value, kv_start, kv_width, 1),
-        ],
-        axis=1,
-    )
+    kv_weights = None
+    for start in range(0, w_key.shape[1], kv_width):
+        option = jnp.concatenate(
+            [w_key[:, start : start + kv_width], w_value[:, start : start + kv_width]], axis=1
+        )
+        kv_weights = option if kv_weights is None else jnp.where(kv_start == start, option, kv_weights)
 
     doc_ends = jnp.cumsum(doc_lengths) - 1
     first_row = seq_i * tokens_here
     query_pos = first_row + jnp.arange(tokens_here, dtype=jnp.int32)
     picker = (doc_ends[:, None] == query_pos[None, :]).astype(jnp.bfloat16)
-    picked = jnp.dot(picker, hidden, preferred_element_type=jnp.float32)
-    picked_square = jnp.mean(picked * picked, axis=-1, keepdims=True)
-    end_terms = (
-        picked * lax.rsqrt(picked_square + 1e-05) * norm_gain.astype(jnp.float32)
-    ).astype(jnp.bfloat16)
+    end_terms = jnp.dot(picker, normed, preferred_element_type=jnp.float32).astype(jnp.bfloat16)
     if n_seq == 8:
         end_rows = seq_reduce_scatter(end_terms).astype(jnp.bfloat16)
     else:

time: 83.9 us -> 89.4 us (1.066)
  local copies, waits for them, and re-layouts: 2.47 us -> 9.92 us
  starting transfers between devices: 24.5 us -> 23 us
  waiting for transfers between devices: 18.3 us -> 17.3 us
    unnamed x21 -> x27, local copies, waits for them, and re-layouts: 1.08 us -> 6.2 us
    slice x0 -> x2, local copies, waits for them, and re-layouts: none -> 3.51 us  [the longest x1 2.34 us: body(): w_value[:, start:start + kv_width]]
    ppermute x3, waiting for transfers between devices: 0.01 us -> 3.28 us  [seq_reduce_scatter(): lax.ppermute(part, 'seq', xor_perm(8, lambda j, m=m: j ^ m))]
    ppermute x1, waiting for transfers between devices: 3.88 us -> 1.21 us  [gather_forward(): lax.ppermute(pair, 'seq', xor_perm(8, lambda j: j ^ 2 if j % 2 == 0 else...]
    ppermute x3, waiting for transfers between devices: 2.37 us -> 0.66 us  [seq_all_reduce(): lax.ppermute(x, 'seq', xor_perm(8, lambda j, m=m: j ^ m))]
    convert_element_type x1, other arithmetic: 1.95 us -> 3.51 us  [rms_norm(): (widened * lax.rsqrt(mean_square + 1e-05) * norm_gain.astype(jnp.float32)...]
    dynamic_slice x1 -> x0, local copies, waits for them, and re-layouts: 1.17 us -> none  [body(): lax.dynamic_slice_in_dim(w_value, kv_start, kv_width, 1)]
    select_n x0 -> x1, other arithmetic: none -> 0.91 us  [body(): jnp.where(kv_start == start, option, kv_weights)]
  transfers between devices with their start and end apart: 23 -> 23, of which waited for: 9 -> 12; matrix products, arithmetic and copies ran while one was open for 20% -> 20% of each run, Pallas kernels for 0% -> 0%
where the time goes in v9:
time: 89.4 us; the launch traced here: 89 us
  starting transfers between devices  23 us (26%)
  waiting for transfers between devices  17.3 us (19%)
  matrix products  16 us (18%)
  between operations  14.7 us (16%)
  local copies, waits for them, and re-layouts  9.92 us (11%)
  other arithmetic  8.09 us (9%)
    unnamed x27, local copies, waits for them, and re-layouts  6.2 us
    ppermute x3, waiting for transfers between devices, gather_pieces(): got = lax.ppermute(pair, 'seq', xor_perm(8, lambda j, m=m: j ^ m))  5.1 us
    dot_general x1, matrix products, body(): jnp.einsum('dc,rce->dre', critic_hidden, critic_down, preferred_element_t...  5.04 us
    ppermute x3, starting transfers between devices, body(): lax.ppermute(kv_own, 'tp', xor_perm(n_tp, lambda j, k=k: j ^ k))  4.45 us
    ppermute x3, starting transfers between devices, group_sum(): lax.ppermute(x, axis, xor_perm(n, lambda j, k=k: j ^ k))  4.39 us
    ppermute x3, starting transfers between devices, seq_reduce_scatter(): lax.ppermute(part, 'seq', xor_perm(8, lambda j, m=m: j ^ m))  4.15 us
    dot_general x8, matrix products, project(): term = jnp.dot(cols, piece, preferred_element_type=jnp.float32)  3.59 us
    ppermute x3, starting transfers between devices, seq_all_reduce(): lax.ppermute(x, 'seq', xor_perm(8, lambda j, m=m: j ^ m))  3.55 us
  transfers between devices with their start and end apart: 23, of which 12 were waited for; matrix products, arithmetic and copies ran while one was open for 20% of the time, Pallas kernels for 0%

profile of v9, /device:TPU:0, one launch (start us, length us, event | category | flops | bytes accessed | tf_op | source)
XLA Modules:
  0.0 89.0 jit_solution(17718484828549283168)
XLA Ops:
  7.2 2.3 %fusion.61 = (bf16[1024,32]{1,0:T(8,128)(2,1)S(1)}, bf16[1024,32]{1,0:T(8,128)(2,1)S(1)}, bf16[1024,32]{1,0:T(8,128)(2,1)}, bf16[1024,32]{1,0:T(8,128)(2,1)S(1)}) fusion(bf16[1024,128]{1,0:T(8,128)(2,1)} %param.13), kind=kLoop, calls=%fused_computation.126 | loop fusion | bytes 524288 | tf_op jit(solution)/shard_map/slice | solution.py:137
  9.6 0.1 copy.39
  9.7 1.2 %fusion.60 = (bf16[1024,32]{1,0:T(8,128)(2,1)S(1)}, bf16[1024,32]{1,0:T(8,128)(2,1)}, bf16[1024,32]{1,0:T(8,128)(2,1)}, bf16[1024,32]{1,0:T(8,128)(2,1)}) fusion(bf16[1024,128]{1,0:T(8,128)(2,1)S(1)} %copy-done.2), kind=kLoop, calls=%fused_computation.125 | loop fusion | bytes 524288 | tf_op jit(solution)/shard_map/slice | solution.py:137
  10.9 1.1 %copy.38 = bf16[1024,32]{0,1:T(8,128)(2,1)S(1)} copy(bf16[1024,32]{1,0:T(8,128)(2,1)} %get-tuple-element.15) | data formatting | bytes 131072
  12.0 1.1 %copy.41 = bf16[1024,32]{0,1:T(8,128)(2,1)S(1)} copy(bf16[1024,32]{1,0:T(8,128)(2,1)} %get-tuple-element.18) | data formatting | bytes 131072
  13.0 1.1 %copy.40 = bf16[1024,32]{0,1:T(8,128)(2,1)S(1)} copy(bf16[1024,32]{1,0:T(8,128)(2,1)} %get-tuple-element.14) | data formatting | bytes 131072
  14.1 0.8 copy.43
  14.9 1.1 %copy.42 = bf16[1024,32]{0,1:T(8,128)(2,1)S(1)} copy(bf16[1024,32]{1,0:T(8,128)(2,1)} %get-tuple-element.13) | data formatting | bytes 131072
  15.9 0.1 copy.45
  16.0 0.1 copy.44
  16.2 0.9 %maximum_select_fusion = bf16[1024,64]{0,1:T(8,128)(2,1)S(1)} fusion(bf16[1024,32]{0,1:T(8,128)(2,1)S(1)} %copy.39, bf16[1024,32]{0,1:T(8,128)(2,1)S(1)} %copy.38, bf16[1024,32]{0,1:T(8,128)(2,1)S(1)} %copy.41, bf16[1024,32]{0,1:T(8,128)(2,1)S(1)} %copy.40, bf16[1024,32]{0,1:T(8,128)(2,1)} %copy.43, bf16[1024,32]{0,1:T(8,128)(2,1)S(1)} %copy.42, ...), kind=kLoop, calls=%fused_computation.56 | loop fusion | flops 1245184 | bytes 655363 | tf_op jit(solution)/shard_map/jit(_where)/select_n | solution.py:139
  17.1 0.6 collective-permute-start
  17.8 2.1 %fusion = f32[128]{0:T(128)S(1)} fusion(bf16[128,8192]{1,0:T(8,128)(2,1)} %param.9), kind=kLoop, calls=%fused_computation.3 | loop fusion | flops 3145600 | bytes 2097664 | tf_op jit(solution)/shard_map/reduce_sum | solution.py:15
  19.9 0.2 reduce-window.7
  20.1 3.5 %fusion.2 = bf16[128,8192]{1,0:T(8,128)(2,1)} fusion(bf16[128,8192]{1,0:T(8,128)(2,1)} %param.9, f32[8192]{0:T(1024)S(1)} %convert_element_type.61, f32[128]{0:T(128)S(1)} %add_rsqrt_fusion), kind=kLoop, calls=%fused_computation.5 | loop fusion | flops 4194304 | bytes 4227584 | tf_op jit(solution)/shard_map/convert_element_type | solution.py:16
  23.8 2.0 %convolution_convert_fusion = bf16[8,8192]{1,0:T(8,128)(2,1)S(1)} fusion(bf16[128,8192]{1,0:T(8,128)(2,1)} %fusion.2, s32[128]{0:T(128)S(1)} %get-tuple-element.56, s32[8]{0:T(128)S(1)} %add_bitcast_fusion), kind=kOutput, calls=%fused_computation | convolution fusion | flops 16843776 | bytes 2228768 | tf_op jit(solution)/shard_map/dot_general | solution.py:145
  25.8 3.5 %collective-permute-start.13 = (bf16[8,2048]{1,0:T(8,128)(2,1)S(1)}, bf16[8,2048]{1,0:T(8,128)(2,1)S(1)}, u32[]{:S(2)}, u32[]{:S(2)}) collective-permute-start(bf16[8,2048]{1,0:T(8,128)(2,1)S(1)} %get-tuple-element.21), channel_id=1, source_target_pairs={{0,24},{4,28},{8,16},{12,20},{16,8},{20,12},{24,0},{28,4},{1,25},{... | collective-permute-start | bytes 98312 | tf_op jit(solution)/shard_map/ppermute | solution.py:37
  29.3 0.5 collective-permute-start.12
  29.8 0.1 collective-permute-start.11
  30.0 1.2 %fusion.36 = f32[128,64]{0,1:T(8,128)S(1)} fusion(bf16[1024,64]{0,1:T(8,128)(2,1)S(1)} %maximum_select_fusion, bf16[128,8192]{1,0:T(8,128)(2,1)} %fusion.2, s32[]{:T(128)S(6)} %select_n.261), kind=kOutput, calls=%fused_computation.50 | convolution fusion | flops 16777216 | bytes 425988 | tf_op jit(solution)/shard_map/dot_general | solution.py:113
  31.2 0.6 collective-permute-done.13
  31.8 2.2 %collective-permute-done.12 = bf16[8,2048]{1,0:T(8,128)(2,1)S(1)} collective-permute-done((bf16[8,2048]{1,0:T(8,128)(2,1)S(1)}, bf16[8,2048]{1,0:T(8,128)(2,1)S(1)}, u32[]{:S(2)}, u32[]{:S(2)}) %collective-permute-start.12) | collective-permute-done | bytes 32800 | tf_op jit(solution)/shard_map/ppermute | solution.py:37
  34.0 0.4 collective-permute-done.11
  34.7 1.1 %collective-permute-done.14 = f32[8,1024]{1,0:T(8,128)S(1)} collective-permute-done((f32[8,1024]{1,0:T(8,128)S(1)}, f32[8,1024]{1,0:T(8,128)S(1)}, u32[]{:S(2)}, u32[]{:S(2)}) %collective-permute-start.14) | collective-permute-done | bytes 32800 | tf_op jit(solution)/shard_map/ppermute | solution.py:42
  35.8 0.4 fusion.43
  36.2 0.2 collective-permute-start.15
  36.4 1.2 %collective-permute-start.1 = (bf16[2048,64]{0,1:T(8,128)(2,1)S(1)}, bf16[2048,64]{0,1:T(8,128)(2,1)S(1)}, u32[]{:S(2)}, u32[]{:S(2)}) collective-permute-start(bf16[2048,64]{0,1:T(8,128)(2,1)S(1)} %pad_maximum_fusion.1), channel_id=1, source_target_pairs={{0,8},{4,20},{8,0},{12,28},{16,24},{20,4},{24,16},{28,12},{1,9},{5... | collective-permute-start | bytes 786440 | tf_op jit(solution)/shard_map/ppermute | solution.py:91
  37.6 0.1 convert_reduce_fusion.1
  37.7 2.0 %collective-permute-start.18 = (f32[8,1152]{1,0:T(8,128)S(1)}, f32[8,1152]{1,0:T(8,128)S(1)}, u32[]{:S(2)}, u32[]{:S(2)}) collective-permute-start(f32[8,1152]{1,0:T(8,128)S(1)} %add.270), channel_id=1, source_target_pairs={{0,24},{4,28},{8,16},{12,20},{16,8},{20,12},{24,0},{28,4},{1,25},{... | collective-permute-start | bytes 110600 | tf_op jit(solution)/shard_map/ppermute | solution.py:27
  39.7 0.5 collective-permute-start.17
  40.1 1.1 %collective-permute-start.16 = (f32[8,1152]{1,0:T(8,128)S(1)}, f32[8,1152]{1,0:T(8,128)S(1)}, u32[]{:S(2)}, u32[]{:S(2)}) collective-permute-start(f32[8,1152]{1,0:T(8,128)S(1)} %add.270), channel_id=1, source_target_pairs={{0,8},{4,12},{8,0},{12,4},{16,24},{20,28},{24,16},{28,20},{1,9},{5... | collective-permute-start | bytes 110600 | tf_op jit(solution)/shard_map/ppermute | solution.py:27
  41.2 1.2 %convolution_add_fusion.1 = f32[128,64]{0,1:T(8,128)S(1)} fusion(f32[128,64]{0,1:T(8,128)S(1)} %fusion.36, bf16[1024,64]{0,1:T(8,128)(2,1)S(1)} %collective-permute-done, bf16[128,8192]{1,0:T(8,128)(2,1)} %fusion.2, s32[]{:T(128)S(6)} %select_n.269), kind=kOutput, calls=%fused_computation.23 | convolution fusion | flops 16785408 | bytes 458756 | tf_op jit(solution)/shard_map/dot_general | solution.py:113
  42.4 1.2 %collective-permute-done.1 = bf16[2048,64]{0,1:T(8,128)(2,1)S(1)} collective-permute-done((bf16[2048,64]{0,1:T(8,128)(2,1)S(1)}, bf16[2048,64]{0,1:T(8,128)(2,1)S(1)}, u32[]{:S(2)}, u32[]{:S(2)}) %collective-permute-start.1) | collective-permute-done | bytes 262176 | tf_op jit(solution)/shard_map/ppermute | solution.py:91
  43.6 0.7 collective-permute-start.2
  44.3 0.7 collective-permute-done.18
  45.0 5.0 %fusion.5 = f32[8,1024]{1,0:T(8,128)S(1)} fusion(bf16[4,1152,1024]{2,1,0:T(8,128)(2,1)} %param.16, pred[8,4]{0,1:T(4,128)(4,1)S(1)} %iota_compare_fusion, f32[8,1152]{1,0:T(8,128)S(1)} %collective-permute-done.18, f32[8,1152]{1,0:T(8,128)S(1)} %collective-permute-done.17, f32[8,1152]{1,0:T(8,128)S(1)} %add.270, f32[8,1152]{1,0:T(8,128)S(1)} %collective-permute-done.16), kind=kOutput, calls=%fused_computation.12 | convolution fusion | flops 75628544 | bytes 9617440 | tf_op jit(solution)/shard_map/dc,rce->dre/dot_general | solution.py:156
  50.0 3.6 %collective-permute-start.19 = (f32[8,1024]{1,0:T(8,128)S(1)}, f32[8,1024]{1,0:T(8,128)S(1)}, u32[]{:S(2)}, u32[]{:S(2)}) collective-permute-start(f32[8,1024]{1,0:T(8,128)S(1)} %fusion.5), channel_id=1, source_target_pairs={{0,3},{1,2},{2,1},{3,0},{4,7},{5,6},{6,5},{7,4},{8,11},{9,10},{10,... | collective-permute-start | bytes 98312 | tf_op jit(solution)/shard_map/ppermute | solution.py:46
  53.6 0.8 collective-permute-start.21
  54.6 0.2 fusion.32
  54.8 0.2 fusion.30
  55.0 1.5 %collective-permute-done.3 = bf16[3072,64]{0,1:T(8,128)(2,1)S(1)} collective-permute-done((bf16[3072,64]{0,1:T(8,128)(2,1)S(1)}, bf16[3072,64]{0,1:T(8,128)(2,1)S(1)}, u32[]{:S(2)}, u32[]{:S(2)}) %collective-permute-start.3) | collective-permute-done | bytes 393248 | tf_op jit(solution)/shard_map/ppermute | solution.py:93
  56.5 0.2 fusion.24
  56.8 0.2 fusion.26
  57.0 0.2 fusion.28
  57.2 0.2 fusion.13
  57.4 3.6 %collective-permute-start.4 = (bf16[128,64]{0,1:T(8,128)(2,1)S(1)}, bf16[128,64]{0,1:T(8,128)(2,1)S(1)}, u32[]{:S(2)}, u32[]{:S(2)}) collective-permute-start(bf16[128,64]{0,1:T(8,128)(2,1)S(1)} %fusion.13), channel_id=1, source_target_pairs={{0,3},{1,2},{2,1},{3,0},{4,7},{5,6},{6,5},{7,4},{8,11},{9,10},{10,... | collective-permute-start | bytes 49160 | tf_op jit(solution)/shard_map/ppermute | solution.py:170
  61.0 0.9 collective-permute-start.6
  61.9 0.6 add_convert_fusion
  62.5 0.6 collective-permute-done.4
  63.2 2.5 %collective-permute-done.5 = bf16[128,64]{0,1:T(8,128)(2,1)S(1)} collective-permute-done((bf16[128,64]{0,1:T(8,128)(2,1)S(1)}, bf16[128,64]{0,1:T(8,128)(2,1)S(1)}, u32[]{:S(2)}, u32[]{:S(2)}) %collective-permute-start.5) | collective-permute-done | bytes 16416 | tf_op jit(solution)/shard_map/ppermute | solution.py:170
  65.9 1.2 %collective-permute-done.7 = bf16[128,256]{0,1:T(8,128)(2,1)S(1)} collective-permute-done((bf16[128,256]{0,1:T(8,128)(2,1)S(1)}, bf16[128,256]{0,1:T(8,128)(2,1)S(1)}, u32[]{:S(2)}, u32[]{:S(2)}) %collective-permute-start.7) | collective-permute-done | bytes 65568 | tf_op jit(solution)/shard_map/ppermute | solution.py:72
  67.1 0.4 collective-permute-start.8
  67.5 1.7 %collective-permute-start.9 = (bf16[256,256]{0,1:T(8,128)(2,1)S(1)}, bf16[256,256]{0,1:T(8,128)(2,1)S(1)}, u32[]{:S(2)}, u32[]{:S(2)}) collective-permute-start(bf16[256,256]{0,1:T(8,128)(2,1)S(1)} %pad_maximum_fusion.2), channel_id=1, source_target_pairs={{0,16},{4,20},{8,24},{12,28},{16,0},{20,4},{24,8},{28,12},{1,17},{... | collective-permute-start | bytes 393224 | tf_op jit(solution)/shard_map/ppermute | solution.py:76
  69.1 1.5 %collective-permute-start.10 = (bf16[256,256]{0,1:T(8,128)(2,1)S(1)}, bf16[256,256]{0,1:T(8,128)(2,1)S(1)}, u32[]{:S(2)}, u32[]{:S(2)}) collective-permute-start(bf16[256,256]{0,1:T(8,128)(2,1)S(1)} %pad_maximum_fusion.2), channel_id=1, source_target_pairs={{0,24},{4,28},{8,16},{12,20},{16,8},{20,12},{24,0},{28,4},{1,25},{... | collective-permute-start | bytes 393224 | tf_op jit(solution)/shard_map/ppermute | solution.py:76
  70.7 2.9 %collective-permute-done.8 = bf16[256,256]{0,1:T(8,128)(2,1)S(1)} collective-permute-done((bf16[256,256]{0,1:T(8,128)(2,1)S(1)}, bf16[256,256]{0,1:T(8,128)(2,1)S(1)}, u32[]{:S(2)}, u32[]{:S(2)}) %collective-permute-start.8) | collective-permute-done | bytes 131104 | tf_op jit(solution)/shard_map/ppermute | solution.py:76
  73.6 2.2 %collective-permute-done.10 = bf16[256,256]{0,1:T(8,128)(2,1)S(1)} collective-permute-done((bf16[256,256]{0,1:T(8,128)(2,1)S(1)}, bf16[256,256]{0,1:T(8,128)(2,1)S(1)}, u32[]{:S(2)}, u32[]{:S(2)}) %collective-permute-start.10) | collective-permute-done | bytes 131104 | tf_op jit(solution)/shard_map/ppermute | solution.py:76
  75.9 3.5 %convolution_convert_fusion.1 = bf16[128,256]{1,0:T(8,128)(2,1)S(1)} fusion(bf16[128,8192]{1,0:T(8,128)(2,1)} %fusion.2, bf16[8192,256]{1,0:T(8,128)(2,1)} %all-gather.2.cloned.1.call-done), kind=kOutput, calls=%fused_computation.11 | convolution fusion | flops 536903680 | bytes 6356992 | tf_op jit(solution)/shard_map/dot_general | solution.py:194
  79.5 0.1 fusion.62
  79.6 0.3 fusion.67
  79.9 0.3 fusion.68
  80.2 0.4 fusion.14
  80.6 0.4 fusion.7
  81.0 0.4 fusion.6
  81.4 0.7 copy.36
  (68 shorter events, 0.8 us)
Async XLA Ops:
  7.2 28.6 %copy-start = (bf16[1024,1152]{1,0:T(8,128)(2,1)S(1)}, bf16[1024,1152]{1,0:T(8,128)(2,1)}, u32[]{:S(2)}) copy-start(bf16[1024,1152]{1,0:T(8,128)(2,1)} %param.15) | copy-start | bytes 7077892
  7.2 2.5 %copy-start.2 = (bf16[1024,128]{1,0:T(8,128)(2,1)S(1)}, bf16[1024,128]{1,0:T(8,128)(2,1)}, u32[]{:S(2)}) copy-start(bf16[1024,128]{1,0:T(8,128)(2,1)} %param.12) | copy-start | bytes 786436
  7.2 68.7 %all-gather.2.cloned.1.call-start = ((), (), s32[]{:S(2)}) async-start(), calls=%async_computation | async-start | bytes 4718592 | tf_op jit(solution)/shard_map/all_gather | solution.py:192
  10.9 6.9 %copy-start.3 = (bf16[8192]{0:T(1024)(128)(2,1)S(1)}, bf16[8192]{0:T(1024)(128)(2,1)}, u32[]{:S(2)}) copy-start(bf16[8192]{0:T(1024)(128)(2,1)} %param.10) | copy-start | bytes 49156
  15.9 4.0 %copy-start.4 = (s32[8]{0:T(128)S(1)}, s32[8]{0:T(128)}, u32[]{:S(2)}) copy-start(s32[8]{0:T(128)} %param.14) | copy-start | bytes 100
  17.1 19.2 %collective-permute-start = (bf16[1024,64]{0,1:T(8,128)(2,1)S(1)}, bf16[1024,64]{0,1:T(8,128)(2,1)S(1)}, u32[]{:S(2)}, u32[]{:S(2)}) collective-permute-start(bf16[1024,64]{0,1:T(8,128)(2,1)S(1)} %maximum_select_fusion), channel_id=1, source_target_pairs={{0,4},{4,0},{8,12},{12,8},{16,20},{20,16},{24,28},{28,24},{1,5},{5... | collective-permute-start | bytes 393224 | tf_op jit(solution)/shard_map/ppermute | solution.py:89
  23.6 7.5 %copy-start.5 = (s32[8]{0:T(128)S(1)}, s32[8]{0:T(128)}, u32[]{:S(2)}) copy-start(s32[8]{0:T(128)} %param.17) | copy-start | bytes 100
  25.8 6.0 %collective-permute-start.13 = (bf16[8,2048]{1,0:T(8,128)(2,1)S(1)}, bf16[8,2048]{1,0:T(8,128)(2,1)S(1)}, u32[]{:S(2)}, u32[]{:S(2)}) collective-permute-start(bf16[8,2048]{1,0:T(8,128)(2,1)S(1)} %get-tuple-element.21), channel_id=1, source_target_pairs={{0,24},{4,28},{8,16},{12,20},{16,8},{20,12},{24,0},{28,4},{1,25},{... | collective-permute-start | bytes 98312 | tf_op jit(solution)/shard_map/ppermute | solution.py:37
  29.3 4.7 %collective-permute-start.12 = (bf16[8,2048]{1,0:T(8,128)(2,1)S(1)}, bf16[8,2048]{1,0:T(8,128)(2,1)S(1)}, u32[]{:S(2)}, u32[]{:S(2)}) collective-permute-start(bf16[8,2048]{1,0:T(8,128)(2,1)S(1)} %get-tuple-element.22), channel_id=1, source_target_pairs={{0,16},{4,20},{8,24},{12,28},{16,0},{20,4},{24,8},{28,12},{1,17},{... | collective-permute-start | bytes 98312 | tf_op jit(solution)/shard_map/ppermute | solution.py:37
  29.8 4.6 %collective-permute-start.11 = (bf16[8,2048]{1,0:T(8,128)(2,1)S(1)}, bf16[8,2048]{1,0:T(8,128)(2,1)S(1)}, u32[]{:S(2)}, u32[]{:S(2)}) collective-permute-start(bf16[8,2048]{1,0:T(8,128)(2,1)S(1)} %get-tuple-element.20), channel_id=1, source_target_pairs={{0,8},{4,12},{8,0},{12,4},{16,24},{20,28},{24,16},{28,20},{1,9},{5... | collective-permute-start | bytes 98312 | tf_op jit(solution)/shard_map/ppermute | solution.py:37
  34.5 1.3 %collective-permute-start.14 = (f32[8,1024]{1,0:T(8,128)S(1)}, f32[8,1024]{1,0:T(8,128)S(1)}, u32[]{:S(2)}, u32[]{:S(2)}) collective-permute-start(f32[8,1024]{1,0:T(8,128)S(1)} %constant_dynamic-slice_fusion), channel_id=1, source_target_pairs={{0,4},{4,0},{8,12},{12,8},{16,20},{20,16},{24,28},{28,24},{1,5},{5... | collective-permute-start | bytes 98312 | tf_op jit(solution)/shard_map/ppermute | solution.py:42
  36.2 1.5 %collective-permute-start.15 = (f32[8,1152]{1,0:T(8,128)S(1)}, f32[8,1152]{1,0:T(8,128)S(1)}, u32[]{:S(2)}, u32[]{:S(2)}) collective-permute-start(f32[8,1152]{1,0:T(8,128)S(1)} %fusion.43), channel_id=1, source_target_pairs={{0,4},{4,0},{8,12},{12,8},{16,20},{20,16},{24,28},{28,24},{1,5},{5... | collective-permute-start | bytes 110600 | tf_op jit(solution)/shard_map/ppermute | solution.py:26
  36.4 7.2 %collective-permute-start.1 = (bf16[2048,64]{0,1:T(8,128)(2,1)S(1)}, bf16[2048,64]{0,1:T(8,128)(2,1)S(1)}, u32[]{:S(2)}, u32[]{:S(2)}) collective-permute-start(bf16[2048,64]{0,1:T(8,128)(2,1)S(1)} %pad_maximum_fusion.1), channel_id=1, source_target_pairs={{0,8},{4,20},{8,0},{12,28},{16,24},{20,4},{24,16},{28,12},{1,9},{5... | collective-permute-start | bytes 786440 | tf_op jit(solution)/shard_map/ppermute | solution.py:91
  37.7 7.3 %collective-permute-start.18 = (f32[8,1152]{1,0:T(8,128)S(1)}, f32[8,1152]{1,0:T(8,128)S(1)}, u32[]{:S(2)}, u32[]{:S(2)}) collective-permute-start(f32[8,1152]{1,0:T(8,128)S(1)} %add.270), channel_id=1, source_target_pairs={{0,24},{4,28},{8,16},{12,20},{16,8},{20,12},{24,0},{28,4},{1,25},{... | collective-permute-start | bytes 110600 | tf_op jit(solution)/shard_map/ppermute | solution.py:27
  39.7 5.3 %collective-permute-start.17 = (f32[8,1152]{1,0:T(8,128)S(1)}, f32[8,1152]{1,0:T(8,128)S(1)}, u32[]{:S(2)}, u32[]{:S(2)}) collective-permute-start(f32[8,1152]{1,0:T(8,128)S(1)} %add.270), channel_id=1, source_target_pairs={{0,16},{4,20},{8,24},{12,28},{16,0},{20,4},{24,8},{28,12},{1,17},{... | collective-permute-start | bytes 110600 | tf_op jit(solution)/shard_map/ppermute | solution.py:27
  40.1 4.9 %collective-permute-start.16 = (f32[8,1152]{1,0:T(8,128)S(1)}, f32[8,1152]{1,0:T(8,128)S(1)}, u32[]{:S(2)}, u32[]{:S(2)}) collective-permute-start(f32[8,1152]{1,0:T(8,128)S(1)} %add.270), channel_id=1, source_target_pairs={{0,8},{4,12},{8,0},{12,4},{16,24},{20,28},{24,16},{28,20},{1,9},{5... | collective-permute-start | bytes 110600 | tf_op jit(solution)/shard_map/ppermute | solution.py:27
  43.6 10.9 %copy-start.1 = (bf16[128,8192]{1,0:T(8,128)(2,1)S(1)}, bf16[128,8192]{1,0:T(8,128)(2,1)}, u32[]{:S(2)}) copy-start(bf16[128,8192]{1,0:T(8,128)(2,1)} %fusion.2) | copy-start | bytes 6291460
  43.6 10.8 %collective-permute-start.2 = (bf16[1024,64]{0,1:T(8,128)(2,1)S(1)}, bf16[1024,64]{0,1:T(8,128)(2,1)S(1)}, u32[]{:S(2)}, u32[]{:S(2)}) collective-permute-start(bf16[1024,64]{0,1:T(8,128)(2,1)S(1)} %slice.160), channel_id=1, source_target_pairs={{0,20},{4,8},{8,28},{12,0},{16,4},{20,24},{24,12},{28,16},{1,21},{... | collective-permute-start | bytes 393224 | tf_op jit(solution)/shard_map/ppermute | solution.py:92
  50.0 11.0 %collective-permute-start.19 = (f32[8,1024]{1,0:T(8,128)S(1)}, f32[8,1024]{1,0:T(8,128)S(1)}, u32[]{:S(2)}, u32[]{:S(2)}) collective-permute-start(f32[8,1024]{1,0:T(8,128)S(1)} %fusion.5), channel_id=1, source_target_pairs={{0,3},{1,2},{2,1},{3,0},{4,7},{5,6},{6,5},{7,4},{8,11},{9,10},{10,... | collective-permute-start | bytes 98312 | tf_op jit(solution)/shard_map/ppermute | solution.py:46
  53.6 8.2 %collective-permute-start.20 = (f32[8,1024]{1,0:T(8,128)S(1)}, f32[8,1024]{1,0:T(8,128)S(1)}, u32[]{:S(2)}, u32[]{:S(2)}) collective-permute-start(f32[8,1024]{1,0:T(8,128)S(1)} %fusion.5), channel_id=1, source_target_pairs={{0,2},{1,3},{2,0},{3,1},{4,6},{5,7},{6,4},{7,5},{8,10},{9,11},{10,... | collective-permute-start | bytes 98312 | tf_op jit(solution)/shard_map/ppermute | solution.py:46
  53.6 8.2 %collective-permute-start.21 = (f32[8,1024]{1,0:T(8,128)S(1)}, f32[8,1024]{1,0:T(8,128)S(1)}, u32[]{:S(2)}, u32[]{:S(2)}) collective-permute-start(f32[8,1024]{1,0:T(8,128)S(1)} %fusion.5), channel_id=1, source_target_pairs={{0,1},{1,0},{2,3},{3,2},{4,5},{5,4},{6,7},{7,6},{8,9},{9,8},{10,11... | collective-permute-start | bytes 98312 | tf_op jit(solution)/shard_map/ppermute | solution.py:46
  54.5 2.1 %collective-permute-start.3 = (bf16[3072,64]{0,1:T(8,128)(2,1)S(1)}, bf16[3072,64]{0,1:T(8,128)(2,1)S(1)}, u32[]{:S(2)}, u32[]{:S(2)}) collective-permute-start(bf16[3072,64]{0,1:T(8,128)(2,1)S(1)} %pad_maximum_fusion), channel_id=1, source_target_pairs={{0,4},{4,0},{8,12},{12,8},{16,20},{20,16},{24,28},{28,24},{1,5},{5... | collective-permute-start | bytes 1179656 | tf_op jit(solution)/shard_map/ppermute | solution.py:93
  57.4 5.7 %collective-permute-start.4 = (bf16[128,64]{0,1:T(8,128)(2,1)S(1)}, bf16[128,64]{0,1:T(8,128)(2,1)S(1)}, u32[]{:S(2)}, u32[]{:S(2)}) collective-permute-start(bf16[128,64]{0,1:T(8,128)(2,1)S(1)} %fusion.13), channel_id=1, source_target_pairs={{0,3},{1,2},{2,1},{3,0},{4,7},{5,6},{6,5},{7,4},{8,11},{9,10},{10,... | collective-permute-start | bytes 49160 | tf_op jit(solution)/shard_map/ppermute | solution.py:170
  61.0 4.6 %collective-permute-start.5 = (bf16[128,64]{0,1:T(8,128)(2,1)S(1)}, bf16[128,64]{0,1:T(8,128)(2,1)S(1)}, u32[]{:S(2)}, u32[]{:S(2)}) collective-permute-start(bf16[128,64]{0,1:T(8,128)(2,1)S(1)} %fusion.13), channel_id=1, source_target_pairs={{0,2},{1,3},{2,0},{3,1},{4,6},{5,7},{6,4},{7,5},{8,10},{9,11},{10,... | collective-permute-start | bytes 49160 | tf_op jit(solution)/shard_map/ppermute | solution.py:170
  61.0 4.6 %collective-permute-start.6 = (bf16[128,64]{0,1:T(8,128)(2,1)S(1)}, bf16[128,64]{0,1:T(8,128)(2,1)S(1)}, u32[]{:S(2)}, u32[]{:S(2)}) collective-permute-start(bf16[128,64]{0,1:T(8,128)(2,1)S(1)} %fusion.13), channel_id=1, source_target_pairs={{0,1},{1,0},{2,3},{3,2},{4,5},{5,4},{6,7},{7,6},{8,9},{9,8},{10,11... | collective-permute-start | bytes 49160 | tf_op jit(solution)/shard_map/ppermute | solution.py:170
  65.8 1.3 %collective-permute-start.7 = (bf16[128,256]{0,1:T(8,128)(2,1)S(1)}, bf16[128,256]{0,1:T(8,128)(2,1)S(1)}, u32[]{:S(2)}, u32[]{:S(2)}) collective-permute-start(bf16[128,256]{0,1:T(8,128)(2,1)S(1)} %constant_dynamic-update-slice_fusion.1), channel_id=1, source_target_pairs={{0,4},{4,0},{8,12},{12,8},{16,20},{20,16},{24,28},{28,24},{1,5},{5... | collective-permute-start | bytes 196616 | tf_op jit(solution)/shard_map/ppermute | solution.py:72
  67.1 6.4 %collective-permute-start.8 = (bf16[256,256]{0,1:T(8,128)(2,1)S(1)}, bf16[256,256]{0,1:T(8,128)(2,1)S(1)}, u32[]{:S(2)}, u32[]{:S(2)}) collective-permute-start(bf16[256,256]{0,1:T(8,128)(2,1)S(1)} %pad_maximum_fusion.2), channel_id=1, source_target_pairs={{0,8},{4,12},{8,0},{12,4},{16,24},{20,28},{24,16},{28,20},{1,9},{5... | collective-permute-start | bytes 393224 | tf_op jit(solution)/shard_map/ppermute | solution.py:76
  67.5 6.1 %collective-permute-start.9 = (bf16[256,256]{0,1:T(8,128)(2,1)S(1)}, bf16[256,256]{0,1:T(8,128)(2,1)S(1)}, u32[]{:S(2)}, u32[]{:S(2)}) collective-permute-start(bf16[256,256]{0,1:T(8,128)(2,1)S(1)} %pad_maximum_fusion.2), channel_id=1, source_target_pairs={{0,16},{4,20},{8,24},{12,28},{16,0},{20,4},{24,8},{28,12},{1,17},{... | collective-permute-start | bytes 393224 | tf_op jit(solution)/shard_map/ppermute | solution.py:76
  69.1 6.7 %collective-permute-start.10 = (bf16[256,256]{0,1:T(8,128)(2,1)S(1)}, bf16[256,256]{0,1:T(8,128)(2,1)S(1)}, u32[]{:S(2)}, u32[]{:S(2)}) collective-permute-start(bf16[256,256]{0,1:T(8,128)(2,1)S(1)} %pad_maximum_fusion.2), channel_id=1, source_target_pairs={{0,24},{4,28},{8,16},{12,20},{16,8},{20,12},{24,0},{28,4},{1,25},{... | collective-permute-start | bytes 393224 | tf_op jit(solution)/shard_map/ppermute | solution.py:76
Sparse Core Ops, SparseCore 0:
  17.8 41.7 all-gather.1

commit v10 on v8

--- a/solution.py
+++ b/solution.py
@@ -143,11 +143,7 @@
     first_row = seq_i * tokens_here
     query_pos = first_row + jnp.arange(tokens_here, dtype=jnp.int32)
     picker = (doc_ends[:, None] == query_pos[None, :]).astype(jnp.bfloat16)
-    picked = jnp.dot(picker, hidden, preferred_element_type=jnp.float32)
-    picked_square = jnp.mean(picked * picked, axis=-1, keepdims=True)
-    end_terms = (
-        picked * lax.rsqrt(picked_square + 1e-05) * norm_gain.astype(jnp.float32)
-    ).astype(jnp.bfloat16)
+    end_terms = jnp.dot(picker, normed, preferred_element_type=jnp.float32).astype(jnp.bfloat16)
     if n_seq == 8:
         end_rows = seq_reduce_scatter(end_terms).astype(jnp.bfloat16)
     else:

time: 83.9 us -> 81.9 us (0.976)
  starting transfers between devices: 24.5 us -> 22.8 us
    ppermute x3, waiting for transfers between devices: 0.01 us -> 4.35 us  [seq_reduce_scatter(): lax.ppermute(part, 'seq', xor_perm(8, lambda j, m=m: j ^ m))]
    ppermute x1, waiting for transfers between devices: 3.88 us -> 0.01 us  [gather_forward(): lax.ppermute(pair, 'seq', xor_perm(8, lambda j: j ^ 2 if j % 2 == 0 else...]
    convert_element_type x1, other arithmetic: 1.95 us -> 3.53 us  [rms_norm(): (widened * lax.rsqrt(mean_square + 1e-05) * norm_gain.astype(jnp.float32)...]
    ppermute x3, waiting for transfers between devices: 2.37 us -> 1.21 us  [seq_all_reduce(): lax.ppermute(x, 'seq', xor_perm(8, lambda j, m=m: j ^ m))]
    ppermute x1, starting transfers between devices: 2.01 us -> 1.11 us  [gather_forward(): lax.ppermute(pair, 'seq', xor_perm(8, lambda j: j ^ 2 if j % 2 == 0 else...]
  transfers between devices with their start and end apart: 23 -> 23, of which waited for: 9 -> 13; matrix products, arithmetic and copies ran while one was open for 20% -> 22% of each run, Pallas kernels for 0% -> 0%
where the time goes in v10:
time: 81.9 us; the launch traced here: 81.6 us
  starting transfers between devices  22.8 us (28%)
  waiting for transfers between devices  18.2 us (22%)
  matrix products  16 us (20%)
  between operations  14.7 us (18%)
  other arithmetic  7.2 us (9%)
  local copies, waits for them, and re-layouts  2.68 us (3%)
    ppermute x3, waiting for transfers between devices, gather_pieces(): got = lax.ppermute(pair, 'seq', xor_perm(8, lambda j, m=m: j ^ m))  5.63 us
    dot_general x1, matrix products, body(): jnp.einsum('dc,rce->dre', critic_hidden, critic_down, preferred_element_t...  5.01 us
    ppermute x3, starting transfers between devices, body(): lax.ppermute(kv_own, 'tp', xor_perm(n_tp, lambda j, k=k: j ^ k))  4.52 us
    ppermute x3, starting transfers between devices, group_sum(): lax.ppermute(x, axis, xor_perm(n, lambda j, k=k: j ^ k))  4.39 us
    ppermute x3, waiting for transfers between devices, seq_reduce_scatter(): lax.ppermute(part, 'seq', xor_perm(8, lambda j, m=m: j ^ m))  4.35 us
    ppermute x3, starting transfers between devices, seq_reduce_scatter(): lax.ppermute(part, 'seq', xor_perm(8, lambda j, m=m: j ^ m))  4.15 us
    dot_general x8, matrix products, project(): term = jnp.dot(cols, piece, preferred_element_type=jnp.float32)  3.6 us
    ppermute x3, starting transfers between devices, seq_all_reduce(): lax.ppermute(x, 'seq', xor_perm(8, lambda j, m=m: j ^ m))  3.55 us
  transfers between devices with their start and end apart: 23, of which 13 were waited for; matrix products, arithmetic and copies ran while one was open for 22% of the time, Pallas kernels for 0%

profile of v10, /device:TPU:0, one launch (start us, length us, event | category | flops | bytes accessed | tf_op | source)
XLA Modules:
  0.0 81.6 jit_solution(7105959094809527394)
XLA Ops:
  7.2 0.0 all-gather.2.cloned.1.call-start
  7.3 1.4 %constant_dynamic-slice_fusion.4 = (bf16[1024,32]{1,0:T(8,128)(2,1)S(1)}, bf16[1024,32]{1,0:T(8,128)(2,1)S(1)}) fusion(bf16[1024,128]{1,0:T(8,128)(2,1)} %param.13, s32[]{:T(128)S(6)} %select_n.247, bf16[1024,128]{1,0:T(8,128)(2,1)} %param.12), kind=kLoop, calls=%fused_computation.111 | loop fusion | bytes 262148 | tf_op jit(solution)/shard_map/dynamic_slice | solution.py:137
  8.7 0.1 copy.27
  8.8 0.1 copy.26
  8.9 0.6 collective-permute-start
  9.5 0.0 all-gather.2.cloned.1.call-update
  9.6 2.1 %fusion = f32[128]{0:T(128)S(1)} fusion(bf16[128,8192]{1,0:T(8,128)(2,1)} %param.9), kind=kLoop, calls=%fused_computation.3 | loop fusion | flops 3145600 | bytes 2097664 | tf_op jit(solution)/shard_map/reduce_sum | solution.py:15
  11.8 0.2 reduce-window.7
  11.9 3.5 %fusion.2 = bf16[128,8192]{1,0:T(8,128)(2,1)} fusion(bf16[128,8192]{1,0:T(8,128)(2,1)} %param.9, f32[8192]{0:T(1024)S(1)} %convert_element_type.61, f32[128]{0:T(128)S(1)} %add_rsqrt_fusion), kind=kLoop, calls=%fused_computation.5 | loop fusion | flops 4194304 | bytes 4227584 | tf_op jit(solution)/shard_map/convert_element_type | solution.py:16
  15.6 2.0 %convolution_convert_fusion = bf16[8,8192]{1,0:T(8,128)(2,1)S(1)} fusion(bf16[128,8192]{1,0:T(8,128)(2,1)} %fusion.2, s32[128]{0:T(128)S(1)} %get-tuple-element.48, s32[8]{0:T(128)S(1)} %add_bitcast_fusion), kind=kOutput, calls=%fused_computation | convolution fusion | flops 16843776 | bytes 2228768 | tf_op jit(solution)/shard_map/dot_general | solution.py:146
  17.6 3.5 %collective-permute-start.13 = (bf16[8,2048]{1,0:T(8,128)(2,1)S(1)}, bf16[8,2048]{1,0:T(8,128)(2,1)S(1)}, u32[]{:S(2)}, u32[]{:S(2)}) collective-permute-start(bf16[8,2048]{1,0:T(8,128)(2,1)S(1)} %get-tuple-element.13), channel_id=1, source_target_pairs={{0,24},{4,28},{8,16},{12,20},{16,8},{20,12},{24,0},{28,4},{1,25},{... | collective-permute-start | bytes 98312 | tf_op jit(solution)/shard_map/ppermute | solution.py:37
  21.2 0.5 collective-permute-start.12
  21.7 0.1 collective-permute-start.11
  21.8 0.1 convert_reduce_fusion
  21.9 1.7 %collective-permute-done.13 = bf16[8,2048]{1,0:T(8,128)(2,1)S(1)} collective-permute-done((bf16[8,2048]{1,0:T(8,128)(2,1)S(1)}, bf16[8,2048]{1,0:T(8,128)(2,1)S(1)}, u32[]{:S(2)}, u32[]{:S(2)}) %collective-permute-start.13) | collective-permute-done | bytes 32800 | tf_op jit(solution)/shard_map/ppermute | solution.py:37
  23.6 2.2 %collective-permute-done.12 = bf16[8,2048]{1,0:T(8,128)(2,1)S(1)} collective-permute-done((bf16[8,2048]{1,0:T(8,128)(2,1)S(1)}, bf16[8,2048]{1,0:T(8,128)(2,1)S(1)}, u32[]{:S(2)}, u32[]{:S(2)}) %collective-permute-start.12) | collective-permute-done | bytes 32800 | tf_op jit(solution)/shard_map/ppermute | solution.py:37
  25.8 0.5 collective-permute-done.11
  26.3 0.1 collective-permute-start.14
  26.4 0.1 convert_reduce_fusion.1
  26.5 1.1 %collective-permute-done.14 = f32[8,1024]{1,0:T(8,128)S(1)} collective-permute-done((f32[8,1024]{1,0:T(8,128)S(1)}, f32[8,1024]{1,0:T(8,128)S(1)}, u32[]{:S(2)}, u32[]{:S(2)}) %collective-permute-start.14) | collective-permute-done | bytes 32800 | tf_op jit(solution)/shard_map/ppermute | solution.py:42
  27.6 0.4 fusion.43
  28.0 0.2 collective-permute-start.15
  28.2 1.1 %collective-permute-start.1 = (bf16[2048,64]{0,1:T(8,128)(2,1)S(1)}, bf16[2048,64]{0,1:T(8,128)(2,1)S(1)}, u32[]{:S(2)}, u32[]{:S(2)}) collective-permute-start(bf16[2048,64]{0,1:T(8,128)(2,1)S(1)} %pad_maximum_fusion.1), channel_id=1, source_target_pairs={{0,8},{4,20},{8,0},{12,28},{16,24},{20,4},{24,16},{28,12},{1,9},{5... | collective-permute-start | bytes 786440 | tf_op jit(solution)/shard_map/ppermute | solution.py:91
  29.3 1.2 %fusion.36 = f32[128,64]{0,1:T(8,128)S(1)} fusion(bf16[128,8192]{1,0:T(8,128)(2,1)} %fusion.2, s32[]{:T(128)S(6)} %select_n.245, bf16[1024,32]{0,1:T(8,128)(2,1)S(1)} %copy.27, bf16[1024,32]{0,1:T(8,128)(2,1)S(1)} %copy.26), kind=kOutput, calls=%fused_computation.50 | convolution fusion | flops 17039360 | bytes 425988 | tf_op jit(solution)/shard_map/dot_general | solution.py:113
  30.6 2.1 %collective-permute-start.18 = (f32[8,1152]{1,0:T(8,128)S(1)}, f32[8,1152]{1,0:T(8,128)S(1)}, u32[]{:S(2)}, u32[]{:S(2)}) collective-permute-start(f32[8,1152]{1,0:T(8,128)S(1)} %add.275), channel_id=1, source_target_pairs={{0,24},{4,28},{8,16},{12,20},{16,8},{20,12},{24,0},{28,4},{1,25},{... | collective-permute-start | bytes 110600 | tf_op jit(solution)/shard_map/ppermute | solution.py:27
  32.7 0.4 collective-permute-start.17
  33.1 1.0 %collective-permute-start.16 = (f32[8,1152]{1,0:T(8,128)S(1)}, f32[8,1152]{1,0:T(8,128)S(1)}, u32[]{:S(2)}, u32[]{:S(2)}) collective-permute-start(f32[8,1152]{1,0:T(8,128)S(1)} %add.275), channel_id=1, source_target_pairs={{0,8},{4,12},{8,0},{12,4},{16,24},{20,28},{24,16},{28,20},{1,9},{5... | collective-permute-start | bytes 110600 | tf_op jit(solution)/shard_map/ppermute | solution.py:27
  34.1 1.2 %convolution_add_fusion.1 = f32[128,64]{0,1:T(8,128)S(1)} fusion(f32[128,64]{0,1:T(8,128)S(1)} %fusion.36, bf16[1024,64]{0,1:T(8,128)(2,1)S(1)} %collective-permute-done, bf16[128,8192]{1,0:T(8,128)(2,1)} %fusion.2, s32[]{:T(128)S(6)} %select_n.248), kind=kOutput, calls=%fused_computation.23 | convolution fusion | flops 16785408 | bytes 458756 | tf_op jit(solution)/shard_map/dot_general | solution.py:113
  35.3 0.5 collective-permute-start.2
  35.9 1.2 %collective-permute-done.18 = f32[8,1152]{1,0:T(8,128)S(1)} collective-permute-done((f32[8,1152]{1,0:T(8,128)S(1)}, f32[8,1152]{1,0:T(8,128)S(1)}, u32[]{:S(2)}, u32[]{:S(2)}) %collective-permute-start.18) | collective-permute-done | bytes 36896 | tf_op jit(solution)/shard_map/ppermute | solution.py:27
  37.0 0.1 collective-permute-done.17
  37.1 5.0 %fusion.5 = f32[8,1024]{1,0:T(8,128)S(1)} fusion(bf16[4,1152,1024]{2,1,0:T(8,128)(2,1)} %param.16, pred[8,4]{0,1:T(4,128)(4,1)S(1)} %iota_compare_fusion, f32[8,1152]{1,0:T(8,128)S(1)} %collective-permute-done.18, f32[8,1152]{1,0:T(8,128)S(1)} %collective-permute-done.17, f32[8,1152]{1,0:T(8,128)S(1)} %add.275, f32[8,1152]{1,0:T(8,128)S(1)} %collective-permute-done.16), kind=kOutput, calls=%fused_computation.12 | convolution fusion | flops 75628544 | bytes 9617440 | tf_op jit(solution)/shard_map/dc,rce->dre/dot_general | solution.py:157
  42.1 3.6 %collective-permute-start.19 = (f32[8,1024]{1,0:T(8,128)S(1)}, f32[8,1024]{1,0:T(8,128)S(1)}, u32[]{:S(2)}, u32[]{:S(2)}) collective-permute-start(f32[8,1024]{1,0:T(8,128)S(1)} %fusion.5), channel_id=1, source_target_pairs={{0,3},{1,2},{2,1},{3,0},{4,7},{5,6},{6,5},{7,4},{8,11},{9,10},{10,... | collective-permute-start | bytes 98312 | tf_op jit(solution)/shard_map/ppermute | solution.py:46
  45.7 0.8 collective-permute-start.21
  46.5 0.1 collective-permute-start.3
  46.6 0.2 fusion.32
  46.8 0.2 fusion.30
  47.0 1.3 %collective-permute-done.3 = bf16[3072,64]{0,1:T(8,128)(2,1)S(1)} collective-permute-done((bf16[3072,64]{0,1:T(8,128)(2,1)S(1)}, bf16[3072,64]{0,1:T(8,128)(2,1)S(1)}, u32[]{:S(2)}, u32[]{:S(2)}) %collective-permute-start.3) | collective-permute-done | bytes 393248 | tf_op jit(solution)/shard_map/ppermute | solution.py:93
  48.4 0.2 fusion.24
  48.6 0.2 fusion.26
  48.8 0.2 fusion.28
  49.0 0.2 fusion.13
  49.3 3.9 %collective-permute-start.4 = (bf16[128,64]{0,1:T(8,128)(2,1)S(1)}, bf16[128,64]{0,1:T(8,128)(2,1)S(1)}, u32[]{:S(2)}, u32[]{:S(2)}) collective-permute-start(bf16[128,64]{0,1:T(8,128)(2,1)S(1)} %fusion.13), channel_id=1, source_target_pairs={{0,3},{1,2},{2,1},{3,0},{4,7},{5,6},{6,5},{7,4},{8,11},{9,10},{10,... | collective-permute-start | bytes 49160 | tf_op jit(solution)/shard_map/ppermute | solution.py:171
  53.1 0.6 collective-permute-start.6
  53.8 0.6 add_convert_fusion
  54.4 0.5 collective-permute-done.4
  55.0 2.8 %collective-permute-done.5 = bf16[128,64]{0,1:T(8,128)(2,1)S(1)} collective-permute-done((bf16[128,64]{0,1:T(8,128)(2,1)S(1)}, bf16[128,64]{0,1:T(8,128)(2,1)S(1)}, u32[]{:S(2)}, u32[]{:S(2)}) %collective-permute-start.5) | collective-permute-done | bytes 16416 | tf_op jit(solution)/shard_map/ppermute | solution.py:171
  57.9 0.1 collective-permute-start.7
  58.0 1.2 %collective-permute-done.7 = bf16[128,256]{0,1:T(8,128)(2,1)S(1)} collective-permute-done((bf16[128,256]{0,1:T(8,128)(2,1)S(1)}, bf16[128,256]{0,1:T(8,128)(2,1)S(1)}, u32[]{:S(2)}, u32[]{:S(2)}) %collective-permute-start.7) | collective-permute-done | bytes 65568 | tf_op jit(solution)/shard_map/ppermute | solution.py:72
  59.2 0.9 %collective-permute-start.8 = (bf16[256,256]{0,1:T(8,128)(2,1)S(1)}, bf16[256,256]{0,1:T(8,128)(2,1)S(1)}, u32[]{:S(2)}, u32[]{:S(2)}) collective-permute-start(bf16[256,256]{0,1:T(8,128)(2,1)S(1)} %pad_maximum_fusion.3), channel_id=1, source_target_pairs={{0,8},{4,12},{8,0},{12,4},{16,24},{20,28},{24,16},{28,20},{1,9},{5... | collective-permute-start | bytes 393224 | tf_op jit(solution)/shard_map/ppermute | solution.py:76
  60.2 1.3 %collective-permute-start.9 = (bf16[256,256]{0,1:T(8,128)(2,1)S(1)}, bf16[256,256]{0,1:T(8,128)(2,1)S(1)}, u32[]{:S(2)}, u32[]{:S(2)}) collective-permute-start(bf16[256,256]{0,1:T(8,128)(2,1)S(1)} %pad_maximum_fusion.3), channel_id=1, source_target_pairs={{0,16},{4,20},{8,24},{12,28},{16,0},{20,4},{24,8},{28,12},{1,17},{... | collective-permute-start | bytes 393224 | tf_op jit(solution)/shard_map/ppermute | solution.py:76
  61.4 1.4 %collective-permute-start.10 = (bf16[256,256]{0,1:T(8,128)(2,1)S(1)}, bf16[256,256]{0,1:T(8,128)(2,1)S(1)}, u32[]{:S(2)}, u32[]{:S(2)}) collective-permute-start(bf16[256,256]{0,1:T(8,128)(2,1)S(1)} %pad_maximum_fusion.3), channel_id=1, source_target_pairs={{0,24},{4,28},{8,16},{12,20},{16,8},{20,12},{24,0},{28,4},{1,25},{... | collective-permute-start | bytes 393224 | tf_op jit(solution)/shard_map/ppermute | solution.py:76
  62.8 2.9 %collective-permute-done.8 = bf16[256,256]{0,1:T(8,128)(2,1)S(1)} collective-permute-done((bf16[256,256]{0,1:T(8,128)(2,1)S(1)}, bf16[256,256]{0,1:T(8,128)(2,1)S(1)}, u32[]{:S(2)}, u32[]{:S(2)}) %collective-permute-start.8) | collective-permute-done | bytes 131104 | tf_op jit(solution)/shard_map/ppermute | solution.py:76
  65.7 1.4 %collective-permute-done.9 = bf16[256,256]{0,1:T(8,128)(2,1)S(1)} collective-permute-done((bf16[256,256]{0,1:T(8,128)(2,1)S(1)}, bf16[256,256]{0,1:T(8,128)(2,1)S(1)}, u32[]{:S(2)}, u32[]{:S(2)}) %collective-permute-start.9) | collective-permute-done | bytes 131104 | tf_op jit(solution)/shard_map/ppermute | solution.py:76
  67.1 1.4 %collective-permute-done.10 = bf16[256,256]{0,1:T(8,128)(2,1)S(1)} collective-permute-done((bf16[256,256]{0,1:T(8,128)(2,1)S(1)}, bf16[256,256]{0,1:T(8,128)(2,1)S(1)}, u32[]{:S(2)}, u32[]{:S(2)}) %collective-permute-start.10) | collective-permute-done | bytes 131104 | tf_op jit(solution)/shard_map/ppermute | solution.py:76
  68.5 0.0 all-gather.2.cloned.1.call-done
  68.5 3.5 %convolution_convert_fusion.1 = bf16[128,256]{1,0:T(8,128)(2,1)S(1)} fusion(bf16[128,8192]{1,0:T(8,128)(2,1)} %fusion.2, bf16[8192,256]{1,0:T(8,128)(2,1)} %all-gather.2.cloned.1.call-done), kind=kOutput, calls=%fused_computation.11 | convolution fusion | flops 536903680 | bytes 6356992 | tf_op jit(solution)/shard_map/dot_general | solution.py:195
  72.1 0.1 fusion.60
  72.2 0.3 fusion.65
  72.5 0.3 fusion.66
  72.8 0.4 fusion.14
  73.2 0.4 fusion.7
  73.6 0.4 fusion.6
  74.0 0.7 copy.24
  (60 shorter events, 0.5 us)
Async XLA Ops:
  7.2 20.4 %copy-start = (bf16[1024,1152]{1,0:T(8,128)(2,1)S(1)}, bf16[1024,1152]{1,0:T(8,128)(2,1)}, u32[]{:S(2)}) copy-start(bf16[1024,1152]{1,0:T(8,128)(2,1)} %param.15) | copy-start | bytes 7077892
  7.2 2.4 %copy-start.2 = (bf16[8192]{0:T(1024)(128)(2,1)S(1)}, bf16[8192]{0:T(1024)(128)(2,1)}, u32[]{:S(2)}) copy-start(bf16[8192]{0:T(1024)(128)(2,1)} %param.10) | copy-start | bytes 49156
  7.2 61.3 %all-gather.2.cloned.1.call-start = ((), (), s32[]{:S(2)}) async-start(), calls=%async_computation | async-start | bytes 4718592 | tf_op jit(solution)/shard_map/all_gather | solution.py:193
  8.7 3.1 %copy-start.3 = (s32[8]{0:T(128)S(1)}, s32[8]{0:T(128)}, u32[]{:S(2)}) copy-start(s32[8]{0:T(128)} %param.14) | copy-start | bytes 100
  8.9 19.2 %collective-permute-start = (bf16[1024,64]{0,1:T(8,128)(2,1)S(1)}, bf16[1024,64]{0,1:T(8,128)(2,1)S(1)}, u32[]{:S(2)}, u32[]{:S(2)}) collective-permute-start(bf16[1024,64]{0,1:T(8,128)(2,1)S(1)} %pad_maximum_fusion.2), channel_id=1, source_target_pairs={{0,4},{4,0},{8,12},{12,8},{16,20},{20,16},{24,28},{28,24},{1,5},{5... | collective-permute-start | bytes 393224 | tf_op jit(solution)/shard_map/ppermute | solution.py:89
  15.5 6.3 %copy-start.4 = (s32[8]{0:T(128)S(1)}, s32[8]{0:T(128)}, u32[]{:S(2)}) copy-start(s32[8]{0:T(128)} %param.17) | copy-start | bytes 100
  17.6 6.0 %collective-permute-start.13 = (bf16[8,2048]{1,0:T(8,128)(2,1)S(1)}, bf16[8,2048]{1,0:T(8,128)(2,1)S(1)}, u32[]{:S(2)}, u32[]{:S(2)}) collective-permute-start(bf16[8,2048]{1,0:T(8,128)(2,1)S(1)} %get-tuple-element.13), channel_id=1, source_target_pairs={{0,24},{4,28},{8,16},{12,20},{16,8},{20,12},{24,0},{28,4},{1,25},{... | collective-permute-start | bytes 98312 | tf_op jit(solution)/shard_map/ppermute | solution.py:37
  21.2 4.7 %collective-permute-start.12 = (bf16[8,2048]{1,0:T(8,128)(2,1)S(1)}, bf16[8,2048]{1,0:T(8,128)(2,1)S(1)}, u32[]{:S(2)}, u32[]{:S(2)}) collective-permute-start(bf16[8,2048]{1,0:T(8,128)(2,1)S(1)} %get-tuple-element.14), channel_id=1, source_target_pairs={{0,16},{4,20},{8,24},{12,28},{16,0},{20,4},{24,8},{28,12},{1,17},{... | collective-permute-start | bytes 98312 | tf_op jit(solution)/shard_map/ppermute | solution.py:37
  21.7 4.6 %collective-permute-start.11 = (bf16[8,2048]{1,0:T(8,128)(2,1)S(1)}, bf16[8,2048]{1,0:T(8,128)(2,1)S(1)}, u32[]{:S(2)}, u32[]{:S(2)}) collective-permute-start(bf16[8,2048]{1,0:T(8,128)(2,1)S(1)} %get-tuple-element.12), channel_id=1, source_target_pairs={{0,8},{4,12},{8,0},{12,4},{16,24},{20,28},{24,16},{28,20},{1,9},{5... | collective-permute-start | bytes 98312 | tf_op jit(solution)/shard_map/ppermute | solution.py:37
  26.3 1.3 %collective-permute-start.14 = (f32[8,1024]{1,0:T(8,128)S(1)}, f32[8,1024]{1,0:T(8,128)S(1)}, u32[]{:S(2)}, u32[]{:S(2)}) collective-permute-start(f32[8,1024]{1,0:T(8,128)S(1)} %constant_dynamic-slice_fusion), channel_id=1, source_target_pairs={{0,4},{4,0},{8,12},{12,8},{16,20},{20,16},{24,28},{28,24},{1,5},{5... | collective-permute-start | bytes 98312 | tf_op jit(solution)/shard_map/ppermute | solution.py:42
  28.0 2.6 %collective-permute-start.15 = (f32[8,1152]{1,0:T(8,128)S(1)}, f32[8,1152]{1,0:T(8,128)S(1)}, u32[]{:S(2)}, u32[]{:S(2)}) collective-permute-start(f32[8,1152]{1,0:T(8,128)S(1)} %fusion.43), channel_id=1, source_target_pairs={{0,4},{4,0},{8,12},{12,8},{16,20},{20,16},{24,28},{28,24},{1,5},{5... | collective-permute-start | bytes 110600 | tf_op jit(solution)/shard_map/ppermute | solution.py:26
  28.2 7.1 %collective-permute-start.1 = (bf16[2048,64]{0,1:T(8,128)(2,1)S(1)}, bf16[2048,64]{0,1:T(8,128)(2,1)S(1)}, u32[]{:S(2)}, u32[]{:S(2)}) collective-permute-start(bf16[2048,64]{0,1:T(8,128)(2,1)S(1)} %pad_maximum_fusion.1), channel_id=1, source_target_pairs={{0,8},{4,20},{8,0},{12,28},{16,24},{20,4},{24,16},{28,12},{1,9},{5... | collective-permute-start | bytes 786440 | tf_op jit(solution)/shard_map/ppermute | solution.py:91
  30.6 6.4 %collective-permute-start.18 = (f32[8,1152]{1,0:T(8,128)S(1)}, f32[8,1152]{1,0:T(8,128)S(1)}, u32[]{:S(2)}, u32[]{:S(2)}) collective-permute-start(f32[8,1152]{1,0:T(8,128)S(1)} %add.275), channel_id=1, source_target_pairs={{0,24},{4,28},{8,16},{12,20},{16,8},{20,12},{24,0},{28,4},{1,25},{... | collective-permute-start | bytes 110600 | tf_op jit(solution)/shard_map/ppermute | solution.py:27
  32.7 4.4 %collective-permute-start.17 = (f32[8,1152]{1,0:T(8,128)S(1)}, f32[8,1152]{1,0:T(8,128)S(1)}, u32[]{:S(2)}, u32[]{:S(2)}) collective-permute-start(f32[8,1152]{1,0:T(8,128)S(1)} %add.275), channel_id=1, source_target_pairs={{0,16},{4,20},{8,24},{12,28},{16,0},{20,4},{24,8},{28,12},{1,17},{... | collective-permute-start | bytes 110600 | tf_op jit(solution)/shard_map/ppermute | solution.py:27
  33.1 4.0 %collective-permute-start.16 = (f32[8,1152]{1,0:T(8,128)S(1)}, f32[8,1152]{1,0:T(8,128)S(1)}, u32[]{:S(2)}, u32[]{:S(2)}) collective-permute-start(f32[8,1152]{1,0:T(8,128)S(1)} %add.275), channel_id=1, source_target_pairs={{0,8},{4,12},{8,0},{12,4},{16,24},{20,28},{24,16},{28,20},{1,9},{5... | collective-permute-start | bytes 110600 | tf_op jit(solution)/shard_map/ppermute | solution.py:27
  35.3 11.3 %copy-start.1 = (bf16[128,8192]{1,0:T(8,128)(2,1)S(1)}, bf16[128,8192]{1,0:T(8,128)(2,1)}, u32[]{:S(2)}) copy-start(bf16[128,8192]{1,0:T(8,128)(2,1)} %fusion.2) | copy-start | bytes 6291460
  35.3 11.1 %collective-permute-start.2 = (bf16[1024,64]{0,1:T(8,128)(2,1)S(1)}, bf16[1024,64]{0,1:T(8,128)(2,1)S(1)}, u32[]{:S(2)}, u32[]{:S(2)}) collective-permute-start(bf16[1024,64]{0,1:T(8,128)(2,1)S(1)} %slice.128), channel_id=1, source_target_pairs={{0,20},{4,8},{8,28},{12,0},{16,4},{20,24},{24,12},{28,16},{1,21},{... | collective-permute-start | bytes 393224 | tf_op jit(solution)/shard_map/ppermute | solution.py:92
  42.1 11.1 %collective-permute-start.19 = (f32[8,1024]{1,0:T(8,128)S(1)}, f32[8,1024]{1,0:T(8,128)S(1)}, u32[]{:S(2)}, u32[]{:S(2)}) collective-permute-start(f32[8,1024]{1,0:T(8,128)S(1)} %fusion.5), channel_id=1, source_target_pairs={{0,3},{1,2},{2,1},{3,0},{4,7},{5,6},{6,5},{7,4},{8,11},{9,10},{10,... | collective-permute-start | bytes 98312 | tf_op jit(solution)/shard_map/ppermute | solution.py:46
  45.7 8.1 %collective-permute-start.20 = (f32[8,1024]{1,0:T(8,128)S(1)}, f32[8,1024]{1,0:T(8,128)S(1)}, u32[]{:S(2)}, u32[]{:S(2)}) collective-permute-start(f32[8,1024]{1,0:T(8,128)S(1)} %fusion.5), channel_id=1, source_target_pairs={{0,2},{1,3},{2,0},{3,1},{4,6},{5,7},{6,4},{7,5},{8,10},{9,11},{10,... | collective-permute-start | bytes 98312 | tf_op jit(solution)/shard_map/ppermute | solution.py:46
  45.7 8.1 %collective-permute-start.21 = (f32[8,1024]{1,0:T(8,128)S(1)}, f32[8,1024]{1,0:T(8,128)S(1)}, u32[]{:S(2)}, u32[]{:S(2)}) collective-permute-start(f32[8,1024]{1,0:T(8,128)S(1)} %fusion.5), channel_id=1, source_target_pairs={{0,1},{1,0},{2,3},{3,2},{4,5},{5,4},{6,7},{7,6},{8,9},{9,8},{10,11... | collective-permute-start | bytes 98312 | tf_op jit(solution)/shard_map/ppermute | solution.py:46
  46.5 1.8 %collective-permute-start.3 = (bf16[3072,64]{0,1:T(8,128)(2,1)S(1)}, bf16[3072,64]{0,1:T(8,128)(2,1)S(1)}, u32[]{:S(2)}, u32[]{:S(2)}) collective-permute-start(bf16[3072,64]{0,1:T(8,128)(2,1)S(1)} %pad_maximum_fusion), channel_id=1, source_target_pairs={{0,4},{4,0},{8,12},{12,8},{16,20},{20,16},{24,28},{28,24},{1,5},{5... | collective-permute-start | bytes 1179656 | tf_op jit(solution)/shard_map/ppermute | solution.py:93
  49.3 5.7 %collective-permute-start.4 = (bf16[128,64]{0,1:T(8,128)(2,1)S(1)}, bf16[128,64]{0,1:T(8,128)(2,1)S(1)}, u32[]{:S(2)}, u32[]{:S(2)}) collective-permute-start(bf16[128,64]{0,1:T(8,128)(2,1)S(1)} %fusion.13), channel_id=1, source_target_pairs={{0,3},{1,2},{2,1},{3,0},{4,7},{5,6},{6,5},{7,4},{8,11},{9,10},{10,... | collective-permute-start | bytes 49160 | tf_op jit(solution)/shard_map/ppermute | solution.py:171
  53.1 4.6 %collective-permute-start.5 = (bf16[128,64]{0,1:T(8,128)(2,1)S(1)}, bf16[128,64]{0,1:T(8,128)(2,1)S(1)}, u32[]{:S(2)}, u32[]{:S(2)}) collective-permute-start(bf16[128,64]{0,1:T(8,128)(2,1)S(1)} %fusion.13), channel_id=1, source_target_pairs={{0,2},{1,3},{2,0},{3,1},{4,6},{5,7},{6,4},{7,5},{8,10},{9,11},{10,... | collective-permute-start | bytes 49160 | tf_op jit(solution)/shard_map/ppermute | solution.py:171
  53.1 4.6 %collective-permute-start.6 = (bf16[128,64]{0,1:T(8,128)(2,1)S(1)}, bf16[128,64]{0,1:T(8,128)(2,1)S(1)}, u32[]{:S(2)}, u32[]{:S(2)}) collective-permute-start(bf16[128,64]{0,1:T(8,128)(2,1)S(1)} %fusion.13), channel_id=1, source_target_pairs={{0,1},{1,0},{2,3},{3,2},{4,5},{5,4},{6,7},{7,6},{8,9},{9,8},{10,11... | collective-permute-start | bytes 49160 | tf_op jit(solution)/shard_map/ppermute | solution.py:171
  57.9 1.3 %collective-permute-start.7 = (bf16[128,256]{0,1:T(8,128)(2,1)S(1)}, bf16[128,256]{0,1:T(8,128)(2,1)S(1)}, u32[]{:S(2)}, u32[]{:S(2)}) collective-permute-start(bf16[128,256]{0,1:T(8,128)(2,1)S(1)} %constant_dynamic-update-slice_fusion.1), channel_id=1, source_target_pairs={{0,4},{4,0},{8,12},{12,8},{16,20},{20,16},{24,28},{28,24},{1,5},{5... | collective-permute-start | bytes 196616 | tf_op jit(solution)/shard_map/ppermute | solution.py:72
  59.2 6.4 %collective-permute-start.8 = (bf16[256,256]{0,1:T(8,128)(2,1)S(1)}, bf16[256,256]{0,1:T(8,128)(2,1)S(1)}, u32[]{:S(2)}, u32[]{:S(2)}) collective-permute-start(bf16[256,256]{0,1:T(8,128)(2,1)S(1)} %pad_maximum_fusion.3), channel_id=1, source_target_pairs={{0,8},{4,12},{8,0},{12,4},{16,24},{20,28},{24,16},{28,20},{1,9},{5... | collective-permute-start | bytes 393224 | tf_op jit(solution)/shard_map/ppermute | solution.py:76
  60.2 6.9 %collective-permute-start.9 = (bf16[256,256]{0,1:T(8,128)(2,1)S(1)}, bf16[256,256]{0,1:T(8,128)(2,1)S(1)}, u32[]{:S(2)}, u32[]{:S(2)}) collective-permute-start(bf16[256,256]{0,1:T(8,128)(2,1)S(1)} %pad_maximum_fusion.3), channel_id=1, source_target_pairs={{0,16},{4,20},{8,24},{12,28},{16,0},{20,4},{24,8},{28,12},{1,17},{... | collective-permute-start | bytes 393224 | tf_op jit(solution)/shard_map/ppermute | solution.py:76
  61.4 7.1 %collective-permute-start.10 = (bf16[256,256]{0,1:T(8,128)(2,1)S(1)}, bf16[256,256]{0,1:T(8,128)(2,1)S(1)}, u32[]{:S(2)}, u32[]{:S(2)}) collective-permute-start(bf16[256,256]{0,1:T(8,128)(2,1)S(1)} %pad_maximum_fusion.3), channel_id=1, source_target_pairs={{0,24},{4,28},{8,16},{12,20},{16,8},{20,12},{24,0},{28,4},{1,25},{... | collective-permute-start | bytes 393224 | tf_op jit(solution)/shard_map/ppermute | solution.py:76
Sparse Core Ops, SparseCore 0:
  9.9 42.1 all-gather.1
